TPU v7x, 128 devices: a whole 4x4x4 slice. The times are simulated.
128 devices in a mesh: row: 32 (over x, z, y_hi), col: 4 (over y_lo, core).
Axes of the slice: x: 4, y: 4 (y_hi: 2, y_lo: 2; y = y_hi * 2 + y_lo), z: 4, core: 2. Of those that a mesh axis runs over, the one named last changes fastest.
Arguments:
- tokens: bfloat16 [256, 8192], P('row', 'col'), may hold values from -6 to 6
- gate_weight: bfloat16 [8192, 14336], P(None, ('row', 'col')), may hold values from -0.0625 to 0.0625
- up_weight: bfloat16 [8192, 14336], P(None, ('row', 'col')), may hold values from -0.0625 to 0.0625
- down_weight: bfloat16 [14336, 8192], P(('row', 'col')), may hold values from -0.1875 to 0.1875
- out_grad: bfloat16 [256, 8192], P('row', 'col'), may hold values from -1.796875 to 1.796875
Outputs:
- output: float32 [256, 8192], P('row', 'col')
- input_grad: float32 [256, 8192], P('row', 'col')
- grad_gate: bfloat16 [8192, 14336], P('col', 'row')
- grad_up: bfloat16 [8192, 14336], P('col', 'row')
- grad_down: bfloat16 [14336, 8192], P('row', 'col')
All inputs are finite; a program needn't handle non-finite values.
Results may differ from a plain program's by a relative error of at most 0.0049.
Values may be sent and summed in bfloat16 or wider, within the bound.
No kernel may reach another device: no remote copies, remote signals or barrier semaphores. Data moves between devices by JAX's collectives and lax.ppermute only.
A program may use at most 64 MiB of HBM per device.

v0:
```python
import jax
import jax.numpy as jnp
from jax import lax
from jax.sharding import PartitionSpec as P


def contract_last(left, right):
    return lax.dot_general(
        left, right, (((1,), (1,)), ((), ())), preferred_element_type=jnp.float32
    )


def contract_first(left, right):
    return lax.dot_general(
        left, right, (((0,), (0,)), ((), ())), preferred_element_type=jnp.float32
    )


def shards(tokens, gate_weight, up_weight, down_weight, out_grad):
    n_row = lax.axis_size("row")
    n_col = lax.axis_size("col")
    col_index = lax.axis_index("col")
    per_row = tokens.shape[0]
    feat_block = tokens.shape[1]
    gate_block, up_block = (
        lax.all_to_all(gate_weight, "col", split_axis=0, concat_axis=1, tiled=True),
        lax.all_to_all(up_weight, "col", split_axis=0, concat_axis=1, tiled=True),
    )
    full_tokens = lax.all_gather(tokens, "row", axis=0, tiled=True)
    count = full_tokens.shape[0]
    share = count // n_col
    gate_part = jnp.dot(full_tokens, gate_block, preferred_element_type=jnp.float32)
    up_part = jnp.dot(full_tokens, up_block, preferred_element_type=jnp.float32)
    gate_sum, up_sum = (
        lax.psum_scatter(gate_part, "col", scatter_dimension=0, tiled=True),
        lax.psum_scatter(up_part, "col", scatter_dimension=0, tiled=True),
    )
    sig = jax.nn.sigmoid(gate_sum)
    hidden_share = (gate_sum * sig * up_sum).astype(jnp.bfloat16)
    hidden = lax.all_gather(hidden_share, "col", axis=0, tiled=True)
    rows_own = down_weight.shape[0]
    hidden_rows = lax.dynamic_slice_in_dim(hidden, col_index * rows_own, rows_own, 1)
    term = jnp.dot(hidden_rows, down_weight, preferred_element_type=jnp.float32)
    arranged = term.reshape(n_row, per_row, n_col, feat_block).transpose(0, 2, 1, 3)
    arranged = arranged.reshape(n_row * n_col * per_row, feat_block)
    output = lax.psum_scatter(arranged, ("row", "col"), scatter_dimension=0, tiled=True)
    stacked = lax.all_gather(out_grad, ("row", "col"), axis=0, tiled=True)
    grad_full = stacked.reshape(n_row, n_col, per_row, feat_block).transpose(0, 2, 1, 3)
    grad_full = grad_full.reshape(count, n_col * feat_block)
    dh_rows = contract_last(grad_full, down_weight)
    grad_rows = contract_first(hidden_rows, grad_full).astype(jnp.bfloat16)
    grad_down = lax.all_to_all(grad_rows, "col", split_axis=1, concat_axis=0, tiled=True)
    dh_block = lax.all_gather(dh_rows, "col", axis=1, tiled=True)
    hidden_grad = lax.dynamic_slice_in_dim(dh_block, col_index * share, share, 0)
    gate_grad = (hidden_grad * up_sum * sig * (1.0 + gate_sum * (1.0 - sig))).astype(jnp.bfloat16)
    up_grad = (hidden_grad * gate_sum * sig).astype(jnp.bfloat16)
    gate_all, up_all = (
        lax.all_gather(gate_grad, "col", axis=0, tiled=True),
        lax.all_gather(up_grad, "col", axis=0, tiled=True),
    )
    input_grad = lax.psum_scatter(
        contract_last(gate_all, gate_block) + contract_last(up_all, up_block),
        "row",
        scatter_dimension=0,
        tiled=True,
    )
    grad_gate = contract_first(full_tokens, gate_all).astype(jnp.bfloat16)
    grad_up = contract_first(full_tokens, up_all).astype(jnp.bfloat16)
    return (output, input_grad, grad_gate, grad_up, grad_down)


def solution(mesh):
    placed = (
        P("row", "col"),
        P(None, ("row", "col")),
        P(None, ("row", "col")),
        P(("row", "col"), None),
        P("row", "col"),
    )
    return jax.shard_map(
        shards,
        mesh=mesh,
        in_specs=placed,
        out_specs=(
            P("row", "col"),
            P("row", "col"),
            P("col", "row"),
            P("col", "row"),
            P("row", "col"),
        ),
        check_vma=False,
    )
```

profile of v0, /device:TPU:8, one launch (start us, length us, event | category | flops | bytes accessed | tf_op | source)
XLA Modules:
  0.0 1056.4 jit_solution(14391260053594187524)
XLA Ops:
  8.7 2.9 copy.31
  11.6 4.7 all-to-all-start
  16.3 2.9 copy.30
  19.2 18.6 %all-to-all-done = bf16[4,2048,112]{1,2,0:T(8,128)(2,1)} async-done(((bf16[4,2048,112]{1,2,0:T(8,128)(2,1)}), bf16[4,2048,112]{1,2,0:T(8,128)(2,1)}, u32[]{:S(2)}, u32[]{:S(2)}) %all-to-all-start) | async-done | bytes 1835040 | tf_op jit(solution)/shard_map/all_to_all | solution.py:26
  37.9 6.0 all-to-all-start.1
  43.9 37.5 %all-gather.3.cloned.1.call-done = bf16[256,2048]{1,0:T(8,128)(2,1)} async-done(((bf16[8,2048]{1,0:T(8,128)(2,1)}), bf16[256,2048]{1,0:T(8,128)(2,1)}) %all-gather.3.cloned.1.call-update) | async-done | bytes 1048592 | tf_op jit(solution)/shard_map/all_gather | solution.py:29
  81.4 3.4 fusion.7
  84.9 3.0 fusion.8
  88.0 59.3 %all-gather.5.cloned.1.call-done = bf16[1024,2048]{1,0:T(8,128)(2,1)} async-done(((bf16[8,2048]{1,0:T(8,128)(2,1)}), bf16[1024,2048]{1,0:T(8,128)(2,1)}) %all-gather.5.cloned.1.call-update) | async-done | bytes 4194320 | tf_op jit(solution)/shard_map/all_gather | solution.py:47
  147.3 3.7 fusion.9
  151.0 7.1 all_gather.21
  158.3 7.8 reduce-scatter.5.cloned.1.call-done
  166.1 22.2 %reduce-scatter.7.cloned.1.call-done = f32[64,448]{1,0:T(8,128)} async-done(((f32[256,448]{1,0:T(8,128)}), f32[64,448]{1,0:T(8,128)}) %reduce-scatter.7.cloned.1.call-update) | async-done | bytes 114704 | tf_op jit(solution)/shard_map/reduce_scatter | solution.py:36
  189.4 6.2 all_gather.22
  197.8 5.9 all_gather.23
  203.7 3.6 convolution_add_fusion
  207.4 5.9 all_gather.19
  213.2 4.5 fusion.3
  217.8 3.2 convolution_convert_fusion
  222.3 6.0 all-to-all-start.2
  232.1 24.7 %all-to-all-done.2 = bf16[112,4,2048]{2,0,1:T(8,128)(2,1)} async-done(((bf16[112,4,2048]{2,0,1:T(8,128)(2,1)}), bf16[112,4,2048]{2,0,1:T(8,128)(2,1)}, u32[]{:S(2)}, u32[]{:S(2)}) %all-to-all-start.2) | async-done | bytes 1835040 | tf_op jit(solution)/shard_map/all_to_all | solution.py:52
  256.7 141.3 %reduce-scatter.11.cloned.1.call-done = f32[8,2048]{1,0:T(8,128)} async-done(((f32[256,2048]{1,0:T(8,128)}), f32[8,2048]{1,0:T(8,128)}) %reduce-scatter.11.cloned.1.call-update) | async-done | bytes 65552 | tf_op jit(solution)/shard_map/reduce_scatter | solution.py:61
  398.0 648.6 %reduce-scatter.9.cloned.1.call-done = f32[8,2048]{1,0:T(8,128)} async-done(((f32[1024,2048]{1,0:T(8,128)}), f32[8,2048]{1,0:T(8,128)}) %reduce-scatter.9.cloned.1.call-update) | async-done | bytes 65552 | tf_op jit(solution)/shard_map/reduce_scatter | solution.py:46
  1046.6 2.9 copy.33
  (26 shorter events, 10.3 us)
Async XLA Ops:
  7.2 140.1 %copy-start = (bf16[112,8192]{1,0:T(8,128)(2,1)S(1)}, bf16[112,8192]{1,0:T(8,128)(2,1)}, u32[]{:S(2)}) copy-start(bf16[112,8192]{1,0:T(8,128)(2,1)} %param.8) | copy-start | bytes 5505028
  7.2 74.2 %all-gather.3.cloned.1.call-start = ((), (), s32[]{:S(2)}) async-start(), calls=%async_computation.7 | async-start | bytes 1081344 | tf_op jit(solution)/shard_map/all_gather | solution.py:29
  7.9 139.4 %all-gather.5.cloned.1.call-start = ((), (), s32[]{:S(2)}) async-start(), calls=%async_computation.11 | async-start | bytes 4227072 | tf_op jit(solution)/shard_map/all_gather | solution.py:47
  11.6 26.3 %all-to-all-start = ((bf16[4,2048,112]{1,2,0:T(8,128)(2,1)}), bf16[4,2048,112]{1,2,0:T(8,128)(2,1)}, u32[]{:S(2)}, u32[]{:S(2)}) async-start(bf16[4,2048,112]{1,2,0:T(8,128)(2,1)} %bitcast.56), calls=%async_computation | async-start | bytes 3670016 | tf_op jit(solution)/shard_map/all_to_all | solution.py:26
  37.9 47.0 %all-to-all-start.1 = ((bf16[4,2048,112]{1,2,0:T(8,128)(2,1)}), bf16[4,2048,112]{1,2,0:T(8,128)(2,1)}, u32[]{:S(2)}, u32[]{:S(2)}) async-start(bf16[4,2048,112]{1,2,0:T(8,128)(2,1)} %bitcast.54), calls=%async_computation.2 | async-start | bytes 3670016 | tf_op jit(solution)/shard_map/all_to_all | solution.py:27
  43.9 122.3 %reduce-scatter.5.cloned.1.call-start = ((), (), s32[]{:S(2)}) async-start(), calls=%async_computation.8 | async-start | bytes 655360 | tf_op jit(solution)/shard_map/reduce_scatter | solution.py:35
  81.4 3.5 copy-start.1
  84.8 103.5 %reduce-scatter.7.cloned.1.call-start = ((), (), s32[]{:S(2)}) async-start(), calls=%async_computation.9 | async-start | bytes 655360 | tf_op jit(solution)/shard_map/reduce_scatter | solution.py:36
  87.9 310.1 %reduce-scatter.11.cloned.1.call-start = ((), (), s32[]{:S(2)}) async-start(), calls=%async_computation.12 | async-start | bytes 2162688 | tf_op jit(solution)/shard_map/reduce_scatter | solution.py:61
  207.3 839.3 %reduce-scatter.9.cloned.1.call-start = ((), (), s32[]{:S(2)}) async-start(), calls=%async_computation.10 | async-start | bytes 8454144 | tf_op jit(solution)/shard_map/reduce_scatter | solution.py:46
  213.2 4.5 copy-start.2
  222.3 34.4 %all-to-all-start.2 = ((bf16[112,4,2048]{2,0,1:T(8,128)(2,1)}), bf16[112,4,2048]{2,0,1:T(8,128)(2,1)}, u32[]{:S(2)}, u32[]{:S(2)}) async-start(bf16[112,4,2048]{2,0,1:T(8,128)(2,1)} %bitcast.55), calls=%async_computation.6 | async-start | bytes 3670016 | tf_op jit(solution)/shard_map/all_to_all | solution.py:52
Sparse Core Ops, SparseCore 0:
  11.1 70.2 all-gather.2
  84.5 62.7 all-gather.4
  150.3 15.8 reduce-scatter.4
  169.0 19.3 reduce-scatter.6
  207.4 190.5 reduce-scatter.10
  400.8 645.7 reduce-scatter.8
where the time goes:
time: 1060 us
  waiting for transfers between devices  961 us (91%)
  matrix products  27.4 us (3%)
  blocking collectives  25 us (2%)
  starting transfers between devices  16.8 us (2%)
  between operations  14.2 us (1%)
    reduce_scatter x1, waiting for transfers between devices, shards(): lax.psum_scatter(arranged, ('row', 'col'), scatter_dimension=0, tiled=True)  649 us
    reduce_scatter x1, waiting for transfers between devices, shards(): lax.psum_scatter(contract_last(gate_all, gate_block) + contract_last(up_a...  141 us
    all_gather x1, waiting for transfers between devices, shards(): stacked = lax.all_gather(out_grad, ('row', 'col'), axis=0, tiled=True)  59.3 us
    all_gather x1, waiting for transfers between devices, shards(): full_tokens = lax.all_gather(tokens, 'row', axis=0, tiled=True)  37.5 us
    all_to_all x1, waiting for transfers between devices, shards(): lax.all_to_all(grad_rows, 'col', split_axis=1, concat_axis=0, tiled=True)  24.7 us
    reduce_scatter x1, waiting for transfers between devices, shards(): lax.psum_scatter(up_part, 'col', scatter_dimension=0, tiled=True)  22.2 us
  transfers between devices with their start and end apart: 9, of which 8 were waited for; matrix products, arithmetic and copies ran while one was open for 3% of the time, Pallas kernels for 0%

commit v1 on v0

v1 whole, which is shorter than its diff:
```python
import jax
import jax.numpy as jnp
from jax import lax
from jax.sharding import PartitionSpec as P


def contract_last(left, right):
    return lax.dot_general(
        left, right, (((1,), (1,)), ((), ())), preferred_element_type=jnp.float32
    )


def contract_first(left, right):
    return lax.dot_general(
        left, right, (((0,), (0,)), ((), ())), preferred_element_type=jnp.float32
    )


def gather_rows(block, axis, n):
    spread = jnp.broadcast_to(block[None], (n,) + block.shape)
    got = lax.all_to_all(spread, axis, split_axis=0, concat_axis=0, tiled=True)
    return got.reshape((n * block.shape[0],) + block.shape[1:])


def reduce_rows(part, axis, n):
    pieces = part.reshape((n, part.shape[0] // n) + part.shape[1:])
    got = lax.all_to_all(pieces, axis, split_axis=0, concat_axis=0, tiled=True)
    return jnp.sum(got, axis=0)


def shards(tokens, gate_weight, up_weight, down_weight, out_grad):
    n_row = lax.axis_size("row")
    n_col = lax.axis_size("col")
    unit = gate_weight.shape[1]
    joined = jnp.concatenate([gate_weight, up_weight], axis=1)
    gu_block = lax.all_to_all(joined, "col", split_axis=0, concat_axis=1, tiled=True)
    feat = gu_block.shape[0]
    down_block = lax.all_to_all(down_weight, "col", split_axis=1, concat_axis=0, tiled=True)

    both = gather_rows(jnp.stack([tokens, out_grad], axis=1), "row", n_row)
    full_tokens = both[:, 0]
    grad_full = both[:, 1]

    gu_part = jnp.dot(full_tokens, gu_block, preferred_element_type=jnp.float32)
    gu_sum = reduce_rows(gu_part, "col", n_col).reshape(-1, n_col, 2, unit)
    gate_sum = gu_sum[:, :, 0].reshape(gu_sum.shape[0], n_col * unit)
    up_sum = gu_sum[:, :, 1].reshape(gu_sum.shape[0], n_col * unit)
    sig = jax.nn.sigmoid(gate_sum)
    hidden_share = (gate_sum * sig * up_sum).astype(jnp.bfloat16)
    hidden = gather_rows(hidden_share, "col", n_col)

    term = jnp.dot(hidden, down_block, preferred_element_type=jnp.float32)
    output = reduce_rows(term, "row", n_row)

    dh_part = contract_last(grad_full, down_block)
    hidden_grad = reduce_rows(dh_part, "col", n_col)
    grad_down = contract_first(hidden, grad_full).astype(jnp.bfloat16)

    gate_grad = (hidden_grad * up_sum * sig * (1.0 + gate_sum * (1.0 - sig))).astype(jnp.bfloat16)
    up_grad = (hidden_grad * gate_sum * sig).astype(jnp.bfloat16)
    grads = gather_rows(jnp.stack([gate_grad, up_grad], axis=1), "col", n_col)
    gate_all = grads[:, 0]
    up_all = grads[:, 1]

    gu4 = gu_block.reshape(feat, n_col, 2, unit)
    gate_block = gu4[:, :, 0].reshape(feat, n_col * unit)
    up_block = gu4[:, :, 1].reshape(feat, n_col * unit)
    in_part = contract_last(gate_all, gate_block) + contract_last(up_all, up_block)
    input_grad = reduce_rows(in_part, "row", n_row)
    grad_gate = contract_first(full_tokens, gate_all).astype(jnp.bfloat16)
    grad_up = contract_first(full_tokens, up_all).astype(jnp.bfloat16)
    return (output, input_grad, grad_gate, grad_up, grad_down)


def solution(mesh):
    placed = (
        P("row", "col"),
        P(None, ("row", "col")),
        P(None, ("row", "col")),
        P(("row", "col"), None),
        P("row", "col"),
    )
    return jax.shard_map(
        shards,
        mesh=mesh,
        in_specs=placed,
        out_specs=(
            P("row", "col"),
            P("row", "col"),
            P("col", "row"),
            P("col", "row"),
            P("row", "col"),
        ),
        check_vma=False,
    )
```

time: 1060 us -> 253 us (0.24)
  waiting for transfers between devices: 961 us -> 154 us
  starting transfers between devices: 16.8 us -> 51.5 us
  blocking collectives: 25 us -> 0 us
  between operations: 14.2 us -> 0.78 us
    reduce_scatter x4 -> x0, waiting for transfers between devices: 820 us -> none  [the longest x1 649 us: shards(): lax.psum_scatter(arranged, ('row', 'col'), scatter_dimension=0, tiled=True)]
    all_to_all x3 -> x9, waiting for transfers between devices: 43.3 us -> 154 us  [the longest x4 62.2 us: reduce_rows(): got = lax.all_to_all(pieces, axis, split_axis=0, concat_axis=0, tiled=True)]
    all_gather x2 -> x0, waiting for transfers between devices: 96.8 us -> none  [the longest x1 59.3 us: shards(): stacked = lax.all_gather(out_grad, ('row', 'col'), axis=0, tiled=True)]
    all_to_all x3 -> x9, starting transfers between devices: 16.6 us -> 51.5 us  [the longest x4 22.3 us: reduce_rows(): got = lax.all_to_all(pieces, axis, split_axis=0, concat_axis=0, tiled=True)]
    all_gather x4 -> x0, blocking collectives: 25 us -> none  [the longest x1 7.11 us: shards(): dh_block = lax.all_gather(dh_rows, 'col', axis=1, tiled=True)]
  transfers between devices with their start and end apart: 9 -> 9, of which waited for: 8 -> 9; matrix products, arithmetic and copies ran while one was open for 3% -> 13% of each run, Pallas kernels for 0% -> 0%
where the time goes in v1:
time: 253 us; the launch traced here: 251 us
  waiting for transfers between devices  154 us (61%)
  starting transfers between devices  51.5 us (20%)
  local copies, waits for them, and re-layouts  18.2 us (7%)
  matrix products  18.1 us (7%)
  other arithmetic  7.98 us (3%)
    all_to_all x4, waiting for transfers between devices, reduce_rows(): got = lax.all_to_all(pieces, axis, split_axis=0, concat_axis=0, tiled=True)  62.2 us
    all_to_all x1, waiting for transfers between devices, shards(): lax.all_to_all(joined, 'col', split_axis=0, concat_axis=1, tiled=True)  35.8 us
    all_to_all x3, waiting for transfers between devices, gather_rows(): got = lax.all_to_all(spread, axis, split_axis=0, concat_axis=0, tiled=True)  34.9 us
    all_to_all x4, starting transfers between devices, reduce_rows(): got = lax.all_to_all(pieces, axis, split_axis=0, concat_axis=0, tiled=True)  22.3 us
    all_to_all x1, waiting for transfers between devices, shards(): lax.all_to_all(down_weight, 'col', split_axis=1, concat_axis=0, tiled=True)  21.2 us
    all_to_all x3, starting transfers between devices, gather_rows(): got = lax.all_to_all(spread, axis, split_axis=0, concat_axis=0, tiled=True)  20.4 us
    dot_general x3, matrix products, contract_first(): lax.dot_general(left, right, (((0,), (0,)), ((), ())), preferred_element_...  5.68 us
    reduce_sum x4, other arithmetic, reduce_rows(): return jnp.sum(got, axis=0)  5.4 us
  transfers between devices with their start and end apart: 9, of which 9 were waited for; matrix products, arithmetic and copies ran while one was open for 13% of the time, Pallas kernels for 0%

profile of v1, /device:TPU:8, one launch (start us, length us, event | category | flops | bytes accessed | tf_op | source)
XLA Modules:
  0.0 250.8 jit_solution(10565330120074351635)
XLA Ops:
  0.6 2.9 %copy.44 = bf16[14,4,8,2048]{3,2,0,1:T(8,128)(2,1)} copy(bf16[14,4,8,2048]{3,2,1,0:T(8,128)(2,1)} %bitcast.94) | data formatting | bytes 3670016 | tf_op jit(solution)/shard_map/all_to_all | solution.py:38
  3.6 4.0 %all-to-all-start.4 = ((bf16[112,4,2048]{2,0,1:T(8,128)(2,1)}), bf16[112,4,2048]{2,0,1:T(8,128)(2,1)S(1)}, u32[]{:S(2)}, u32[]{:S(2)}) async-start(bf16[112,4,2048]{2,0,1:T(8,128)(2,1)} %bitcast.77), calls=%async_computation.4 | async-start | bytes 3670016 | tf_op jit(solution)/shard_map/all_to_all | solution.py:38
  7.6 21.2 %all-to-all-done.4 = bf16[112,4,2048]{2,0,1:T(8,128)(2,1)S(1)} async-done(((bf16[112,4,2048]{2,0,1:T(8,128)(2,1)}), bf16[112,4,2048]{2,0,1:T(8,128)(2,1)S(1)}, u32[]{:S(2)}, u32[]{:S(2)}) %all-to-all-start.4) | async-done | bytes 1835040 | tf_op jit(solution)/shard_map/all_to_all | solution.py:38
  30.7 10.3 %all-to-all-start = ((bf16[32,8,2,2048]{3,1,2,0:T(8,128)(2,1)}), bf16[32,8,2,2048]{3,1,2,0:T(8,128)(2,1)S(1)}, u32[]{:S(2)}, u32[]{:S(2)}) async-start(bf16[32,8,2,2048]{3,1,2,0:T(8,128)(2,1)} %broadcast_in_dim.6), calls=%async_computation | async-start | bytes 4194304 | tf_op jit(solution)/shard_map/all_to_all | solution.py:21
  41.1 2.4 pad_maximum_fusion
  45.7 27.1 %all-to-all-done = bf16[32,8,2,2048]{3,1,2,0:T(8,128)(2,1)S(1)} async-done(((bf16[32,8,2,2048]{3,1,2,0:T(8,128)(2,1)}), bf16[32,8,2,2048]{3,1,2,0:T(8,128)(2,1)S(1)}, u32[]{:S(2)}, u32[]{:S(2)}) %all-to-all-start) | async-done | bytes 2097184 | tf_op jit(solution)/shard_map/all_to_all | solution.py:21
  74.2 4.8 %all-to-all-start.1 = ((bf16[4,2048,224]{1,2,0:T(8,128)(2,1)}), bf16[4,2048,224]{1,2,0:T(8,128)(2,1)}, u32[]{:S(2)}, u32[]{:S(2)}) async-start(bf16[4,2048,224]{1,2,0:T(8,128)(2,1)} %bitcast.82), calls=%async_computation.1 | async-start | bytes 7340032 | tf_op jit(solution)/shard_map/all_to_all | solution.py:36
  84.1 35.8 %all-to-all-done.1 = bf16[4,2048,224]{1,2,0:T(8,128)(2,1)} async-done(((bf16[4,2048,224]{1,2,0:T(8,128)(2,1)}), bf16[4,2048,224]{1,2,0:T(8,128)(2,1)}, u32[]{:S(2)}, u32[]{:S(2)}) %all-to-all-start.1) | async-done | bytes 3670048 | tf_op jit(solution)/shard_map/all_to_all | solution.py:36
  120.0 5.1 %all-to-all-start.6 = ((f32[4,64,448]{2,1,0:T(8,128)}), f32[4,64,448]{2,1,0:T(8,128)S(1)}, u32[]{:S(2)}, u32[]{:S(2)}) async-start(f32[4,64,448]{2,1,0:T(8,128)} %fusion.17), calls=%async_computation.6 | async-start | bytes 1048576 | tf_op jit(solution)/shard_map/all_to_all | solution.py:27
  125.1 4.6 %fusion.15 = f32[4,64,896]{2,1,0:T(8,128)} fusion(bf16[4,64,2048]{2,1,0:T(8,128)(2,1)} %bitcast.95, bf16[2048,896,1]{0,1,2:T(8,128)(2,1)} %bitcast.6), kind=kOutput, calls=%fused_computation.33 | convolution fusion | flops 939524096 | bytes 5636096 | tf_op jit(solution)/shard_map/dot_general | solution.py:44
  129.6 2.6 %all-to-all-done.6 = f32[4,64,448]{2,1,0:T(8,128)S(1)} async-done(((f32[4,64,448]{2,1,0:T(8,128)}), f32[4,64,448]{2,1,0:T(8,128)S(1)}, u32[]{:S(2)}, u32[]{:S(2)}) %all-to-all-start.6) | async-done | bytes 458784 | tf_op jit(solution)/shard_map/all_to_all | solution.py:27
  132.2 5.1 %all-to-all-start.2 = ((f32[4,64,896]{2,1,0:T(8,128)}), f32[4,64,896]{2,1,0:T(8,128)S(1)}, u32[]{:S(2)}, u32[]{:S(2)}) async-start(f32[4,64,896]{2,1,0:T(8,128)} %fusion.15), calls=%async_computation.2 | async-start | bytes 1835008 | tf_op jit(solution)/shard_map/all_to_all | solution.py:27
  138.0 10.7 %all-to-all-done.2 = f32[4,64,896]{2,1,0:T(8,128)S(1)} async-done(((f32[4,64,896]{2,1,0:T(8,128)}), f32[4,64,896]{2,1,0:T(8,128)S(1)}, u32[]{:S(2)}, u32[]{:S(2)}) %all-to-all-start.2) | async-done | bytes 917536 | tf_op jit(solution)/shard_map/all_to_all | solution.py:27
  151.5 5.0 %all-to-all-start.3 = ((bf16[4,64,448]{2,1,0:T(8,128)(2,1)}), bf16[4,64,448]{2,1,0:T(8,128)(2,1)S(1)}, u32[]{:S(2)}, u32[]{:S(2)}) async-start(bf16[4,64,448]{2,1,0:T(8,128)(2,1)} %broadcast_in_dim.7), calls=%async_computation.3 | async-start | bytes 524288 | tf_op jit(solution)/shard_map/all_to_all | solution.py:21
  156.7 4.3 %all-to-all-done.3 = bf16[4,64,448]{2,1,0:T(8,128)(2,1)S(1)} async-done(((bf16[4,64,448]{2,1,0:T(8,128)(2,1)}), bf16[4,64,448]{2,1,0:T(8,128)(2,1)S(1)}, u32[]{:S(2)}, u32[]{:S(2)}) %all-to-all-start.3) | async-done | bytes 229408 | tf_op jit(solution)/shard_map/all_to_all | solution.py:21
  161.8 5.1 %all-to-all-start.7 = ((bf16[4,64,2,448]{3,1,2,0:T(8,128)(2,1)}), bf16[4,64,2,448]{3,1,2,0:T(8,128)(2,1)S(1)}, u32[]{:S(2)}, u32[]{:S(2)}) async-start(bf16[4,64,2,448]{3,1,2,0:T(8,128)(2,1)} %broadcast_in_dim.8), calls=%async_computation.7 | async-start | bytes 1048576 | tf_op jit(solution)/shard_map/all_to_all | solution.py:21
  166.8 3.5 %fusion.16 = f32[32,8,2048]{2,1,0:T(8,128)} fusion(bf16[32,8,448]{2,1,0:T(8,128)(2,1)S(1)} %bitcast.92, bf16[448,2048,1]{1,0,2:T(8,128)(2,1)} %bitcast.86), kind=kOutput, calls=%fused_computation.34 | convolution fusion | flops 469762048 | bytes 4161536 | tf_op jit(solution)/shard_map/dot_general | solution.py:52
  170.4 3.6 %all-to-all-done.7 = bf16[4,64,2,448]{3,1,2,0:T(8,128)(2,1)S(1)} async-done(((bf16[4,64,2,448]{3,1,2,0:T(8,128)(2,1)}), bf16[4,64,2,448]{3,1,2,0:T(8,128)(2,1)S(1)}, u32[]{:S(2)}, u32[]{:S(2)}) %all-to-all-start.7) | async-done | bytes 458784 | tf_op jit(solution)/shard_map/all_to_all | solution.py:21
  174.0 6.6 %all-to-all-start.5 = ((f32[32,8,2048]{2,1,0:T(8,128)}), f32[32,8,2048]{2,1,0:T(8,128)}, u32[]{:S(2)}, u32[]{:S(2)}) async-start(f32[32,8,2048]{2,1,0:T(8,128)} %fusion.16), calls=%async_computation.5 | async-start | bytes 4194304 | tf_op jit(solution)/shard_map/all_to_all | solution.py:27
  180.6 2.5 %fusion.13 = (bf16[2048,4,1,112]{0,3,2,1:T(8,128)(2,1)S(1)}, bf16[2048,4,1,112]{0,3,2,1:T(8,128)(2,1)S(1)}) fusion(bf16[2048,4,2,112]{0,3,2,1:T(8,128)(2,1)} %bitcast.17), kind=kLoop, calls=%fused_computation.31 | loop fusion | bytes 7340032 | tf_op jit(solution)/shard_map/slice | solution.py:67
  186.0 26.3 %all-to-all-done.5 = f32[32,8,2048]{2,1,0:T(8,128)} async-done(((f32[32,8,2048]{2,1,0:T(8,128)}), f32[32,8,2048]{2,1,0:T(8,128)}, u32[]{:S(2)}, u32[]{:S(2)}) %all-to-all-start.5) | async-done | bytes 2097184 | tf_op jit(solution)/shard_map/all_to_all | solution.py:27
  212.3 5.6 %all-to-all-start.8 = ((f32[32,8,2048]{2,1,0:T(8,128)}), f32[32,8,2048]{2,1,0:T(8,128)}, u32[]{:S(2)}, u32[]{:S(2)}) async-start(f32[32,8,2048]{2,1,0:T(8,128)} %fusion), calls=%async_computation.8 | async-start | bytes 4194304 | tf_op jit(solution)/shard_map/all_to_all | solution.py:27
  225.9 22.5 %all-to-all-done.8 = f32[32,8,2048]{2,1,0:T(8,128)} async-done(((f32[32,8,2048]{2,1,0:T(8,128)}), f32[32,8,2048]{2,1,0:T(8,128)}, u32[]{:S(2)}, u32[]{:S(2)}) %all-to-all-start.8) | async-done | bytes 2097184 | tf_op jit(solution)/shard_map/all_to_all | solution.py:27
  248.5 2.3 reduce_sum.42
  (38 shorter events, 26.0 us)
Async XLA Ops:
  3.6 4.0 %copy-start.4 = (bf16[8,2048]{1,0:T(8,128)(2,1)S(1)}, bf16[8,2048]{1,0:T(8,128)(2,1)}, u32[]{:S(2)}) copy-start(bf16[8,2048]{1,0:T(8,128)(2,1)} %param.9) | copy-start | bytes 98308
  3.6 4.0 %copy-start.5 = (bf16[8,2048]{1,0:T(8,128)(2,1)S(1)}, bf16[8,2048]{1,0:T(8,128)(2,1)}, u32[]{:S(2)}) copy-start(bf16[8,2048]{1,0:T(8,128)(2,1)} %param.5) | copy-start | bytes 98308
  3.6 25.3 %all-to-all-start.4 = ((bf16[112,4,2048]{2,0,1:T(8,128)(2,1)}), bf16[112,4,2048]{2,0,1:T(8,128)(2,1)S(1)}, u32[]{:S(2)}, u32[]{:S(2)}) async-start(bf16[112,4,2048]{2,0,1:T(8,128)(2,1)} %bitcast.77), calls=%async_computation.4 | async-start | bytes 3670016 | tf_op jit(solution)/shard_map/all_to_all | solution.py:38
  28.8 1.9 copy-start.1
  30.7 42.1 %all-to-all-start = ((bf16[32,8,2,2048]{3,1,2,0:T(8,128)(2,1)}), bf16[32,8,2,2048]{3,1,2,0:T(8,128)(2,1)S(1)}, u32[]{:S(2)}, u32[]{:S(2)}) async-start(bf16[32,8,2,2048]{3,1,2,0:T(8,128)(2,1)} %broadcast_in_dim.6), calls=%async_computation | async-start | bytes 4194304 | tf_op jit(solution)/shard_map/all_to_all | solution.py:21
  72.8 1.4 copy-start
  74.2 45.8 %all-to-all-start.1 = ((bf16[4,2048,224]{1,2,0:T(8,128)(2,1)}), bf16[4,2048,224]{1,2,0:T(8,128)(2,1)}, u32[]{:S(2)}, u32[]{:S(2)}) async-start(bf16[4,2048,224]{1,2,0:T(8,128)(2,1)} %bitcast.82), calls=%async_computation.1 | async-start | bytes 7340032 | tf_op jit(solution)/shard_map/all_to_all | solution.py:36
  80.7 1.9 copy-start.2
  120.0 12.3 %all-to-all-start.6 = ((f32[4,64,448]{2,1,0:T(8,128)}), f32[4,64,448]{2,1,0:T(8,128)S(1)}, u32[]{:S(2)}, u32[]{:S(2)}) async-start(f32[4,64,448]{2,1,0:T(8,128)} %fusion.17), calls=%async_computation.6 | async-start | bytes 1048576 | tf_op jit(solution)/shard_map/all_to_all | solution.py:27
  132.2 16.5 %all-to-all-start.2 = ((f32[4,64,896]{2,1,0:T(8,128)}), f32[4,64,896]{2,1,0:T(8,128)S(1)}, u32[]{:S(2)}, u32[]{:S(2)}) async-start(f32[4,64,896]{2,1,0:T(8,128)} %fusion.15), calls=%async_computation.2 | async-start | bytes 1835008 | tf_op jit(solution)/shard_map/all_to_all | solution.py:27
  138.0 18.5 %copy-start.3 = (f32[64,448]{1,0:T(8,128)S(1)}, f32[64,448]{1,0:T(8,128)}, u32[]{:S(2)}) copy-start(f32[64,448]{1,0:T(8,128)} %reduce_sum.40) | copy-start | bytes 344068
  151.5 9.4 %all-to-all-start.3 = ((bf16[4,64,448]{2,1,0:T(8,128)(2,1)}), bf16[4,64,448]{2,1,0:T(8,128)(2,1)S(1)}, u32[]{:S(2)}, u32[]{:S(2)}) async-start(bf16[4,64,448]{2,1,0:T(8,128)(2,1)} %broadcast_in_dim.7), calls=%async_computation.3 | async-start | bytes 524288 | tf_op jit(solution)/shard_map/all_to_all | solution.py:21
  161.8 12.3 %all-to-all-start.7 = ((bf16[4,64,2,448]{3,1,2,0:T(8,128)(2,1)}), bf16[4,64,2,448]{3,1,2,0:T(8,128)(2,1)S(1)}, u32[]{:S(2)}, u32[]{:S(2)}) async-start(bf16[4,64,2,448]{3,1,2,0:T(8,128)(2,1)} %broadcast_in_dim.8), calls=%async_computation.7 | async-start | bytes 1048576 | tf_op jit(solution)/shard_map/all_to_all | solution.py:21
  174.0 38.3 %all-to-all-start.5 = ((f32[32,8,2048]{2,1,0:T(8,128)}), f32[32,8,2048]{2,1,0:T(8,128)}, u32[]{:S(2)}, u32[]{:S(2)}) async-start(f32[32,8,2048]{2,1,0:T(8,128)} %fusion.16), calls=%async_computation.5 | async-start | bytes 4194304 | tf_op jit(solution)/shard_map/all_to_all | solution.py:27
  212.3 36.1 %all-to-all-start.8 = ((f32[32,8,2048]{2,1,0:T(8,128)}), f32[32,8,2048]{2,1,0:T(8,128)}, u32[]{:S(2)}, u32[]{:S(2)}) async-start(f32[32,8,2048]{2,1,0:T(8,128)} %fusion), calls=%async_computation.8 | async-start | bytes 4194304 | tf_op jit(solution)/shard_map/all_to_all | solution.py:27

commit v2 on v1

--- a/solution.py
+++ b/solution.py
@@ -28,47 +28,84 @@
     return jnp.sum(got, axis=0)
 
 
+def swap(x, k, n):
+    return lax.ppermute(x, "col", perm=[(i, i ^ k) for i in range(n)])
+
+
+def piece(x, index, size, axis):
+    return lax.dynamic_slice_in_dim(x, index * size, size, axis)
+
+
+def col_scatter(x, axis, n):
+    me = lax.axis_index("col")
+    size = x.shape[axis] // n
+    got = [piece(x, me, size, axis)]
+    for k in range(1, n):
+        got.append(swap(piece(x, me ^ k, size, axis), k, n))
+    stacked = jnp.stack(got)
+    order = jnp.arange(n, dtype=jnp.int32) ^ me
+    return jnp.take(stacked, order, axis=0)
+
+
+def col_gather(x, n):
+    me = lax.axis_index("col")
+    got = [x] + [swap(x, k, n) for k in range(1, n)]
+    stacked = jnp.stack(got)
+    order = jnp.arange(n, dtype=jnp.int32) ^ me
+    return jnp.take(stacked, order, axis=0)
+
+
+def col_reduce(x, n):
+    me = lax.axis_index("col")
+    size = x.shape[0] // n
+    total = piece(x, me, size, 0)
+    for k in range(1, n):
+        total = total + swap(piece(x, me ^ k, size, 0), k, n)
+    return total
+
+
 def shards(tokens, gate_weight, up_weight, down_weight, out_grad):
     n_row = lax.axis_size("row")
     n_col = lax.axis_size("col")
     unit = gate_weight.shape[1]
     joined = jnp.concatenate([gate_weight, up_weight], axis=1)
-    gu_block = lax.all_to_all(joined, "col", split_axis=0, concat_axis=1, tiled=True)
-    feat = gu_block.shape[0]
-    down_block = lax.all_to_all(down_weight, "col", split_axis=1, concat_axis=0, tiled=True)
+    gu_stack = col_scatter(joined, 0, n_col)
+    feat = gu_stack.shape[1]
+    gu_block = gu_stack.reshape(n_col, feat, 2, unit)
+    gate_block = gu_block[:, :, 0].transpose(1, 0, 2).reshape(feat, n_col * unit)
+    up_block = gu_block[:, :, 1].transpose(1, 0, 2).reshape(feat, n_col * unit)
+    down_block = col_scatter(down_weight, 1, n_col).reshape(n_col * unit, feat)
 
     both = gather_rows(jnp.stack([tokens, out_grad], axis=1), "row", n_row)
     full_tokens = both[:, 0]
     grad_full = both[:, 1]
 
-    gu_part = jnp.dot(full_tokens, gu_block, preferred_element_type=jnp.float32)
-    gu_sum = reduce_rows(gu_part, "col", n_col).reshape(-1, n_col, 2, unit)
-    gate_sum = gu_sum[:, :, 0].reshape(gu_sum.shape[0], n_col * unit)
-    up_sum = gu_sum[:, :, 1].reshape(gu_sum.shape[0], n_col * unit)
+    gu_w = jnp.concatenate([gate_block, up_block], axis=1)
+    gu_part = jnp.dot(full_tokens, gu_w, preferred_element_type=jnp.float32)
+    gu_sum = col_reduce(gu_part, n_col)
+    gate_sum = gu_sum[:, : n_col * unit]
+    up_sum = gu_sum[:, n_col * unit :]
     sig = jax.nn.sigmoid(gate_sum)
     hidden_share = (gate_sum * sig * up_sum).astype(jnp.bfloat16)
-    hidden = gather_rows(hidden_share, "col", n_col)
+    hidden = col_gather(hidden_share, n_col).reshape(-1, n_col * unit)
 
     term = jnp.dot(hidden, down_block, preferred_element_type=jnp.float32)
     output = reduce_rows(term, "row", n_row)
 
     dh_part = contract_last(grad_full, down_block)
-    hidden_grad = reduce_rows(dh_part, "col", n_col)
+    hidden_grad = col_reduce(dh_part, n_col)
     grad_down = contract_first(hidden, grad_full).astype(jnp.bfloat16)
 
     gate_grad = (hidden_grad * up_sum * sig * (1.0 + gate_sum * (1.0 - sig))).astype(jnp.bfloat16)
     up_grad = (hidden_grad * gate_sum * sig).astype(jnp.bfloat16)
-    grads = gather_rows(jnp.stack([gate_grad, up_grad], axis=1), "col", n_col)
-    gate_all = grads[:, 0]
-    up_all = grads[:, 1]
+    grads = col_gather(jnp.concatenate([gate_grad, up_grad], axis=1), n_col)
+    grads = grads.reshape(-1, 2 * n_col * unit)
 
-    gu4 = gu_block.reshape(feat, n_col, 2, unit)
-    gate_block = gu4[:, :, 0].reshape(feat, n_col * unit)
-    up_block = gu4[:, :, 1].reshape(feat, n_col * unit)
-    in_part = contract_last(gate_all, gate_block) + contract_last(up_all, up_block)
+    in_part = contract_last(grads, gu_w)
     input_grad = reduce_rows(in_part, "row", n_row)
-    grad_gate = contract_first(full_tokens, gate_all).astype(jnp.bfloat16)
-    grad_up = contract_first(full_tokens, up_all).astype(jnp.bfloat16)
+    grad_gu = contract_first(full_tokens, grads)
+    grad_gate = grad_gu[:, : n_col * unit].astype(jnp.bfloat16)
+    grad_up = grad_gu[:, n_col * unit :].astype(jnp.bfloat16)
     return (output, input_grad, grad_gate, grad_up, grad_down)
 
 

time: 253 us -> 232 us (0.917)
  waiting for transfers between devices: 154 us -> 129 us
  starting transfers between devices: 51.5 us -> 40 us
  local copies, waits for them, and re-layouts: 18.2 us -> 29.4 us
  other arithmetic: 7.98 us -> 15.7 us
  matrix products: 18.1 us -> 13.8 us
    ppermute x0 -> x18, waiting for transfers between devices: none -> 107 us  [swap(): return lax.ppermute(x, 'col', perm=[(i, i ^ k) for i in range(n)])]
    all_to_all x2 -> x0, waiting for transfers between devices: 57.1 us -> none  [the longest x1 35.8 us: shards(): lax.all_to_all(joined, 'col', split_axis=0, concat_axis=1, tiled=True)]
    all_to_all x4 -> x2, waiting for transfers between devices: 62.2 us -> 22.2 us  [reduce_rows(): got = lax.all_to_all(pieces, axis, split_axis=0, concat_axis=0, tiled=True)]
    all_to_all x3 -> x1, waiting for transfers between devices: 34.9 us -> 0.01 us  [gather_rows(): got = lax.all_to_all(spread, axis, split_axis=0, concat_axis=0, tiled=True)]
    ppermute x0 -> x18, starting transfers between devices: none -> 11 us  [swap(): return lax.ppermute(x, 'col', perm=[(i, i ^ k) for i in range(n)])]
    all_to_all x3 -> x1, starting transfers between devices: 20.4 us -> 10 us  [gather_rows(): got = lax.all_to_all(spread, axis, split_axis=0, concat_axis=0, tiled=True)]
    all_to_all x2 -> x0, starting transfers between devices: 8.8 us -> none  [the longest x1 4.78 us: shards(): lax.all_to_all(joined, 'col', split_axis=0, concat_axis=1, tiled=True)]
    gather x0 -> x4, local copies, waits for them, and re-layouts: none -> 7.72 us  [the longest x2 6.53 us: col_scatter(): return jnp.take(stacked, order, axis=0)]
  transfers between devices with their start and end apart: 9 -> 21, of which waited for: 9 -> 10; matrix products, arithmetic and copies ran while one was open for 13% -> 19% of each run, Pallas kernels for 0% -> 0%
where the time goes in v2:
time: 232 us; the launch traced here: 229 us
  waiting for transfers between devices  129 us (56%)
  starting transfers between devices  40 us (17%)
  local copies, waits for them, and re-layouts  29.4 us (13%)
  other arithmetic  15.7 us (7%)
  matrix products  13.8 us (6%)
    ppermute x18, waiting for transfers between devices, swap(): return lax.ppermute(x, 'col', perm=[(i, i ^ k) for i in range(n)])  107 us
    all_to_all x2, waiting for transfers between devices, reduce_rows(): got = lax.all_to_all(pieces, axis, split_axis=0, concat_axis=0, tiled=True)  22.2 us
    all_to_all x2, starting transfers between devices, reduce_rows(): got = lax.all_to_all(pieces, axis, split_axis=0, concat_axis=0, tiled=True)  19 us
    ppermute x18, starting transfers between devices, swap(): return lax.ppermute(x, 'col', perm=[(i, i ^ k) for i in range(n)])  11 us
    all_to_all x1, starting transfers between devices, gather_rows(): got = lax.all_to_all(spread, axis, split_axis=0, concat_axis=0, tiled=True)  10 us
    gather x2, local copies, waits for them, and re-layouts, col_scatter(): return jnp.take(stacked, order, axis=0)  6.53 us
    dot_general x2, matrix products, contract_last(): lax.dot_general(left, right, (((1,), (1,)), ((), ())), preferred_element_...  5.72 us
    select_n x2, other arithmetic, col_scatter(): return jnp.take(stacked, order, axis=0)  5.42 us
  transfers between devices with their start and end apart: 21, of which 10 were waited for; matrix products, arithmetic and copies ran while one was open for 19% of the time, Pallas kernels for 0%

profile of v2, /device:TPU:8, one launch (start us, length us, event | category | flops | bytes accessed | tf_op | source)
XLA Modules:
  0.0 228.9 jit_solution(17357124269370909201)
XLA Ops:
  0.7 2.7 %dynamic-slice_bitcast_fusion.1 = (bf16[1,112,2048]{2,1,0:T(8,128)(2,1)S(1)}, bf16[112,2048]{1,0:T(8,128)(2,1)}, bf16[112,2048]{1,0:T(8,128)(2,1)}, bf16[112,2048]{1,0:T(8,128)(2,1)}) fusion(bf16[112,8192]{1,0:T(8,128)(2,1)} %param.8, s32[]{:T(128)S(6)} %select_n.121, s32[]{:T(128)S(6)} %select_n.122, s32[]{:T(128)S(6)} %select_n.124, s32[]{:T(128)S(6)} %select_n.123), kind=kLoop, calls=%fused_computation.21 | loop fusion | bytes 3670032 | tf_op jit(solution)/shard_map/stack | solution.py:45
  10.6 10.0 %all-to-all-start = ((bf16[32,8,2,2048]{3,1,2,0:T(8,128)(2,1)}), bf16[32,8,2,2048]{3,1,2,0:T(8,128)(2,1)}, u32[]{:S(2)}, u32[]{:S(2)}) async-start(bf16[32,8,2,2048]{3,1,2,0:T(8,128)(2,1)} %broadcast_in_dim.55), calls=%async_computation | async-start | bytes 4194304 | tf_op jit(solution)/shard_map/all_to_all | solution.py:21
  21.0 61.4 %collective-permute-done.10 = bf16[112,2048]{1,0:T(8,128)(2,1)S(1)} collective-permute-done((bf16[112,2048]{1,0:T(8,128)(2,1)}, bf16[112,2048]{1,0:T(8,128)(2,1)S(1)}, u32[]{:S(2)}, u32[]{:S(2)}) %collective-permute-start.10) | collective-permute-done | bytes 458784 | tf_op jit(solution)/shard_map/ppermute | solution.py:32
  86.7 3.0 %broadcast_select_fusion.1 = bf16[4,112,2048]{2,1,0:T(8,128)(2,1)} fusion(bf16[4,112,2048]{2,1,0:T(8,128)(2,1)} %gather_fusion.2, pred[4]{0:T(512)(128)(4,1)S(1)} %compare_and_fusion), kind=kLoop, calls=%fused_computation.14 | loop fusion | flops 917504 | bytes 3670020 | tf_op jit(solution)/shard_map/jit(_take)/select_n | solution.py:47
  89.7 3.3 %pad_maximum_fusion = bf16[4,2048,224]{1,2,0:T(8,128)(2,1)} fusion(bf16[1,2048,224]{1,2,0:T(8,128)(2,1)} %bitcast.7, bf16[1,2048,224]{1,2,0:T(8,128)(2,1)} %bitcast.6, bf16[1,2048,224]{1,2,0:T(8,128)(2,1)} %bitcast.5, bf16[1,2048,224]{1,2,0:T(8,128)(2,1)S(1)} %get-tuple-element.11), kind=kLoop, calls=%fused_computation.4 | loop fusion | flops 5505024 | bytes 7340032 | tf_op jit(solution)/shard_map/stack | solution.py:45
  93.0 4.6 %gather_fusion = bf16[4,2048,224]{1,2,0:T(8,128)(2,1)} fusion(bf16[4,2048,224]{1,2,0:T(8,128)(2,1)} %pad_maximum_fusion, s32[1024]{0:T(1024)S(1)} %pad_clamp_fusion), kind=kCustom, calls=%fused_computation | custom fusion | bytes 7340048 | tf_op jit(solution)/shard_map/jit(_take)/gather | solution.py:47
  97.7 2.5 %broadcast_select_fusion = bf16[4,2048,2,112]{1,3,2,0:T(8,128)(2,1)S(1)} fusion(bf16[4,2048,2,112]{1,3,2,0:T(8,128)(2,1)} %bitcast.60, pred[4]{0:T(512)(128)(4,1)S(1)} %compare_and_fusion), kind=kLoop, calls=%fused_computation.8 | loop fusion | flops 1835008 | bytes 7340036 | tf_op jit(solution)/shard_map/jit(_take)/select_n | solution.py:47
  101.7 3.8 %copy.30 = bf16[2048,448]{1,0:T(8,128)(2,1)} copy(bf16[2048,448]{0,1:T(8,128)(2,1)} %bitcast.66) | data formatting | bytes 3670016 | tf_op jit(solution)/shard_map/reshape | solution.py:76
  105.5 2.4 %copy.29 = bf16[2048,448]{1,0:T(8,128)(2,1)} copy(bf16[2048,448]{0,1:T(8,128)(2,1)S(1)} %bitcast.65) | data formatting | bytes 3670016 | tf_op jit(solution)/shard_map/reshape | solution.py:75
  117.1 2.9 %collective-permute-done.5 = f32[64,896]{1,0:T(8,128)S(1)} collective-permute-done((f32[64,896]{1,0:T(8,128)S(1)}, f32[64,896]{1,0:T(8,128)S(1)}, u32[]{:S(2)}, u32[]{:S(2)}) %collective-permute-start.5) | collective-permute-done | bytes 229408 | tf_op jit(solution)/shard_map/ppermute | solution.py:32
  120.4 5.1 %collective-permute-done.4 = f32[64,896]{1,0:T(8,128)S(1)} collective-permute-done((f32[64,896]{1,0:T(8,128)S(1)}, f32[64,896]{1,0:T(8,128)S(1)}, u32[]{:S(2)}, u32[]{:S(2)}) %collective-permute-start.4) | collective-permute-done | bytes 229408 | tf_op jit(solution)/shard_map/ppermute | solution.py:32
  125.5 2.2 collective-permute-done.14
  127.8 3.1 %collective-permute-done.13 = f32[64,448]{1,0:T(8,128)S(1)} collective-permute-done((f32[64,448]{1,0:T(8,128)S(1)}, f32[64,448]{1,0:T(8,128)S(1)}, u32[]{:S(2)}, u32[]{:S(2)}) %collective-permute-start.13) | collective-permute-done | bytes 114720 | tf_op jit(solution)/shard_map/ppermute | solution.py:32
  133.0 2.5 %collective-permute-done.8 = bf16[64,448]{1,0:T(8,128)(2,1)S(1)} collective-permute-done((bf16[64,448]{1,0:T(8,128)(2,1)S(1)}, bf16[64,448]{1,0:T(8,128)(2,1)S(1)}, u32[]{:S(2)}, u32[]{:S(2)}) %collective-permute-start.8) | collective-permute-done | bytes 57376 | tf_op jit(solution)/shard_map/ppermute | solution.py:32
  137.7 3.6 %fusion.13 = f32[32,8,2048]{2,1,0:T(8,128)} fusion(bf16[32,8,448]{2,1,0:T(8,128)(2,1)S(1)} %bitcast.69, bf16[448,2048,1]{1,0,2:T(8,128)(2,1)} %bitcast.67), kind=kOutput, calls=%fused_computation.59 | convolution fusion | flops 469762048 | bytes 4161536 | tf_op jit(solution)/shard_map/dot_general | solution.py:92
  141.3 10.0 %all-to-all-start.1 = ((f32[32,8,2048]{2,1,0:T(8,128)}), f32[32,8,2048]{2,1,0:T(8,128)}, u32[]{:S(2)}, u32[]{:S(2)}) async-start(f32[32,8,2048]{2,1,0:T(8,128)} %fusion.13), calls=%async_computation.1 | async-start | bytes 4194304 | tf_op jit(solution)/shard_map/all_to_all | solution.py:27
  153.6 25.0 %collective-permute-done.17 = bf16[64,896]{1,0:T(8,128)(2,1)S(1)} collective-permute-done((bf16[64,896]{1,0:T(8,128)(2,1)S(1)}, bf16[64,896]{1,0:T(8,128)(2,1)S(1)}, u32[]{:S(2)}, u32[]{:S(2)}) %collective-permute-start.17) | collective-permute-done | bytes 114720 | tf_op jit(solution)/shard_map/ppermute | solution.py:32
  178.6 3.3 %collective-permute-done.16 = bf16[64,896]{1,0:T(8,128)(2,1)S(1)} collective-permute-done((bf16[64,896]{1,0:T(8,128)(2,1)S(1)}, bf16[64,896]{1,0:T(8,128)(2,1)S(1)}, u32[]{:S(2)}, u32[]{:S(2)}) %collective-permute-start.16) | collective-permute-done | bytes 114720 | tf_op jit(solution)/shard_map/ppermute | solution.py:32
  182.6 5.0 %fusion = f32[32,8,2048]{2,1,0:T(8,128)} fusion(bf16[2048,448]{1,0:T(8,128)(2,1)} %copy.30, bf16[2048,448]{1,0:T(8,128)(2,1)} %copy.29, bf16[32,8,896]{2,1,0:T(8,128)(2,1)S(1)} %bitcast.71, pred[32]{0:T(512)(128)(4,1)S(1)} %broadcast_in_dim.62), kind=kOutput, calls=%fused_computation.6 | convolution fusion | flops 947093504 | bytes 6225952 | tf_op jit(solution)/shard_map/dot_general | solution.py:8
  187.6 8.9 %all-to-all-start.2 = ((f32[32,8,2048]{2,1,0:T(8,128)}), f32[32,8,2048]{2,1,0:T(8,128)}, u32[]{:S(2)}, u32[]{:S(2)}) async-start(f32[32,8,2048]{2,1,0:T(8,128)} %fusion), calls=%async_computation.2 | async-start | bytes 4194304 | tf_op jit(solution)/shard_map/all_to_all | solution.py:27
  199.7 2.3 %fusion.11 = (bf16[2048,448]{0,1:T(8,128)(2,1)}, bf16[2048,448]{0,1:T(8,128)(2,1)}) fusion(bf16[2048,896]{0,1:T(8,128)(2,1)S(1)} %convolution_convert_fusion), kind=kLoop, calls=%fused_computation.57 | loop fusion | bytes 7340032 | tf_op jit(solution)/shard_map/slice | solution.py:108
  202.1 2.3 %reduce_sum.18 = f32[8,2048]{1,0:T(8,128)} reduce(f32[32,8,2048]{2,1,0:T(8,128)} %all-to-all-done.1, f32[]{:T(128)} %constant.73.clone.1), dimensions={0}, to_apply=%region_0.1 | reduce | flops 507904 | bytes 2162692 | tf_op jit(solution)/shard_map/reduce_sum | solution.py:28
  204.4 22.2 %all-to-all-done.2 = f32[32,8,2048]{2,1,0:T(8,128)} async-done(((f32[32,8,2048]{2,1,0:T(8,128)}), f32[32,8,2048]{2,1,0:T(8,128)}, u32[]{:S(2)}, u32[]{:S(2)}) %all-to-all-start.2) | async-done | bytes 2097184 | tf_op jit(solution)/shard_map/all_to_all | solution.py:27
  226.6 2.3 %reduce_sum.19 = f32[8,2048]{1,0:T(8,128)} reduce(f32[32,8,2048]{2,1,0:T(8,128)} %all-to-all-done.2, f32[]{:T(128)} %constant.73.clone.1), dimensions={0}, to_apply=%region_1.2 | reduce | flops 507904 | bytes 2162692 | tf_op jit(solution)/shard_map/reduce_sum | solution.py:28
  (79 shorter events, 33.5 us)
Async XLA Ops:
  3.4 17.4 %collective-permute-start.11 = (bf16[112,2048]{1,0:T(8,128)(2,1)}, bf16[112,2048]{1,0:T(8,128)(2,1)}, u32[]{:S(2)}, u32[]{:S(2)}) collective-permute-start(bf16[112,2048]{1,0:T(8,128)(2,1)} %get-tuple-element.17), channel_id=1, source_target_pairs={{0,3},{1,2},{2,1},{3,0},{4,7},{5,6},{6,5},{7,4},{8,11},{9,10},{10,... | collective-permute-start | bytes 1376264 | tf_op jit(solution)/shard_map/ppermute | solution.py:32
  5.0 4.1 %copy-start.7 = (bf16[8,2048]{1,0:T(8,128)(2,1)S(1)}, bf16[8,2048]{1,0:T(8,128)(2,1)}, u32[]{:S(2)}) copy-start(bf16[8,2048]{1,0:T(8,128)(2,1)} %param.9) | copy-start | bytes 98308
  5.0 4.1 %copy-start.8 = (bf16[8,2048]{1,0:T(8,128)(2,1)S(1)}, bf16[8,2048]{1,0:T(8,128)(2,1)}, u32[]{:S(2)}) copy-start(bf16[8,2048]{1,0:T(8,128)(2,1)} %param.5) | copy-start | bytes 98308
  6.6 83.1 %collective-permute-start.2 = (bf16[2048,224]{0,1:T(8,128)(2,1)}, bf16[2048,224]{0,1:T(8,128)(2,1)}, u32[]{:S(2)}, u32[]{:S(2)}) collective-permute-start(bf16[2048,224]{0,1:T(8,128)(2,1)} %get-tuple-element.12), channel_id=1, source_target_pairs={{0,3},{1,2},{2,1},{3,0},{4,7},{5,6},{6,5},{7,4},{8,11},{9,10},{10,... | collective-permute-start | bytes 2752520 | tf_op jit(solution)/shard_map/ppermute | solution.py:32
  7.0 82.7 %collective-permute-start.1 = (bf16[2048,224]{0,1:T(8,128)(2,1)}, bf16[2048,224]{0,1:T(8,128)(2,1)}, u32[]{:S(2)}, u32[]{:S(2)}) collective-permute-start(bf16[2048,224]{0,1:T(8,128)(2,1)} %get-tuple-element.13), channel_id=1, source_target_pairs={{0,2},{1,3},{2,0},{3,1},{4,6},{5,7},{6,4},{7,5},{8,10},{9,11},{10,... | collective-permute-start | bytes 2752520 | tf_op jit(solution)/shard_map/ppermute | solution.py:32
  8.1 74.3 %collective-permute-start.10 = (bf16[112,2048]{1,0:T(8,128)(2,1)}, bf16[112,2048]{1,0:T(8,128)(2,1)S(1)}, u32[]{:S(2)}, u32[]{:S(2)}) collective-permute-start(bf16[112,2048]{1,0:T(8,128)(2,1)} %get-tuple-element.18), channel_id=1, source_target_pairs={{0,2},{1,3},{2,0},{3,1},{4,6},{5,7},{6,4},{7,5},{8,10},{9,11},{10,... | collective-permute-start | bytes 1376264 | tf_op jit(solution)/shard_map/ppermute | solution.py:32
  9.0 73.4 %collective-permute-start.9 = (bf16[112,2048]{1,0:T(8,128)(2,1)}, bf16[112,2048]{1,0:T(8,128)(2,1)S(1)}, u32[]{:S(2)}, u32[]{:S(2)}) collective-permute-start(bf16[112,2048]{1,0:T(8,128)(2,1)} %get-tuple-element.16), channel_id=1, source_target_pairs={{0,1},{1,0},{2,3},{3,2},{4,5},{5,4},{6,7},{7,6},{8,9},{9,8},{10,11... | collective-permute-start | bytes 1376264 | tf_op jit(solution)/shard_map/ppermute | solution.py:32
  10.6 97.3 %all-to-all-start = ((bf16[32,8,2,2048]{3,1,2,0:T(8,128)(2,1)}), bf16[32,8,2,2048]{3,1,2,0:T(8,128)(2,1)}, u32[]{:S(2)}, u32[]{:S(2)}) async-start(bf16[32,8,2,2048]{3,1,2,0:T(8,128)(2,1)} %broadcast_in_dim.55), calls=%async_computation | async-start | bytes 4194304 | tf_op jit(solution)/shard_map/all_to_all | solution.py:21
  20.7 69.0 %collective-permute-start = (bf16[2048,224]{0,1:T(8,128)(2,1)}, bf16[2048,224]{0,1:T(8,128)(2,1)}, u32[]{:S(2)}, u32[]{:S(2)}) collective-permute-start(bf16[2048,224]{0,1:T(8,128)(2,1)} %get-tuple-element.14), channel_id=1, source_target_pairs={{0,1},{1,0},{2,3},{3,2},{4,5},{5,4},{6,7},{7,6},{8,9},{9,8},{10,11... | collective-permute-start | bytes 2752520 | tf_op jit(solution)/shard_map/ppermute | solution.py:32
  110.8 3.5 %copy-start = (bf16[4,112,2048]{2,1,0:T(8,128)(2,1)S(1)}, bf16[4,112,2048]{2,1,0:T(8,128)(2,1)}, u32[]{:S(2)}) copy-start(bf16[4,112,2048]{2,1,0:T(8,128)(2,1)} %broadcast_select_fusion.1) | copy-start | bytes 5505028
  112.3 7.7 %collective-permute-start.5 = (f32[64,896]{1,0:T(8,128)S(1)}, f32[64,896]{1,0:T(8,128)S(1)}, u32[]{:S(2)}, u32[]{:S(2)}) collective-permute-start(f32[64,896]{1,0:T(8,128)S(1)} %get-tuple-element.20), channel_id=1, source_target_pairs={{0,3},{1,2},{2,1},{3,0},{4,7},{5,6},{6,5},{7,4},{8,11},{9,10},{10,... | collective-permute-start | bytes 688136 | tf_op jit(solution)/shard_map/ppermute | solution.py:32
  112.4 13.1 %collective-permute-start.4 = (f32[64,896]{1,0:T(8,128)S(1)}, f32[64,896]{1,0:T(8,128)S(1)}, u32[]{:S(2)}, u32[]{:S(2)}) collective-permute-start(f32[64,896]{1,0:T(8,128)S(1)} %get-tuple-element.21), channel_id=1, source_target_pairs={{0,2},{1,3},{2,0},{3,1},{4,6},{5,7},{6,4},{7,5},{8,10},{9,11},{10,... | collective-permute-start | bytes 688136 | tf_op jit(solution)/shard_map/ppermute | solution.py:32
  114.1 11.4 %collective-permute-start.3 = (f32[64,896]{1,0:T(8,128)S(1)}, f32[64,896]{1,0:T(8,128)S(1)}, u32[]{:S(2)}, u32[]{:S(2)}) collective-permute-start(f32[64,896]{1,0:T(8,128)S(1)} %get-tuple-element.19), channel_id=1, source_target_pairs={{0,1},{1,0},{2,3},{3,2},{4,5},{5,4},{6,7},{7,6},{8,9},{9,8},{10,11... | collective-permute-start | bytes 688136 | tf_op jit(solution)/shard_map/ppermute | solution.py:32
  115.0 12.7 %collective-permute-start.14 = (f32[64,448]{1,0:T(8,128)S(1)}, f32[64,448]{1,0:T(8,128)S(1)}, u32[]{:S(2)}, u32[]{:S(2)}) collective-permute-start(f32[64,448]{1,0:T(8,128)S(1)} %get-tuple-element.24), channel_id=1, source_target_pairs={{0,3},{1,2},{2,1},{3,0},{4,7},{5,6},{6,5},{7,4},{8,11},{9,10},{10,... | collective-permute-start | bytes 344072 | tf_op jit(solution)/shard_map/ppermute | solution.py:32
  115.5 15.3 %collective-permute-start.13 = (f32[64,448]{1,0:T(8,128)S(1)}, f32[64,448]{1,0:T(8,128)S(1)}, u32[]{:S(2)}, u32[]{:S(2)}) collective-permute-start(f32[64,448]{1,0:T(8,128)S(1)} %get-tuple-element.23), channel_id=1, source_target_pairs={{0,2},{1,3},{2,0},{3,1},{4,6},{5,7},{6,4},{7,5},{8,10},{9,11},{10,... | collective-permute-start | bytes 344072 | tf_op jit(solution)/shard_map/ppermute | solution.py:32
  120.0 10.8 %collective-permute-start.12 = (f32[64,448]{1,0:T(8,128)S(1)}, f32[64,448]{1,0:T(8,128)S(1)}, u32[]{:S(2)}, u32[]{:S(2)}) collective-permute-start(f32[64,448]{1,0:T(8,128)S(1)} %get-tuple-element.22), channel_id=1, source_target_pairs={{0,1},{1,0},{2,3},{3,2},{4,5},{5,4},{6,7},{7,6},{8,9},{9,8},{10,11... | collective-permute-start | bytes 344072 | tf_op jit(solution)/shard_map/ppermute | solution.py:32
  131.1 4.4 %collective-permute-start.8 = (bf16[64,448]{1,0:T(8,128)(2,1)S(1)}, bf16[64,448]{1,0:T(8,128)(2,1)S(1)}, u32[]{:S(2)}, u32[]{:S(2)}) collective-permute-start(bf16[64,448]{1,0:T(8,128)(2,1)S(1)} %get-tuple-element.26), channel_id=1, source_target_pairs={{0,3},{1,2},{2,1},{3,0},{4,7},{5,6},{6,5},{7,4},{8,11},{9,10},{10,... | collective-permute-start | bytes 172040 | tf_op jit(solution)/shard_map/ppermute | solution.py:32
  131.4 5.5 %collective-permute-start.7 = (bf16[64,448]{1,0:T(8,128)(2,1)S(1)}, bf16[64,448]{1,0:T(8,128)(2,1)S(1)}, u32[]{:S(2)}, u32[]{:S(2)}) collective-permute-start(bf16[64,448]{1,0:T(8,128)(2,1)S(1)} %get-tuple-element.26), channel_id=1, source_target_pairs={{0,2},{1,3},{2,0},{3,1},{4,6},{5,7},{6,4},{7,5},{8,10},{9,11},{10,... | collective-permute-start | bytes 172040 | tf_op jit(solution)/shard_map/ppermute | solution.py:32
  132.6 4.3 %collective-permute-start.6 = (bf16[64,448]{1,0:T(8,128)(2,1)S(1)}, bf16[64,448]{1,0:T(8,128)(2,1)S(1)}, u32[]{:S(2)}, u32[]{:S(2)}) collective-permute-start(bf16[64,448]{1,0:T(8,128)(2,1)S(1)} %get-tuple-element.26), channel_id=1, source_target_pairs={{0,1},{1,0},{2,3},{3,2},{4,5},{5,4},{6,7},{7,6},{8,9},{9,8},{10,11... | collective-permute-start | bytes 172040 | tf_op jit(solution)/shard_map/ppermute | solution.py:32
  141.3 46.3 %all-to-all-start.1 = ((f32[32,8,2048]{2,1,0:T(8,128)}), f32[32,8,2048]{2,1,0:T(8,128)}, u32[]{:S(2)}, u32[]{:S(2)}) async-start(f32[32,8,2048]{2,1,0:T(8,128)} %fusion.13), calls=%async_computation.1 | async-start | bytes 4194304 | tf_op jit(solution)/shard_map/all_to_all | solution.py:27
  151.6 27.0 %collective-permute-start.17 = (bf16[64,896]{1,0:T(8,128)(2,1)S(1)}, bf16[64,896]{1,0:T(8,128)(2,1)S(1)}, u32[]{:S(2)}, u32[]{:S(2)}) collective-permute-start(bf16[64,896]{1,0:T(8,128)(2,1)S(1)} %pad_maximum_fusion.7), channel_id=1, source_target_pairs={{0,3},{1,2},{2,1},{3,0},{4,7},{5,6},{6,5},{7,4},{8,11},{9,10},{10,... | collective-permute-start | bytes 344072 | tf_op jit(solution)/shard_map/ppermute | solution.py:32
  152.4 29.5 %collective-permute-start.16 = (bf16[64,896]{1,0:T(8,128)(2,1)S(1)}, bf16[64,896]{1,0:T(8,128)(2,1)S(1)}, u32[]{:S(2)}, u32[]{:S(2)}) collective-permute-start(bf16[64,896]{1,0:T(8,128)(2,1)S(1)} %pad_maximum_fusion.7), channel_id=1, source_target_pairs={{0,2},{1,3},{2,0},{3,1},{4,6},{5,7},{6,4},{7,5},{8,10},{9,11},{10,... | collective-permute-start | bytes 344072 | tf_op jit(solution)/shard_map/ppermute | solution.py:32
  153.1 28.8 %collective-permute-start.15 = (bf16[64,896]{1,0:T(8,128)(2,1)S(1)}, bf16[64,896]{1,0:T(8,128)(2,1)S(1)}, u32[]{:S(2)}, u32[]{:S(2)}) collective-permute-start(bf16[64,896]{1,0:T(8,128)(2,1)S(1)} %pad_maximum_fusion.7), channel_id=1, source_target_pairs={{0,1},{1,0},{2,3},{3,2},{4,5},{5,4},{6,7},{7,6},{8,9},{9,8},{10,11... | collective-permute-start | bytes 344072 | tf_op jit(solution)/shard_map/ppermute | solution.py:32
  187.6 39.0 %all-to-all-start.2 = ((f32[32,8,2048]{2,1,0:T(8,128)}), f32[32,8,2048]{2,1,0:T(8,128)}, u32[]{:S(2)}, u32[]{:S(2)}) async-start(f32[32,8,2048]{2,1,0:T(8,128)} %fusion), calls=%async_computation.2 | async-start | bytes 4194304 | tf_op jit(solution)/shard_map/all_to_all | solution.py:27
  (6 other events, 11.0 us)

commit v3 on v2

--- a/solution.py
+++ b/solution.py
@@ -36,23 +36,30 @@
     return lax.dynamic_slice_in_dim(x, index * size, size, axis)
 
 
+def place(pieces, me, axis):
+    shape = list(pieces[0].shape)
+    shape.insert(axis, len(pieces))
+    out = jnp.zeros(shape, pieces[0].dtype)
+    for k, p in enumerate(pieces):
+        start = [0] * len(shape)
+        start[axis] = me ^ k
+        out = lax.dynamic_update_slice(out, jnp.expand_dims(p, axis), start)
+    return out
+
+
 def col_scatter(x, axis, n):
     me = lax.axis_index("col")
     size = x.shape[axis] // n
     got = [piece(x, me, size, axis)]
     for k in range(1, n):
         got.append(swap(piece(x, me ^ k, size, axis), k, n))
-    stacked = jnp.stack(got)
-    order = jnp.arange(n, dtype=jnp.int32) ^ me
-    return jnp.take(stacked, order, axis=0)
+    return got
 
 
 def col_gather(x, n):
     me = lax.axis_index("col")
     got = [x] + [swap(x, k, n) for k in range(1, n)]
-    stacked = jnp.stack(got)
-    order = jnp.arange(n, dtype=jnp.int32) ^ me
-    return jnp.take(stacked, order, axis=0)
+    return place(got, me, 0)
 
 
 def col_reduce(x, n):
@@ -67,45 +74,54 @@
 def shards(tokens, gate_weight, up_weight, down_weight, out_grad):
     n_row = lax.axis_size("row")
     n_col = lax.axis_size("col")
+    me = lax.axis_index("col")
     unit = gate_weight.shape[1]
     joined = jnp.concatenate([gate_weight, up_weight], axis=1)
-    gu_stack = col_scatter(joined, 0, n_col)
-    feat = gu_stack.shape[1]
-    gu_block = gu_stack.reshape(n_col, feat, 2, unit)
-    gate_block = gu_block[:, :, 0].transpose(1, 0, 2).reshape(feat, n_col * unit)
-    up_block = gu_block[:, :, 1].transpose(1, 0, 2).reshape(feat, n_col * unit)
-    down_block = col_scatter(down_weight, 1, n_col).reshape(n_col * unit, feat)
+    gu_rel = col_scatter(joined, 0, n_col)
+    down_rel = col_scatter(down_weight, 1, n_col)
 
     both = gather_rows(jnp.stack([tokens, out_grad], axis=1), "row", n_row)
     full_tokens = both[:, 0]
     grad_full = both[:, 1]
+    count = full_tokens.shape[0]
 
-    gu_w = jnp.concatenate([gate_block, up_block], axis=1)
-    gu_part = jnp.dot(full_tokens, gu_w, preferred_element_type=jnp.float32)
+    gu_part = place([jnp.dot(full_tokens, w, preferred_element_type=jnp.float32) for w in gu_rel], me, 1)
     gu_sum = col_reduce(gu_part, n_col)
-    gate_sum = gu_sum[:, : n_col * unit]
-    up_sum = gu_sum[:, n_col * unit :]
+    share = gu_sum.shape[0]
+    gate_sum = gu_sum[:, :, :unit].reshape(share, n_col * unit)
+    up_sum = gu_sum[:, :, unit:].reshape(share, n_col * unit)
     sig = jax.nn.sigmoid(gate_sum)
     hidden_share = (gate_sum * sig * up_sum).astype(jnp.bfloat16)
-    hidden = col_gather(hidden_share, n_col).reshape(-1, n_col * unit)
+    hidden = col_gather(hidden_share, n_col).reshape(count, n_col * unit)
 
-    term = jnp.dot(hidden, down_block, preferred_element_type=jnp.float32)
+    term = None
+    for k, w in enumerate(down_rel):
+        h = lax.dynamic_slice_in_dim(hidden, (me ^ k) * unit, unit, 1)
+        t = jnp.dot(h, w, preferred_element_type=jnp.float32)
+        term = t if term is None else term + t
     output = reduce_rows(term, "row", n_row)
 
-    dh_part = contract_last(grad_full, down_block)
-    hidden_grad = col_reduce(dh_part, n_col)
+    dh_part = place([contract_last(grad_full, w) for w in down_rel], me, 1)
+    hidden_grad = col_reduce(dh_part, n_col).reshape(share, n_col * unit)
     grad_down = contract_first(hidden, grad_full).astype(jnp.bfloat16)
 
     gate_grad = (hidden_grad * up_sum * sig * (1.0 + gate_sum * (1.0 - sig))).astype(jnp.bfloat16)
     up_grad = (hidden_grad * gate_sum * sig).astype(jnp.bfloat16)
-    grads = col_gather(jnp.concatenate([gate_grad, up_grad], axis=1), n_col)
-    grads = grads.reshape(-1, 2 * n_col * unit)
+    joined_grad = jnp.concatenate(
+        [gate_grad.reshape(share, n_col, unit), up_grad.reshape(share, n_col, unit)], axis=2
+    )
+    grads = col_gather(joined_grad, n_col).reshape(count, n_col, 2 * unit)
 
-    in_part = contract_last(grads, gu_w)
+    in_part = None
+    for k, w in enumerate(gu_rel):
+        g = lax.dynamic_index_in_dim(grads, me ^ k, 1, keepdims=False)
+        t = contract_last(g, w)
+        in_part = t if in_part is None else in_part + t
     input_grad = reduce_rows(in_part, "row", n_row)
-    grad_gu = contract_first(full_tokens, grads)
-    grad_gate = grad_gu[:, : n_col * unit].astype(jnp.bfloat16)
-    grad_up = grad_gu[:, n_col * unit :].astype(jnp.bfloat16)
+    grad_gu = contract_first(full_tokens, grads.reshape(count, n_col * 2 * unit))
+    grad_gu = grad_gu.reshape(-1, n_col, 2 * unit)
+    grad_gate = grad_gu[:, :, :unit].reshape(-1, n_col * unit).astype(jnp.bfloat16)
+    grad_up = grad_gu[:, :, unit:].reshape(-1, n_col * unit).astype(jnp.bfloat16)
     return (output, input_grad, grad_gate, grad_up, grad_down)
 
 

time: 232 us -> 209 us (0.901)
  waiting for transfers between devices: 129 us -> 112 us
  matrix products: 13.8 us -> 26.6 us
  local copies, waits for them, and re-layouts: 29.4 us -> 19.3 us
  other arithmetic: 15.7 us -> 6.58 us
    ppermute x18, waiting for transfers between devices: 107 us -> 48.2 us  [swap(): return lax.ppermute(x, 'col', perm=[(i, i ^ k) for i in range(n)])]
    all_to_all x2, waiting for transfers between devices: 22.2 us -> 44.1 us  [reduce_rows(): got = lax.all_to_all(pieces, axis, split_axis=0, concat_axis=0, tiled=True)]
    all_to_all x1, waiting for transfers between devices: 0.01 us -> 19.7 us  [gather_rows(): got = lax.all_to_all(spread, axis, split_axis=0, concat_axis=0, tiled=True)]
    gather x4 -> x0, local copies, waits for them, and re-layouts: 7.72 us -> none  [the longest x2 6.53 us: col_scatter(): return jnp.take(stacked, order, axis=0)]
    dot_general x2 -> x8, matrix products: 5.03 us -> 12 us  [the longest x4 6.6 us: shards(): jnp.dot(full_tokens, w, preferred_element_type=jnp.float32)]
    dot_general x2 -> x8, matrix products: 5.72 us -> 11.6 us  [contract_last(): lax.dot_general(left, right, (((1,), (1,)), ((), ())), preferred_element_...]
    reshape x2 -> x4, local copies, waits for them, and re-layouts: 6.23 us -> 0.47 us  [the longest x2 0.23 us: shards(): gate_sum = gu_sum[:, :, :unit].reshape(share, n_col * unit)]
    select_n x5 -> x0, other arithmetic: 5.64 us -> none  [the longest x2 5.42 us: col_scatter(): return jnp.take(stacked, order, axis=0)]
  transfers between devices with their start and end apart: 21 -> 21, of which waited for: 10 -> 11; matrix products, arithmetic and copies ran while one was open for 19% -> 23% of each run, Pallas kernels for 0% -> 0%
where the time goes in v3:
time: 209 us; the launch traced here: 208 us
  waiting for transfers between devices  112 us (54%)
  starting transfers between devices  42 us (20%)
  matrix products  26.6 us (13%)
  local copies, waits for them, and re-layouts  19.3 us (9%)
  other arithmetic  6.58 us (3%)
    ppermute x18, waiting for transfers between devices, swap(): return lax.ppermute(x, 'col', perm=[(i, i ^ k) for i in range(n)])  48.2 us
    all_to_all x2, waiting for transfers between devices, reduce_rows(): got = lax.all_to_all(pieces, axis, split_axis=0, concat_axis=0, tiled=True)  44.1 us
    all_to_all x1, waiting for transfers between devices, gather_rows(): got = lax.all_to_all(spread, axis, split_axis=0, concat_axis=0, tiled=True)  19.7 us
    all_to_all x2, starting transfers between devices, reduce_rows(): got = lax.all_to_all(pieces, axis, split_axis=0, concat_axis=0, tiled=True)  16.2 us
    ppermute x18, starting transfers between devices, swap(): return lax.ppermute(x, 'col', perm=[(i, i ^ k) for i in range(n)])  15.7 us
    dot_general x8, matrix products, contract_last(): lax.dot_general(left, right, (((1,), (1,)), ((), ())), preferred_element_...  11.6 us
    all_to_all x1, starting transfers between devices, gather_rows(): got = lax.all_to_all(spread, axis, split_axis=0, concat_axis=0, tiled=True)  10.2 us
    dot_general x4, matrix products, shards(): jnp.dot(full_tokens, w, preferred_element_type=jnp.float32)  6.6 us
  transfers between devices with their start and end apart: 21, of which 11 were waited for; matrix products, arithmetic and copies ran while one was open for 23% of the time, Pallas kernels for 0%

profile of v3, /device:TPU:8, one launch (start us, length us, event | category | flops | bytes accessed | tf_op | source)
XLA Modules:
  0.0 207.6 jit_solution(13056755435723356855)
XLA Ops:
  3.0 10.2 %all-to-all-start = ((bf16[32,8,2,2048]{3,1,2,0:T(8,128)(2,1)}), bf16[32,8,2,2048]{3,1,2,0:T(8,128)(2,1)}, u32[]{:S(2)}, u32[]{:S(2)}) async-start(bf16[32,8,2,2048]{3,1,2,0:T(8,128)(2,1)} %broadcast_in_dim.66), calls=%async_computation | async-start | bytes 4194304 | tf_op jit(solution)/shard_map/all_to_all | solution.py:21
  14.6 2.8 %constant_dynamic-update-slice_fusion = bf16[8192,224]{0,1:T(8,128)(2,1)} fusion(bf16[8192,224]{0,1:T(8,128)(2,1)} %constant_dynamic-update-slice_fusion.1, bf16[8192,112]{0,1:T(8,128)(2,1)} %param.7), kind=kLoop, calls=%fused_computation.97 | loop fusion | bytes 3670016 | tf_op jit(solution)/shard_map/concatenate | solution.py:79
  17.4 3.4 %constant_dynamic-slice_fusion.9 = (bf16[2048,224]{0,1:T(8,128)(2,1)S(1)}, bf16[2048,224]{0,1:T(8,128)(2,1)}, bf16[2048,224]{0,1:T(8,128)(2,1)}) fusion(bf16[8192,224]{0,1:T(8,128)(2,1)} %constant_dynamic-update-slice_fusion, s32[]{:T(128)S(6)} %select_n.79, s32[]{:T(128)S(6)} %select_n.77, s32[]{:T(128)S(6)} %select_n.75), kind=kLoop, calls=%fused_computation.92 | loop fusion | bytes 5505036 | tf_op jit(solution)/shard_map/dynamic_slice | solution.py:36
  25.1 19.7 %all-to-all-done = bf16[32,8,2,2048]{3,1,2,0:T(8,128)(2,1)} async-done(((bf16[32,8,2,2048]{3,1,2,0:T(8,128)(2,1)}), bf16[32,8,2,2048]{3,1,2,0:T(8,128)(2,1)}, u32[]{:S(2)}, u32[]{:S(2)}) %all-to-all-start) | async-done | bytes 2097184 | tf_op jit(solution)/shard_map/all_to_all | solution.py:21
  50.1 8.7 %collective-permute-done.1 = bf16[2048,224]{0,1:T(8,128)(2,1)} collective-permute-done((bf16[2048,224]{0,1:T(8,128)(2,1)}, bf16[2048,224]{0,1:T(8,128)(2,1)}, u32[]{:S(2)}, u32[]{:S(2)}) %collective-permute-start.1) | collective-permute-done | bytes 917536 | tf_op jit(solution)/shard_map/ppermute | solution.py:32
  60.4 15.8 %collective-permute-done.2 = bf16[2048,224]{0,1:T(8,128)(2,1)} collective-permute-done((bf16[2048,224]{0,1:T(8,128)(2,1)S(1)}, bf16[2048,224]{0,1:T(8,128)(2,1)}, u32[]{:S(2)}, u32[]{:S(2)}) %collective-permute-start.2) | collective-permute-done | bytes 917536 | tf_op jit(solution)/shard_map/ppermute | solution.py:32
  77.9 2.1 %collective-permute-start.3 = (f32[64,4,224]{2,0,1:T(8,128)S(1)}, f32[64,4,224]{2,0,1:T(8,128)S(1)}, u32[]{:S(2)}, u32[]{:S(2)}) collective-permute-start(f32[64,4,224]{2,0,1:T(8,128)S(1)} %get-tuple-element.15), channel_id=1, source_target_pairs={{0,1},{1,0},{2,3},{3,2},{4,5},{5,4},{6,7},{7,6},{8,9},{9,8},{10,11... | collective-permute-start | bytes 688136 | tf_op jit(solution)/shard_map/ppermute | solution.py:32
  81.6 1.8 collective-permute-start.4
  84.8 3.3 %collective-permute-done.10 = bf16[112,2048]{1,0:T(8,128)(2,1)S(1)} collective-permute-done((bf16[112,2048]{1,0:T(8,128)(2,1)}, bf16[112,2048]{1,0:T(8,128)(2,1)S(1)}, u32[]{:S(2)}, u32[]{:S(2)}) %collective-permute-start.10) | collective-permute-done | bytes 458784 | tf_op jit(solution)/shard_map/ppermute | solution.py:32
  88.6 7.2 %collective-permute-done.11 = bf16[112,2048]{1,0:T(8,128)(2,1)S(1)} collective-permute-done((bf16[112,2048]{1,0:T(8,128)(2,1)S(1)}, bf16[112,2048]{1,0:T(8,128)(2,1)S(1)}, u32[]{:S(2)}, u32[]{:S(2)}) %collective-permute-start.11) | collective-permute-done | bytes 458784 | tf_op jit(solution)/shard_map/ppermute | solution.py:32
  96.2 2.4 %collective-permute-start.12 = (f32[64,4,112]{2,0,1:T(8,128)S(1)}, f32[64,4,112]{2,0,1:T(8,128)S(1)}, u32[]{:S(2)}, u32[]{:S(2)}) collective-permute-start(f32[64,4,112]{2,0,1:T(8,128)S(1)} %get-tuple-element.18), channel_id=1, source_target_pairs={{0,1},{1,0},{2,3},{3,2},{4,5},{5,4},{6,7},{7,6},{8,9},{9,8},{10,11... | collective-permute-start | bytes 344072 | tf_op jit(solution)/shard_map/ppermute | solution.py:32
  101.4 7.8 %collective-permute-done.4 = f32[64,4,224]{2,0,1:T(8,128)S(1)} collective-permute-done((f32[64,4,224]{2,0,1:T(8,128)S(1)}, f32[64,4,224]{2,0,1:T(8,128)S(1)}, u32[]{:S(2)}, u32[]{:S(2)}) %collective-permute-start.4) | collective-permute-done | bytes 229408 | tf_op jit(solution)/shard_map/ppermute | solution.py:32
  109.8 3.9 %collective-permute-done.13 = f32[64,4,112]{2,0,1:T(8,128)S(1)} collective-permute-done((f32[64,4,112]{2,0,1:T(8,128)S(1)}, f32[64,4,112]{2,0,1:T(8,128)S(1)}, u32[]{:S(2)}, u32[]{:S(2)}) %collective-permute-start.13) | collective-permute-done | bytes 114720 | tf_op jit(solution)/shard_map/ppermute | solution.py:32
  118.0 1.9 collective-permute-start.17
  123.5 1.8 fusion.1
  125.4 11.4 %all-to-all-start.1 = ((f32[32,8,2048]{2,1,0:T(8,128)}), f32[32,8,2048]{2,1,0:T(8,128)}, u32[]{:S(2)}, u32[]{:S(2)}) async-start(f32[32,8,2048]{2,1,0:T(8,128)} %fusion.1), calls=%async_computation.1 | async-start | bytes 4194304 | tf_op jit(solution)/shard_map/all_to_all | solution.py:27
  145.1 3.0 %fusion.3 = f32[32,8,2048]{2,1,0:T(8,128)} fusion(f32[256,2048]{1,0:T(8,128)S(1)} %fusion.27, f32[256,2048]{1,0:T(8,128)S(1)} %convolution_add_fusion.3, bf16[2048,224]{0,1:T(8,128)(2,1)} %collective-permute-done.1, bf16[256,4,224]{2,0,1:T(8,128)(2,1)S(1)} %bitcast.134, s32[]{:T(128)S(6)} %select_n.78), kind=kOutput, calls=%fused_computation.8 | convolution fusion | flops 235929600 | bytes 7340036 | tf_op jit(solution)/shard_map/dot_general | solution.py:8
  148.1 21.7 %all-to-all-done.1 = f32[32,8,2048]{2,1,0:T(8,128)} async-done(((f32[32,8,2048]{2,1,0:T(8,128)}), f32[32,8,2048]{2,1,0:T(8,128)}, u32[]{:S(2)}, u32[]{:S(2)}) %all-to-all-start.1) | async-done | bytes 2097184 | tf_op jit(solution)/shard_map/all_to_all | solution.py:27
  169.8 4.8 %all-to-all-start.2 = ((f32[32,8,2048]{2,1,0:T(8,128)}), f32[32,8,2048]{2,1,0:T(8,128)}, u32[]{:S(2)}, u32[]{:S(2)}) async-start(f32[32,8,2048]{2,1,0:T(8,128)} %fusion.3), calls=%async_computation.2 | async-start | bytes 4194304 | tf_op jit(solution)/shard_map/all_to_all | solution.py:27
  174.6 1.9 convolution_convert_fusion.1
  178.2 2.3 %fusion.54 = (bf16[2048,4,112]{0,2,1:T(8,128)(2,1)}, bf16[2048,4,112]{0,2,1:T(8,128)(2,1)}) fusion(bf16[2048,4,224]{0,2,1:T(8,128)(2,1)S(1)} %convolution_convert_fusion), kind=kLoop, calls=%fused_computation.100 | loop fusion | bytes 7340032 | tf_op jit(solution)/shard_map/slice | solution.py:124
  180.5 2.3 %reduce_sum.18 = f32[8,2048]{1,0:T(8,128)} reduce(f32[32,8,2048]{2,1,0:T(8,128)} %all-to-all-done.1, f32[]{:T(128)} %constant.16.clone.1), dimensions={0}, to_apply=%region_0.0 | reduce | flops 507904 | bytes 2162692 | tf_op jit(solution)/shard_map/reduce_sum | solution.py:28
  182.8 22.5 %all-to-all-done.2 = f32[32,8,2048]{2,1,0:T(8,128)} async-done(((f32[32,8,2048]{2,1,0:T(8,128)}), f32[32,8,2048]{2,1,0:T(8,128)}, u32[]{:S(2)}, u32[]{:S(2)}) %all-to-all-start.2) | async-done | bytes 2097184 | tf_op jit(solution)/shard_map/all_to_all | solution.py:27
  205.3 2.3 %reduce_sum.19 = f32[8,2048]{1,0:T(8,128)} reduce(f32[32,8,2048]{2,1,0:T(8,128)} %all-to-all-done.2, f32[]{:T(128)} %constant.16.clone.1), dimensions={0}, to_apply=%region_1.2 | reduce | flops 507904 | bytes 2162692 | tf_op jit(solution)/shard_map/reduce_sum | solution.py:28
  (84 shorter events, 41.5 us)
Async XLA Ops:
  3.0 10.2 %copy-start.1 = (bf16[8192,112]{0,1:T(8,128)(2,1)S(1)}, bf16[8192,112]{0,1:T(8,128)(2,1)}, u32[]{:S(2)}) copy-start(bf16[8192,112]{0,1:T(8,128)(2,1)} %param.6) | copy-start | bytes 5505028
  3.0 41.8 %all-to-all-start = ((bf16[32,8,2,2048]{3,1,2,0:T(8,128)(2,1)}), bf16[32,8,2,2048]{3,1,2,0:T(8,128)(2,1)}, u32[]{:S(2)}, u32[]{:S(2)}) async-start(bf16[32,8,2,2048]{3,1,2,0:T(8,128)(2,1)} %broadcast_in_dim.66), calls=%async_computation | async-start | bytes 4194304 | tf_op jit(solution)/shard_map/all_to_all | solution.py:21
  17.4 5.3 %copy-start = (bf16[112,8192]{1,0:T(8,128)(2,1)S(1)}, bf16[112,8192]{1,0:T(8,128)(2,1)}, u32[]{:S(2)}) copy-start(bf16[112,8192]{1,0:T(8,128)(2,1)} %param.8) | copy-start | bytes 5505028
  20.8 27.5 %collective-permute-start = (bf16[2048,224]{0,1:T(8,128)(2,1)}, bf16[2048,224]{0,1:T(8,128)(2,1)}, u32[]{:S(2)}, u32[]{:S(2)}) collective-permute-start(bf16[2048,224]{0,1:T(8,128)(2,1)} %get-tuple-element.11), channel_id=1, source_target_pairs={{0,1},{1,0},{2,3},{3,2},{4,5},{5,4},{6,7},{7,6},{8,9},{9,8},{10,11... | collective-permute-start | bytes 2752520 | tf_op jit(solution)/shard_map/ppermute | solution.py:32
  20.8 37.9 %collective-permute-start.1 = (bf16[2048,224]{0,1:T(8,128)(2,1)}, bf16[2048,224]{0,1:T(8,128)(2,1)}, u32[]{:S(2)}, u32[]{:S(2)}) collective-permute-start(bf16[2048,224]{0,1:T(8,128)(2,1)} %get-tuple-element.10), channel_id=1, source_target_pairs={{0,2},{1,3},{2,0},{3,1},{4,6},{5,7},{6,4},{7,5},{8,10},{9,11},{10,... | collective-permute-start | bytes 2752520 | tf_op jit(solution)/shard_map/ppermute | solution.py:32
  22.2 54.0 %collective-permute-start.2 = (bf16[2048,224]{0,1:T(8,128)(2,1)S(1)}, bf16[2048,224]{0,1:T(8,128)(2,1)}, u32[]{:S(2)}, u32[]{:S(2)}) collective-permute-start(bf16[2048,224]{0,1:T(8,128)(2,1)S(1)} %get-tuple-element.9), channel_id=1, source_target_pairs={{0,3},{1,2},{2,1},{3,0},{4,7},{5,6},{6,5},{7,4},{8,11},{9,10},{10,... | collective-permute-start | bytes 2752520 | tf_op jit(solution)/shard_map/ppermute | solution.py:32
  23.8 64.4 %collective-permute-start.10 = (bf16[112,2048]{1,0:T(8,128)(2,1)}, bf16[112,2048]{1,0:T(8,128)(2,1)S(1)}, u32[]{:S(2)}, u32[]{:S(2)}) collective-permute-start(bf16[112,2048]{1,0:T(8,128)(2,1)} %get-tuple-element.12), channel_id=1, source_target_pairs={{0,2},{1,3},{2,0},{3,1},{4,6},{5,7},{6,4},{7,5},{8,10},{9,11},{10,... | collective-permute-start | bytes 1376264 | tf_op jit(solution)/shard_map/ppermute | solution.py:32
  25.1 56.4 %collective-permute-start.9 = (bf16[112,2048]{1,0:T(8,128)(2,1)}, bf16[112,2048]{1,0:T(8,128)(2,1)}, u32[]{:S(2)}, u32[]{:S(2)}) collective-permute-start(bf16[112,2048]{1,0:T(8,128)(2,1)} %get-tuple-element.13), channel_id=1, source_target_pairs={{0,1},{1,0},{2,3},{3,2},{4,5},{5,4},{6,7},{7,6},{8,9},{9,8},{10,11... | collective-permute-start | bytes 1376264 | tf_op jit(solution)/shard_map/ppermute | solution.py:32
  48.3 47.4 %collective-permute-start.11 = (bf16[112,2048]{1,0:T(8,128)(2,1)S(1)}, bf16[112,2048]{1,0:T(8,128)(2,1)S(1)}, u32[]{:S(2)}, u32[]{:S(2)}) collective-permute-start(bf16[112,2048]{1,0:T(8,128)(2,1)S(1)} %copy-done.4), channel_id=1, source_target_pairs={{0,3},{1,2},{2,1},{3,0},{4,7},{5,6},{6,5},{7,4},{8,11},{9,10},{10,... | collective-permute-start | bytes 1376264 | tf_op jit(solution)/shard_map/ppermute | solution.py:32
  77.9 20.7 %collective-permute-start.3 = (f32[64,4,224]{2,0,1:T(8,128)S(1)}, f32[64,4,224]{2,0,1:T(8,128)S(1)}, u32[]{:S(2)}, u32[]{:S(2)}) collective-permute-start(f32[64,4,224]{2,0,1:T(8,128)S(1)} %get-tuple-element.15), channel_id=1, source_target_pairs={{0,1},{1,0},{2,3},{3,2},{4,5},{5,4},{6,7},{7,6},{8,9},{9,8},{10,11... | collective-permute-start | bytes 688136 | tf_op jit(solution)/shard_map/ppermute | solution.py:32
  80.0 21.3 %collective-permute-start.5 = (f32[64,4,224]{2,0,1:T(8,128)S(1)}, f32[64,4,224]{2,0,1:T(8,128)S(1)}, u32[]{:S(2)}, u32[]{:S(2)}) collective-permute-start(f32[64,4,224]{2,0,1:T(8,128)S(1)} %get-tuple-element.16), channel_id=1, source_target_pairs={{0,3},{1,2},{2,1},{3,0},{4,7},{5,6},{6,5},{7,4},{8,11},{9,10},{10,... | collective-permute-start | bytes 688136 | tf_op jit(solution)/shard_map/ppermute | solution.py:32
  81.6 27.6 %collective-permute-start.4 = (f32[64,4,224]{2,0,1:T(8,128)S(1)}, f32[64,4,224]{2,0,1:T(8,128)S(1)}, u32[]{:S(2)}, u32[]{:S(2)}) collective-permute-start(f32[64,4,224]{2,0,1:T(8,128)S(1)} %get-tuple-element.17), channel_id=1, source_target_pairs={{0,2},{1,3},{2,0},{3,1},{4,6},{5,7},{6,4},{7,5},{8,10},{9,11},{10,... | collective-permute-start | bytes 688136 | tf_op jit(solution)/shard_map/ppermute | solution.py:32
  95.7 18.1 %copy-start.2 = (bf16[112,2048]{1,0:T(8,128)(2,1)}, bf16[112,2048]{1,0:T(8,128)(2,1)S(1)}, u32[]{:S(2)}) copy-start(bf16[112,2048]{1,0:T(8,128)(2,1)S(1)} %collective-permute-done.11) | copy-start | bytes 1376260
  96.2 13.1 %collective-permute-start.12 = (f32[64,4,112]{2,0,1:T(8,128)S(1)}, f32[64,4,112]{2,0,1:T(8,128)S(1)}, u32[]{:S(2)}, u32[]{:S(2)}) collective-permute-start(f32[64,4,112]{2,0,1:T(8,128)S(1)} %get-tuple-element.18), channel_id=1, source_target_pairs={{0,1},{1,0},{2,3},{3,2},{4,5},{5,4},{6,7},{7,6},{8,9},{9,8},{10,11... | collective-permute-start | bytes 344072 | tf_op jit(solution)/shard_map/ppermute | solution.py:32
  98.6 11.1 %collective-permute-start.14 = (f32[64,4,112]{2,0,1:T(8,128)S(1)}, f32[64,4,112]{2,0,1:T(8,128)S(1)}, u32[]{:S(2)}, u32[]{:S(2)}) collective-permute-start(f32[64,4,112]{2,0,1:T(8,128)S(1)} %get-tuple-element.19), channel_id=1, source_target_pairs={{0,3},{1,2},{2,1},{3,0},{4,7},{5,6},{6,5},{7,4},{8,11},{9,10},{10,... | collective-permute-start | bytes 344072 | tf_op jit(solution)/shard_map/ppermute | solution.py:32
  98.7 15.1 %collective-permute-start.13 = (f32[64,4,112]{2,0,1:T(8,128)S(1)}, f32[64,4,112]{2,0,1:T(8,128)S(1)}, u32[]{:S(2)}, u32[]{:S(2)}) collective-permute-start(f32[64,4,112]{2,0,1:T(8,128)S(1)} %get-tuple-element.20), channel_id=1, source_target_pairs={{0,2},{1,3},{2,0},{3,1},{4,6},{5,7},{6,4},{7,5},{8,10},{9,11},{10,... | collective-permute-start | bytes 344072 | tf_op jit(solution)/shard_map/ppermute | solution.py:32
  114.7 5.2 %collective-permute-start.8 = (bf16[64,448]{1,0:T(8,128)(2,1)S(1)}, bf16[64,448]{1,0:T(8,128)(2,1)S(1)}, u32[]{:S(2)}, u32[]{:S(2)}) collective-permute-start(bf16[64,448]{1,0:T(8,128)(2,1)S(1)} %multiply_convert_fusion.2), channel_id=1, source_target_pairs={{0,3},{1,2},{2,1},{3,0},{4,7},{5,6},{6,5},{7,4},{8,11},{9,10},{10,... | collective-permute-start | bytes 172040 | tf_op jit(solution)/shard_map/ppermute | solution.py:32
  114.8 5.1 %collective-permute-start.7 = (bf16[64,448]{1,0:T(8,128)(2,1)S(1)}, bf16[64,448]{1,0:T(8,128)(2,1)S(1)}, u32[]{:S(2)}, u32[]{:S(2)}) collective-permute-start(bf16[64,448]{1,0:T(8,128)(2,1)S(1)} %multiply_convert_fusion.2), channel_id=1, source_target_pairs={{0,2},{1,3},{2,0},{3,1},{4,6},{5,7},{6,4},{7,5},{8,10},{9,11},{10,... | collective-permute-start | bytes 172040 | tf_op jit(solution)/shard_map/ppermute | solution.py:32
  115.4 2.6 %collective-permute-start.6 = (bf16[64,448]{1,0:T(8,128)(2,1)S(1)}, bf16[64,448]{1,0:T(8,128)(2,1)S(1)}, u32[]{:S(2)}, u32[]{:S(2)}) collective-permute-start(bf16[64,448]{1,0:T(8,128)(2,1)S(1)} %multiply_convert_fusion.2), channel_id=1, source_target_pairs={{0,1},{1,0},{2,3},{3,2},{4,5},{5,4},{6,7},{7,6},{8,9},{9,8},{10,11... | collective-permute-start | bytes 172040 | tf_op jit(solution)/shard_map/ppermute | solution.py:32
  117.4 20.7 %collective-permute-start.16 = (bf16[64,4,224]{2,0,1:T(8,128)(2,1)}, bf16[64,4,224]{2,0,1:T(8,128)(2,1)}, u32[]{:S(2)}, u32[]{:S(2)}) collective-permute-start(bf16[64,4,224]{2,0,1:T(8,128)(2,1)} %get-tuple-element.24), channel_id=1, source_target_pairs={{0,2},{1,3},{2,0},{3,1},{4,6},{5,7},{6,4},{7,5},{8,10},{9,11},{10,... | collective-permute-start | bytes 344072 | tf_op jit(solution)/shard_map/ppermute | solution.py:32
  117.7 19.4 %collective-permute-start.15 = (bf16[64,4,224]{2,0,1:T(8,128)(2,1)}, bf16[64,4,224]{2,0,1:T(8,128)(2,1)}, u32[]{:S(2)}, u32[]{:S(2)}) collective-permute-start(bf16[64,4,224]{2,0,1:T(8,128)(2,1)} %get-tuple-element.24), channel_id=1, source_target_pairs={{0,1},{1,0},{2,3},{3,2},{4,5},{5,4},{6,7},{7,6},{8,9},{9,8},{10,11... | collective-permute-start | bytes 344072 | tf_op jit(solution)/shard_map/ppermute | solution.py:32
  118.0 21.2 %collective-permute-start.17 = (bf16[64,4,224]{2,0,1:T(8,128)(2,1)}, bf16[64,4,224]{2,0,1:T(8,128)(2,1)}, u32[]{:S(2)}, u32[]{:S(2)}) collective-permute-start(bf16[64,4,224]{2,0,1:T(8,128)(2,1)} %get-tuple-element.24), channel_id=1, source_target_pairs={{0,3},{1,2},{2,1},{3,0},{4,7},{5,6},{6,5},{7,4},{8,11},{9,10},{10,... | collective-permute-start | bytes 344072 | tf_op jit(solution)/shard_map/ppermute | solution.py:32
  125.4 44.4 %all-to-all-start.1 = ((f32[32,8,2048]{2,1,0:T(8,128)}), f32[32,8,2048]{2,1,0:T(8,128)}, u32[]{:S(2)}, u32[]{:S(2)}) async-start(f32[32,8,2048]{2,1,0:T(8,128)} %fusion.1), calls=%async_computation.1 | async-start | bytes 4194304 | tf_op jit(solution)/shard_map/all_to_all | solution.py:27
  169.8 35.5 %all-to-all-start.2 = ((f32[32,8,2048]{2,1,0:T(8,128)}), f32[32,8,2048]{2,1,0:T(8,128)}, u32[]{:S(2)}, u32[]{:S(2)}) async-start(f32[32,8,2048]{2,1,0:T(8,128)} %fusion.3), calls=%async_computation.2 | async-start | bytes 4194304 | tf_op jit(solution)/shard_map/all_to_all | solution.py:27
  (2 other events, 3.4 us)

commit v4 on v3

--- a/solution.py
+++ b/solution.py
@@ -77,10 +77,15 @@
     me = lax.axis_index("col")
     unit = gate_weight.shape[1]
     joined = jnp.concatenate([gate_weight, up_weight], axis=1)
-    gu_rel = col_scatter(joined, 0, n_col)
-    down_rel = col_scatter(down_weight, 1, n_col)
+    feat = joined.shape[0] // n_col
+    gu_out = [piece(joined, me ^ k, feat, 0) for k in range(n_col)]
+    down_out = [piece(down_weight, me ^ k, feat, 1) for k in range(n_col)]
+    pair = jnp.stack([tokens, out_grad], axis=1)
+    gu_out, down_out, pair = lax.optimization_barrier((gu_out, down_out, pair))
+    gu_rel = [gu_out[0]] + [swap(gu_out[k], k, n_col) for k in range(1, n_col)]
+    down_rel = [down_out[0]] + [swap(down_out[k], k, n_col) for k in range(1, n_col)]
 
-    both = gather_rows(jnp.stack([tokens, out_grad], axis=1), "row", n_row)
+    both = gather_rows(pair, "row", n_row)
     full_tokens = both[:, 0]
     grad_full = both[:, 1]
     count = full_tokens.shape[0]

time: 209 us -> 223 us (1.067)
  waiting for transfers between devices: 112 us -> 124 us
  local copies, waits for them, and re-layouts: 19.3 us -> 22.6 us
  other arithmetic: 6.58 us -> 8.91 us
  matrix products: 26.6 us -> 24.3 us
    all_to_all x1, waiting for transfers between devices: 19.7 us -> 27.9 us  [gather_rows(): got = lax.all_to_all(spread, axis, split_axis=0, concat_axis=0, tiled=True)]
    unnamed x11 -> x25, local copies, waits for them, and re-layouts: 1.4 us -> 6.16 us
    all_to_all x2, waiting for transfers between devices: 44.1 us -> 46.5 us  [reduce_rows(): got = lax.all_to_all(pieces, axis, split_axis=0, concat_axis=0, tiled=True)]
  transfers between devices with their start and end apart: 21 -> 21, of which waited for: 11 -> 11; matrix products, arithmetic and copies ran while one was open for 23% -> 17% of each run, Pallas kernels for 0% -> 0%
where the time goes in v4:
time: 223 us; the launch traced here: 222 us
  waiting for transfers between devices  124 us (56%)
  starting transfers between devices  41.8 us (19%)
  matrix products  24.3 us (11%)
  local copies, waits for them, and re-layouts  22.6 us (10%)
  other arithmetic  8.91 us (4%)
    ppermute x18, waiting for transfers between devices, swap(): return lax.ppermute(x, 'col', perm=[(i, i ^ k) for i in range(n)])  49.2 us
    all_to_all x2, waiting for transfers between devices, reduce_rows(): got = lax.all_to_all(pieces, axis, split_axis=0, concat_axis=0, tiled=True)  46.5 us
    all_to_all x1, waiting for transfers between devices, gather_rows(): got = lax.all_to_all(spread, axis, split_axis=0, concat_axis=0, tiled=True)  27.9 us
    ppermute x18, starting transfers between devices, swap(): return lax.ppermute(x, 'col', perm=[(i, i ^ k) for i in range(n)])  16.1 us
    all_to_all x2, starting transfers between devices, reduce_rows(): got = lax.all_to_all(pieces, axis, split_axis=0, concat_axis=0, tiled=True)  15.7 us
    dot_general x8, matrix products, contract_last(): lax.dot_general(left, right, (((1,), (1,)), ((), ())), preferred_element_...  10.5 us
    all_to_all x1, starting transfers between devices, gather_rows(): got = lax.all_to_all(spread, axis, split_axis=0, concat_axis=0, tiled=True)  10 us
    unnamed x25, local copies, waits for them, and re-layouts  6.16 us
  transfers between devices with their start and end apart: 21, of which 11 were waited for; matrix products, arithmetic and copies ran while one was open for 17% of the time, Pallas kernels for 0%

profile of v4, /device:TPU:8, one launch (start us, length us, event | category | flops | bytes accessed | tf_op | source)
XLA Modules:
  0.0 222.3 jit_solution(17550736072050899116)
XLA Ops:
  0.7 3.1 %constant_dynamic-update-slice_fusion.1 = bf16[8192,224]{0,1:T(8,128)(2,1)} fusion(bf16[8192,112]{0,1:T(8,128)(2,1)} %param.6), kind=kLoop, calls=%fused_computation.94 | loop fusion | bytes 3670016
  11.8 10.0 %all-to-all-start = ((bf16[32,8,2,2048]{3,1,2,0:T(8,128)(2,1)}), bf16[32,8,2,2048]{3,1,2,0:T(8,128)(2,1)}, u32[]{:S(2)}, u32[]{:S(2)}) async-start(bf16[32,8,2,2048]{3,1,2,0:T(8,128)(2,1)} %broadcast_in_dim.66), calls=%async_computation | async-start | bytes 4194304 | tf_op jit(solution)/shard_map/all_to_all | solution.py:21
  25.5 27.9 %all-to-all-done = bf16[32,8,2,2048]{3,1,2,0:T(8,128)(2,1)} async-done(((bf16[32,8,2,2048]{3,1,2,0:T(8,128)(2,1)}), bf16[32,8,2,2048]{3,1,2,0:T(8,128)(2,1)}, u32[]{:S(2)}, u32[]{:S(2)}) %all-to-all-start) | async-done | bytes 2097184 | tf_op jit(solution)/shard_map/all_to_all | solution.py:21
  53.3 1.7 copy.80
  57.7 9.7 %collective-permute-done.1 = bf16[2048,224]{0,1:T(8,128)(2,1)} collective-permute-done((bf16[2048,224]{0,1:T(8,128)(2,1)}, bf16[2048,224]{0,1:T(8,128)(2,1)}, u32[]{:S(2)}, u32[]{:S(2)}) %collective-permute-start.1) | collective-permute-done | bytes 917536 | tf_op jit(solution)/shard_map/ppermute | solution.py:32
  69.0 15.8 %collective-permute-done.2 = bf16[2048,224]{0,1:T(8,128)(2,1)} collective-permute-done((bf16[2048,224]{0,1:T(8,128)(2,1)}, bf16[2048,224]{0,1:T(8,128)(2,1)}, u32[]{:S(2)}, u32[]{:S(2)}) %collective-permute-start.2) | collective-permute-done | bytes 917536 | tf_op jit(solution)/shard_map/ppermute | solution.py:32
  86.5 2.1 collective-permute-start.3
  89.2 1.8 collective-permute-start.4
  92.4 4.4 %collective-permute-done.10 = bf16[112,2048]{1,0:T(8,128)(2,1)} collective-permute-done((bf16[112,2048]{1,0:T(8,128)(2,1)}, bf16[112,2048]{1,0:T(8,128)(2,1)}, u32[]{:S(2)}, u32[]{:S(2)}) %collective-permute-start.10) | collective-permute-done | bytes 458784 | tf_op jit(solution)/shard_map/ppermute | solution.py:32
  98.3 6.0 %collective-permute-done.11 = bf16[112,2048]{1,0:T(8,128)(2,1)S(1)} collective-permute-done((bf16[112,2048]{1,0:T(8,128)(2,1)S(1)}, bf16[112,2048]{1,0:T(8,128)(2,1)S(1)}, u32[]{:S(2)}, u32[]{:S(2)}) %collective-permute-start.11) | collective-permute-done | bytes 458784 | tf_op jit(solution)/shard_map/ppermute | solution.py:32
  104.8 2.4 %collective-permute-start.12 = (f32[64,4,112]{2,0,1:T(8,128)S(1)}, f32[64,4,112]{2,0,1:T(8,128)S(1)}, u32[]{:S(2)}, u32[]{:S(2)}) collective-permute-start(f32[64,4,112]{2,0,1:T(8,128)S(1)} %get-tuple-element.38), channel_id=1, source_target_pairs={{0,1},{1,0},{2,3},{3,2},{4,5},{5,4},{6,7},{7,6},{8,9},{9,8},{10,11... | collective-permute-start | bytes 344072 | tf_op jit(solution)/shard_map/ppermute | solution.py:32
  110.0 7.8 %collective-permute-done.4 = f32[64,4,224]{2,0,1:T(8,128)S(1)} collective-permute-done((f32[64,4,224]{2,0,1:T(8,128)S(1)}, f32[64,4,224]{2,0,1:T(8,128)S(1)}, u32[]{:S(2)}, u32[]{:S(2)}) %collective-permute-start.4) | collective-permute-done | bytes 229408 | tf_op jit(solution)/shard_map/ppermute | solution.py:32
  118.4 3.9 %collective-permute-done.13 = f32[64,4,112]{2,0,1:T(8,128)S(1)} collective-permute-done((f32[64,4,112]{2,0,1:T(8,128)S(1)}, f32[64,4,112]{2,0,1:T(8,128)S(1)}, u32[]{:S(2)}, u32[]{:S(2)}) %collective-permute-start.13) | collective-permute-done | bytes 114720 | tf_op jit(solution)/shard_map/ppermute | solution.py:32
  130.3 1.9 collective-permute-start.17
  135.4 2.8 %fusion.1 = f32[32,8,2048]{2,1,0:T(8,128)} fusion(f32[256,2048]{1,0:T(8,128)S(1)} %fusion.33, f32[256,2048]{1,0:T(8,128)S(1)} %convolution_add_fusion.1, bf16[112,2048]{1,0:T(8,128)(2,1)} %collective-permute-done.10, bf16[256,448]{1,0:T(8,128)(2,1)S(1)} %bitcast.132, s32[]{:T(128)S(6)} %select_n.87), kind=kOutput, calls=%fused_computation.5 | convolution fusion | flops 118489088 | bytes 6815748 | tf_op jit(solution)/shard_map/dot_general | solution.py:105
  138.3 11.0 %all-to-all-start.1 = ((f32[32,8,2048]{2,1,0:T(8,128)}), f32[32,8,2048]{2,1,0:T(8,128)}, u32[]{:S(2)}, u32[]{:S(2)}) async-start(f32[32,8,2048]{2,1,0:T(8,128)} %fusion.1), calls=%async_computation.1 | async-start | bytes 4194304 | tf_op jit(solution)/shard_map/all_to_all | solution.py:27
  157.3 3.1 %fusion.3 = f32[32,8,2048]{2,1,0:T(8,128)} fusion(f32[256,2048]{1,0:T(8,128)S(1)} %fusion.22, f32[256,2048]{1,0:T(8,128)S(1)} %convolution_add_fusion.3, bf16[2048,224]{0,1:T(8,128)(2,1)} %collective-permute-done.1, bf16[256,4,224]{2,0,1:T(8,128)(2,1)S(1)} %bitcast.138, s32[]{:T(128)S(6)} %select_n.79), kind=kOutput, calls=%fused_computation.8 | convolution fusion | flops 235929600 | bytes 7340036 | tf_op jit(solution)/shard_map/dot_general | solution.py:8
  160.4 22.5 %all-to-all-done.1 = f32[32,8,2048]{2,1,0:T(8,128)} async-done(((f32[32,8,2048]{2,1,0:T(8,128)}), f32[32,8,2048]{2,1,0:T(8,128)}, u32[]{:S(2)}, u32[]{:S(2)}) %all-to-all-start.1) | async-done | bytes 2097184 | tf_op jit(solution)/shard_map/all_to_all | solution.py:27
  182.9 4.8 %all-to-all-start.2 = ((f32[32,8,2048]{2,1,0:T(8,128)}), f32[32,8,2048]{2,1,0:T(8,128)}, u32[]{:S(2)}, u32[]{:S(2)}) async-start(f32[32,8,2048]{2,1,0:T(8,128)} %fusion.3), calls=%async_computation.2 | async-start | bytes 4194304 | tf_op jit(solution)/shard_map/all_to_all | solution.py:27
  187.7 1.9 convolution_convert_fusion.1
  191.3 2.3 %fusion.48 = (bf16[2048,4,112]{0,2,1:T(8,128)(2,1)}, bf16[2048,4,112]{0,2,1:T(8,128)(2,1)}) fusion(bf16[2048,4,224]{0,2,1:T(8,128)(2,1)S(1)} %convolution_convert_fusion), kind=kLoop, calls=%fused_computation.96 | loop fusion | bytes 7340032 | tf_op jit(solution)/shard_map/slice | solution.py:129
  193.6 2.3 %reduce_sum.18 = f32[8,2048]{1,0:T(8,128)} reduce(f32[32,8,2048]{2,1,0:T(8,128)} %all-to-all-done.1, f32[]{:T(128)} %constant.16.clone.1), dimensions={0}, to_apply=%region_0.0 | reduce | flops 507904 | bytes 2162692 | tf_op jit(solution)/shard_map/reduce_sum | solution.py:28
  195.9 24.0 %all-to-all-done.2 = f32[32,8,2048]{2,1,0:T(8,128)} async-done(((f32[32,8,2048]{2,1,0:T(8,128)}), f32[32,8,2048]{2,1,0:T(8,128)}, u32[]{:S(2)}, u32[]{:S(2)}) %all-to-all-start.2) | async-done | bytes 2097184 | tf_op jit(solution)/shard_map/all_to_all | solution.py:27
  220.0 2.3 %reduce_sum.19 = f32[8,2048]{1,0:T(8,128)} reduce(f32[32,8,2048]{2,1,0:T(8,128)} %all-to-all-done.2, f32[]{:T(128)} %constant.16.clone.1), dimensions={0}, to_apply=%region_1.2 | reduce | flops 507904 | bytes 2162692 | tf_op jit(solution)/shard_map/reduce_sum | solution.py:28
  (98 shorter events, 45.5 us)
Async XLA Ops:
  8.4 80.3 %copy-start.3 = (bf16[112,2048]{1,0:T(8,128)(2,1)}, bf16[112,2048]{1,0:T(8,128)(2,1)S(1)}, u32[]{:S(2)}) copy-start(bf16[112,2048]{1,0:T(8,128)(2,1)S(1)} %get-tuple-element.19) | copy-start | bytes 1376260
  11.8 41.6 %all-to-all-start = ((bf16[32,8,2,2048]{3,1,2,0:T(8,128)(2,1)}), bf16[32,8,2,2048]{3,1,2,0:T(8,128)(2,1)}, u32[]{:S(2)}, u32[]{:S(2)}) async-start(bf16[32,8,2,2048]{3,1,2,0:T(8,128)(2,1)} %broadcast_in_dim.66), calls=%async_computation | async-start | bytes 4194304 | tf_op jit(solution)/shard_map/all_to_all | solution.py:21
  21.8 33.8 %collective-permute-start = (bf16[2048,224]{0,1:T(8,128)(2,1)}, bf16[2048,224]{0,1:T(8,128)(2,1)}, u32[]{:S(2)}, u32[]{:S(2)}) collective-permute-start(bf16[2048,224]{0,1:T(8,128)(2,1)} %get-tuple-element.16), channel_id=1, source_target_pairs={{0,1},{1,0},{2,3},{3,2},{4,5},{5,4},{6,7},{7,6},{8,9},{9,8},{10,11... | collective-permute-start | bytes 2752520 | tf_op jit(solution)/shard_map/ppermute | solution.py:32
  21.9 45.5 %collective-permute-start.1 = (bf16[2048,224]{0,1:T(8,128)(2,1)}, bf16[2048,224]{0,1:T(8,128)(2,1)}, u32[]{:S(2)}, u32[]{:S(2)}) collective-permute-start(bf16[2048,224]{0,1:T(8,128)(2,1)} %get-tuple-element.17), channel_id=1, source_target_pairs={{0,2},{1,3},{2,0},{3,1},{4,6},{5,7},{6,4},{7,5},{8,10},{9,11},{10,... | collective-permute-start | bytes 2752520 | tf_op jit(solution)/shard_map/ppermute | solution.py:32
  23.3 61.5 %collective-permute-start.2 = (bf16[2048,224]{0,1:T(8,128)(2,1)}, bf16[2048,224]{0,1:T(8,128)(2,1)}, u32[]{:S(2)}, u32[]{:S(2)}) collective-permute-start(bf16[2048,224]{0,1:T(8,128)(2,1)} %get-tuple-element.18), channel_id=1, source_target_pairs={{0,3},{1,2},{2,1},{3,0},{4,7},{5,6},{6,5},{7,4},{8,11},{9,10},{10,... | collective-permute-start | bytes 2752520 | tf_op jit(solution)/shard_map/ppermute | solution.py:32
  23.7 65.4 %collective-permute-start.9 = (bf16[112,2048]{1,0:T(8,128)(2,1)}, bf16[112,2048]{1,0:T(8,128)(2,1)}, u32[]{:S(2)}, u32[]{:S(2)}) collective-permute-start(bf16[112,2048]{1,0:T(8,128)(2,1)} %get-tuple-element.20), channel_id=1, source_target_pairs={{0,1},{1,0},{2,3},{3,2},{4,5},{5,4},{6,7},{7,6},{8,9},{9,8},{10,11... | collective-permute-start | bytes 1376264 | tf_op jit(solution)/shard_map/ppermute | solution.py:32
  24.1 72.7 %collective-permute-start.10 = (bf16[112,2048]{1,0:T(8,128)(2,1)}, bf16[112,2048]{1,0:T(8,128)(2,1)}, u32[]{:S(2)}, u32[]{:S(2)}) collective-permute-start(bf16[112,2048]{1,0:T(8,128)(2,1)} %get-tuple-element.21), channel_id=1, source_target_pairs={{0,2},{1,3},{2,0},{3,1},{4,6},{5,7},{6,4},{7,5},{8,10},{9,11},{10,... | collective-permute-start | bytes 1376264 | tf_op jit(solution)/shard_map/ppermute | solution.py:32
  56.1 48.3 %collective-permute-start.11 = (bf16[112,2048]{1,0:T(8,128)(2,1)S(1)}, bf16[112,2048]{1,0:T(8,128)(2,1)S(1)}, u32[]{:S(2)}, u32[]{:S(2)}) collective-permute-start(bf16[112,2048]{1,0:T(8,128)(2,1)S(1)} %copy-done.7), channel_id=1, source_target_pairs={{0,3},{1,2},{2,1},{3,0},{4,7},{5,6},{6,5},{7,4},{8,11},{9,10},{10,... | collective-permute-start | bytes 1376264 | tf_op jit(solution)/shard_map/ppermute | solution.py:32
  86.5 20.7 %collective-permute-start.3 = (f32[64,4,224]{2,0,1:T(8,128)S(1)}, f32[64,4,224]{2,0,1:T(8,128)S(1)}, u32[]{:S(2)}, u32[]{:S(2)}) collective-permute-start(f32[64,4,224]{2,0,1:T(8,128)S(1)} %get-tuple-element.35), channel_id=1, source_target_pairs={{0,1},{1,0},{2,3},{3,2},{4,5},{5,4},{6,7},{7,6},{8,9},{9,8},{10,11... | collective-permute-start | bytes 688136 | tf_op jit(solution)/shard_map/ppermute | solution.py:32
  88.7 21.3 %collective-permute-start.5 = (f32[64,4,224]{2,0,1:T(8,128)S(1)}, f32[64,4,224]{2,0,1:T(8,128)S(1)}, u32[]{:S(2)}, u32[]{:S(2)}) collective-permute-start(f32[64,4,224]{2,0,1:T(8,128)S(1)} %get-tuple-element.36), channel_id=1, source_target_pairs={{0,3},{1,2},{2,1},{3,0},{4,7},{5,6},{6,5},{7,4},{8,11},{9,10},{10,... | collective-permute-start | bytes 688136 | tf_op jit(solution)/shard_map/ppermute | solution.py:32
  89.2 28.7 %collective-permute-start.4 = (f32[64,4,224]{2,0,1:T(8,128)S(1)}, f32[64,4,224]{2,0,1:T(8,128)S(1)}, u32[]{:S(2)}, u32[]{:S(2)}) collective-permute-start(f32[64,4,224]{2,0,1:T(8,128)S(1)} %get-tuple-element.37), channel_id=1, source_target_pairs={{0,2},{1,3},{2,0},{3,1},{4,6},{5,7},{6,4},{7,5},{8,10},{9,11},{10,... | collective-permute-start | bytes 688136 | tf_op jit(solution)/shard_map/ppermute | solution.py:32
  104.3 18.7 %copy-start.8 = (bf16[112,2048]{1,0:T(8,128)(2,1)}, bf16[112,2048]{1,0:T(8,128)(2,1)S(1)}, u32[]{:S(2)}) copy-start(bf16[112,2048]{1,0:T(8,128)(2,1)S(1)} %collective-permute-done.11) | copy-start | bytes 1376260
  104.8 13.1 %collective-permute-start.12 = (f32[64,4,112]{2,0,1:T(8,128)S(1)}, f32[64,4,112]{2,0,1:T(8,128)S(1)}, u32[]{:S(2)}, u32[]{:S(2)}) collective-permute-start(f32[64,4,112]{2,0,1:T(8,128)S(1)} %get-tuple-element.38), channel_id=1, source_target_pairs={{0,1},{1,0},{2,3},{3,2},{4,5},{5,4},{6,7},{7,6},{8,9},{9,8},{10,11... | collective-permute-start | bytes 344072 | tf_op jit(solution)/shard_map/ppermute | solution.py:32
  107.3 11.1 %collective-permute-start.14 = (f32[64,4,112]{2,0,1:T(8,128)S(1)}, f32[64,4,112]{2,0,1:T(8,128)S(1)}, u32[]{:S(2)}, u32[]{:S(2)}) collective-permute-start(f32[64,4,112]{2,0,1:T(8,128)S(1)} %get-tuple-element.39), channel_id=1, source_target_pairs={{0,3},{1,2},{2,1},{3,0},{4,7},{5,6},{6,5},{7,4},{8,11},{9,10},{10,... | collective-permute-start | bytes 344072 | tf_op jit(solution)/shard_map/ppermute | solution.py:32
  107.3 15.0 %collective-permute-start.13 = (f32[64,4,112]{2,0,1:T(8,128)S(1)}, f32[64,4,112]{2,0,1:T(8,128)S(1)}, u32[]{:S(2)}, u32[]{:S(2)}) collective-permute-start(f32[64,4,112]{2,0,1:T(8,128)S(1)} %get-tuple-element.40), channel_id=1, source_target_pairs={{0,2},{1,3},{2,0},{3,1},{4,6},{5,7},{6,4},{7,5},{8,10},{9,11},{10,... | collective-permute-start | bytes 344072 | tf_op jit(solution)/shard_map/ppermute | solution.py:32
  126.1 6.2 %collective-permute-start.8 = (bf16[64,448]{1,0:T(8,128)(2,1)S(1)}, bf16[64,448]{1,0:T(8,128)(2,1)S(1)}, u32[]{:S(2)}, u32[]{:S(2)}) collective-permute-start(bf16[64,448]{1,0:T(8,128)(2,1)S(1)} %multiply_convert_fusion.2), channel_id=1, source_target_pairs={{0,3},{1,2},{2,1},{3,0},{4,7},{5,6},{6,5},{7,4},{8,11},{9,10},{10,... | collective-permute-start | bytes 172040 | tf_op jit(solution)/shard_map/ppermute | solution.py:32
  126.2 6.0 %collective-permute-start.7 = (bf16[64,448]{1,0:T(8,128)(2,1)S(1)}, bf16[64,448]{1,0:T(8,128)(2,1)S(1)}, u32[]{:S(2)}, u32[]{:S(2)}) collective-permute-start(bf16[64,448]{1,0:T(8,128)(2,1)S(1)} %multiply_convert_fusion.2), channel_id=1, source_target_pairs={{0,2},{1,3},{2,0},{3,1},{4,6},{5,7},{6,4},{7,5},{8,10},{9,11},{10,... | collective-permute-start | bytes 172040 | tf_op jit(solution)/shard_map/ppermute | solution.py:32
  126.8 3.5 %collective-permute-start.6 = (bf16[64,448]{1,0:T(8,128)(2,1)S(1)}, bf16[64,448]{1,0:T(8,128)(2,1)S(1)}, u32[]{:S(2)}, u32[]{:S(2)}) collective-permute-start(bf16[64,448]{1,0:T(8,128)(2,1)S(1)} %multiply_convert_fusion.2), channel_id=1, source_target_pairs={{0,1},{1,0},{2,3},{3,2},{4,5},{5,4},{6,7},{7,6},{8,9},{9,8},{10,11... | collective-permute-start | bytes 172040 | tf_op jit(solution)/shard_map/ppermute | solution.py:32
  129.7 21.7 %collective-permute-start.16 = (bf16[64,4,224]{2,0,1:T(8,128)(2,1)}, bf16[64,4,224]{2,0,1:T(8,128)(2,1)}, u32[]{:S(2)}, u32[]{:S(2)}) collective-permute-start(bf16[64,4,224]{2,0,1:T(8,128)(2,1)} %get-tuple-element.44), channel_id=1, source_target_pairs={{0,2},{1,3},{2,0},{3,1},{4,6},{5,7},{6,4},{7,5},{8,10},{9,11},{10,... | collective-permute-start | bytes 344072 | tf_op jit(solution)/shard_map/ppermute | solution.py:32
  130.0 20.4 %collective-permute-start.15 = (bf16[64,4,224]{2,0,1:T(8,128)(2,1)}, bf16[64,4,224]{2,0,1:T(8,128)(2,1)}, u32[]{:S(2)}, u32[]{:S(2)}) collective-permute-start(bf16[64,4,224]{2,0,1:T(8,128)(2,1)} %get-tuple-element.44), channel_id=1, source_target_pairs={{0,1},{1,0},{2,3},{3,2},{4,5},{5,4},{6,7},{7,6},{8,9},{9,8},{10,11... | collective-permute-start | bytes 344072 | tf_op jit(solution)/shard_map/ppermute | solution.py:32
  130.3 22.2 %collective-permute-start.17 = (bf16[64,4,224]{2,0,1:T(8,128)(2,1)}, bf16[64,4,224]{2,0,1:T(8,128)(2,1)}, u32[]{:S(2)}, u32[]{:S(2)}) collective-permute-start(bf16[64,4,224]{2,0,1:T(8,128)(2,1)} %get-tuple-element.44), channel_id=1, source_target_pairs={{0,3},{1,2},{2,1},{3,0},{4,7},{5,6},{6,5},{7,4},{8,11},{9,10},{10,... | collective-permute-start | bytes 344072 | tf_op jit(solution)/shard_map/ppermute | solution.py:32
  138.3 44.6 %all-to-all-start.1 = ((f32[32,8,2048]{2,1,0:T(8,128)}), f32[32,8,2048]{2,1,0:T(8,128)}, u32[]{:S(2)}, u32[]{:S(2)}) async-start(f32[32,8,2048]{2,1,0:T(8,128)} %fusion.1), calls=%async_computation.1 | async-start | bytes 4194304 | tf_op jit(solution)/shard_map/all_to_all | solution.py:27
  160.4 27.3 %copy-start.2 = (bf16[4,64,448]{2,1,0:T(8,128)(2,1)S(1)}, bf16[4,64,448]{2,1,0:T(8,128)(2,1)}, u32[]{:S(2)}) copy-start(bf16[4,64,448]{2,1,0:T(8,128)(2,1)} %copy-done.1) | copy-start | bytes 688132
  182.9 37.1 %all-to-all-start.2 = ((f32[32,8,2048]{2,1,0:T(8,128)}), f32[32,8,2048]{2,1,0:T(8,128)}, u32[]{:S(2)}, u32[]{:S(2)}) async-start(f32[32,8,2048]{2,1,0:T(8,128)} %fusion.3), calls=%async_computation.2 | async-start | bytes 4194304 | tf_op jit(solution)/shard_map/all_to_all | solution.py:27
  (9 other events, 25.1 us)

commit v5 on v3

--- a/solution.py
+++ b/solution.py
@@ -23,9 +23,9 @@
 
 
 def reduce_rows(part, axis, n):
-    pieces = part.reshape((n, part.shape[0] // n) + part.shape[1:])
+    pieces = part.reshape((n, part.shape[0] // n) + part.shape[1:]).astype(jnp.bfloat16)
     got = lax.all_to_all(pieces, axis, split_axis=0, concat_axis=0, tiled=True)
-    return jnp.sum(got, axis=0)
+    return jnp.sum(got.astype(jnp.float32), axis=0)
 
 
 def swap(x, k, n):

time: 209 us -> 184 us (0.88)
  waiting for transfers between devices: 112 us -> 88.7 us
  other arithmetic: 6.58 us -> 4.05 us
    all_to_all x2, waiting for transfers between devices: 44.1 us -> 19.6 us  [reduce_rows(): got = lax.all_to_all(pieces, axis, split_axis=0, concat_axis=0, tiled=True)]
  transfers between devices with their start and end apart: 21 -> 21, of which waited for: 11 -> 12; matrix products, arithmetic and copies ran while one was open for 23% -> 25% of each run, Pallas kernels for 0% -> 0%
where the time goes in v5:
time: 184 us; the launch traced here: 182 us
  waiting for transfers between devices  88.7 us (48%)
  starting transfers between devices  41.5 us (23%)
  matrix products  26.1 us (14%)
  local copies, waits for them, and re-layouts  20.3 us (11%)
  other arithmetic  4.05 us (2%)
    ppermute x18, waiting for transfers between devices, swap(): return lax.ppermute(x, 'col', perm=[(i, i ^ k) for i in range(n)])  49.6 us
    all_to_all x2, waiting for transfers between devices, reduce_rows(): got = lax.all_to_all(pieces, axis, split_axis=0, concat_axis=0, tiled=True)  19.6 us
    all_to_all x1, waiting for transfers between devices, gather_rows(): got = lax.all_to_all(spread, axis, split_axis=0, concat_axis=0, tiled=True)  19.5 us
    ppermute x18, starting transfers between devices, swap(): return lax.ppermute(x, 'col', perm=[(i, i ^ k) for i in range(n)])  15.8 us
    all_to_all x2, starting transfers between devices, reduce_rows(): got = lax.all_to_all(pieces, axis, split_axis=0, concat_axis=0, tiled=True)  15.5 us
    dot_general x8, matrix products, contract_last(): lax.dot_general(left, right, (((1,), (1,)), ((), ())), preferred_element_...  11.6 us
    all_to_all x1, starting transfers between devices, gather_rows(): got = lax.all_to_all(spread, axis, split_axis=0, concat_axis=0, tiled=True)  10.2 us
    dot_general x4, matrix products, shards(): jnp.dot(full_tokens, w, preferred_element_type=jnp.float32)  5.42 us
  transfers between devices with their start and end apart: 21, of which 12 were waited for; matrix products, arithmetic and copies ran while one was open for 25% of the time, Pallas kernels for 0%

profile of v5, /device:TPU:8, one launch (start us, length us, event | category | flops | bytes accessed | tf_op | source)
XLA Modules:
  0.0 181.7 jit_solution(9573635960918639842)
XLA Ops:
  3.0 10.2 %all-to-all-start = ((bf16[32,8,2,2048]{3,1,2,0:T(8,128)(2,1)}), bf16[32,8,2,2048]{3,1,2,0:T(8,128)(2,1)}, u32[]{:S(2)}, u32[]{:S(2)}) async-start(bf16[32,8,2,2048]{3,1,2,0:T(8,128)(2,1)} %broadcast_in_dim.66), calls=%async_computation | async-start | bytes 4194304 | tf_op jit(solution)/shard_map/all_to_all | solution.py:21
  14.6 2.9 %constant_dynamic-update-slice_fusion = bf16[8192,224]{0,1:T(8,128)(2,1)} fusion(bf16[8192,224]{0,1:T(8,128)(2,1)} %constant_dynamic-update-slice_fusion.1, bf16[8192,112]{0,1:T(8,128)(2,1)} %param.7), kind=kLoop, calls=%fused_computation.101 | loop fusion | bytes 3670016 | tf_op jit(solution)/shard_map/concatenate | solution.py:79
  17.4 3.5 %constant_dynamic-slice_fusion.9 = (bf16[2048,224]{0,1:T(8,128)(2,1)}, bf16[2048,224]{0,1:T(8,128)(2,1)}, bf16[2048,224]{0,1:T(8,128)(2,1)}) fusion(bf16[8192,224]{0,1:T(8,128)(2,1)} %constant_dynamic-update-slice_fusion, s32[]{:T(128)S(6)} %select_n.79, s32[]{:T(128)S(6)} %select_n.77, s32[]{:T(128)S(6)} %select_n.75), kind=kLoop, calls=%fused_computation.96 | loop fusion | bytes 5505036 | tf_op jit(solution)/shard_map/dynamic_slice | solution.py:36
  25.3 19.5 %all-to-all-done = bf16[32,8,2,2048]{3,1,2,0:T(8,128)(2,1)} async-done(((bf16[32,8,2,2048]{3,1,2,0:T(8,128)(2,1)}), bf16[32,8,2,2048]{3,1,2,0:T(8,128)(2,1)}, u32[]{:S(2)}, u32[]{:S(2)}) %all-to-all-start) | async-done | bytes 2097184 | tf_op jit(solution)/shard_map/all_to_all | solution.py:21
  50.1 8.6 %collective-permute-done.1 = bf16[2048,224]{0,1:T(8,128)(2,1)S(1)} collective-permute-done((bf16[2048,224]{0,1:T(8,128)(2,1)}, bf16[2048,224]{0,1:T(8,128)(2,1)S(1)}, u32[]{:S(2)}, u32[]{:S(2)}) %collective-permute-start.1) | collective-permute-done | bytes 917536 | tf_op jit(solution)/shard_map/ppermute | solution.py:32
  59.1 17.1 %collective-permute-done.2 = bf16[2048,224]{0,1:T(8,128)(2,1)} collective-permute-done((bf16[2048,224]{0,1:T(8,128)(2,1)}, bf16[2048,224]{0,1:T(8,128)(2,1)}, u32[]{:S(2)}, u32[]{:S(2)}) %collective-permute-start.2) | collective-permute-done | bytes 917536 | tf_op jit(solution)/shard_map/ppermute | solution.py:32
  77.9 2.1 %collective-permute-start.3 = (f32[64,4,224]{2,0,1:T(8,128)S(1)}, f32[64,4,224]{2,0,1:T(8,128)S(1)}, u32[]{:S(2)}, u32[]{:S(2)}) collective-permute-start(f32[64,4,224]{2,0,1:T(8,128)S(1)} %get-tuple-element.15), channel_id=1, source_target_pairs={{0,1},{1,0},{2,3},{3,2},{4,5},{5,4},{6,7},{7,6},{8,9},{9,8},{10,11... | collective-permute-start | bytes 688136 | tf_op jit(solution)/shard_map/ppermute | solution.py:32
  81.6 1.8 collective-permute-start.4
  84.8 3.3 %collective-permute-done.10 = bf16[112,2048]{1,0:T(8,128)(2,1)S(1)} collective-permute-done((bf16[112,2048]{1,0:T(8,128)(2,1)}, bf16[112,2048]{1,0:T(8,128)(2,1)S(1)}, u32[]{:S(2)}, u32[]{:S(2)}) %collective-permute-start.10) | collective-permute-done | bytes 458784 | tf_op jit(solution)/shard_map/ppermute | solution.py:32
  88.6 7.2 %collective-permute-done.11 = bf16[112,2048]{1,0:T(8,128)(2,1)S(1)} collective-permute-done((bf16[112,2048]{1,0:T(8,128)(2,1)S(1)}, bf16[112,2048]{1,0:T(8,128)(2,1)S(1)}, u32[]{:S(2)}, u32[]{:S(2)}) %collective-permute-start.11) | collective-permute-done | bytes 458784 | tf_op jit(solution)/shard_map/ppermute | solution.py:32
  96.2 2.4 %collective-permute-start.12 = (f32[64,4,112]{2,0,1:T(8,128)S(1)}, f32[64,4,112]{2,0,1:T(8,128)S(1)}, u32[]{:S(2)}, u32[]{:S(2)}) collective-permute-start(f32[64,4,112]{2,0,1:T(8,128)S(1)} %get-tuple-element.18), channel_id=1, source_target_pairs={{0,1},{1,0},{2,3},{3,2},{4,5},{5,4},{6,7},{7,6},{8,9},{9,8},{10,11... | collective-permute-start | bytes 344072 | tf_op jit(solution)/shard_map/ppermute | solution.py:32
  101.4 7.8 %collective-permute-done.4 = f32[64,4,224]{2,0,1:T(8,128)S(1)} collective-permute-done((f32[64,4,224]{2,0,1:T(8,128)S(1)}, f32[64,4,224]{2,0,1:T(8,128)S(1)}, u32[]{:S(2)}, u32[]{:S(2)}) %collective-permute-start.4) | collective-permute-done | bytes 229408 | tf_op jit(solution)/shard_map/ppermute | solution.py:32
  109.8 3.9 %collective-permute-done.13 = f32[64,4,112]{2,0,1:T(8,128)S(1)} collective-permute-done((f32[64,4,112]{2,0,1:T(8,128)S(1)}, f32[64,4,112]{2,0,1:T(8,128)S(1)}, u32[]{:S(2)}, u32[]{:S(2)}) %collective-permute-start.13) | collective-permute-done | bytes 114720 | tf_op jit(solution)/shard_map/ppermute | solution.py:32
  117.7 1.9 %collective-permute-start.17 = (bf16[64,4,224]{2,0,1:T(8,128)(2,1)S(1)}, bf16[64,4,224]{2,0,1:T(8,128)(2,1)}, u32[]{:S(2)}, u32[]{:S(2)}) collective-permute-start(bf16[64,4,224]{2,0,1:T(8,128)(2,1)S(1)} %get-tuple-element.24), channel_id=1, source_target_pairs={{0,3},{1,2},{2,1},{3,0},{4,7},{5,6},{6,5},{7,4},{8,11},{9,10},{10,... | collective-permute-start | bytes 344072 | tf_op jit(solution)/shard_map/ppermute | solution.py:32
  119.8 1.9 %convolution_convert_fusion.1 = bf16[448,2048]{1,0:T(8,128)(2,1)} fusion(bf16[256,448]{1,0:T(8,128)(2,1)S(1)} %bitcast.125, bf16[256,2,2048]{2,0,1:T(8,128)(2,1)S(1)} %bitcast.123), kind=kOutput, calls=%fused_computation.1 | convolution fusion | flops 470679552 | bytes 3145728 | tf_op jit(solution)/shard_map/dot_general | solution.py:14
  126.8 11.5 %all-to-all-start.1 = ((bf16[32,8,2048]{2,1,0:T(8,128)(2,1)}), bf16[32,8,2048]{2,1,0:T(8,128)(2,1)}, u32[]{:S(2)}, u32[]{:S(2)}) async-start(bf16[32,8,2048]{2,1,0:T(8,128)(2,1)} %fusion.4), calls=%async_computation.1 | async-start | bytes 2097152 | tf_op jit(solution)/shard_map/all_to_all | solution.py:27
  139.7 2.9 %fusion.19 = f32[256,2048]{1,0:T(8,128)} fusion(bf16[8192,224]{0,1:T(8,128)(2,1)} %constant_dynamic-update-slice_fusion, s32[]{:T(128)S(6)} %select_n.36, bf16[256,4,224]{2,0,1:T(8,128)(2,1)S(1)} %bitcast.131, s32[]{:T(128)S(6)} %select_n.74), kind=kOutput, calls=%fused_computation.37 | convolution fusion | flops 234881024 | bytes 3145736 | tf_op jit(solution)/shard_map/dot_general | solution.py:8
  143.8 2.0 %copy.74 = bf16[896,256]{1,0:T(8,128)(2,1)} copy(bf16[896,256]{0,1:T(8,128)(2,1)} %bitcast.137) | data formatting | bytes 917504 | tf_op jit(solution)/shard_map/dot_general | solution.py:14
  150.8 7.0 %all-to-all-done.1 = bf16[32,8,2048]{2,1,0:T(8,128)(2,1)} async-done(((bf16[32,8,2048]{2,1,0:T(8,128)(2,1)}), bf16[32,8,2048]{2,1,0:T(8,128)(2,1)}, u32[]{:S(2)}, u32[]{:S(2)}) %all-to-all-start.1) | async-done | bytes 1048608 | tf_op jit(solution)/shard_map/all_to_all | solution.py:27
  157.8 4.0 %all-to-all-start.2 = ((bf16[32,8,2048]{2,1,0:T(8,128)(2,1)}), bf16[32,8,2048]{2,1,0:T(8,128)(2,1)S(1)}, u32[]{:S(2)}, u32[]{:S(2)}) async-start(bf16[32,8,2048]{2,1,0:T(8,128)(2,1)} %fusion.5), calls=%async_computation.2 | async-start | bytes 2097152 | tf_op jit(solution)/shard_map/all_to_all | solution.py:27
  161.8 2.1 %convolution_convert_fusion = bf16[2048,4,224]{0,2,1:T(8,128)(2,1)S(1)} fusion(bf16[4,224,256]{2,1,0:T(8,128)(2,1)} %bitcast.130, bf16[256,2,2048]{2,0,1:T(8,128)(2,1)S(1)} %bitcast.124), kind=kOutput, calls=%fused_computation | convolution fusion | flops 941359104 | bytes 5177344 | tf_op jit(solution)/shard_map/dot_general | solution.py:14
  163.9 2.3 %fusion.56 = (bf16[2048,4,112]{0,2,1:T(8,128)(2,1)}, bf16[2048,4,112]{0,2,1:T(8,128)(2,1)}) fusion(bf16[2048,4,224]{0,2,1:T(8,128)(2,1)S(1)} %convolution_convert_fusion), kind=kLoop, calls=%fused_computation.104 | loop fusion | bytes 7340032 | tf_op jit(solution)/shard_map/slice | solution.py:124
  166.3 2.0 %convert_reduce_fusion.1 = f32[8,2048]{1,0:T(8,128)} fusion(bf16[32,8,2048]{2,1,0:T(8,128)(2,1)} %all-to-all-done.1), kind=kLoop, calls=%fused_computation.14 | loop fusion | flops 1032192 | bytes 1114112 | tf_op jit(solution)/shard_map/reduce_sum | solution.py:28
  168.3 12.6 %all-to-all-done.2 = bf16[32,8,2048]{2,1,0:T(8,128)(2,1)S(1)} async-done(((bf16[32,8,2048]{2,1,0:T(8,128)(2,1)}), bf16[32,8,2048]{2,1,0:T(8,128)(2,1)S(1)}, u32[]{:S(2)}, u32[]{:S(2)}) %all-to-all-start.2) | async-done | bytes 1048608 | tf_op jit(solution)/shard_map/all_to_all | solution.py:27
  (90 shorter events, 40.0 us)
Async XLA Ops:
  3.0 10.2 %copy-start.2 = (bf16[8192,112]{0,1:T(8,128)(2,1)S(1)}, bf16[8192,112]{0,1:T(8,128)(2,1)}, u32[]{:S(2)}) copy-start(bf16[8192,112]{0,1:T(8,128)(2,1)} %param.6) | copy-start | bytes 5505028
  3.0 41.8 %all-to-all-start = ((bf16[32,8,2,2048]{3,1,2,0:T(8,128)(2,1)}), bf16[32,8,2,2048]{3,1,2,0:T(8,128)(2,1)}, u32[]{:S(2)}, u32[]{:S(2)}) async-start(bf16[32,8,2,2048]{3,1,2,0:T(8,128)(2,1)} %broadcast_in_dim.66), calls=%async_computation | async-start | bytes 4194304 | tf_op jit(solution)/shard_map/all_to_all | solution.py:21
  20.9 27.4 %collective-permute-start = (bf16[2048,224]{0,1:T(8,128)(2,1)}, bf16[2048,224]{0,1:T(8,128)(2,1)}, u32[]{:S(2)}, u32[]{:S(2)}) collective-permute-start(bf16[2048,224]{0,1:T(8,128)(2,1)} %get-tuple-element.11), channel_id=1, source_target_pairs={{0,1},{1,0},{2,3},{3,2},{4,5},{5,4},{6,7},{7,6},{8,9},{9,8},{10,11... | collective-permute-start | bytes 2752520 | tf_op jit(solution)/shard_map/ppermute | solution.py:32
  20.9 37.7 %collective-permute-start.1 = (bf16[2048,224]{0,1:T(8,128)(2,1)}, bf16[2048,224]{0,1:T(8,128)(2,1)S(1)}, u32[]{:S(2)}, u32[]{:S(2)}) collective-permute-start(bf16[2048,224]{0,1:T(8,128)(2,1)} %get-tuple-element.10), channel_id=1, source_target_pairs={{0,2},{1,3},{2,0},{3,1},{4,6},{5,7},{6,4},{7,5},{8,10},{9,11},{10,... | collective-permute-start | bytes 2752520 | tf_op jit(solution)/shard_map/ppermute | solution.py:32
  22.3 53.9 %collective-permute-start.2 = (bf16[2048,224]{0,1:T(8,128)(2,1)}, bf16[2048,224]{0,1:T(8,128)(2,1)}, u32[]{:S(2)}, u32[]{:S(2)}) collective-permute-start(bf16[2048,224]{0,1:T(8,128)(2,1)} %get-tuple-element.9), channel_id=1, source_target_pairs={{0,3},{1,2},{2,1},{3,0},{4,7},{5,6},{6,5},{7,4},{8,11},{9,10},{10,... | collective-permute-start | bytes 2752520 | tf_op jit(solution)/shard_map/ppermute | solution.py:32
  23.9 64.2 %collective-permute-start.10 = (bf16[112,2048]{1,0:T(8,128)(2,1)}, bf16[112,2048]{1,0:T(8,128)(2,1)S(1)}, u32[]{:S(2)}, u32[]{:S(2)}) collective-permute-start(bf16[112,2048]{1,0:T(8,128)(2,1)} %get-tuple-element.12), channel_id=1, source_target_pairs={{0,2},{1,3},{2,0},{3,1},{4,6},{5,7},{6,4},{7,5},{8,10},{9,11},{10,... | collective-permute-start | bytes 1376264 | tf_op jit(solution)/shard_map/ppermute | solution.py:32
  25.3 56.3 %collective-permute-start.9 = (bf16[112,2048]{1,0:T(8,128)(2,1)}, bf16[112,2048]{1,0:T(8,128)(2,1)}, u32[]{:S(2)}, u32[]{:S(2)}) collective-permute-start(bf16[112,2048]{1,0:T(8,128)(2,1)} %get-tuple-element.13), channel_id=1, source_target_pairs={{0,1},{1,0},{2,3},{3,2},{4,5},{5,4},{6,7},{7,6},{8,9},{9,8},{10,11... | collective-permute-start | bytes 1376264 | tf_op jit(solution)/shard_map/ppermute | solution.py:32
  48.4 47.4 %collective-permute-start.11 = (bf16[112,2048]{1,0:T(8,128)(2,1)S(1)}, bf16[112,2048]{1,0:T(8,128)(2,1)S(1)}, u32[]{:S(2)}, u32[]{:S(2)}) collective-permute-start(bf16[112,2048]{1,0:T(8,128)(2,1)S(1)} %copy-done.7), channel_id=1, source_target_pairs={{0,3},{1,2},{2,1},{3,0},{4,7},{5,6},{6,5},{7,4},{8,11},{9,10},{10,... | collective-permute-start | bytes 1376264 | tf_op jit(solution)/shard_map/ppermute | solution.py:32
  58.6 19.2 %copy-start.3 = (bf16[2048,224]{0,1:T(8,128)(2,1)}, bf16[2048,224]{0,1:T(8,128)(2,1)S(1)}, u32[]{:S(2)}) copy-start(bf16[2048,224]{0,1:T(8,128)(2,1)S(1)} %collective-permute-done.1) | copy-start | bytes 2752516
  77.9 20.7 %collective-permute-start.3 = (f32[64,4,224]{2,0,1:T(8,128)S(1)}, f32[64,4,224]{2,0,1:T(8,128)S(1)}, u32[]{:S(2)}, u32[]{:S(2)}) collective-permute-start(f32[64,4,224]{2,0,1:T(8,128)S(1)} %get-tuple-element.15), channel_id=1, source_target_pairs={{0,1},{1,0},{2,3},{3,2},{4,5},{5,4},{6,7},{7,6},{8,9},{9,8},{10,11... | collective-permute-start | bytes 688136 | tf_op jit(solution)/shard_map/ppermute | solution.py:32
  80.1 21.3 %collective-permute-start.5 = (f32[64,4,224]{2,0,1:T(8,128)S(1)}, f32[64,4,224]{2,0,1:T(8,128)S(1)}, u32[]{:S(2)}, u32[]{:S(2)}) collective-permute-start(f32[64,4,224]{2,0,1:T(8,128)S(1)} %get-tuple-element.16), channel_id=1, source_target_pairs={{0,3},{1,2},{2,1},{3,0},{4,7},{5,6},{6,5},{7,4},{8,11},{9,10},{10,... | collective-permute-start | bytes 688136 | tf_op jit(solution)/shard_map/ppermute | solution.py:32
  81.6 27.6 %collective-permute-start.4 = (f32[64,4,224]{2,0,1:T(8,128)S(1)}, f32[64,4,224]{2,0,1:T(8,128)S(1)}, u32[]{:S(2)}, u32[]{:S(2)}) collective-permute-start(f32[64,4,224]{2,0,1:T(8,128)S(1)} %get-tuple-element.17), channel_id=1, source_target_pairs={{0,2},{1,3},{2,0},{3,1},{4,6},{5,7},{6,4},{7,5},{8,10},{9,11},{10,... | collective-permute-start | bytes 688136 | tf_op jit(solution)/shard_map/ppermute | solution.py:32
  95.7 18.1 %copy-start.5 = (bf16[112,2048]{1,0:T(8,128)(2,1)}, bf16[112,2048]{1,0:T(8,128)(2,1)S(1)}, u32[]{:S(2)}) copy-start(bf16[112,2048]{1,0:T(8,128)(2,1)S(1)} %collective-permute-done.11) | copy-start | bytes 1376260
  96.2 13.1 %collective-permute-start.12 = (f32[64,4,112]{2,0,1:T(8,128)S(1)}, f32[64,4,112]{2,0,1:T(8,128)S(1)}, u32[]{:S(2)}, u32[]{:S(2)}) collective-permute-start(f32[64,4,112]{2,0,1:T(8,128)S(1)} %get-tuple-element.18), channel_id=1, source_target_pairs={{0,1},{1,0},{2,3},{3,2},{4,5},{5,4},{6,7},{7,6},{8,9},{9,8},{10,11... | collective-permute-start | bytes 344072 | tf_op jit(solution)/shard_map/ppermute | solution.py:32
  98.7 11.1 %collective-permute-start.14 = (f32[64,4,112]{2,0,1:T(8,128)S(1)}, f32[64,4,112]{2,0,1:T(8,128)S(1)}, u32[]{:S(2)}, u32[]{:S(2)}) collective-permute-start(f32[64,4,112]{2,0,1:T(8,128)S(1)} %get-tuple-element.19), channel_id=1, source_target_pairs={{0,3},{1,2},{2,1},{3,0},{4,7},{5,6},{6,5},{7,4},{8,11},{9,10},{10,... | collective-permute-start | bytes 344072 | tf_op jit(solution)/shard_map/ppermute | solution.py:32
  98.7 15.1 %collective-permute-start.13 = (f32[64,4,112]{2,0,1:T(8,128)S(1)}, f32[64,4,112]{2,0,1:T(8,128)S(1)}, u32[]{:S(2)}, u32[]{:S(2)}) collective-permute-start(f32[64,4,112]{2,0,1:T(8,128)S(1)} %get-tuple-element.20), channel_id=1, source_target_pairs={{0,2},{1,3},{2,0},{3,1},{4,6},{5,7},{6,4},{7,5},{8,10},{9,11},{10,... | collective-permute-start | bytes 344072 | tf_op jit(solution)/shard_map/ppermute | solution.py:32
  114.7 5.2 %collective-permute-start.8 = (bf16[64,448]{1,0:T(8,128)(2,1)S(1)}, bf16[64,448]{1,0:T(8,128)(2,1)S(1)}, u32[]{:S(2)}, u32[]{:S(2)}) collective-permute-start(bf16[64,448]{1,0:T(8,128)(2,1)S(1)} %multiply_convert_fusion.2), channel_id=1, source_target_pairs={{0,3},{1,2},{2,1},{3,0},{4,7},{5,6},{6,5},{7,4},{8,11},{9,10},{10,... | collective-permute-start | bytes 172040 | tf_op jit(solution)/shard_map/ppermute | solution.py:32
  114.8 5.0 %collective-permute-start.7 = (bf16[64,448]{1,0:T(8,128)(2,1)S(1)}, bf16[64,448]{1,0:T(8,128)(2,1)S(1)}, u32[]{:S(2)}, u32[]{:S(2)}) collective-permute-start(bf16[64,448]{1,0:T(8,128)(2,1)S(1)} %multiply_convert_fusion.2), channel_id=1, source_target_pairs={{0,2},{1,3},{2,0},{3,1},{4,6},{5,7},{6,4},{7,5},{8,10},{9,11},{10,... | collective-permute-start | bytes 172040 | tf_op jit(solution)/shard_map/ppermute | solution.py:32
  115.4 2.3 %collective-permute-start.6 = (bf16[64,448]{1,0:T(8,128)(2,1)S(1)}, bf16[64,448]{1,0:T(8,128)(2,1)S(1)}, u32[]{:S(2)}, u32[]{:S(2)}) collective-permute-start(bf16[64,448]{1,0:T(8,128)(2,1)S(1)} %multiply_convert_fusion.2), channel_id=1, source_target_pairs={{0,1},{1,0},{2,3},{3,2},{4,5},{5,4},{6,7},{7,6},{8,9},{9,8},{10,11... | collective-permute-start | bytes 172040 | tf_op jit(solution)/shard_map/ppermute | solution.py:32
  116.7 21.7 %collective-permute-start.16 = (bf16[64,4,224]{2,0,1:T(8,128)(2,1)S(1)}, bf16[64,4,224]{2,0,1:T(8,128)(2,1)S(1)}, u32[]{:S(2)}, u32[]{:S(2)}) collective-permute-start(bf16[64,4,224]{2,0,1:T(8,128)(2,1)S(1)} %get-tuple-element.24), channel_id=1, source_target_pairs={{0,2},{1,3},{2,0},{3,1},{4,6},{5,7},{6,4},{7,5},{8,10},{9,11},{10,... | collective-permute-start | bytes 344072 | tf_op jit(solution)/shard_map/ppermute | solution.py:32
  117.1 21.2 %collective-permute-start.15 = (bf16[64,4,224]{2,0,1:T(8,128)(2,1)S(1)}, bf16[64,4,224]{2,0,1:T(8,128)(2,1)S(1)}, u32[]{:S(2)}, u32[]{:S(2)}) collective-permute-start(bf16[64,4,224]{2,0,1:T(8,128)(2,1)S(1)} %get-tuple-element.24), channel_id=1, source_target_pairs={{0,1},{1,0},{2,3},{3,2},{4,5},{5,4},{6,7},{7,6},{8,9},{9,8},{10,11... | collective-permute-start | bytes 344072 | tf_op jit(solution)/shard_map/ppermute | solution.py:32
  117.7 20.9 %collective-permute-start.17 = (bf16[64,4,224]{2,0,1:T(8,128)(2,1)S(1)}, bf16[64,4,224]{2,0,1:T(8,128)(2,1)}, u32[]{:S(2)}, u32[]{:S(2)}) collective-permute-start(bf16[64,4,224]{2,0,1:T(8,128)(2,1)S(1)} %get-tuple-element.24), channel_id=1, source_target_pairs={{0,3},{1,2},{2,1},{3,0},{4,7},{5,6},{6,5},{7,4},{8,11},{9,10},{10,... | collective-permute-start | bytes 344072 | tf_op jit(solution)/shard_map/ppermute | solution.py:32
  126.8 31.0 %all-to-all-start.1 = ((bf16[32,8,2048]{2,1,0:T(8,128)(2,1)}), bf16[32,8,2048]{2,1,0:T(8,128)(2,1)}, u32[]{:S(2)}, u32[]{:S(2)}) async-start(bf16[32,8,2048]{2,1,0:T(8,128)(2,1)} %fusion.4), calls=%async_computation.1 | async-start | bytes 2097152 | tf_op jit(solution)/shard_map/all_to_all | solution.py:27
  157.8 23.1 %all-to-all-start.2 = ((bf16[32,8,2048]{2,1,0:T(8,128)(2,1)}), bf16[32,8,2048]{2,1,0:T(8,128)(2,1)S(1)}, u32[]{:S(2)}, u32[]{:S(2)}) async-start(bf16[32,8,2048]{2,1,0:T(8,128)(2,1)} %fusion.5), calls=%async_computation.2 | async-start | bytes 2097152 | tf_op jit(solution)/shard_map/all_to_all | solution.py:27
  (5 other events, 12.3 us)

commit v6 on v5

--- a/solution.py
+++ b/solution.py
@@ -99,7 +99,6 @@
         h = lax.dynamic_slice_in_dim(hidden, (me ^ k) * unit, unit, 1)
         t = jnp.dot(h, w, preferred_element_type=jnp.float32)
         term = t if term is None else term + t
-    output = reduce_rows(term, "row", n_row)
 
     dh_part = place([contract_last(grad_full, w) for w in down_rel], me, 1)
     hidden_grad = col_reduce(dh_part, n_col).reshape(share, n_col * unit)
@@ -117,7 +116,9 @@
         g = lax.dynamic_index_in_dim(grads, me ^ k, 1, keepdims=False)
         t = contract_last(g, w)
         in_part = t if in_part is None else in_part + t
-    input_grad = reduce_rows(in_part, "row", n_row)
+    summed = reduce_rows(jnp.stack([term, in_part], axis=1), "row", n_row)
+    output = summed[:, 0]
+    input_grad = summed[:, 1]
     grad_gu = contract_first(full_tokens, grads.reshape(count, n_col * 2 * unit))
     grad_gu = grad_gu.reshape(-1, n_col, 2 * unit)
     grad_gate = grad_gu[:, :, :unit].reshape(-1, n_col * unit).astype(jnp.bfloat16)

time: 184 us -> 180 us (0.978)
  waiting for transfers between devices: 88.7 us -> 96.1 us
  starting transfers between devices: 41.5 us -> 36.3 us
  local copies, waits for them, and re-layouts: 20.3 us -> 17.4 us
  matrix products: 26.1 us -> 23.8 us
    all_to_all x2 -> x1, waiting for transfers between devices: 19.6 us -> 26.4 us  [reduce_rows(): got = lax.all_to_all(pieces, axis, split_axis=0, concat_axis=0, tiled=True)]
    all_to_all x2 -> x1, starting transfers between devices: 15.5 us -> 11.8 us  [reduce_rows(): got = lax.all_to_all(pieces, axis, split_axis=0, concat_axis=0, tiled=True)]
  transfers between devices with their start and end apart: 21 -> 20, of which waited for: 12 -> 9; matrix products, arithmetic and copies ran while one was open for 25% -> 18% of each run, Pallas kernels for 0% -> 0%
where the time goes in v6:
time: 180 us; the launch traced here: 179 us
  waiting for transfers between devices  96.1 us (53%)
  starting transfers between devices  36.3 us (20%)
  matrix products  23.8 us (13%)
  local copies, waits for them, and re-layouts  17.4 us (10%)
  other arithmetic  4.7 us (3%)
    ppermute x18, waiting for transfers between devices, swap(): return lax.ppermute(x, 'col', perm=[(i, i ^ k) for i in range(n)])  50.2 us
    all_to_all x1, waiting for transfers between devices, reduce_rows(): got = lax.all_to_all(pieces, axis, split_axis=0, concat_axis=0, tiled=True)  26.4 us
    all_to_all x1, waiting for transfers between devices, gather_rows(): got = lax.all_to_all(spread, axis, split_axis=0, concat_axis=0, tiled=True)  19.4 us
    ppermute x18, starting transfers between devices, swap(): return lax.ppermute(x, 'col', perm=[(i, i ^ k) for i in range(n)])  14.3 us
    all_to_all x1, starting transfers between devices, reduce_rows(): got = lax.all_to_all(pieces, axis, split_axis=0, concat_axis=0, tiled=True)  11.8 us
    dot_general x8, matrix products, contract_last(): lax.dot_general(left, right, (((1,), (1,)), ((), ())), preferred_element_...  10.3 us
    all_to_all x1, starting transfers between devices, gather_rows(): got = lax.all_to_all(spread, axis, split_axis=0, concat_axis=0, tiled=True)  10.2 us
    dot_general x4, matrix products, shards(): jnp.dot(full_tokens, w, preferred_element_type=jnp.float32)  5.43 us
  transfers between devices with their start and end apart: 20, of which 9 were waited for; matrix products, arithmetic and copies ran while one was open for 18% of the time, Pallas kernels for 0%

profile of v6, /device:TPU:8, one launch (start us, length us, event | category | flops | bytes accessed | tf_op | source)
XLA Modules:
  0.0 179.2 jit_solution(3445474637950149272)
XLA Ops:
  3.0 10.2 %all-to-all-start = ((bf16[32,8,2,2048]{3,1,2,0:T(8,128)(2,1)}), bf16[32,8,2,2048]{3,1,2,0:T(8,128)(2,1)}, u32[]{:S(2)}, u32[]{:S(2)}) async-start(bf16[32,8,2,2048]{3,1,2,0:T(8,128)(2,1)} %broadcast_in_dim.66), calls=%async_computation | async-start | bytes 4194304 | tf_op jit(solution)/shard_map/all_to_all | solution.py:21
  14.6 2.8 %constant_dynamic-update-slice_fusion = bf16[8192,224]{0,1:T(8,128)(2,1)} fusion(bf16[8192,224]{0,1:T(8,128)(2,1)} %constant_dynamic-update-slice_fusion.1, bf16[8192,112]{0,1:T(8,128)(2,1)} %param.7), kind=kLoop, calls=%fused_computation.103 | loop fusion | bytes 3670016 | tf_op jit(solution)/shard_map/concatenate | solution.py:79
  17.4 3.5 %constant_dynamic-slice_fusion.10 = (bf16[2048,224]{0,1:T(8,128)(2,1)}, bf16[2048,224]{0,1:T(8,128)(2,1)}, bf16[2048,224]{0,1:T(8,128)(2,1)}) fusion(bf16[8192,224]{0,1:T(8,128)(2,1)} %constant_dynamic-update-slice_fusion, s32[]{:T(128)S(6)} %select_n.77, s32[]{:T(128)S(6)} %select_n.79, s32[]{:T(128)S(6)} %select_n.75), kind=kLoop, calls=%fused_computation.99 | loop fusion | bytes 5505036 | tf_op jit(solution)/shard_map/dynamic_slice | solution.py:36
  25.4 19.4 %all-to-all-done = bf16[32,8,2,2048]{3,1,2,0:T(8,128)(2,1)} async-done(((bf16[32,8,2,2048]{3,1,2,0:T(8,128)(2,1)}), bf16[32,8,2,2048]{3,1,2,0:T(8,128)(2,1)}, u32[]{:S(2)}, u32[]{:S(2)}) %all-to-all-start) | async-done | bytes 2097184 | tf_op jit(solution)/shard_map/all_to_all | solution.py:21
  44.8 1.7 copy.82
  46.6 1.7 fusion.9
  48.4 1.6 fusion.8
  50.1 8.5 %collective-permute-done.1 = bf16[2048,224]{0,1:T(8,128)(2,1)S(1)} collective-permute-done((bf16[2048,224]{0,1:T(8,128)(2,1)}, bf16[2048,224]{0,1:T(8,128)(2,1)S(1)}, u32[]{:S(2)}, u32[]{:S(2)}) %collective-permute-start.1) | collective-permute-done | bytes 917536 | tf_op jit(solution)/shard_map/ppermute | solution.py:32
  59.1 17.1 %collective-permute-done.2 = bf16[2048,224]{0,1:T(8,128)(2,1)} collective-permute-done((bf16[2048,224]{0,1:T(8,128)(2,1)}, bf16[2048,224]{0,1:T(8,128)(2,1)}, u32[]{:S(2)}, u32[]{:S(2)}) %collective-permute-start.2) | collective-permute-done | bytes 917536 | tf_op jit(solution)/shard_map/ppermute | solution.py:32
  76.2 1.6 fusion.6
  77.9 2.4 %collective-permute-start.3 = (f32[64,4,224]{2,0,1:T(8,128)S(1)}, f32[64,4,224]{2,0,1:T(8,128)S(1)}, u32[]{:S(2)}, u32[]{:S(2)}) collective-permute-start(f32[64,4,224]{2,0,1:T(8,128)S(1)} %get-tuple-element.15), channel_id=1, source_target_pairs={{0,1},{1,0},{2,3},{3,2},{4,5},{5,4},{6,7},{7,6},{8,9},{9,8},{10,11... | collective-permute-start | bytes 688136 | tf_op jit(solution)/shard_map/ppermute | solution.py:32
  81.9 1.8 %collective-permute-start.4 = (f32[64,4,224]{2,0,1:T(8,128)S(1)}, f32[64,4,224]{2,0,1:T(8,128)S(1)}, u32[]{:S(2)}, u32[]{:S(2)}) collective-permute-start(f32[64,4,224]{2,0,1:T(8,128)S(1)} %get-tuple-element.17), channel_id=1, source_target_pairs={{0,2},{1,3},{2,0},{3,1},{4,6},{5,7},{6,4},{7,5},{8,10},{9,11},{10,... | collective-permute-start | bytes 688136 | tf_op jit(solution)/shard_map/ppermute | solution.py:32
  85.1 12.8 %collective-permute-done.10 = bf16[112,2048]{1,0:T(8,128)(2,1)S(1)} collective-permute-done((bf16[112,2048]{1,0:T(8,128)(2,1)S(1)}, bf16[112,2048]{1,0:T(8,128)(2,1)S(1)}, u32[]{:S(2)}, u32[]{:S(2)}) %collective-permute-start.10) | collective-permute-done | bytes 458784 | tf_op jit(solution)/shard_map/ppermute | solution.py:32
  100.2 1.9 %collective-permute-start.13 = (f32[64,4,112]{2,0,1:T(8,128)S(1)}, f32[64,4,112]{2,0,1:T(8,128)S(1)}, u32[]{:S(2)}, u32[]{:S(2)}) collective-permute-start(f32[64,4,112]{2,0,1:T(8,128)S(1)} %get-tuple-element.20), channel_id=1, source_target_pairs={{0,2},{1,3},{2,0},{3,1},{4,6},{5,7},{6,4},{7,5},{8,10},{9,11},{10,... | collective-permute-start | bytes 344072 | tf_op jit(solution)/shard_map/ppermute | solution.py:32
  102.1 7.1 %collective-permute-done.4 = f32[64,4,224]{2,0,1:T(8,128)S(1)} collective-permute-done((f32[64,4,224]{2,0,1:T(8,128)S(1)}, f32[64,4,224]{2,0,1:T(8,128)S(1)}, u32[]{:S(2)}, u32[]{:S(2)}) %collective-permute-start.4) | collective-permute-done | bytes 229408 | tf_op jit(solution)/shard_map/ppermute | solution.py:32
  109.8 3.9 %collective-permute-done.13 = f32[64,4,112]{2,0,1:T(8,128)S(1)} collective-permute-done((f32[64,4,112]{2,0,1:T(8,128)S(1)}, f32[64,4,112]{2,0,1:T(8,128)S(1)}, u32[]{:S(2)}, u32[]{:S(2)}) %collective-permute-start.13) | collective-permute-done | bytes 114720 | tf_op jit(solution)/shard_map/ppermute | solution.py:32
  117.6 1.9 %collective-permute-start.17 = (bf16[64,4,224]{2,0,1:T(8,128)(2,1)S(1)}, bf16[64,4,224]{2,0,1:T(8,128)(2,1)S(1)}, u32[]{:S(2)}, u32[]{:S(2)}) collective-permute-start(bf16[64,4,224]{2,0,1:T(8,128)(2,1)S(1)} %get-tuple-element.26), channel_id=1, source_target_pairs={{0,3},{1,2},{2,1},{3,0},{4,7},{5,6},{6,5},{7,4},{8,11},{9,10},{10,... | collective-permute-start | bytes 344072 | tf_op jit(solution)/shard_map/ppermute | solution.py:32
  125.4 1.6 fusion.19
  128.7 1.7 convolution_add_fusion.3
  132.4 11.8 %all-to-all-start.1 = ((bf16[32,8,2,2048]{3,1,2,0:T(8,128)(2,1)}), bf16[32,8,2,2048]{3,1,2,0:T(8,128)(2,1)}, u32[]{:S(2)}, u32[]{:S(2)}) async-start(bf16[32,8,2,2048]{3,1,2,0:T(8,128)(2,1)} %pad_maximum_fusion), calls=%async_computation.1 | async-start | bytes 4194304 | tf_op jit(solution)/shard_map/all_to_all | solution.py:27
  144.3 1.9 %convolution_convert_fusion.1 = bf16[448,2048]{1,0:T(8,128)(2,1)} fusion(bf16[256,448]{1,0:T(8,128)(2,1)S(1)} %bitcast.137, bf16[256,2,2048]{2,0,1:T(8,128)(2,1)S(1)} %bitcast.131), kind=kOutput, calls=%fused_computation.2 | convolution fusion | flops 470679552 | bytes 3145728 | tf_op jit(solution)/shard_map/dot_general | solution.py:14
  147.9 2.3 %fusion.56 = (bf16[2048,4,112]{0,2,1:T(8,128)(2,1)}, bf16[2048,4,112]{0,2,1:T(8,128)(2,1)}) fusion(bf16[2048,4,224]{0,2,1:T(8,128)(2,1)S(1)} %convolution_convert_fusion), kind=kLoop, calls=%fused_computation.106 | loop fusion | bytes 7340032 | tf_op jit(solution)/shard_map/slice | solution.py:125
  150.2 26.4 %all-to-all-done.1 = bf16[32,8,2,2048]{3,1,2,0:T(8,128)(2,1)} async-done(((bf16[32,8,2,2048]{3,1,2,0:T(8,128)(2,1)}), bf16[32,8,2,2048]{3,1,2,0:T(8,128)(2,1)}, u32[]{:S(2)}, u32[]{:S(2)}) %all-to-all-start.1) | async-done | bytes 2097184 | tf_op jit(solution)/shard_map/all_to_all | solution.py:27
  176.6 1.9 %convert_reduce_fusion = f32[8,2,2048]{2,0,1:T(8,128)S(1)} fusion(bf16[32,8,2,2048]{3,1,2,0:T(8,128)(2,1)} %all-to-all-done.1), kind=kLoop, calls=%fused_computation | loop fusion | flops 2064384 | bytes 2228224 | tf_op jit(solution)/shard_map/reduce_sum | solution.py:28
  (83 shorter events, 30.3 us)
Async XLA Ops:
  3.0 10.2 %copy-start.1 = (bf16[8192,112]{0,1:T(8,128)(2,1)S(1)}, bf16[8192,112]{0,1:T(8,128)(2,1)}, u32[]{:S(2)}) copy-start(bf16[8192,112]{0,1:T(8,128)(2,1)} %param.6) | copy-start | bytes 5505028
  3.0 41.8 %all-to-all-start = ((bf16[32,8,2,2048]{3,1,2,0:T(8,128)(2,1)}), bf16[32,8,2,2048]{3,1,2,0:T(8,128)(2,1)}, u32[]{:S(2)}, u32[]{:S(2)}) async-start(bf16[32,8,2,2048]{3,1,2,0:T(8,128)(2,1)} %broadcast_in_dim.66), calls=%async_computation | async-start | bytes 4194304 | tf_op jit(solution)/shard_map/all_to_all | solution.py:21
  17.4 5.4 %copy-start = (bf16[112,8192]{1,0:T(8,128)(2,1)S(1)}, bf16[112,8192]{1,0:T(8,128)(2,1)}, u32[]{:S(2)}) copy-start(bf16[112,8192]{1,0:T(8,128)(2,1)} %param.8) | copy-start | bytes 5505028
  20.9 27.4 %collective-permute-start = (bf16[2048,224]{0,1:T(8,128)(2,1)}, bf16[2048,224]{0,1:T(8,128)(2,1)}, u32[]{:S(2)}, u32[]{:S(2)}) collective-permute-start(bf16[2048,224]{0,1:T(8,128)(2,1)} %get-tuple-element.11), channel_id=1, source_target_pairs={{0,1},{1,0},{2,3},{3,2},{4,5},{5,4},{6,7},{7,6},{8,9},{9,8},{10,11... | collective-permute-start | bytes 2752520 | tf_op jit(solution)/shard_map/ppermute | solution.py:32
  20.9 37.7 %collective-permute-start.1 = (bf16[2048,224]{0,1:T(8,128)(2,1)}, bf16[2048,224]{0,1:T(8,128)(2,1)S(1)}, u32[]{:S(2)}, u32[]{:S(2)}) collective-permute-start(bf16[2048,224]{0,1:T(8,128)(2,1)} %get-tuple-element.9), channel_id=1, source_target_pairs={{0,2},{1,3},{2,0},{3,1},{4,6},{5,7},{6,4},{7,5},{8,10},{9,11},{10,... | collective-permute-start | bytes 2752520 | tf_op jit(solution)/shard_map/ppermute | solution.py:32
  22.3 53.9 %collective-permute-start.2 = (bf16[2048,224]{0,1:T(8,128)(2,1)}, bf16[2048,224]{0,1:T(8,128)(2,1)}, u32[]{:S(2)}, u32[]{:S(2)}) collective-permute-start(bf16[2048,224]{0,1:T(8,128)(2,1)} %get-tuple-element.10), channel_id=1, source_target_pairs={{0,3},{1,2},{2,1},{3,0},{4,7},{5,6},{6,5},{7,4},{8,11},{9,10},{10,... | collective-permute-start | bytes 2752520 | tf_op jit(solution)/shard_map/ppermute | solution.py:32
  23.9 74.5 %collective-permute-start.11 = (bf16[112,2048]{1,0:T(8,128)(2,1)}, bf16[112,2048]{1,0:T(8,128)(2,1)}, u32[]{:S(2)}, u32[]{:S(2)}) collective-permute-start(bf16[112,2048]{1,0:T(8,128)(2,1)} %get-tuple-element.12), channel_id=1, source_target_pairs={{0,3},{1,2},{2,1},{3,0},{4,7},{5,6},{6,5},{7,4},{8,11},{9,10},{10,... | collective-permute-start | bytes 1376264 | tf_op jit(solution)/shard_map/ppermute | solution.py:32
  25.1 56.7 %collective-permute-start.9 = (bf16[112,2048]{1,0:T(8,128)(2,1)}, bf16[112,2048]{1,0:T(8,128)(2,1)}, u32[]{:S(2)}, u32[]{:S(2)}) collective-permute-start(bf16[112,2048]{1,0:T(8,128)(2,1)} %get-tuple-element.13), channel_id=1, source_target_pairs={{0,1},{1,0},{2,3},{3,2},{4,5},{5,4},{6,7},{7,6},{8,9},{9,8},{10,11... | collective-permute-start | bytes 1376264 | tf_op jit(solution)/shard_map/ppermute | solution.py:32
  46.5 1.8 %copy-start.4 = (bf16[112,2048]{1,0:T(8,128)(2,1)S(1)}, bf16[112,2048]{1,0:T(8,128)(2,1)}, u32[]{:S(2)}) copy-start(bf16[112,2048]{1,0:T(8,128)(2,1)} %get-tuple-element.14) | copy-start | bytes 1376260
  48.3 49.6 %collective-permute-start.10 = (bf16[112,2048]{1,0:T(8,128)(2,1)S(1)}, bf16[112,2048]{1,0:T(8,128)(2,1)S(1)}, u32[]{:S(2)}, u32[]{:S(2)}) collective-permute-start(bf16[112,2048]{1,0:T(8,128)(2,1)S(1)} %copy-done.4), channel_id=1, source_target_pairs={{0,2},{1,3},{2,0},{3,1},{4,6},{5,7},{6,4},{7,5},{8,10},{9,11},{10,... | collective-permute-start | bytes 1376264 | tf_op jit(solution)/shard_map/ppermute | solution.py:32
  58.6 19.2 %copy-start.2 = (bf16[2048,224]{0,1:T(8,128)(2,1)}, bf16[2048,224]{0,1:T(8,128)(2,1)S(1)}, u32[]{:S(2)}) copy-start(bf16[2048,224]{0,1:T(8,128)(2,1)S(1)} %collective-permute-done.1) | copy-start | bytes 2752516
  77.9 22.3 %collective-permute-start.3 = (f32[64,4,224]{2,0,1:T(8,128)S(1)}, f32[64,4,224]{2,0,1:T(8,128)S(1)}, u32[]{:S(2)}, u32[]{:S(2)}) collective-permute-start(f32[64,4,224]{2,0,1:T(8,128)S(1)} %get-tuple-element.15), channel_id=1, source_target_pairs={{0,1},{1,0},{2,3},{3,2},{4,5},{5,4},{6,7},{7,6},{8,9},{9,8},{10,11... | collective-permute-start | bytes 688136 | tf_op jit(solution)/shard_map/ppermute | solution.py:32
  80.3 21.8 %collective-permute-start.5 = (f32[64,4,224]{2,0,1:T(8,128)S(1)}, f32[64,4,224]{2,0,1:T(8,128)S(1)}, u32[]{:S(2)}, u32[]{:S(2)}) collective-permute-start(f32[64,4,224]{2,0,1:T(8,128)S(1)} %get-tuple-element.16), channel_id=1, source_target_pairs={{0,3},{1,2},{2,1},{3,0},{4,7},{5,6},{6,5},{7,4},{8,11},{9,10},{10,... | collective-permute-start | bytes 688136 | tf_op jit(solution)/shard_map/ppermute | solution.py:32
  81.9 27.3 %collective-permute-start.4 = (f32[64,4,224]{2,0,1:T(8,128)S(1)}, f32[64,4,224]{2,0,1:T(8,128)S(1)}, u32[]{:S(2)}, u32[]{:S(2)}) collective-permute-start(f32[64,4,224]{2,0,1:T(8,128)S(1)} %get-tuple-element.17), channel_id=1, source_target_pairs={{0,2},{1,3},{2,0},{3,1},{4,6},{5,7},{6,4},{7,5},{8,10},{9,11},{10,... | collective-permute-start | bytes 688136 | tf_op jit(solution)/shard_map/ppermute | solution.py:32
  99.9 9.4 %collective-permute-start.12 = (f32[64,4,112]{2,0,1:T(8,128)S(1)}, f32[64,4,112]{2,0,1:T(8,128)S(1)}, u32[]{:S(2)}, u32[]{:S(2)}) collective-permute-start(f32[64,4,112]{2,0,1:T(8,128)S(1)} %get-tuple-element.18), channel_id=1, source_target_pairs={{0,1},{1,0},{2,3},{3,2},{4,5},{5,4},{6,7},{7,6},{8,9},{9,8},{10,11... | collective-permute-start | bytes 344072 | tf_op jit(solution)/shard_map/ppermute | solution.py:32
  100.0 9.8 %collective-permute-start.14 = (f32[64,4,112]{2,0,1:T(8,128)S(1)}, f32[64,4,112]{2,0,1:T(8,128)S(1)}, u32[]{:S(2)}, u32[]{:S(2)}) collective-permute-start(f32[64,4,112]{2,0,1:T(8,128)S(1)} %get-tuple-element.19), channel_id=1, source_target_pairs={{0,3},{1,2},{2,1},{3,0},{4,7},{5,6},{6,5},{7,4},{8,11},{9,10},{10,... | collective-permute-start | bytes 344072 | tf_op jit(solution)/shard_map/ppermute | solution.py:32
  100.2 13.5 %collective-permute-start.13 = (f32[64,4,112]{2,0,1:T(8,128)S(1)}, f32[64,4,112]{2,0,1:T(8,128)S(1)}, u32[]{:S(2)}, u32[]{:S(2)}) collective-permute-start(f32[64,4,112]{2,0,1:T(8,128)S(1)} %get-tuple-element.20), channel_id=1, source_target_pairs={{0,2},{1,3},{2,0},{3,1},{4,6},{5,7},{6,4},{7,5},{8,10},{9,11},{10,... | collective-permute-start | bytes 344072 | tf_op jit(solution)/shard_map/ppermute | solution.py:32
  114.6 5.2 %collective-permute-start.8 = (bf16[64,448]{1,0:T(8,128)(2,1)S(1)}, bf16[64,448]{1,0:T(8,128)(2,1)S(1)}, u32[]{:S(2)}, u32[]{:S(2)}) collective-permute-start(bf16[64,448]{1,0:T(8,128)(2,1)S(1)} %multiply_convert_fusion.2), channel_id=1, source_target_pairs={{0,3},{1,2},{2,1},{3,0},{4,7},{5,6},{6,5},{7,4},{8,11},{9,10},{10,... | collective-permute-start | bytes 172040 | tf_op jit(solution)/shard_map/ppermute | solution.py:32
  114.7 5.0 %collective-permute-start.7 = (bf16[64,448]{1,0:T(8,128)(2,1)S(1)}, bf16[64,448]{1,0:T(8,128)(2,1)S(1)}, u32[]{:S(2)}, u32[]{:S(2)}) collective-permute-start(bf16[64,448]{1,0:T(8,128)(2,1)S(1)} %multiply_convert_fusion.2), channel_id=1, source_target_pairs={{0,2},{1,3},{2,0},{3,1},{4,6},{5,7},{6,4},{7,5},{8,10},{9,11},{10,... | collective-permute-start | bytes 172040 | tf_op jit(solution)/shard_map/ppermute | solution.py:32
  115.4 2.3 %collective-permute-start.6 = (bf16[64,448]{1,0:T(8,128)(2,1)S(1)}, bf16[64,448]{1,0:T(8,128)(2,1)S(1)}, u32[]{:S(2)}, u32[]{:S(2)}) collective-permute-start(bf16[64,448]{1,0:T(8,128)(2,1)S(1)} %multiply_convert_fusion.2), channel_id=1, source_target_pairs={{0,1},{1,0},{2,3},{3,2},{4,5},{5,4},{6,7},{7,6},{8,9},{9,8},{10,11... | collective-permute-start | bytes 172040 | tf_op jit(solution)/shard_map/ppermute | solution.py:32
  116.7 8.4 %collective-permute-start.16 = (bf16[64,4,224]{2,0,1:T(8,128)(2,1)S(1)}, bf16[64,4,224]{2,0,1:T(8,128)(2,1)S(1)}, u32[]{:S(2)}, u32[]{:S(2)}) collective-permute-start(bf16[64,4,224]{2,0,1:T(8,128)(2,1)S(1)} %get-tuple-element.26), channel_id=1, source_target_pairs={{0,2},{1,3},{2,0},{3,1},{4,6},{5,7},{6,4},{7,5},{8,10},{9,11},{10,... | collective-permute-start | bytes 344072 | tf_op jit(solution)/shard_map/ppermute | solution.py:32
  117.1 7.9 %collective-permute-start.15 = (bf16[64,4,224]{2,0,1:T(8,128)(2,1)S(1)}, bf16[64,4,224]{2,0,1:T(8,128)(2,1)S(1)}, u32[]{:S(2)}, u32[]{:S(2)}) collective-permute-start(bf16[64,4,224]{2,0,1:T(8,128)(2,1)S(1)} %get-tuple-element.26), channel_id=1, source_target_pairs={{0,1},{1,0},{2,3},{3,2},{4,5},{5,4},{6,7},{7,6},{8,9},{9,8},{10,11... | collective-permute-start | bytes 344072 | tf_op jit(solution)/shard_map/ppermute | solution.py:32
  117.6 7.6 %collective-permute-start.17 = (bf16[64,4,224]{2,0,1:T(8,128)(2,1)S(1)}, bf16[64,4,224]{2,0,1:T(8,128)(2,1)S(1)}, u32[]{:S(2)}, u32[]{:S(2)}) collective-permute-start(bf16[64,4,224]{2,0,1:T(8,128)(2,1)S(1)} %get-tuple-element.26), channel_id=1, source_target_pairs={{0,3},{1,2},{2,1},{3,0},{4,7},{5,6},{6,5},{7,4},{8,11},{9,10},{10,... | collective-permute-start | bytes 344072 | tf_op jit(solution)/shard_map/ppermute | solution.py:32
  132.4 44.2 %all-to-all-start.1 = ((bf16[32,8,2,2048]{3,1,2,0:T(8,128)(2,1)}), bf16[32,8,2,2048]{3,1,2,0:T(8,128)(2,1)}, u32[]{:S(2)}, u32[]{:S(2)}) async-start(bf16[32,8,2,2048]{3,1,2,0:T(8,128)(2,1)} %pad_maximum_fusion), calls=%async_computation.1 | async-start | bytes 4194304 | tf_op jit(solution)/shard_map/all_to_all | solution.py:27
  (1 other events, 1.7 us)

commit v7 on v5

--- a/solution.py
+++ b/solution.py
@@ -26,6 +26,29 @@
     pieces = part.reshape((n, part.shape[0] // n) + part.shape[1:]).astype(jnp.bfloat16)
     got = lax.all_to_all(pieces, axis, split_axis=0, concat_axis=0, tiled=True)
     return jnp.sum(got.astype(jnp.float32), axis=0)
+
+
+def row_tree(part, axis):
+    me = lax.axis_index(axis)
+    n = lax.axis_size(axis)
+    y, z, x = me % 2, (me // 2) % 4, me // 8
+    rows = part.shape[0] // n
+    view = part.reshape((4, 4, 2, rows) + part.shape[1:])
+
+    def swap_row(v, mask):
+        return lax.ppermute(v.astype(jnp.bfloat16), axis, perm=[(i, i ^ mask) for i in range(n)])
+
+    acc = lax.dynamic_index_in_dim(view, y, 2, keepdims=False)
+    acc = acc + swap_row(lax.dynamic_index_in_dim(view, y ^ 1, 2, keepdims=False), 1).astype(jnp.float32)
+    total = lax.dynamic_index_in_dim(acc, z, 1, keepdims=False)
+    for k in range(1, 4):
+        sent = lax.dynamic_index_in_dim(acc, z ^ k, 1, keepdims=False)
+        total = total + swap_row(sent, k << 1).astype(jnp.float32)
+    out = lax.dynamic_index_in_dim(total, x, 0, keepdims=False)
+    for k in range(1, 4):
+        sent = lax.dynamic_index_in_dim(total, x ^ k, 0, keepdims=False)
+        out = out + swap_row(sent, k << 3).astype(jnp.float32)
+    return out
 
 
 def swap(x, k, n):
@@ -99,7 +122,7 @@
         h = lax.dynamic_slice_in_dim(hidden, (me ^ k) * unit, unit, 1)
         t = jnp.dot(h, w, preferred_element_type=jnp.float32)
         term = t if term is None else term + t
-    output = reduce_rows(term, "row", n_row)
+    output = row_tree(term, "row")
 
     dh_part = place([contract_last(grad_full, w) for w in down_rel], me, 1)
     hidden_grad = col_reduce(dh_part, n_col).reshape(share, n_col * unit)

time: 184 us -> 184 us (level)
  starting transfers between devices: 41.5 us -> 47 us
  waiting for transfers between devices: 88.7 us -> 84.6 us
    all_to_all x2 -> x1, waiting for transfers between devices: 19.6 us -> 0.01 us  [reduce_rows(): got = lax.all_to_all(pieces, axis, split_axis=0, concat_axis=0, tiled=True)]
    ppermute x0 -> x7, waiting for transfers between devices: none -> 16.2 us  [swap_row(): lax.ppermute(v.astype(jnp.bfloat16), axis, perm=[(i, i ^ mask) for i in r...]
    ppermute x0 -> x7, starting transfers between devices: none -> 13.2 us  [swap_row(): lax.ppermute(v.astype(jnp.bfloat16), axis, perm=[(i, i ^ mask) for i in r...]
    all_to_all x2 -> x1, starting transfers between devices: 15.5 us -> 8.02 us  [reduce_rows(): got = lax.all_to_all(pieces, axis, split_axis=0, concat_axis=0, tiled=True)]
    unnamed x17 -> x23, local copies, waits for them, and re-layouts: 1.52 us -> 4.28 us
    add x0 -> x3, other arithmetic: none -> 2.37 us  [the longest x1 1.67 us: row_tree(): acc + swap_row(lax.dynamic_index_in_dim(view, y ^ 1, 2, keepdims=False),...]
    reduce_sum x2 -> x1, other arithmetic: 2.79 us -> 0.78 us  [reduce_rows(): return jnp.sum(got.astype(jnp.float32), axis=0)]
    all_to_all x1, waiting for transfers between devices: 19.5 us -> 17.6 us  [gather_rows(): got = lax.all_to_all(spread, axis, split_axis=0, concat_axis=0, tiled=True)]
  transfers between devices with their start and end apart: 21 -> 27, of which waited for: 12 -> 13; matrix products, arithmetic and copies ran while one was open for 25% -> 24% of each run, Pallas kernels for 0% -> 0%
where the time goes in v7:
time: 184 us; the launch traced here: 183 us
  waiting for transfers between devices  84.6 us (46%)
  starting transfers between devices  47 us (26%)
  matrix products  25.7 us (14%)
  local copies, waits for them, and re-layouts  19.7 us (11%)
  other arithmetic  4.41 us (2%)
    ppermute x18, waiting for transfers between devices, swap(): return lax.ppermute(x, 'col', perm=[(i, i ^ k) for i in range(n)])  50.9 us
    all_to_all x1, waiting for transfers between devices, gather_rows(): got = lax.all_to_all(spread, axis, split_axis=0, concat_axis=0, tiled=True)  17.6 us
    ppermute x7, waiting for transfers between devices, swap_row(): lax.ppermute(v.astype(jnp.bfloat16), axis, perm=[(i, i ^ mask) for i in r...  16.2 us
    ppermute x18, starting transfers between devices, swap(): return lax.ppermute(x, 'col', perm=[(i, i ^ k) for i in range(n)])  15.8 us
    ppermute x7, starting transfers between devices, swap_row(): lax.ppermute(v.astype(jnp.bfloat16), axis, perm=[(i, i ^ mask) for i in r...  13.2 us
    dot_general x8, matrix products, contract_last(): lax.dot_general(left, right, (((1,), (1,)), ((), ())), preferred_element_...  12.3 us
    all_to_all x1, starting transfers between devices, gather_rows(): got = lax.all_to_all(spread, axis, split_axis=0, concat_axis=0, tiled=True)  9.9 us
    all_to_all x1, starting transfers between devices, reduce_rows(): got = lax.all_to_all(pieces, axis, split_axis=0, concat_axis=0, tiled=True)  8.02 us
  transfers between devices with their start and end apart: 27, of which 13 were waited for; matrix products, arithmetic and copies ran while one was open for 24% of the time, Pallas kernels for 0%

profile of v7, /device:TPU:8, one launch (start us, length us, event | category | flops | bytes accessed | tf_op | source)
XLA Modules:
  0.0 182.5 jit_solution(5451116207758672549)
XLA Ops:
  3.0 9.9 %all-to-all-start = ((bf16[32,8,2,2048]{3,1,2,0:T(8,128)(2,1)}), bf16[32,8,2,2048]{3,1,2,0:T(8,128)(2,1)S(1)}, u32[]{:S(2)}, u32[]{:S(2)}) async-start(bf16[32,8,2,2048]{3,1,2,0:T(8,128)(2,1)} %broadcast_in_dim.66), calls=%async_computation | async-start | bytes 4194304 | tf_op jit(solution)/shard_map/all_to_all | solution.py:21
  12.9 2.9 %constant_dynamic-update-slice_fusion.1 = bf16[8192,224]{0,1:T(8,128)(2,1)} fusion(bf16[8192,112]{0,1:T(8,128)(2,1)} %param.6), kind=kLoop, calls=%fused_computation.122 | loop fusion | bytes 3670016
  15.8 2.9 %constant_dynamic-update-slice_fusion = bf16[8192,224]{0,1:T(8,128)(2,1)} fusion(bf16[8192,224]{0,1:T(8,128)(2,1)} %constant_dynamic-update-slice_fusion.1, bf16[8192,112]{0,1:T(8,128)(2,1)} %param.7), kind=kLoop, calls=%fused_computation.121 | loop fusion | bytes 3670016 | tf_op jit(solution)/shard_map/concatenate | solution.py:102
  18.7 3.5 %constant_dynamic-slice_fusion.11 = (bf16[2048,224]{0,1:T(8,128)(2,1)}, bf16[2048,224]{0,1:T(8,128)(2,1)}, bf16[2048,224]{0,1:T(8,128)(2,1)}) fusion(bf16[8192,224]{0,1:T(8,128)(2,1)} %constant_dynamic-update-slice_fusion, s32[]{:T(128)S(6)} %select_n.130, s32[]{:T(128)S(6)} %select_n.128, s32[]{:T(128)S(6)} %select_n.126), kind=kLoop, calls=%fused_computation.116 | loop fusion | bytes 5505036 | tf_op jit(solution)/shard_map/dynamic_slice | solution.py:59
  26.5 17.6 %all-to-all-done = bf16[32,8,2,2048]{3,1,2,0:T(8,128)(2,1)S(1)} async-done(((bf16[32,8,2,2048]{3,1,2,0:T(8,128)(2,1)}), bf16[32,8,2,2048]{3,1,2,0:T(8,128)(2,1)S(1)}, u32[]{:S(2)}, u32[]{:S(2)}) %all-to-all-start) | async-done | bytes 2097184 | tf_op jit(solution)/shard_map/all_to_all | solution.py:21
  44.3 2.4 %fusion.7 = f32[256,4,224]{2,0,1:T(8,128)S(1)} fusion(f32[256,4,224]{2,0,1:T(8,128)S(1)} %broadcast_in_dim.65, s32[]{:T(128)S(6)} %select_n.125, bf16[8192,224]{0,1:T(8,128)(2,1)} %constant_dynamic-update-slice_fusion, s32[]{:T(128)S(6)} %select_n.124, bf16[256,2,2048]{2,0,1:T(8,128)(2,1)S(1)} %bitcast.142), kind=kOutput, calls=%fused_computation.19 | convolution fusion | flops 234881024 | bytes 2228232 | tf_op jit(solution)/shard_map/dot_general | solution.py:111
  48.6 9.9 %collective-permute-done.1 = bf16[2048,224]{0,1:T(8,128)(2,1)S(1)} collective-permute-done((bf16[2048,224]{0,1:T(8,128)(2,1)}, bf16[2048,224]{0,1:T(8,128)(2,1)S(1)}, u32[]{:S(2)}, u32[]{:S(2)}) %collective-permute-start.1) | collective-permute-done | bytes 917536 | tf_op jit(solution)/shard_map/ppermute | solution.py:55
  58.9 17.1 %collective-permute-done.2 = bf16[2048,224]{0,1:T(8,128)(2,1)} collective-permute-done((bf16[2048,224]{0,1:T(8,128)(2,1)}, bf16[2048,224]{0,1:T(8,128)(2,1)}, u32[]{:S(2)}, u32[]{:S(2)}) %collective-permute-start.2) | collective-permute-done | bytes 917536 | tf_op jit(solution)/shard_map/ppermute | solution.py:55
  77.7 2.1 %collective-permute-start.3 = (f32[64,4,224]{2,0,1:T(8,128)S(1)}, f32[64,4,224]{2,0,1:T(8,128)S(1)}, u32[]{:S(2)}, u32[]{:S(2)}) collective-permute-start(f32[64,4,224]{2,0,1:T(8,128)S(1)} %get-tuple-element.18), channel_id=1, source_target_pairs={{0,1},{1,0},{2,3},{3,2},{4,5},{5,4},{6,7},{7,6},{8,9},{9,8},{10,11... | collective-permute-start | bytes 688136 | tf_op jit(solution)/shard_map/ppermute | solution.py:55
  84.7 3.3 %collective-permute-done.10 = bf16[112,2048]{1,0:T(8,128)(2,1)S(1)} collective-permute-done((bf16[112,2048]{1,0:T(8,128)(2,1)}, bf16[112,2048]{1,0:T(8,128)(2,1)S(1)}, u32[]{:S(2)}, u32[]{:S(2)}) %collective-permute-start.10) | collective-permute-done | bytes 458784 | tf_op jit(solution)/shard_map/ppermute | solution.py:55
  88.4 7.1 %collective-permute-done.11 = bf16[112,2048]{1,0:T(8,128)(2,1)S(1)} collective-permute-done((bf16[112,2048]{1,0:T(8,128)(2,1)S(1)}, bf16[112,2048]{1,0:T(8,128)(2,1)S(1)}, u32[]{:S(2)}, u32[]{:S(2)}) %collective-permute-start.11) | collective-permute-done | bytes 458784 | tf_op jit(solution)/shard_map/ppermute | solution.py:55
  96.0 2.4 %collective-permute-start.19 = (f32[64,4,112]{2,0,1:T(8,128)S(1)}, f32[64,4,112]{2,0,1:T(8,128)S(1)}, u32[]{:S(2)}, u32[]{:S(2)}) collective-permute-start(f32[64,4,112]{2,0,1:T(8,128)S(1)} %get-tuple-element.21), channel_id=1, source_target_pairs={{0,1},{1,0},{2,3},{3,2},{4,5},{5,4},{6,7},{7,6},{8,9},{9,8},{10,11... | collective-permute-start | bytes 344072 | tf_op jit(solution)/shard_map/ppermute | solution.py:55
  101.2 7.9 %collective-permute-done.4 = f32[64,4,224]{2,0,1:T(8,128)S(1)} collective-permute-done((f32[64,4,224]{2,0,1:T(8,128)S(1)}, f32[64,4,224]{2,0,1:T(8,128)S(1)}, u32[]{:S(2)}, u32[]{:S(2)}) %collective-permute-start.4) | collective-permute-done | bytes 229408 | tf_op jit(solution)/shard_map/ppermute | solution.py:55
  109.6 3.9 %collective-permute-done.20 = f32[64,4,112]{2,0,1:T(8,128)S(1)} collective-permute-done((f32[64,4,112]{2,0,1:T(8,128)S(1)}, f32[64,4,112]{2,0,1:T(8,128)S(1)}, u32[]{:S(2)}, u32[]{:S(2)}) %collective-permute-start.20) | collective-permute-done | bytes 114720 | tf_op jit(solution)/shard_map/ppermute | solution.py:55
  127.9 4.5 %collective-permute-start.12 = (bf16[4,4,8,2048]{3,2,0,1:T(8,128)(2,1)}, bf16[4,4,8,2048]{3,2,0,1:T(8,128)(2,1)}, u32[]{:S(2)}, u32[]{:S(2)}) collective-permute-start(bf16[4,4,8,2048]{3,2,0,1:T(8,128)(2,1)} %fusion.25), channel_id=1, source_target_pairs={{0,4},{4,0},{8,12},{12,8},{16,20},{20,16},{24,28},{28,24},{32,36},... | collective-permute-start | bytes 1572872 | tf_op jit(solution)/shard_map/ppermute | solution.py:39
  133.3 3.0 %fusion.17 = f32[256,2048]{1,0:T(8,128)} fusion(bf16[8192,224]{0,1:T(8,128)(2,1)} %constant_dynamic-update-slice_fusion, s32[]{:T(128)S(6)} %select_n.124, bf16[256,4,224]{2,0,1:T(8,128)(2,1)S(1)} %bitcast.160, s32[]{:T(128)S(6)} %select_n.125), kind=kOutput, calls=%fused_computation.36 | convolution fusion | flops 234881024 | bytes 3145736 | tf_op jit(solution)/shard_map/dot_general | solution.py:8
  137.3 2.3 %convolution_add_fusion.3 = f32[256,2048]{1,0:T(8,128)S(1)} fusion(f32[256,2048]{1,0:T(8,128)} %fusion.17, bf16[2048,224]{0,1:T(8,128)(2,1)} %collective-permute-done, bf16[256,4,224]{2,0,1:T(8,128)(2,1)S(1)} %bitcast.161, s32[]{:T(128)S(6)} %select_n.127), kind=kOutput, calls=%fused_computation.7 | convolution fusion | flops 235405312 | bytes 5242884 | tf_op jit(solution)/shard_map/dot_general | solution.py:8
  142.8 8.0 %all-to-all-start.1 = ((bf16[32,8,2048]{2,1,0:T(8,128)(2,1)}), bf16[32,8,2048]{2,1,0:T(8,128)(2,1)S(1)}, u32[]{:S(2)}, u32[]{:S(2)}) async-start(bf16[32,8,2048]{2,1,0:T(8,128)(2,1)} %fusion.3), calls=%async_computation.1 | async-start | bytes 2097152 | tf_op jit(solution)/shard_map/all_to_all | solution.py:27
  154.5 2.1 %collective-permute-start.15 = (bf16[4,8,2048]{2,1,0:T(8,128)(2,1)S(1)}, bf16[4,8,2048]{2,1,0:T(8,128)(2,1)S(1)}, u32[]{:S(2)}, u32[]{:S(2)}) collective-permute-start(bf16[4,8,2048]{2,1,0:T(8,128)(2,1)S(1)} %get-tuple-element.16), channel_id=1, source_target_pairs={{0,24},{4,28},{8,16},{12,20},{16,8},{20,12},{24,0},{28,4},{32,56},... | collective-permute-start | bytes 393224 | tf_op jit(solution)/shard_map/ppermute | solution.py:39
  158.3 9.8 %collective-permute-done.13 = bf16[4,8,2048]{2,1,0:T(8,128)(2,1)S(1)} collective-permute-done((bf16[4,8,2048]{2,1,0:T(8,128)(2,1)S(1)}, bf16[4,8,2048]{2,1,0:T(8,128)(2,1)S(1)}, u32[]{:S(2)}, u32[]{:S(2)}) %collective-permute-start.13) | collective-permute-done | bytes 131104 | tf_op jit(solution)/shard_map/ppermute | solution.py:39
  168.1 4.3 %collective-permute-done.15 = bf16[4,8,2048]{2,1,0:T(8,128)(2,1)S(1)} collective-permute-done((bf16[4,8,2048]{2,1,0:T(8,128)(2,1)S(1)}, bf16[4,8,2048]{2,1,0:T(8,128)(2,1)S(1)}, u32[]{:S(2)}, u32[]{:S(2)}) %collective-permute-start.15) | collective-permute-done | bytes 131104 | tf_op jit(solution)/shard_map/ppermute | solution.py:39
  173.7 2.0 %collective-permute-start.18 = (bf16[8,2048]{1,0:T(8,128)(2,1)S(1)}, bf16[8,2048]{1,0:T(8,128)(2,1)S(1)}, u32[]{:S(2)}, u32[]{:S(2)}) collective-permute-start(bf16[8,2048]{1,0:T(8,128)(2,1)S(1)} %get-tuple-element.28), channel_id=1, source_target_pairs={{0,96},{4,100},{8,104},{12,108},{16,112},{20,116},{24,120},{28,124... | collective-permute-start | bytes 98312 | tf_op jit(solution)/shard_map/ppermute | solution.py:39
  176.6 2.3 %fusion.65 = (bf16[2048,4,112]{0,2,1:T(8,128)(2,1)}, bf16[2048,4,112]{0,2,1:T(8,128)(2,1)}) fusion(bf16[2048,4,224]{0,2,1:T(8,128)(2,1)S(1)} %convolution_convert_fusion), kind=kLoop, calls=%fused_computation.124 | loop fusion | bytes 7340032 | tf_op jit(solution)/shard_map/slice | solution.py:147
  178.9 2.2 %collective-permute-done.17 = bf16[8,2048]{1,0:T(8,128)(2,1)S(1)} collective-permute-done((bf16[8,2048]{1,0:T(8,128)(2,1)S(1)}, bf16[8,2048]{1,0:T(8,128)(2,1)S(1)}, u32[]{:S(2)}, u32[]{:S(2)}) %collective-permute-start.17) | collective-permute-done | bytes 32800 | tf_op jit(solution)/shard_map/ppermute | solution.py:39
  (113 shorter events, 48.0 us)
Async XLA Ops:
  3.0 41.1 %all-to-all-start = ((bf16[32,8,2,2048]{3,1,2,0:T(8,128)(2,1)}), bf16[32,8,2,2048]{3,1,2,0:T(8,128)(2,1)S(1)}, u32[]{:S(2)}, u32[]{:S(2)}) async-start(bf16[32,8,2,2048]{3,1,2,0:T(8,128)(2,1)} %broadcast_in_dim.66), calls=%async_computation | async-start | bytes 4194304 | tf_op jit(solution)/shard_map/all_to_all | solution.py:21
  22.2 24.6 %collective-permute-start = (bf16[2048,224]{0,1:T(8,128)(2,1)}, bf16[2048,224]{0,1:T(8,128)(2,1)}, u32[]{:S(2)}, u32[]{:S(2)}) collective-permute-start(bf16[2048,224]{0,1:T(8,128)(2,1)} %get-tuple-element.11), channel_id=1, source_target_pairs={{0,1},{1,0},{2,3},{3,2},{4,5},{5,4},{6,7},{7,6},{8,9},{9,8},{10,11... | collective-permute-start | bytes 2752520 | tf_op jit(solution)/shard_map/ppermute | solution.py:55
  22.2 36.3 %collective-permute-start.1 = (bf16[2048,224]{0,1:T(8,128)(2,1)}, bf16[2048,224]{0,1:T(8,128)(2,1)S(1)}, u32[]{:S(2)}, u32[]{:S(2)}) collective-permute-start(bf16[2048,224]{0,1:T(8,128)(2,1)} %get-tuple-element.10), channel_id=1, source_target_pairs={{0,2},{1,3},{2,0},{3,1},{4,6},{5,7},{6,4},{7,5},{8,10},{9,11},{10,... | collective-permute-start | bytes 2752520 | tf_op jit(solution)/shard_map/ppermute | solution.py:55
  23.5 52.4 %collective-permute-start.2 = (bf16[2048,224]{0,1:T(8,128)(2,1)}, bf16[2048,224]{0,1:T(8,128)(2,1)}, u32[]{:S(2)}, u32[]{:S(2)}) collective-permute-start(bf16[2048,224]{0,1:T(8,128)(2,1)} %get-tuple-element.9), channel_id=1, source_target_pairs={{0,3},{1,2},{2,1},{3,0},{4,7},{5,6},{6,5},{7,4},{8,11},{9,10},{10,... | collective-permute-start | bytes 2752520 | tf_op jit(solution)/shard_map/ppermute | solution.py:55
  25.2 62.8 %collective-permute-start.10 = (bf16[112,2048]{1,0:T(8,128)(2,1)}, bf16[112,2048]{1,0:T(8,128)(2,1)S(1)}, u32[]{:S(2)}, u32[]{:S(2)}) collective-permute-start(bf16[112,2048]{1,0:T(8,128)(2,1)} %get-tuple-element.12), channel_id=1, source_target_pairs={{0,2},{1,3},{2,0},{3,1},{4,6},{5,7},{6,4},{7,5},{8,10},{9,11},{10,... | collective-permute-start | bytes 1376264 | tf_op jit(solution)/shard_map/ppermute | solution.py:55
  26.5 54.8 %collective-permute-start.9 = (bf16[112,2048]{1,0:T(8,128)(2,1)}, bf16[112,2048]{1,0:T(8,128)(2,1)}, u32[]{:S(2)}, u32[]{:S(2)}) collective-permute-start(bf16[112,2048]{1,0:T(8,128)(2,1)} %get-tuple-element.13), channel_id=1, source_target_pairs={{0,1},{1,0},{2,3},{3,2},{4,5},{5,4},{6,7},{7,6},{8,9},{9,8},{10,11... | collective-permute-start | bytes 1376264 | tf_op jit(solution)/shard_map/ppermute | solution.py:55
  46.8 48.7 %collective-permute-start.11 = (bf16[112,2048]{1,0:T(8,128)(2,1)S(1)}, bf16[112,2048]{1,0:T(8,128)(2,1)S(1)}, u32[]{:S(2)}, u32[]{:S(2)}) collective-permute-start(bf16[112,2048]{1,0:T(8,128)(2,1)S(1)} %copy-done.8), channel_id=1, source_target_pairs={{0,3},{1,2},{2,1},{3,0},{4,7},{5,6},{6,5},{7,4},{8,11},{9,10},{10,... | collective-permute-start | bytes 1376264 | tf_op jit(solution)/shard_map/ppermute | solution.py:55
  77.7 20.8 %collective-permute-start.3 = (f32[64,4,224]{2,0,1:T(8,128)S(1)}, f32[64,4,224]{2,0,1:T(8,128)S(1)}, u32[]{:S(2)}, u32[]{:S(2)}) collective-permute-start(f32[64,4,224]{2,0,1:T(8,128)S(1)} %get-tuple-element.18), channel_id=1, source_target_pairs={{0,1},{1,0},{2,3},{3,2},{4,5},{5,4},{6,7},{7,6},{8,9},{9,8},{10,11... | collective-permute-start | bytes 688136 | tf_op jit(solution)/shard_map/ppermute | solution.py:55
  79.9 21.3 %collective-permute-start.5 = (f32[64,4,224]{2,0,1:T(8,128)S(1)}, f32[64,4,224]{2,0,1:T(8,128)S(1)}, u32[]{:S(2)}, u32[]{:S(2)}) collective-permute-start(f32[64,4,224]{2,0,1:T(8,128)S(1)} %get-tuple-element.19), channel_id=1, source_target_pairs={{0,3},{1,2},{2,1},{3,0},{4,7},{5,6},{6,5},{7,4},{8,11},{9,10},{10,... | collective-permute-start | bytes 688136 | tf_op jit(solution)/shard_map/ppermute | solution.py:55
  81.4 27.6 %collective-permute-start.4 = (f32[64,4,224]{2,0,1:T(8,128)S(1)}, f32[64,4,224]{2,0,1:T(8,128)S(1)}, u32[]{:S(2)}, u32[]{:S(2)}) collective-permute-start(f32[64,4,224]{2,0,1:T(8,128)S(1)} %get-tuple-element.20), channel_id=1, source_target_pairs={{0,2},{1,3},{2,0},{3,1},{4,6},{5,7},{6,4},{7,5},{8,10},{9,11},{10,... | collective-permute-start | bytes 688136 | tf_op jit(solution)/shard_map/ppermute | solution.py:55
  96.0 13.1 %collective-permute-start.19 = (f32[64,4,112]{2,0,1:T(8,128)S(1)}, f32[64,4,112]{2,0,1:T(8,128)S(1)}, u32[]{:S(2)}, u32[]{:S(2)}) collective-permute-start(f32[64,4,112]{2,0,1:T(8,128)S(1)} %get-tuple-element.21), channel_id=1, source_target_pairs={{0,1},{1,0},{2,3},{3,2},{4,5},{5,4},{6,7},{7,6},{8,9},{9,8},{10,11... | collective-permute-start | bytes 344072 | tf_op jit(solution)/shard_map/ppermute | solution.py:55
  98.5 11.1 %collective-permute-start.21 = (f32[64,4,112]{2,0,1:T(8,128)S(1)}, f32[64,4,112]{2,0,1:T(8,128)S(1)}, u32[]{:S(2)}, u32[]{:S(2)}) collective-permute-start(f32[64,4,112]{2,0,1:T(8,128)S(1)} %get-tuple-element.22), channel_id=1, source_target_pairs={{0,3},{1,2},{2,1},{3,0},{4,7},{5,6},{6,5},{7,4},{8,11},{9,10},{10,... | collective-permute-start | bytes 344072 | tf_op jit(solution)/shard_map/ppermute | solution.py:55
  98.5 15.0 %collective-permute-start.20 = (f32[64,4,112]{2,0,1:T(8,128)S(1)}, f32[64,4,112]{2,0,1:T(8,128)S(1)}, u32[]{:S(2)}, u32[]{:S(2)}) collective-permute-start(f32[64,4,112]{2,0,1:T(8,128)S(1)} %get-tuple-element.23), channel_id=1, source_target_pairs={{0,2},{1,3},{2,0},{3,1},{4,6},{5,7},{6,4},{7,5},{8,10},{9,11},{10,... | collective-permute-start | bytes 344072 | tf_op jit(solution)/shard_map/ppermute | solution.py:55
  116.5 16.0 %collective-permute-start.23 = (bf16[64,4,224]{2,0,1:T(8,128)(2,1)S(1)}, bf16[64,4,224]{2,0,1:T(8,128)(2,1)S(1)}, u32[]{:S(2)}, u32[]{:S(2)}) collective-permute-start(bf16[64,4,224]{2,0,1:T(8,128)(2,1)S(1)} %get-tuple-element.30), channel_id=1, source_target_pairs={{0,2},{1,3},{2,0},{3,1},{4,6},{5,7},{6,4},{7,5},{8,10},{9,11},{10,... | collective-permute-start | bytes 344072 | tf_op jit(solution)/shard_map/ppermute | solution.py:55
  116.9 15.5 %collective-permute-start.22 = (bf16[64,4,224]{2,0,1:T(8,128)(2,1)S(1)}, bf16[64,4,224]{2,0,1:T(8,128)(2,1)S(1)}, u32[]{:S(2)}, u32[]{:S(2)}) collective-permute-start(bf16[64,4,224]{2,0,1:T(8,128)(2,1)S(1)} %get-tuple-element.30), channel_id=1, source_target_pairs={{0,1},{1,0},{2,3},{3,2},{4,5},{5,4},{6,7},{7,6},{8,9},{9,8},{10,11... | collective-permute-start | bytes 344072 | tf_op jit(solution)/shard_map/ppermute | solution.py:55
  117.5 15.2 %collective-permute-start.24 = (bf16[64,4,224]{2,0,1:T(8,128)(2,1)S(1)}, bf16[64,4,224]{2,0,1:T(8,128)(2,1)S(1)}, u32[]{:S(2)}, u32[]{:S(2)}) collective-permute-start(bf16[64,4,224]{2,0,1:T(8,128)(2,1)S(1)} %get-tuple-element.30), channel_id=1, source_target_pairs={{0,3},{1,2},{2,1},{3,0},{4,7},{5,6},{6,5},{7,4},{8,11},{9,10},{10,... | collective-permute-start | bytes 344072 | tf_op jit(solution)/shard_map/ppermute | solution.py:55
  127.9 23.0 %collective-permute-start.12 = (bf16[4,4,8,2048]{3,2,0,1:T(8,128)(2,1)}, bf16[4,4,8,2048]{3,2,0,1:T(8,128)(2,1)}, u32[]{:S(2)}, u32[]{:S(2)}) collective-permute-start(bf16[4,4,8,2048]{3,2,0,1:T(8,128)(2,1)} %fusion.25), channel_id=1, source_target_pairs={{0,4},{4,0},{8,12},{12,8},{16,20},{20,16},{24,28},{28,24},{32,36},... | collective-permute-start | bytes 1572872 | tf_op jit(solution)/shard_map/ppermute | solution.py:39
  142.8 38.9 %all-to-all-start.1 = ((bf16[32,8,2048]{2,1,0:T(8,128)(2,1)}), bf16[32,8,2048]{2,1,0:T(8,128)(2,1)S(1)}, u32[]{:S(2)}, u32[]{:S(2)}) async-start(bf16[32,8,2048]{2,1,0:T(8,128)(2,1)} %fusion.3), calls=%async_computation.1 | async-start | bytes 2097152 | tf_op jit(solution)/shard_map/all_to_all | solution.py:27
  152.6 15.5 %collective-permute-start.13 = (bf16[4,8,2048]{2,1,0:T(8,128)(2,1)S(1)}, bf16[4,8,2048]{2,1,0:T(8,128)(2,1)S(1)}, u32[]{:S(2)}, u32[]{:S(2)}) collective-permute-start(bf16[4,8,2048]{2,1,0:T(8,128)(2,1)S(1)} %get-tuple-element.15), channel_id=1, source_target_pairs={{0,8},{4,12},{8,0},{12,4},{16,24},{20,28},{24,16},{28,20},{32,40},... | collective-permute-start | bytes 393224 | tf_op jit(solution)/shard_map/ppermute | solution.py:39
  154.5 17.8 %collective-permute-start.15 = (bf16[4,8,2048]{2,1,0:T(8,128)(2,1)S(1)}, bf16[4,8,2048]{2,1,0:T(8,128)(2,1)S(1)}, u32[]{:S(2)}, u32[]{:S(2)}) collective-permute-start(bf16[4,8,2048]{2,1,0:T(8,128)(2,1)S(1)} %get-tuple-element.16), channel_id=1, source_target_pairs={{0,24},{4,28},{8,16},{12,20},{16,8},{20,12},{24,0},{28,4},{32,56},... | collective-permute-start | bytes 393224 | tf_op jit(solution)/shard_map/ppermute | solution.py:39
  156.6 15.8 %collective-permute-start.14 = (bf16[4,8,2048]{2,1,0:T(8,128)(2,1)S(1)}, bf16[4,8,2048]{2,1,0:T(8,128)(2,1)S(1)}, u32[]{:S(2)}, u32[]{:S(2)}) collective-permute-start(bf16[4,8,2048]{2,1,0:T(8,128)(2,1)S(1)} %get-tuple-element.17), channel_id=1, source_target_pairs={{0,16},{4,20},{8,24},{12,28},{16,0},{20,4},{24,8},{28,12},{32,48},... | collective-permute-start | bytes 393224 | tf_op jit(solution)/shard_map/ppermute | solution.py:39
  172.4 6.5 %collective-permute-start.16 = (bf16[8,2048]{1,0:T(8,128)(2,1)S(1)}, bf16[8,2048]{1,0:T(8,128)(2,1)S(1)}, u32[]{:S(2)}, u32[]{:S(2)}) collective-permute-start(bf16[8,2048]{1,0:T(8,128)(2,1)S(1)} %get-tuple-element.27), channel_id=1, source_target_pairs={{0,32},{4,36},{8,40},{12,44},{16,48},{20,52},{24,56},{28,60},{32,0... | collective-permute-start | bytes 98312 | tf_op jit(solution)/shard_map/ppermute | solution.py:39
  173.7 5.2 %collective-permute-start.18 = (bf16[8,2048]{1,0:T(8,128)(2,1)S(1)}, bf16[8,2048]{1,0:T(8,128)(2,1)S(1)}, u32[]{:S(2)}, u32[]{:S(2)}) collective-permute-start(bf16[8,2048]{1,0:T(8,128)(2,1)S(1)} %get-tuple-element.28), channel_id=1, source_target_pairs={{0,96},{4,100},{8,104},{12,108},{16,112},{20,116},{24,120},{28,124... | collective-permute-start | bytes 98312 | tf_op jit(solution)/shard_map/ppermute | solution.py:39
  175.7 5.4 %collective-permute-start.17 = (bf16[8,2048]{1,0:T(8,128)(2,1)S(1)}, bf16[8,2048]{1,0:T(8,128)(2,1)S(1)}, u32[]{:S(2)}, u32[]{:S(2)}) collective-permute-start(bf16[8,2048]{1,0:T(8,128)(2,1)S(1)} %get-tuple-element.29), channel_id=1, source_target_pairs={{0,64},{4,68},{8,72},{12,76},{16,80},{20,84},{24,88},{28,92},{32,9... | collective-permute-start | bytes 98312 | tf_op jit(solution)/shard_map/ppermute | solution.py:39
  (14 other events, 132.1 us)

commit v8 on v6

--- a/solution.py
+++ b/solution.py
@@ -80,7 +80,11 @@
     gu_rel = col_scatter(joined, 0, n_col)
     down_rel = col_scatter(down_weight, 1, n_col)
 
-    both = gather_rows(jnp.stack([tokens, out_grad], axis=1), "row", n_row)
+    pair = jnp.stack([tokens, out_grad], axis=1)
+    pair, gu_near, down_near = lax.optimization_barrier((pair, gu_rel[1], down_rel[1]))
+    gu_rel[1] = gu_near
+    down_rel[1] = down_near
+    both = gather_rows(pair, "row", n_row)
     full_tokens = both[:, 0]
     grad_full = both[:, 1]
     count = full_tokens.shape[0]

time: 180 us -> 190 us (1.056)
  waiting for transfers between devices: 96.1 us -> 108 us
    all_to_all x1, waiting for transfers between devices: 19.4 us -> 29.8 us  [gather_rows(): got = lax.all_to_all(spread, axis, split_axis=0, concat_axis=0, tiled=True)]
  transfers between devices with their start and end apart: 20 -> 20, of which waited for: 9 -> 11; matrix products, arithmetic and copies ran while one was open for 18% -> 13% of each run, Pallas kernels for 0% -> 0%
where the time goes in v8:
time: 190 us; the launch traced here: 189 us
  waiting for transfers between devices  108 us (57%)
  starting transfers between devices  35.3 us (19%)
  matrix products  23.6 us (12%)
  local copies, waits for them, and re-layouts  17.3 us (9%)
  other arithmetic  3.94 us (2%)
    ppermute x18, waiting for transfers between devices, swap(): return lax.ppermute(x, 'col', perm=[(i, i ^ k) for i in range(n)])  51.8 us
    all_to_all x1, waiting for transfers between devices, gather_rows(): got = lax.all_to_all(spread, axis, split_axis=0, concat_axis=0, tiled=True)  29.8 us
    all_to_all x1, waiting for transfers between devices, reduce_rows(): got = lax.all_to_all(pieces, axis, split_axis=0, concat_axis=0, tiled=True)  26.6 us
    ppermute x18, starting transfers between devices, swap(): return lax.ppermute(x, 'col', perm=[(i, i ^ k) for i in range(n)])  14.4 us
    all_to_all x1, starting transfers between devices, reduce_rows(): got = lax.all_to_all(pieces, axis, split_axis=0, concat_axis=0, tiled=True)  10.9 us
    dot_general x8, matrix products, contract_last(): lax.dot_general(left, right, (((1,), (1,)), ((), ())), preferred_element_...  10.2 us
    all_to_all x1, starting transfers between devices, gather_rows(): got = lax.all_to_all(spread, axis, split_axis=0, concat_axis=0, tiled=True)  10 us
    dot_general x4, matrix products, shards(): jnp.dot(full_tokens, w, preferred_element_type=jnp.float32)  5.38 us
  transfers between devices with their start and end apart: 20, of which 11 were waited for; matrix products, arithmetic and copies ran while one was open for 13% of the time, Pallas kernels for 0%

profile of v8, /device:TPU:8, one launch (start us, length us, event | category | flops | bytes accessed | tf_op | source)
XLA Modules:
  0.0 189.3 jit_solution(12851373178898013196)
XLA Ops:
  0.7 3.0 %constant_dynamic-update-slice_fusion.1 = bf16[8192,224]{0,1:T(8,128)(2,1)} fusion(bf16[8192,112]{0,1:T(8,128)(2,1)} %param.6), kind=kLoop, calls=%fused_computation.104 | loop fusion | bytes 3670016
  5.0 3.4 %constant_dynamic-slice_fusion.9 = (bf16[2048,224]{0,1:T(8,128)(2,1)}, bf16[2048,224]{0,1:T(8,128)(2,1)}, bf16[2048,224]{0,1:T(8,128)(2,1)S(1)}) fusion(bf16[8192,224]{0,1:T(8,128)(2,1)} %constant_dynamic-update-slice_fusion, s32[]{:T(128)S(6)} %select_n.77, s32[]{:T(128)S(6)} %select_n.79, s32[]{:T(128)S(6)} %select_n.36), kind=kLoop, calls=%fused_computation.98 | loop fusion | bytes 5505036 | tf_op jit(solution)/shard_map/dynamic_slice | solution.py:36
  10.0 1.7 collective-permute-done.1
  13.3 10.0 %all-to-all-start = ((bf16[32,8,2,2048]{3,1,2,0:T(8,128)(2,1)}), bf16[32,8,2,2048]{3,1,2,0:T(8,128)(2,1)}, u32[]{:S(2)}, u32[]{:S(2)}) async-start(bf16[32,8,2,2048]{3,1,2,0:T(8,128)(2,1)} %broadcast_in_dim.66), calls=%async_computation | async-start | bytes 4194304 | tf_op jit(solution)/shard_map/all_to_all | solution.py:21
  24.8 1.7 collective-permute-start.11
  27.2 29.8 %all-to-all-done = bf16[32,8,2,2048]{3,1,2,0:T(8,128)(2,1)} async-done(((bf16[32,8,2,2048]{3,1,2,0:T(8,128)(2,1)}), bf16[32,8,2,2048]{3,1,2,0:T(8,128)(2,1)}, u32[]{:S(2)}, u32[]{:S(2)}) %all-to-all-start) | async-done | bytes 2097184 | tf_op jit(solution)/shard_map/all_to_all | solution.py:21
  57.0 1.7 copy.82
  58.8 1.6 fusion.9
  60.4 1.6 fusion.8
  62.1 6.9 %collective-permute-done.2 = bf16[2048,224]{0,1:T(8,128)(2,1)S(1)} collective-permute-done((bf16[2048,224]{0,1:T(8,128)(2,1)}, bf16[2048,224]{0,1:T(8,128)(2,1)S(1)}, u32[]{:S(2)}, u32[]{:S(2)}) %collective-permute-start.2) | collective-permute-done | bytes 917536 | tf_op jit(solution)/shard_map/ppermute | solution.py:32
  69.5 17.8 %collective-permute-done.3 = bf16[2048,224]{0,1:T(8,128)(2,1)} collective-permute-done((bf16[2048,224]{0,1:T(8,128)(2,1)}, bf16[2048,224]{0,1:T(8,128)(2,1)}, u32[]{:S(2)}, u32[]{:S(2)}) %collective-permute-start.3) | collective-permute-done | bytes 917536 | tf_op jit(solution)/shard_map/ppermute | solution.py:32
  89.0 1.7 collective-permute-start.4
  90.7 1.7 collective-permute-start.5
  95.4 12.9 %collective-permute-done.10 = bf16[112,2048]{1,0:T(8,128)(2,1)S(1)} collective-permute-done((bf16[112,2048]{1,0:T(8,128)(2,1)}, bf16[112,2048]{1,0:T(8,128)(2,1)S(1)}, u32[]{:S(2)}, u32[]{:S(2)}) %collective-permute-start.10) | collective-permute-done | bytes 458784 | tf_op jit(solution)/shard_map/ppermute | solution.py:32
  110.5 2.0 %collective-permute-start.13 = (f32[64,4,112]{2,0,1:T(8,128)S(1)}, f32[64,4,112]{2,0,1:T(8,128)S(1)}, u32[]{:S(2)}, u32[]{:S(2)}) collective-permute-start(f32[64,4,112]{2,0,1:T(8,128)S(1)} %get-tuple-element.26), channel_id=1, source_target_pairs={{0,2},{1,3},{2,0},{3,1},{4,6},{5,7},{6,4},{7,5},{8,10},{9,11},{10,... | collective-permute-start | bytes 344072 | tf_op jit(solution)/shard_map/ppermute | solution.py:32
  112.5 7.0 %collective-permute-done.5 = f32[64,4,224]{2,0,1:T(8,128)S(1)} collective-permute-done((f32[64,4,224]{2,0,1:T(8,128)S(1)}, f32[64,4,224]{2,0,1:T(8,128)S(1)}, u32[]{:S(2)}, u32[]{:S(2)}) %collective-permute-start.5) | collective-permute-done | bytes 229408 | tf_op jit(solution)/shard_map/ppermute | solution.py:32
  120.9 3.6 %collective-permute-done.13 = f32[64,4,112]{2,0,1:T(8,128)S(1)} collective-permute-done((f32[64,4,112]{2,0,1:T(8,128)S(1)}, f32[64,4,112]{2,0,1:T(8,128)S(1)}, u32[]{:S(2)}, u32[]{:S(2)}) %collective-permute-start.13) | collective-permute-done | bytes 114720 | tf_op jit(solution)/shard_map/ppermute | solution.py:32
  128.4 1.9 %collective-permute-start.17 = (bf16[64,4,224]{2,0,1:T(8,128)(2,1)S(1)}, bf16[64,4,224]{2,0,1:T(8,128)(2,1)S(1)}, u32[]{:S(2)}, u32[]{:S(2)}) collective-permute-start(bf16[64,4,224]{2,0,1:T(8,128)(2,1)S(1)} %get-tuple-element.32), channel_id=1, source_target_pairs={{0,3},{1,2},{2,1},{3,0},{4,7},{5,6},{6,5},{7,4},{8,11},{9,10},{10,... | collective-permute-start | bytes 344072 | tf_op jit(solution)/shard_map/ppermute | solution.py:32
  139.6 1.7 fusion.29
  143.3 10.9 %all-to-all-start.1 = ((bf16[32,8,2,2048]{3,1,2,0:T(8,128)(2,1)}), bf16[32,8,2,2048]{3,1,2,0:T(8,128)(2,1)}, u32[]{:S(2)}, u32[]{:S(2)}) async-start(bf16[32,8,2,2048]{3,1,2,0:T(8,128)(2,1)} %pad_maximum_fusion), calls=%async_computation.1 | async-start | bytes 4194304 | tf_op jit(solution)/shard_map/all_to_all | solution.py:27
  154.2 1.9 %convolution_convert_fusion.1 = bf16[448,2048]{1,0:T(8,128)(2,1)} fusion(bf16[256,448]{1,0:T(8,128)(2,1)S(1)} %bitcast.137, bf16[256,2,2048]{2,0,1:T(8,128)(2,1)S(1)} %bitcast.131), kind=kOutput, calls=%fused_computation.2 | convolution fusion | flops 470679552 | bytes 3145728 | tf_op jit(solution)/shard_map/dot_general | solution.py:14
  157.9 2.3 %fusion.56 = (bf16[2048,4,112]{0,2,1:T(8,128)(2,1)}, bf16[2048,4,112]{0,2,1:T(8,128)(2,1)}) fusion(bf16[2048,4,224]{0,2,1:T(8,128)(2,1)S(1)} %convolution_convert_fusion), kind=kLoop, calls=%fused_computation.106 | loop fusion | bytes 7340032 | tf_op jit(solution)/shard_map/slice | solution.py:129
  160.2 26.6 %all-to-all-done.1 = bf16[32,8,2,2048]{3,1,2,0:T(8,128)(2,1)} async-done(((bf16[32,8,2,2048]{3,1,2,0:T(8,128)(2,1)}), bf16[32,8,2,2048]{3,1,2,0:T(8,128)(2,1)}, u32[]{:S(2)}, u32[]{:S(2)}) %all-to-all-start.1) | async-done | bytes 2097184 | tf_op jit(solution)/shard_map/all_to_all | solution.py:27
  186.7 1.9 %convert_reduce_fusion = f32[8,2,2048]{2,0,1:T(8,128)S(1)} fusion(bf16[32,8,2,2048]{3,1,2,0:T(8,128)(2,1)} %all-to-all-done.1), kind=kLoop, calls=%fused_computation | loop fusion | flops 2064384 | bytes 2228224 | tf_op jit(solution)/shard_map/reduce_sum | solution.py:28
  (85 shorter events, 32.7 us)
Async XLA Ops:
  0.6 3.1 %copy-start.1 = (bf16[8192,112]{0,1:T(8,128)(2,1)S(1)}, bf16[8192,112]{0,1:T(8,128)(2,1)}, u32[]{:S(2)}) copy-start(bf16[8192,112]{0,1:T(8,128)(2,1)} %param.7) | copy-start | bytes 5505028
  5.0 3.4 %copy-start = (bf16[112,8192]{1,0:T(8,128)(2,1)S(1)}, bf16[112,8192]{1,0:T(8,128)(2,1)}, u32[]{:S(2)}) copy-start(bf16[112,8192]{1,0:T(8,128)(2,1)} %param.8) | copy-start | bytes 5505028
  8.4 3.3 %collective-permute-start = (bf16[2048,224]{0,1:T(8,128)(2,1)S(1)}, bf16[2048,224]{0,1:T(8,128)(2,1)}, u32[]{:S(2)}, u32[]{:S(2)}) collective-permute-start(bf16[2048,224]{0,1:T(8,128)(2,1)S(1)} %get-tuple-element.17), channel_id=1, source_target_pairs={{0,1},{1,0},{2,3},{3,2},{4,5},{5,4},{6,7},{7,6},{8,9},{9,8},{10,11... | collective-permute-start | bytes 2752520 | tf_op jit(solution)/shard_map/ppermute | solution.py:32
  9.5 2.2 %collective-permute-start.1 = (bf16[112,2048]{1,0:T(8,128)(2,1)S(1)}, bf16[112,2048]{1,0:T(8,128)(2,1)}, u32[]{:S(2)}, u32[]{:S(2)}) collective-permute-start(bf16[112,2048]{1,0:T(8,128)(2,1)S(1)} %get-tuple-element.19), channel_id=1, source_target_pairs={{0,1},{1,0},{2,3},{3,2},{4,5},{5,4},{6,7},{7,6},{8,9},{9,8},{10,11... | collective-permute-start | bytes 1376264 | tf_op jit(solution)/shard_map/ppermute | solution.py:32
  13.3 43.6 %all-to-all-start = ((bf16[32,8,2,2048]{3,1,2,0:T(8,128)(2,1)}), bf16[32,8,2,2048]{3,1,2,0:T(8,128)(2,1)}, u32[]{:S(2)}, u32[]{:S(2)}) async-start(bf16[32,8,2,2048]{3,1,2,0:T(8,128)(2,1)} %broadcast_in_dim.66), calls=%async_computation | async-start | bytes 4194304 | tf_op jit(solution)/shard_map/all_to_all | solution.py:21
  23.3 45.7 %collective-permute-start.2 = (bf16[2048,224]{0,1:T(8,128)(2,1)}, bf16[2048,224]{0,1:T(8,128)(2,1)S(1)}, u32[]{:S(2)}, u32[]{:S(2)}) collective-permute-start(bf16[2048,224]{0,1:T(8,128)(2,1)} %get-tuple-element.15), channel_id=1, source_target_pairs={{0,2},{1,3},{2,0},{3,1},{4,6},{5,7},{6,4},{7,5},{8,10},{9,11},{10,... | collective-permute-start | bytes 2752520 | tf_op jit(solution)/shard_map/ppermute | solution.py:32
  24.8 62.5 %collective-permute-start.3 = (bf16[2048,224]{0,1:T(8,128)(2,1)}, bf16[2048,224]{0,1:T(8,128)(2,1)}, u32[]{:S(2)}, u32[]{:S(2)}) collective-permute-start(bf16[2048,224]{0,1:T(8,128)(2,1)} %get-tuple-element.16), channel_id=1, source_target_pairs={{0,3},{1,2},{2,1},{3,0},{4,7},{5,6},{6,5},{7,4},{8,11},{9,10},{10,... | collective-permute-start | bytes 2752520 | tf_op jit(solution)/shard_map/ppermute | solution.py:32
  24.8 84.0 %collective-permute-start.11 = (bf16[112,2048]{1,0:T(8,128)(2,1)}, bf16[112,2048]{1,0:T(8,128)(2,1)}, u32[]{:S(2)}, u32[]{:S(2)}) collective-permute-start(bf16[112,2048]{1,0:T(8,128)(2,1)} %get-tuple-element.18), channel_id=1, source_target_pairs={{0,3},{1,2},{2,1},{3,0},{4,7},{5,6},{6,5},{7,4},{8,11},{9,10},{10,... | collective-permute-start | bytes 1376264 | tf_op jit(solution)/shard_map/ppermute | solution.py:32
  26.5 81.8 %collective-permute-start.10 = (bf16[112,2048]{1,0:T(8,128)(2,1)}, bf16[112,2048]{1,0:T(8,128)(2,1)S(1)}, u32[]{:S(2)}, u32[]{:S(2)}) collective-permute-start(bf16[112,2048]{1,0:T(8,128)(2,1)} %get-tuple-element.20), channel_id=1, source_target_pairs={{0,2},{1,3},{2,0},{3,1},{4,6},{5,7},{6,4},{7,5},{8,10},{9,11},{10,... | collective-permute-start | bytes 1376264 | tf_op jit(solution)/shard_map/ppermute | solution.py:32
  69.0 19.9 %copy-start.2 = (bf16[2048,224]{0,1:T(8,128)(2,1)}, bf16[2048,224]{0,1:T(8,128)(2,1)S(1)}, u32[]{:S(2)}) copy-start(bf16[2048,224]{0,1:T(8,128)(2,1)S(1)} %collective-permute-done.2) | copy-start | bytes 2752516
  89.0 21.4 %collective-permute-start.4 = (f32[64,4,224]{2,0,1:T(8,128)S(1)}, f32[64,4,224]{2,0,1:T(8,128)S(1)}, u32[]{:S(2)}, u32[]{:S(2)}) collective-permute-start(f32[64,4,224]{2,0,1:T(8,128)S(1)} %get-tuple-element.21), channel_id=1, source_target_pairs={{0,1},{1,0},{2,3},{3,2},{4,5},{5,4},{6,7},{7,6},{8,9},{9,8},{10,11... | collective-permute-start | bytes 688136 | tf_op jit(solution)/shard_map/ppermute | solution.py:32
  90.7 21.8 %collective-permute-start.6 = (f32[64,4,224]{2,0,1:T(8,128)S(1)}, f32[64,4,224]{2,0,1:T(8,128)S(1)}, u32[]{:S(2)}, u32[]{:S(2)}) collective-permute-start(f32[64,4,224]{2,0,1:T(8,128)S(1)} %get-tuple-element.22), channel_id=1, source_target_pairs={{0,3},{1,2},{2,1},{3,0},{4,7},{5,6},{6,5},{7,4},{8,11},{9,10},{10,... | collective-permute-start | bytes 688136 | tf_op jit(solution)/shard_map/ppermute | solution.py:32
  90.7 28.8 %collective-permute-start.5 = (f32[64,4,224]{2,0,1:T(8,128)S(1)}, f32[64,4,224]{2,0,1:T(8,128)S(1)}, u32[]{:S(2)}, u32[]{:S(2)}) collective-permute-start(f32[64,4,224]{2,0,1:T(8,128)S(1)} %get-tuple-element.23), channel_id=1, source_target_pairs={{0,2},{1,3},{2,0},{3,1},{4,6},{5,7},{6,4},{7,5},{8,10},{9,11},{10,... | collective-permute-start | bytes 688136 | tf_op jit(solution)/shard_map/ppermute | solution.py:32
  110.3 9.4 %collective-permute-start.12 = (f32[64,4,112]{2,0,1:T(8,128)S(1)}, f32[64,4,112]{2,0,1:T(8,128)S(1)}, u32[]{:S(2)}, u32[]{:S(2)}) collective-permute-start(f32[64,4,112]{2,0,1:T(8,128)S(1)} %get-tuple-element.24), channel_id=1, source_target_pairs={{0,1},{1,0},{2,3},{3,2},{4,5},{5,4},{6,7},{7,6},{8,9},{9,8},{10,11... | collective-permute-start | bytes 344072 | tf_op jit(solution)/shard_map/ppermute | solution.py:32
  110.4 10.5 %collective-permute-start.14 = (f32[64,4,112]{2,0,1:T(8,128)S(1)}, f32[64,4,112]{2,0,1:T(8,128)S(1)}, u32[]{:S(2)}, u32[]{:S(2)}) collective-permute-start(f32[64,4,112]{2,0,1:T(8,128)S(1)} %get-tuple-element.25), channel_id=1, source_target_pairs={{0,3},{1,2},{2,1},{3,0},{4,7},{5,6},{6,5},{7,4},{8,11},{9,10},{10,... | collective-permute-start | bytes 344072 | tf_op jit(solution)/shard_map/ppermute | solution.py:32
  110.5 14.0 %collective-permute-start.13 = (f32[64,4,112]{2,0,1:T(8,128)S(1)}, f32[64,4,112]{2,0,1:T(8,128)S(1)}, u32[]{:S(2)}, u32[]{:S(2)}) collective-permute-start(f32[64,4,112]{2,0,1:T(8,128)S(1)} %get-tuple-element.26), channel_id=1, source_target_pairs={{0,2},{1,3},{2,0},{3,1},{4,6},{5,7},{6,4},{7,5},{8,10},{9,11},{10,... | collective-permute-start | bytes 344072 | tf_op jit(solution)/shard_map/ppermute | solution.py:32
  125.4 5.1 %collective-permute-start.9 = (bf16[64,448]{1,0:T(8,128)(2,1)S(1)}, bf16[64,448]{1,0:T(8,128)(2,1)S(1)}, u32[]{:S(2)}, u32[]{:S(2)}) collective-permute-start(bf16[64,448]{1,0:T(8,128)(2,1)S(1)} %multiply_convert_fusion.2), channel_id=1, source_target_pairs={{0,3},{1,2},{2,1},{3,0},{4,7},{5,6},{6,5},{7,4},{8,11},{9,10},{10,... | collective-permute-start | bytes 172040 | tf_op jit(solution)/shard_map/ppermute | solution.py:32
  125.5 5.0 %collective-permute-start.8 = (bf16[64,448]{1,0:T(8,128)(2,1)S(1)}, bf16[64,448]{1,0:T(8,128)(2,1)S(1)}, u32[]{:S(2)}, u32[]{:S(2)}) collective-permute-start(bf16[64,448]{1,0:T(8,128)(2,1)S(1)} %multiply_convert_fusion.2), channel_id=1, source_target_pairs={{0,2},{1,3},{2,0},{3,1},{4,6},{5,7},{6,4},{7,5},{8,10},{9,11},{10,... | collective-permute-start | bytes 172040 | tf_op jit(solution)/shard_map/ppermute | solution.py:32
  126.5 1.9 %collective-permute-start.7 = (bf16[64,448]{1,0:T(8,128)(2,1)S(1)}, bf16[64,448]{1,0:T(8,128)(2,1)S(1)}, u32[]{:S(2)}, u32[]{:S(2)}) collective-permute-start(bf16[64,448]{1,0:T(8,128)(2,1)S(1)} %multiply_convert_fusion.2), channel_id=1, source_target_pairs={{0,1},{1,0},{2,3},{3,2},{4,5},{5,4},{6,7},{7,6},{8,9},{9,8},{10,11... | collective-permute-start | bytes 172040 | tf_op jit(solution)/shard_map/ppermute | solution.py:32
  127.4 8.3 %collective-permute-start.16 = (bf16[64,4,224]{2,0,1:T(8,128)(2,1)S(1)}, bf16[64,4,224]{2,0,1:T(8,128)(2,1)S(1)}, u32[]{:S(2)}, u32[]{:S(2)}) collective-permute-start(bf16[64,4,224]{2,0,1:T(8,128)(2,1)S(1)} %get-tuple-element.32), channel_id=1, source_target_pairs={{0,2},{1,3},{2,0},{3,1},{4,6},{5,7},{6,4},{7,5},{8,10},{9,11},{10,... | collective-permute-start | bytes 344072 | tf_op jit(solution)/shard_map/ppermute | solution.py:32
  127.8 7.8 %collective-permute-start.15 = (bf16[64,4,224]{2,0,1:T(8,128)(2,1)S(1)}, bf16[64,4,224]{2,0,1:T(8,128)(2,1)S(1)}, u32[]{:S(2)}, u32[]{:S(2)}) collective-permute-start(bf16[64,4,224]{2,0,1:T(8,128)(2,1)S(1)} %get-tuple-element.32), channel_id=1, source_target_pairs={{0,1},{1,0},{2,3},{3,2},{4,5},{5,4},{6,7},{7,6},{8,9},{9,8},{10,11... | collective-permute-start | bytes 344072 | tf_op jit(solution)/shard_map/ppermute | solution.py:32
  128.4 7.8 %collective-permute-start.17 = (bf16[64,4,224]{2,0,1:T(8,128)(2,1)S(1)}, bf16[64,4,224]{2,0,1:T(8,128)(2,1)S(1)}, u32[]{:S(2)}, u32[]{:S(2)}) collective-permute-start(bf16[64,4,224]{2,0,1:T(8,128)(2,1)S(1)} %get-tuple-element.32), channel_id=1, source_target_pairs={{0,3},{1,2},{2,1},{3,0},{4,7},{5,6},{6,5},{7,4},{8,11},{9,10},{10,... | collective-permute-start | bytes 344072 | tf_op jit(solution)/shard_map/ppermute | solution.py:32
  139.6 1.7 copy-start.3
  143.3 43.4 %all-to-all-start.1 = ((bf16[32,8,2,2048]{3,1,2,0:T(8,128)(2,1)}), bf16[32,8,2,2048]{3,1,2,0:T(8,128)(2,1)}, u32[]{:S(2)}, u32[]{:S(2)}) async-start(bf16[32,8,2,2048]{3,1,2,0:T(8,128)(2,1)} %pad_maximum_fusion), calls=%async_computation.1 | async-start | bytes 4194304 | tf_op jit(solution)/shard_map/all_to_all | solution.py:27
  (2 other events, 3.1 us)

commit v9 on v6

--- a/solution.py
+++ b/solution.py
@@ -76,8 +76,12 @@
     n_col = lax.axis_size("col")
     me = lax.axis_index("col")
     unit = gate_weight.shape[1]
-    joined = jnp.concatenate([gate_weight, up_weight], axis=1)
-    gu_rel = col_scatter(joined, 0, n_col)
+    feat = gate_weight.shape[0] // n_col
+
+    def gu_piece(index):
+        return jnp.stack([piece(gate_weight, index, feat, 0), piece(up_weight, index, feat, 0)])
+
+    gu_rel = [gu_piece(me)] + [swap(gu_piece(me ^ k), k, n_col) for k in range(1, n_col)]
     down_rel = col_scatter(down_weight, 1, n_col)
 
     both = gather_rows(jnp.stack([tokens, out_grad], axis=1), "row", n_row)
@@ -85,7 +89,18 @@
     grad_full = both[:, 1]
     count = full_tokens.shape[0]
 
-    gu_part = place([jnp.dot(full_tokens, w, preferred_element_type=jnp.float32) for w in gu_rel], me, 1)
+    gu_part = place(
+        [
+            jnp.concatenate(
+                [jnp.dot(full_tokens, w[0], preferred_element_type=jnp.float32),
+                 jnp.dot(full_tokens, w[1], preferred_element_type=jnp.float32)],
+                axis=1,
+            )
+            for w in gu_rel
+        ],
+        me,
+        1,
+    )
     gu_sum = col_reduce(gu_part, n_col)
     share = gu_sum.shape[0]
     gate_sum = gu_sum[:, :, :unit].reshape(share, n_col * unit)
@@ -114,7 +129,7 @@
     in_part = None
     for k, w in enumerate(gu_rel):
         g = lax.dynamic_index_in_dim(grads, me ^ k, 1, keepdims=False)
-        t = contract_last(g, w)
+        t = contract_last(g[:, :unit], w[0]) + contract_last(g[:, unit:], w[1])
         in_part = t if in_part is None else in_part + t
     summed = reduce_rows(jnp.stack([term, in_part], axis=1), "row", n_row)
     output = summed[:, 0]

time: 180 us -> 196 us (1.089)
  matrix products: 23.8 us -> 37.3 us
  local copies, waits for them, and re-layouts: 17.4 us -> 12.9 us
  waiting for transfers between devices: 96.1 us -> 100 us
  other arithmetic: 4.7 us -> 7.79 us
    dot_general x8 -> x12, matrix products: 10.3 us -> 17.4 us  [contract_last(): lax.dot_general(left, right, (((1,), (1,)), ((), ())), preferred_element_...]
    dot_general x4 -> x8, matrix products: 5.43 us -> 9.91 us  [the longest x4 4.96 us: shards(): jnp.dot(full_tokens, w[1], preferred_element_type=jnp.float32)]
    dynamic_slice x4 -> x3, local copies, waits for them, and re-layouts: 4.74 us -> 1.27 us  [piece(): return lax.dynamic_slice_in_dim(x, index * size, size, axis)]
    another operation x0 -> x3, other arithmetic: none -> 3.01 us  [gu_piece(): jnp.stack([piece(gate_weight, index, feat, 0), piece(up_weight, index, fe...]
    concatenate x1 -> x0, local copies, waits for them, and re-layouts: 2.85 us -> none  [shards(): joined = jnp.concatenate([gate_weight, up_weight], axis=1)]
    all_to_all x1, waiting for transfers between devices: 19.4 us -> 22.1 us  [gather_rows(): got = lax.all_to_all(spread, axis, split_axis=0, concat_axis=0, tiled=True)]
    another operation x0 -> x1, local copies, waits for them, and re-layouts: none -> 2.01 us  [gu_piece(): jnp.stack([piece(gate_weight, index, feat, 0), piece(up_weight, index, fe...]
  transfers between devices with their start and end apart: 20 -> 20, of which waited for: 9 -> 8; matrix products, arithmetic and copies ran while one was open for 18% -> 20% of each run, Pallas kernels for 0% -> 0%
where the time goes in v9:
time: 196 us; the launch traced here: 194 us
  waiting for transfers between devices  100 us (51%)
  matrix products  37.3 us (19%)
  starting transfers between devices  35 us (18%)
  local copies, waits for them, and re-layouts  12.9 us (7%)
  other arithmetic  7.79 us (4%)
    ppermute x18, waiting for transfers between devices, swap(): return lax.ppermute(x, 'col', perm=[(i, i ^ k) for i in range(n)])  51.1 us
    all_to_all x1, waiting for transfers between devices, reduce_rows(): got = lax.all_to_all(pieces, axis, split_axis=0, concat_axis=0, tiled=True)  27 us
    all_to_all x1, waiting for transfers between devices, gather_rows(): got = lax.all_to_all(spread, axis, split_axis=0, concat_axis=0, tiled=True)  22.1 us
    dot_general x12, matrix products, contract_last(): lax.dot_general(left, right, (((1,), (1,)), ((), ())), preferred_element_...  17.4 us
    ppermute x18, starting transfers between devices, swap(): return lax.ppermute(x, 'col', perm=[(i, i ^ k) for i in range(n)])  12.7 us
    all_to_all x1, starting transfers between devices, reduce_rows(): got = lax.all_to_all(pieces, axis, split_axis=0, concat_axis=0, tiled=True)  12.3 us
    all_to_all x1, starting transfers between devices, gather_rows(): got = lax.all_to_all(spread, axis, split_axis=0, concat_axis=0, tiled=True)  10 us
    dot_general x4, matrix products, shards(): t = jnp.dot(h, w, preferred_element_type=jnp.float32)  6.99 us
  transfers between devices with their start and end apart: 20, of which 8 were waited for; matrix products, arithmetic and copies ran while one was open for 20% of the time, Pallas kernels for 0%

profile of v9, /device:TPU:8, one launch (start us, length us, event | category | flops | bytes accessed | tf_op | source)
XLA Modules:
  0.0 194.4 jit_solution(14408106478877431001)
XLA Ops:
  1.4 1.6 broadcast_in_dim.66
  3.0 10.0 %all-to-all-start = ((bf16[32,8,2,2048]{3,1,2,0:T(8,128)(2,1)}), bf16[32,8,2,2048]{3,1,2,0:T(8,128)(2,1)}, u32[]{:S(2)}, u32[]{:S(2)}) async-start(bf16[32,8,2,2048]{3,1,2,0:T(8,128)(2,1)} %broadcast_in_dim.66), calls=%async_computation | async-start | bytes 4194304 | tf_op jit(solution)/shard_map/all_to_all | solution.py:21
  13.1 2.0 %dynamic-slice_bitcast_fusion.2 = (bf16[1,2048,112]{1,2,0:T(8,128)(2,1)S(1)}, bf16[1,2048,112]{1,2,0:T(8,128)(2,1)S(1)}, bf16[1,2048,112]{1,2,0:T(8,128)(2,1)S(1...) fusion(bf16[8192,112]{0,1:T(8,128)(2,1)} %param.7, ...), kind=kLoop, calls=%fused_computation.56 | loop fusion | bytes 5505036 | tf_op jit(solution)/shard_map/stack | solution.py:82
  22.5 22.1 %all-to-all-done = bf16[32,8,2,2048]{3,1,2,0:T(8,128)(2,1)} async-done(((bf16[32,8,2,2048]{3,1,2,0:T(8,128)(2,1)}), bf16[32,8,2,2048]{3,1,2,0:T(8,128)(2,1)}, u32[]{:S(2)}, u32[]{:S(2)}) %all-to-all-start) | async-done | bytes 2097184 | tf_op jit(solution)/shard_map/all_to_all | solution.py:21
  44.6 1.8 copy.82
  46.4 12.1 %collective-permute-done.1 = bf16[2,2048,112]{1,2,0:T(8,128)(2,1)S(1)} collective-permute-done((bf16[2,2048,112]{1,2,0:T(8,128)(2,1)}, bf16[2,2048,112]{1,2,0:T(8,128)(2,1)S(1)}, u32[]{:S(2)}, u32[]{:S(2)}) %collective-permute-start.1) | collective-permute-done | bytes 917536 | tf_op jit(solution)/shard_map/ppermute | solution.py:32
  64.3 1.5 fusion.27
  66.0 29.7 %collective-permute-done.2 = bf16[2,2048,112]{1,2,0:T(8,128)(2,1)} collective-permute-done((bf16[2,2048,112]{1,2,0:T(8,128)(2,1)}, bf16[2,2048,112]{1,2,0:T(8,128)(2,1)}, u32[]{:S(2)}, u32[]{:S(2)}) %collective-permute-start.2) | collective-permute-done | bytes 917536 | tf_op jit(solution)/shard_map/ppermute | solution.py:32
  109.9 3.3 %collective-permute-done.5 = f32[64,4,224]{2,0,1:T(8,128)S(1)} collective-permute-done((f32[64,4,224]{2,0,1:T(8,128)S(1)}, f32[64,4,224]{2,0,1:T(8,128)S(1)}, u32[]{:S(2)}, u32[]{:S(2)}) %collective-permute-start.5) | collective-permute-done | bytes 229408 | tf_op jit(solution)/shard_map/ppermute | solution.py:32
  113.3 4.5 %collective-permute-done.13 = f32[64,4,112]{2,0,1:T(8,128)S(1)} collective-permute-done((f32[64,4,112]{2,0,1:T(8,128)S(1)}, f32[64,4,112]{2,0,1:T(8,128)S(1)}, u32[]{:S(2)}, u32[]{:S(2)}) %collective-permute-start.13) | collective-permute-done | bytes 114720 | tf_op jit(solution)/shard_map/ppermute | solution.py:32
  125.4 1.5 fusion.43
  126.9 1.5 convolution_add_fusion.5
  128.4 1.5 fusion.40
  129.9 2.5 %fusion.6 = bf16[32,8,1,2048]{3,1,2,0:T(8,128)(2,1)} fusion(f32[256,2048]{1,0:T(8,128)S(1)} %fusion.40, f32[256,2048]{1,0:T(8,128)S(1)} %convolution_add_fusion.5, bf16[112,2048]{1,0:T(8,128)(2,1)} %collective-permute-done.10, bf16[256,448]{1,0:T(8,128)(2,1)S(1)} %bitcast.154, s32[]{:T(128)S(6)} %select_n.91), kind=kOutput, calls=%fused_computation.15 | convolution fusion | flops 119013376 | bytes 5767172 | tf_op jit(solution)/shard_map/dot_general | solution.py:115
  134.5 2.8 %convolution_add_fusion.3 = f32[256,2048]{1,0:T(8,128)} fusion(f32[256,2048]{1,0:T(8,128)S(1)} %fusion.36, bf16[8192,112]{0,1:T(8,128)(2,1)} %param.7, s32[]{:T(128)S(6)} %select_n.36, bf16[256,224]{0,1:T(8,128)(2,1)S(1)} %bitcast.166), kind=kOutput, calls=%fused_computation.6 | convolution fusion | flops 117964800 | bytes 4710404 | tf_op jit(solution)/shard_map/dot_general | solution.py:8
  137.7 1.5 fusion.29
  141.6 1.6 convolution_add_fusion
  143.3 1.7 fusion.7
  145.1 1.5 pad_maximum_fusion
  146.6 12.3 %all-to-all-start.1 = ((bf16[32,8,2,2048]{3,1,2,0:T(8,128)(2,1)}), bf16[32,8,2,2048]{3,1,2,0:T(8,128)(2,1)}, u32[]{:S(2)}, u32[]{:S(2)}) async-start(bf16[32,8,2,2048]{3,1,2,0:T(8,128)(2,1)} %pad_maximum_fusion), calls=%async_computation.1 | async-start | bytes 4194304 | tf_op jit(solution)/shard_map/all_to_all | solution.py:27
  158.9 1.9 convolution_convert_fusion.1
  162.5 2.3 %fusion.73 = (bf16[2048,4,112]{0,2,1:T(8,128)(2,1)}, bf16[2048,4,112]{0,2,1:T(8,128)(2,1)}) fusion(bf16[2048,4,224]{0,2,1:T(8,128)(2,1)S(1)} %convolution_convert_fusion), kind=kLoop, calls=%fused_computation.143 | loop fusion | bytes 7340032 | tf_op jit(solution)/shard_map/slice | solution.py:140
  164.8 27.0 %all-to-all-done.1 = bf16[32,8,2,2048]{3,1,2,0:T(8,128)(2,1)} async-done(((bf16[32,8,2,2048]{3,1,2,0:T(8,128)(2,1)}), bf16[32,8,2,2048]{3,1,2,0:T(8,128)(2,1)}, u32[]{:S(2)}, u32[]{:S(2)}) %all-to-all-start.1) | async-done | bytes 2097184 | tf_op jit(solution)/shard_map/all_to_all | solution.py:27
  191.8 1.9 convert_reduce_fusion
  (109 shorter events, 42.9 us)
Async XLA Ops:
  3.0 41.6 %all-to-all-start = ((bf16[32,8,2,2048]{3,1,2,0:T(8,128)(2,1)}), bf16[32,8,2,2048]{3,1,2,0:T(8,128)(2,1)}, u32[]{:S(2)}, u32[]{:S(2)}) async-start(bf16[32,8,2,2048]{3,1,2,0:T(8,128)(2,1)} %broadcast_in_dim.66), calls=%async_computation | async-start | bytes 4194304 | tf_op jit(solution)/shard_map/all_to_all | solution.py:21
  15.1 3.4 %copy-start.2 = (bf16[112,8192]{1,0:T(8,128)(2,1)S(1)}, bf16[112,8192]{1,0:T(8,128)(2,1)}, u32[]{:S(2)}) copy-start(bf16[112,8192]{1,0:T(8,128)(2,1)} %param.8) | copy-start | bytes 5505028
  16.1 42.4 %collective-permute-start.1 = (bf16[2,2048,112]{1,2,0:T(8,128)(2,1)}, bf16[2,2048,112]{1,2,0:T(8,128)(2,1)S(1)}, u32[]{:S(2)}, u32[]{:S(2)}) collective-permute-start(bf16[2,2048,112]{1,2,0:T(8,128)(2,1)} %pad_maximum_fusion.2), channel_id=1, source_target_pairs={{0,2},{1,3},{2,0},{3,1},{4,6},{5,7},{6,4},{7,5},{8,10},{9,11},{10,... | collective-permute-start | bytes 2752520 | tf_op jit(solution)/shard_map/ppermute | solution.py:32
  18.4 41.2 %collective-permute-start = (bf16[2,2048,112]{1,2,0:T(8,128)(2,1)}, bf16[2,2048,112]{1,2,0:T(8,128)(2,1)}, u32[]{:S(2)}, u32[]{:S(2)}) collective-permute-start(bf16[2,2048,112]{1,2,0:T(8,128)(2,1)} %pad_maximum_fusion.1), channel_id=1, source_target_pairs={{0,1},{1,0},{2,3},{3,2},{4,5},{5,4},{6,7},{7,6},{8,9},{9,8},{10,11... | collective-permute-start | bytes 2752520 | tf_op jit(solution)/shard_map/ppermute | solution.py:32
  19.6 82.2 %collective-permute-start.9 = (bf16[112,2048]{1,0:T(8,128)(2,1)}, bf16[112,2048]{1,0:T(8,128)(2,1)}, u32[]{:S(2)}, u32[]{:S(2)}) collective-permute-start(bf16[112,2048]{1,0:T(8,128)(2,1)} %get-tuple-element.10), channel_id=1, source_target_pairs={{0,1},{1,0},{2,3},{3,2},{4,5},{5,4},{6,7},{7,6},{8,9},{9,8},{10,11... | collective-permute-start | bytes 1376264 | tf_op jit(solution)/shard_map/ppermute | solution.py:32
  20.1 84.5 %collective-permute-start.10 = (bf16[112,2048]{1,0:T(8,128)(2,1)}, bf16[112,2048]{1,0:T(8,128)(2,1)}, u32[]{:S(2)}, u32[]{:S(2)}) collective-permute-start(bf16[112,2048]{1,0:T(8,128)(2,1)} %get-tuple-element.11), channel_id=1, source_target_pairs={{0,2},{1,3},{2,0},{3,1},{4,6},{5,7},{6,4},{7,5},{8,10},{9,11},{10,... | collective-permute-start | bytes 1376264 | tf_op jit(solution)/shard_map/ppermute | solution.py:32
  20.8 85.3 %collective-permute-start.11 = (bf16[112,2048]{1,0:T(8,128)(2,1)}, bf16[112,2048]{1,0:T(8,128)(2,1)}, u32[]{:S(2)}, u32[]{:S(2)}) collective-permute-start(bf16[112,2048]{1,0:T(8,128)(2,1)} %get-tuple-element.9), channel_id=1, source_target_pairs={{0,3},{1,2},{2,1},{3,0},{4,7},{5,6},{6,5},{7,4},{8,11},{9,10},{10,... | collective-permute-start | bytes 1376264 | tf_op jit(solution)/shard_map/ppermute | solution.py:32
  58.5 37.2 %collective-permute-start.2 = (bf16[2,2048,112]{1,2,0:T(8,128)(2,1)}, bf16[2,2048,112]{1,2,0:T(8,128)(2,1)}, u32[]{:S(2)}, u32[]{:S(2)}) collective-permute-start(bf16[2,2048,112]{1,2,0:T(8,128)(2,1)} %pad_maximum_fusion.3), channel_id=1, source_target_pairs={{0,3},{1,2},{2,1},{3,0},{4,7},{5,6},{6,5},{7,4},{8,11},{9,10},{10,... | collective-permute-start | bytes 2752520 | tf_op jit(solution)/shard_map/ppermute | solution.py:32
  99.1 9.4 %collective-permute-start.3 = (f32[64,4,224]{2,0,1:T(8,128)S(1)}, f32[64,4,224]{2,0,1:T(8,128)S(1)}, u32[]{:S(2)}, u32[]{:S(2)}) collective-permute-start(f32[64,4,224]{2,0,1:T(8,128)S(1)} %get-tuple-element.18), channel_id=1, source_target_pairs={{0,1},{1,0},{2,3},{3,2},{4,5},{5,4},{6,7},{7,6},{8,9},{9,8},{10,11... | collective-permute-start | bytes 688136 | tf_op jit(solution)/shard_map/ppermute | solution.py:32
  100.2 9.7 %collective-permute-start.4 = (f32[64,4,224]{2,0,1:T(8,128)S(1)}, f32[64,4,224]{2,0,1:T(8,128)S(1)}, u32[]{:S(2)}, u32[]{:S(2)}) collective-permute-start(f32[64,4,224]{2,0,1:T(8,128)S(1)} %get-tuple-element.20), channel_id=1, source_target_pairs={{0,2},{1,3},{2,0},{3,1},{4,6},{5,7},{6,4},{7,5},{8,10},{9,11},{10,... | collective-permute-start | bytes 688136 | tf_op jit(solution)/shard_map/ppermute | solution.py:32
  101.8 11.4 %collective-permute-start.5 = (f32[64,4,224]{2,0,1:T(8,128)S(1)}, f32[64,4,224]{2,0,1:T(8,128)S(1)}, u32[]{:S(2)}, u32[]{:S(2)}) collective-permute-start(f32[64,4,224]{2,0,1:T(8,128)S(1)} %get-tuple-element.19), channel_id=1, source_target_pairs={{0,3},{1,2},{2,1},{3,0},{4,7},{5,6},{6,5},{7,4},{8,11},{9,10},{10,... | collective-permute-start | bytes 688136 | tf_op jit(solution)/shard_map/ppermute | solution.py:32
  107.6 5.6 %collective-permute-start.12 = (f32[64,4,112]{2,0,1:T(8,128)S(1)}, f32[64,4,112]{2,0,1:T(8,128)S(1)}, u32[]{:S(2)}, u32[]{:S(2)}) collective-permute-start(f32[64,4,112]{2,0,1:T(8,128)S(1)} %get-tuple-element.25), channel_id=1, source_target_pairs={{0,1},{1,0},{2,3},{3,2},{4,5},{5,4},{6,7},{7,6},{8,9},{9,8},{10,11... | collective-permute-start | bytes 344072 | tf_op jit(solution)/shard_map/ppermute | solution.py:32
  108.4 9.3 %collective-permute-start.13 = (f32[64,4,112]{2,0,1:T(8,128)S(1)}, f32[64,4,112]{2,0,1:T(8,128)S(1)}, u32[]{:S(2)}, u32[]{:S(2)}) collective-permute-start(f32[64,4,112]{2,0,1:T(8,128)S(1)} %get-tuple-element.27), channel_id=1, source_target_pairs={{0,2},{1,3},{2,0},{3,1},{4,6},{5,7},{6,4},{7,5},{8,10},{9,11},{10,... | collective-permute-start | bytes 344072 | tf_op jit(solution)/shard_map/ppermute | solution.py:32
  108.5 10.3 %collective-permute-start.14 = (f32[64,4,112]{2,0,1:T(8,128)S(1)}, f32[64,4,112]{2,0,1:T(8,128)S(1)}, u32[]{:S(2)}, u32[]{:S(2)}) collective-permute-start(f32[64,4,112]{2,0,1:T(8,128)S(1)} %get-tuple-element.26), channel_id=1, source_target_pairs={{0,3},{1,2},{2,1},{3,0},{4,7},{5,6},{6,5},{7,4},{8,11},{9,10},{10,... | collective-permute-start | bytes 344072 | tf_op jit(solution)/shard_map/ppermute | solution.py:32
  119.8 3.8 %collective-permute-start.6 = (bf16[64,448]{1,0:T(8,128)(2,1)S(1)}, bf16[64,448]{1,0:T(8,128)(2,1)S(1)}, u32[]{:S(2)}, u32[]{:S(2)}) collective-permute-start(bf16[64,448]{1,0:T(8,128)(2,1)S(1)} %multiply_convert_fusion.2), channel_id=1, source_target_pairs={{0,1},{1,0},{2,3},{3,2},{4,5},{5,4},{6,7},{7,6},{8,9},{9,8},{10,11... | collective-permute-start | bytes 172040 | tf_op jit(solution)/shard_map/ppermute | solution.py:32
  120.6 4.8 %collective-permute-start.7 = (bf16[64,448]{1,0:T(8,128)(2,1)S(1)}, bf16[64,448]{1,0:T(8,128)(2,1)S(1)}, u32[]{:S(2)}, u32[]{:S(2)}) collective-permute-start(bf16[64,448]{1,0:T(8,128)(2,1)S(1)} %multiply_convert_fusion.2), channel_id=1, source_target_pairs={{0,2},{1,3},{2,0},{3,1},{4,6},{5,7},{6,4},{7,5},{8,10},{9,11},{10,... | collective-permute-start | bytes 172040 | tf_op jit(solution)/shard_map/ppermute | solution.py:32
  120.8 4.5 %collective-permute-start.8 = (bf16[64,448]{1,0:T(8,128)(2,1)S(1)}, bf16[64,448]{1,0:T(8,128)(2,1)S(1)}, u32[]{:S(2)}, u32[]{:S(2)}) collective-permute-start(bf16[64,448]{1,0:T(8,128)(2,1)S(1)} %multiply_convert_fusion.2), channel_id=1, source_target_pairs={{0,3},{1,2},{2,1},{3,0},{4,7},{5,6},{6,5},{7,4},{8,11},{9,10},{10,... | collective-permute-start | bytes 172040 | tf_op jit(solution)/shard_map/ppermute | solution.py:32
  122.1 10.3 %collective-permute-start.15 = (bf16[64,4,224]{2,0,1:T(8,128)(2,1)S(1)}, bf16[64,4,224]{2,0,1:T(8,128)(2,1)S(1)}, u32[]{:S(2)}, u32[]{:S(2)}) collective-permute-start(bf16[64,4,224]{2,0,1:T(8,128)(2,1)S(1)} %get-tuple-element.33), channel_id=1, source_target_pairs={{0,1},{1,0},{2,3},{3,2},{4,5},{5,4},{6,7},{7,6},{8,9},{9,8},{10,11... | collective-permute-start | bytes 344072 | tf_op jit(solution)/shard_map/ppermute | solution.py:32
  122.9 9.6 %collective-permute-start.16 = (bf16[64,4,224]{2,0,1:T(8,128)(2,1)S(1)}, bf16[64,4,224]{2,0,1:T(8,128)(2,1)S(1)}, u32[]{:S(2)}, u32[]{:S(2)}) collective-permute-start(bf16[64,4,224]{2,0,1:T(8,128)(2,1)S(1)} %get-tuple-element.33), channel_id=1, source_target_pairs={{0,2},{1,3},{2,0},{3,1},{4,6},{5,7},{6,4},{7,5},{8,10},{9,11},{10,... | collective-permute-start | bytes 344072 | tf_op jit(solution)/shard_map/ppermute | solution.py:32
  123.5 9.1 %collective-permute-start.17 = (bf16[64,4,224]{2,0,1:T(8,128)(2,1)S(1)}, bf16[64,4,224]{2,0,1:T(8,128)(2,1)S(1)}, u32[]{:S(2)}, u32[]{:S(2)}) collective-permute-start(bf16[64,4,224]{2,0,1:T(8,128)(2,1)S(1)} %get-tuple-element.33), channel_id=1, source_target_pairs={{0,3},{1,2},{2,1},{3,0},{4,7},{5,6},{6,5},{7,4},{8,11},{9,10},{10,... | collective-permute-start | bytes 344072 | tf_op jit(solution)/shard_map/ppermute | solution.py:32
  137.6 1.6 copy-start.4
  141.6 1.7 copy-start
  143.3 1.7 copy-start.1
  146.6 45.3 %all-to-all-start.1 = ((bf16[32,8,2,2048]{3,1,2,0:T(8,128)(2,1)}), bf16[32,8,2,2048]{3,1,2,0:T(8,128)(2,1)}, u32[]{:S(2)}, u32[]{:S(2)}) async-start(bf16[32,8,2,2048]{3,1,2,0:T(8,128)(2,1)} %pad_maximum_fusion), calls=%async_computation.1 | async-start | bytes 4194304 | tf_op jit(solution)/shard_map/all_to_all | solution.py:27
  (1 other events, 1.0 us)

commit v10 on v9

--- a/solution.py
+++ b/solution.py
@@ -81,8 +81,10 @@
     def gu_piece(index):
         return jnp.stack([piece(gate_weight, index, feat, 0), piece(up_weight, index, feat, 0)])
 
-    gu_rel = [gu_piece(me)] + [swap(gu_piece(me ^ k), k, n_col) for k in range(1, n_col)]
     down_rel = col_scatter(down_weight, 1, n_col)
+    gu_out = [gu_piece(me ^ k) for k in range(n_col)]
+    gu_out, down_rel = lax.optimization_barrier((gu_out, down_rel))
+    gu_rel = [gu_out[0]] + [swap(gu_out[k], k, n_col) for k in range(1, n_col)]
 
     both = gather_rows(jnp.stack([tokens, out_grad], axis=1), "row", n_row)
     full_tokens = both[:, 0]

time: 196 us -> 213 us (1.087)
  local copies, waits for them, and re-layouts: 12.9 us -> 29.7 us
  other arithmetic: 7.79 us -> 13.8 us
  waiting for transfers between devices: 100 us -> 95.1 us
    all_to_all x1, waiting for transfers between devices: 22.1 us -> 7.66 us  [gather_rows(): got = lax.all_to_all(spread, axis, split_axis=0, concat_axis=0, tiled=True)]
    ppermute x18, waiting for transfers between devices: 51.1 us -> 60.5 us  [swap(): return lax.ppermute(x, 'col', perm=[(i, i ^ k) for i in range(n)])]
    broadcast_in_dim x4, local copies, waits for them, and re-layouts: 0.51 us -> 7.08 us  [place(): out = lax.dynamic_update_slice(out, jnp.expand_dims(p, axis), start)]
    dynamic_slice x5, local copies, waits for them, and re-layouts: 0.44 us -> 6.12 us  [shards(): g = lax.dynamic_index_in_dim(grads, me ^ k, 1, keepdims=False)]
    broadcast_in_dim x4, other arithmetic: 0.07 us -> 3.77 us  [place(): out = lax.dynamic_update_slice(out, jnp.expand_dims(p, axis), start)]
    all_to_all x1, starting transfers between devices: 12.3 us -> 10.1 us  [reduce_rows(): got = lax.all_to_all(pieces, axis, split_axis=0, concat_axis=0, tiled=True)]
  transfers between devices with their start and end apart: 20 -> 20, of which waited for: 8 -> 9; matrix products, arithmetic and copies ran while one was open for 20% -> 20% of each run, Pallas kernels for 0% -> 0%
where the time goes in v10:
time: 213 us; the launch traced here: 212 us
  waiting for transfers between devices  95.1 us (45%)
  matrix products  38.2 us (18%)
  starting transfers between devices  33.6 us (16%)
  local copies, waits for them, and re-layouts  29.7 us (14%)
  other arithmetic  13.8 us (6%)
    ppermute x18, waiting for transfers between devices, swap(): return lax.ppermute(x, 'col', perm=[(i, i ^ k) for i in range(n)])  60.5 us
    all_to_all x1, waiting for transfers between devices, reduce_rows(): got = lax.all_to_all(pieces, axis, split_axis=0, concat_axis=0, tiled=True)  26.9 us
    dot_general x12, matrix products, contract_last(): lax.dot_general(left, right, (((1,), (1,)), ((), ())), preferred_element_...  17.2 us
    ppermute x18, starting transfers between devices, swap(): return lax.ppermute(x, 'col', perm=[(i, i ^ k) for i in range(n)])  13.5 us
    all_to_all x1, starting transfers between devices, reduce_rows(): got = lax.all_to_all(pieces, axis, split_axis=0, concat_axis=0, tiled=True)  10.1 us
    all_to_all x1, starting transfers between devices, gather_rows(): got = lax.all_to_all(spread, axis, split_axis=0, concat_axis=0, tiled=True)  10 us
    all_to_all x1, waiting for transfers between devices, gather_rows(): got = lax.all_to_all(spread, axis, split_axis=0, concat_axis=0, tiled=True)  7.66 us
    broadcast_in_dim x4, local copies, waits for them, and re-layouts, place(): out = lax.dynamic_update_slice(out, jnp.expand_dims(p, axis), start)  7.08 us
  transfers between devices with their start and end apart: 20, of which 9 were waited for; matrix products, arithmetic and copies ran while one was open for 20% of the time, Pallas kernels for 0%

profile of v10, /device:TPU:8, one launch (start us, length us, event | category | flops | bytes accessed | tf_op | source)
XLA Modules:
  0.0 211.7 jit_solution(2005922081808293139)
XLA Ops:
  0.7 2.6 %constant_dynamic-slice_fusion.10 = (bf16[112,2048]{1,0:T(8,128)(2,1)}, bf16[112,2048]{1,0:T(8,128)(2,1)}, bf16[112,2048]{1,0:T(8,128)(2,1)S(1)}, bf16[112,2048]{1,0:T(8,128)(2,1)}) fusion(bf16[112,8192]{1,0:T(8,128)(2,1)} %param.8, s32[]{:T(128)S(6)} %select_n.39, s32[]{:T(128)S(6)} %select_n.37, s32[]{:T(128)S(6)} %select_n.36, s32[]{:T(128)S(6)} %select_n.38), kind=kLoop, calls=%fused_computation.140 | loop fusion | bytes 3670032 | tf_op jit(solution)/shard_map/dynamic_slice | solution.py:36
  6.7 10.0 %all-to-all-start = ((bf16[32,8,2,2048]{3,1,2,0:T(8,128)(2,1)}), bf16[32,8,2,2048]{3,1,2,0:T(8,128)(2,1)}, u32[]{:S(2)}, u32[]{:S(2)}) async-start(bf16[32,8,2,2048]{3,1,2,0:T(8,128)(2,1)} %broadcast_in_dim.66), calls=%async_computation | async-start | bytes 4194304 | tf_op jit(solution)/shard_map/all_to_all | solution.py:21
  16.8 2.5 %dynamic-slice_bitcast_fusion = (bf16[1,2048,112]{1,2,0:T(8,128)(2,1)S(1)}, bf16[1,2048,112]{1,2,0:T(8,128)(2,1)S(1)}, bf16[1,2048,112]{1,2,0:T(8,128)(2,1)S(1)}...) fusion(bf16[8192,112]{0,1:T(8,128)(2,1)} %param.7, ...), kind=kLoop, calls=%fused_computation.60 | loop fusion | bytes 7340048 | tf_op jit(solution)/shard_map/stack | solution.py:82
  22.4 19.3 %collective-permute-done.2 = bf16[112,2048]{1,0:T(8,128)(2,1)} collective-permute-done((bf16[112,2048]{1,0:T(8,128)(2,1)}, bf16[112,2048]{1,0:T(8,128)(2,1)}, u32[]{:S(2)}, u32[]{:S(2)}) %collective-permute-start.2) | collective-permute-done | bytes 458784 | tf_op jit(solution)/shard_map/ppermute | solution.py:32
  43.1 2.0 collective-permute-start.4
  45.1 7.7 %all-to-all-done = bf16[32,8,2,2048]{3,1,2,0:T(8,128)(2,1)} async-done(((bf16[32,8,2,2048]{3,1,2,0:T(8,128)(2,1)}), bf16[32,8,2,2048]{3,1,2,0:T(8,128)(2,1)}, u32[]{:S(2)}, u32[]{:S(2)}) %all-to-all-start) | async-done | bytes 2097184 | tf_op jit(solution)/shard_map/all_to_all | solution.py:21
  52.7 1.8 copy.82
  54.6 13.4 %collective-permute-done.5 = bf16[2,2048,112]{1,2,0:T(8,128)(2,1)} collective-permute-done((bf16[2,2048,112]{1,2,0:T(8,128)(2,1)}, bf16[2,2048,112]{1,2,0:T(8,128)(2,1)}, u32[]{:S(2)}, u32[]{:S(2)}) %collective-permute-start.5) | collective-permute-done | bytes 917536 | tf_op jit(solution)/shard_map/ppermute | solution.py:32
  71.0 17.2 %collective-permute-done.4 = bf16[2,2048,112]{1,2,0:T(8,128)(2,1)} collective-permute-done((bf16[2,2048,112]{1,2,0:T(8,128)(2,1)}, bf16[2,2048,112]{1,2,0:T(8,128)(2,1)}, u32[]{:S(2)}, u32[]{:S(2)}) %collective-permute-start.4) | collective-permute-done | bytes 917536 | tf_op jit(solution)/shard_map/ppermute | solution.py:32
  88.1 2.1 %fusion.18 = f32[256,112]{0,1:T(8,128)} fusion(bf16[2,2048,112]{1,2,0:T(8,128)(2,1)} %collective-permute-done.4, bf16[256,2,2048]{2,0,1:T(8,128)(2,1)S(1)} %bitcast.155), kind=kOutput, calls=%fused_computation.33 | convolution fusion | flops 117440512 | bytes 1622016 | tf_op jit(solution)/shard_map/dot_general | solution.py:98
  91.0 1.8 copy.56
  95.0 1.8 copy.55
  102.7 1.8 copy.54
  106.2 1.8 copy.53
  119.5 4.5 %collective-permute-done.8 = f32[64,4,224]{2,0,1:T(8,128)S(1)} collective-permute-done((f32[64,4,224]{2,0,1:T(8,128)S(1)}, f32[64,4,224]{2,0,1:T(8,128)S(1)}, u32[]{:S(2)}, u32[]{:S(2)}) %collective-permute-start.8) | collective-permute-done | bytes 229408 | tf_op jit(solution)/shard_map/ppermute | solution.py:32
  124.1 3.8 %collective-permute-done.13 = f32[64,4,112]{2,0,1:T(8,128)S(1)} collective-permute-done((f32[64,4,112]{2,0,1:T(8,128)S(1)}, f32[64,4,112]{2,0,1:T(8,128)S(1)}, u32[]{:S(2)}, u32[]{:S(2)}) %collective-permute-start.13) | collective-permute-done | bytes 114720 | tf_op jit(solution)/shard_map/ppermute | solution.py:32
  128.0 1.7 collective-permute-done.14
  151.3 1.8 convolution_add_fusion.3
  162.8 1.7 fusion.8
  166.1 10.1 %all-to-all-start.1 = ((bf16[32,8,2,2048]{3,1,2,0:T(8,128)(2,1)}), bf16[32,8,2,2048]{3,1,2,0:T(8,128)(2,1)}, u32[]{:S(2)}, u32[]{:S(2)}) async-start(bf16[32,8,2,2048]{3,1,2,0:T(8,128)(2,1)} %pad_maximum_fusion), calls=%async_computation.1 | async-start | bytes 4194304 | tf_op jit(solution)/shard_map/all_to_all | solution.py:27
  176.3 1.9 convolution_convert_fusion.1
  179.9 2.3 %fusion.72 = (bf16[2048,4,112]{0,2,1:T(8,128)(2,1)}, bf16[2048,4,112]{0,2,1:T(8,128)(2,1)}) fusion(bf16[2048,4,224]{0,2,1:T(8,128)(2,1)S(1)} %convolution_convert_fusion), kind=kLoop, calls=%fused_computation.145 | loop fusion | bytes 7340032 | tf_op jit(solution)/shard_map/slice | solution.py:142
  182.2 26.9 %all-to-all-done.1 = bf16[32,8,2,2048]{3,1,2,0:T(8,128)(2,1)} async-done(((bf16[32,8,2,2048]{3,1,2,0:T(8,128)(2,1)}), bf16[32,8,2,2048]{3,1,2,0:T(8,128)(2,1)}, u32[]{:S(2)}, u32[]{:S(2)}) %all-to-all-start.1) | async-done | bytes 2097184 | tf_op jit(solution)/shard_map/all_to_all | solution.py:27
  209.1 1.9 convert_reduce_fusion
  (126 shorter events, 68.0 us)
Async XLA Ops:
  0.6 4.5 %copy-start.12 = (bf16[8,2048]{1,0:T(8,128)(2,1)S(1)}, bf16[8,2048]{1,0:T(8,128)(2,1)}, u32[]{:S(2)}) copy-start(bf16[8,2048]{1,0:T(8,128)(2,1)} %param.5) | copy-start | bytes 98308
  3.3 108.9 %copy-start.4 = (bf16[112,2048]{1,0:T(8,128)(2,1)}, bf16[112,2048]{1,0:T(8,128)(2,1)S(1)}, u32[]{:S(2)}) copy-start(bf16[112,2048]{1,0:T(8,128)(2,1)S(1)} %get-tuple-element.17) | copy-start | bytes 1376260
  3.3 19.1 %collective-permute-start = (bf16[112,2048]{1,0:T(8,128)(2,1)}, bf16[112,2048]{1,0:T(8,128)(2,1)}, u32[]{:S(2)}, u32[]{:S(2)}) collective-permute-start(bf16[112,2048]{1,0:T(8,128)(2,1)} %get-tuple-element.26), channel_id=1, source_target_pairs={{0,1},{1,0},{2,3},{3,2},{4,5},{5,4},{6,7},{7,6},{8,9},{9,8},{10,11... | collective-permute-start | bytes 1376264 | tf_op jit(solution)/shard_map/ppermute | solution.py:32
  3.3 19.1 %collective-permute-start.1 = (bf16[112,2048]{1,0:T(8,128)(2,1)}, bf16[112,2048]{1,0:T(8,128)(2,1)}, u32[]{:S(2)}, u32[]{:S(2)}) collective-permute-start(bf16[112,2048]{1,0:T(8,128)(2,1)} %get-tuple-element.28), channel_id=1, source_target_pairs={{0,2},{1,3},{2,0},{3,1},{4,6},{5,7},{6,4},{7,5},{8,10},{9,11},{10,... | collective-permute-start | bytes 1376264 | tf_op jit(solution)/shard_map/ppermute | solution.py:32
  3.7 38.1 %collective-permute-start.2 = (bf16[112,2048]{1,0:T(8,128)(2,1)}, bf16[112,2048]{1,0:T(8,128)(2,1)}, u32[]{:S(2)}, u32[]{:S(2)}) collective-permute-start(bf16[112,2048]{1,0:T(8,128)(2,1)} %get-tuple-element.25), channel_id=1, source_target_pairs={{0,3},{1,2},{2,1},{3,0},{4,7},{5,6},{6,5},{7,4},{8,11},{9,10},{10,... | collective-permute-start | bytes 1376264 | tf_op jit(solution)/shard_map/ppermute | solution.py:32
  6.7 46.0 %all-to-all-start = ((bf16[32,8,2,2048]{3,1,2,0:T(8,128)(2,1)}), bf16[32,8,2,2048]{3,1,2,0:T(8,128)(2,1)}, u32[]{:S(2)}, u32[]{:S(2)}) async-start(bf16[32,8,2,2048]{3,1,2,0:T(8,128)(2,1)} %broadcast_in_dim.66), calls=%async_computation | async-start | bytes 4194304 | tf_op jit(solution)/shard_map/all_to_all | solution.py:21
  41.7 26.3 %collective-permute-start.5 = (bf16[2,2048,112]{1,2,0:T(8,128)(2,1)}, bf16[2,2048,112]{1,2,0:T(8,128)(2,1)}, u32[]{:S(2)}, u32[]{:S(2)}) collective-permute-start(bf16[2,2048,112]{1,2,0:T(8,128)(2,1)} %pad_maximum_fusion.4), channel_id=1, source_target_pairs={{0,3},{1,2},{2,1},{3,0},{4,7},{5,6},{6,5},{7,4},{8,11},{9,10},{10,... | collective-permute-start | bytes 2752520 | tf_op jit(solution)/shard_map/ppermute | solution.py:32
  43.1 45.1 %collective-permute-start.4 = (bf16[2,2048,112]{1,2,0:T(8,128)(2,1)}, bf16[2,2048,112]{1,2,0:T(8,128)(2,1)}, u32[]{:S(2)}, u32[]{:S(2)}) collective-permute-start(bf16[2,2048,112]{1,2,0:T(8,128)(2,1)} %pad_maximum_fusion.3), channel_id=1, source_target_pairs={{0,2},{1,3},{2,0},{3,1},{4,6},{5,7},{6,4},{7,5},{8,10},{9,11},{10,... | collective-permute-start | bytes 2752520 | tf_op jit(solution)/shard_map/ppermute | solution.py:32
  45.1 54.0 %collective-permute-start.3 = (bf16[2,2048,112]{1,2,0:T(8,128)(2,1)}, bf16[2,2048,112]{1,2,0:T(8,128)(2,1)}, u32[]{:S(2)}, u32[]{:S(2)}) collective-permute-start(bf16[2,2048,112]{1,2,0:T(8,128)(2,1)} %pad_maximum_fusion.2), channel_id=1, source_target_pairs={{0,1},{1,0},{2,3},{3,2},{4,5},{5,4},{6,7},{7,6},{8,9},{9,8},{10,11... | collective-permute-start | bytes 2752520 | tf_op jit(solution)/shard_map/ppermute | solution.py:32
  110.2 7.7 %collective-permute-start.6 = (f32[64,4,224]{2,0,1:T(8,128)S(1)}, f32[64,4,224]{2,0,1:T(8,128)S(1)}, u32[]{:S(2)}, u32[]{:S(2)}) collective-permute-start(f32[64,4,224]{2,0,1:T(8,128)S(1)} %get-tuple-element.37), channel_id=1, source_target_pairs={{0,1},{1,0},{2,3},{3,2},{4,5},{5,4},{6,7},{7,6},{8,9},{9,8},{10,11... | collective-permute-start | bytes 688136 | tf_op jit(solution)/shard_map/ppermute | solution.py:32
  110.3 9.3 %collective-permute-start.7 = (f32[64,4,224]{2,0,1:T(8,128)S(1)}, f32[64,4,224]{2,0,1:T(8,128)S(1)}, u32[]{:S(2)}, u32[]{:S(2)}) collective-permute-start(f32[64,4,224]{2,0,1:T(8,128)S(1)} %get-tuple-element.39), channel_id=1, source_target_pairs={{0,2},{1,3},{2,0},{3,1},{4,6},{5,7},{6,4},{7,5},{8,10},{9,11},{10,... | collective-permute-start | bytes 688136 | tf_op jit(solution)/shard_map/ppermute | solution.py:32
  110.7 13.4 %collective-permute-start.8 = (f32[64,4,224]{2,0,1:T(8,128)S(1)}, f32[64,4,224]{2,0,1:T(8,128)S(1)}, u32[]{:S(2)}, u32[]{:S(2)}) collective-permute-start(f32[64,4,224]{2,0,1:T(8,128)S(1)} %get-tuple-element.38), channel_id=1, source_target_pairs={{0,3},{1,2},{2,1},{3,0},{4,7},{5,6},{6,5},{7,4},{8,11},{9,10},{10,... | collective-permute-start | bytes 688136 | tf_op jit(solution)/shard_map/ppermute | solution.py:32
  117.0 7.1 %collective-permute-start.12 = (f32[64,4,112]{2,0,1:T(8,128)S(1)}, f32[64,4,112]{2,0,1:T(8,128)S(1)}, u32[]{:S(2)}, u32[]{:S(2)}) collective-permute-start(f32[64,4,112]{2,0,1:T(8,128)S(1)} %get-tuple-element.44), channel_id=1, source_target_pairs={{0,1},{1,0},{2,3},{3,2},{4,5},{5,4},{6,7},{7,6},{8,9},{9,8},{10,11... | collective-permute-start | bytes 344072 | tf_op jit(solution)/shard_map/ppermute | solution.py:32
  117.5 10.5 %collective-permute-start.13 = (f32[64,4,112]{2,0,1:T(8,128)S(1)}, f32[64,4,112]{2,0,1:T(8,128)S(1)}, u32[]{:S(2)}, u32[]{:S(2)}) collective-permute-start(f32[64,4,112]{2,0,1:T(8,128)S(1)} %get-tuple-element.46), channel_id=1, source_target_pairs={{0,2},{1,3},{2,0},{3,1},{4,6},{5,7},{6,4},{7,5},{8,10},{9,11},{10,... | collective-permute-start | bytes 344072 | tf_op jit(solution)/shard_map/ppermute | solution.py:32
  117.8 11.8 %collective-permute-start.14 = (f32[64,4,112]{2,0,1:T(8,128)S(1)}, f32[64,4,112]{2,0,1:T(8,128)S(1)}, u32[]{:S(2)}, u32[]{:S(2)}) collective-permute-start(f32[64,4,112]{2,0,1:T(8,128)S(1)} %get-tuple-element.45), channel_id=1, source_target_pairs={{0,3},{1,2},{2,1},{3,0},{4,7},{5,6},{6,5},{7,4},{8,11},{9,10},{10,... | collective-permute-start | bytes 344072 | tf_op jit(solution)/shard_map/ppermute | solution.py:32
  133.4 4.4 %collective-permute-start.9 = (bf16[64,448]{1,0:T(8,128)(2,1)S(1)}, bf16[64,448]{1,0:T(8,128)(2,1)S(1)}, u32[]{:S(2)}, u32[]{:S(2)}) collective-permute-start(bf16[64,448]{1,0:T(8,128)(2,1)S(1)} %multiply_convert_fusion.2), channel_id=1, source_target_pairs={{0,1},{1,0},{2,3},{3,2},{4,5},{5,4},{6,7},{7,6},{8,9},{9,8},{10,11... | collective-permute-start | bytes 172040 | tf_op jit(solution)/shard_map/ppermute | solution.py:32
  133.8 5.3 %collective-permute-start.10 = (bf16[64,448]{1,0:T(8,128)(2,1)S(1)}, bf16[64,448]{1,0:T(8,128)(2,1)S(1)}, u32[]{:S(2)}, u32[]{:S(2)}) collective-permute-start(bf16[64,448]{1,0:T(8,128)(2,1)S(1)} %multiply_convert_fusion.2), channel_id=1, source_target_pairs={{0,2},{1,3},{2,0},{3,1},{4,6},{5,7},{6,4},{7,5},{8,10},{9,11},{10,... | collective-permute-start | bytes 172040 | tf_op jit(solution)/shard_map/ppermute | solution.py:32
  134.2 5.0 %collective-permute-start.11 = (bf16[64,448]{1,0:T(8,128)(2,1)S(1)}, bf16[64,448]{1,0:T(8,128)(2,1)S(1)}, u32[]{:S(2)}, u32[]{:S(2)}) collective-permute-start(bf16[64,448]{1,0:T(8,128)(2,1)S(1)} %multiply_convert_fusion.2), channel_id=1, source_target_pairs={{0,3},{1,2},{2,1},{3,0},{4,7},{5,6},{6,5},{7,4},{8,11},{9,10},{10,... | collective-permute-start | bytes 172040 | tf_op jit(solution)/shard_map/ppermute | solution.py:32
  136.3 9.1 %collective-permute-start.15 = (bf16[64,4,224]{2,0,1:T(8,128)(2,1)S(1)}, bf16[64,4,224]{2,0,1:T(8,128)(2,1)S(1)}, u32[]{:S(2)}, u32[]{:S(2)}) collective-permute-start(bf16[64,4,224]{2,0,1:T(8,128)(2,1)S(1)} %get-tuple-element.52), channel_id=1, source_target_pairs={{0,1},{1,0},{2,3},{3,2},{4,5},{5,4},{6,7},{7,6},{8,9},{9,8},{10,11... | collective-permute-start | bytes 344072 | tf_op jit(solution)/shard_map/ppermute | solution.py:32
  137.1 8.4 %collective-permute-start.16 = (bf16[64,4,224]{2,0,1:T(8,128)(2,1)S(1)}, bf16[64,4,224]{2,0,1:T(8,128)(2,1)S(1)}, u32[]{:S(2)}, u32[]{:S(2)}) collective-permute-start(bf16[64,4,224]{2,0,1:T(8,128)(2,1)S(1)} %get-tuple-element.52), channel_id=1, source_target_pairs={{0,2},{1,3},{2,0},{3,1},{4,6},{5,7},{6,4},{7,5},{8,10},{9,11},{10,... | collective-permute-start | bytes 344072 | tf_op jit(solution)/shard_map/ppermute | solution.py:32
  137.8 7.9 %collective-permute-start.17 = (bf16[64,4,224]{2,0,1:T(8,128)(2,1)S(1)}, bf16[64,4,224]{2,0,1:T(8,128)(2,1)S(1)}, u32[]{:S(2)}, u32[]{:S(2)}) collective-permute-start(bf16[64,4,224]{2,0,1:T(8,128)(2,1)S(1)} %get-tuple-element.52), channel_id=1, source_target_pairs={{0,3},{1,2},{2,1},{3,0},{4,7},{5,6},{6,5},{7,4},{8,11},{9,10},{10,... | collective-permute-start | bytes 344072 | tf_op jit(solution)/shard_map/ppermute | solution.py:32
  139.2 4.7 %copy-start.2 = (bf16[4,64,448]{2,1,0:T(8,128)(2,1)}, bf16[4,64,448]{2,1,0:T(8,128)(2,1)S(1)}, u32[]{:S(2)}) copy-start(bf16[4,64,448]{2,1,0:T(8,128)(2,1)S(1)} %bitcast_dynamic-update-slice_fusion) | copy-start | bytes 688132
  166.1 10.2 %copy-start.3 = (bf16[4,64,448]{2,1,0:T(8,128)(2,1)S(1)}, bf16[4,64,448]{2,1,0:T(8,128)(2,1)}, u32[]{:S(2)}) copy-start(bf16[4,64,448]{2,1,0:T(8,128)(2,1)} %copy-done.2) | copy-start | bytes 688132
  166.1 43.0 %all-to-all-start.1 = ((bf16[32,8,2,2048]{3,1,2,0:T(8,128)(2,1)}), bf16[32,8,2,2048]{3,1,2,0:T(8,128)(2,1)}, u32[]{:S(2)}, u32[]{:S(2)}) async-start(bf16[32,8,2,2048]{3,1,2,0:T(8,128)(2,1)} %pad_maximum_fusion), calls=%async_computation.1 | async-start | bytes 4194304 | tf_op jit(solution)/shard_map/all_to_all | solution.py:27
  (9 other events, 19.9 us)

commit v11 on v9

--- a/solution.py
+++ b/solution.py
@@ -82,7 +82,10 @@
         return jnp.stack([piece(gate_weight, index, feat, 0), piece(up_weight, index, feat, 0)])
 
     gu_rel = [gu_piece(me)] + [swap(gu_piece(me ^ k), k, n_col) for k in range(1, n_col)]
-    down_rel = col_scatter(down_weight, 1, n_col)
+    down_out = [piece(down_weight, me ^ k, feat, 1) for k in range(n_col)]
+    down_out, first = lax.optimization_barrier((down_out, gu_rel[2]))
+    gu_rel[2] = first
+    down_rel = [down_out[0]] + [swap(down_out[k], k, n_col) for k in range(1, n_col)]
 
     both = gather_rows(jnp.stack([tokens, out_grad], axis=1), "row", n_row)
     full_tokens = both[:, 0]

time: 196 us -> 193 us (0.985)
  waiting for transfers between devices: 100 us -> 83.4 us
  local copies, waits for them, and re-layouts: 12.9 us -> 18.3 us
  starting transfers between devices: 35 us -> 38.5 us
  matrix products: 37.3 us -> 40.6 us
    all_to_all x1, waiting for transfers between devices: 22.1 us -> 0.01 us  [gather_rows(): got = lax.all_to_all(spread, axis, split_axis=0, concat_axis=0, tiled=True)]
    ppermute x18, waiting for transfers between devices: 51.1 us -> 56.4 us  [swap(): return lax.ppermute(x, 'col', perm=[(i, i ^ k) for i in range(n)])]
    ppermute x18, starting transfers between devices: 12.7 us -> 16.2 us  [swap(): return lax.ppermute(x, 'col', perm=[(i, i ^ k) for i in range(n)])]
    broadcast_in_dim x4, local copies, waits for them, and re-layouts: 0.51 us -> 3.1 us  [place(): out = lax.dynamic_update_slice(out, jnp.expand_dims(p, axis), start)]
    dot_general x12, matrix products: 17.4 us -> 19.6 us  [contract_last(): lax.dot_general(left, right, (((1,), (1,)), ((), ())), preferred_element_...]
  transfers between devices with their start and end apart: 20 -> 20, of which waited for: 8 -> 9; matrix products, arithmetic and copies ran while one was open for 20% -> 23% of each run, Pallas kernels for 0% -> 0%
where the time goes in v11:
time: 193 us; the launch traced here: 191 us
  waiting for transfers between devices  83.4 us (43%)
  matrix products  40.6 us (21%)
  starting transfers between devices  38.5 us (20%)
  local copies, waits for them, and re-layouts  18.3 us (9%)
  other arithmetic  9.15 us (5%)
    ppermute x18, waiting for transfers between devices, swap(): return lax.ppermute(x, 'col', perm=[(i, i ^ k) for i in range(n)])  56.4 us
    all_to_all x1, waiting for transfers between devices, reduce_rows(): got = lax.all_to_all(pieces, axis, split_axis=0, concat_axis=0, tiled=True)  27 us
    dot_general x12, matrix products, contract_last(): lax.dot_general(left, right, (((1,), (1,)), ((), ())), preferred_element_...  19.6 us
    ppermute x18, starting transfers between devices, swap(): return lax.ppermute(x, 'col', perm=[(i, i ^ k) for i in range(n)])  16.2 us
    all_to_all x1, starting transfers between devices, reduce_rows(): got = lax.all_to_all(pieces, axis, split_axis=0, concat_axis=0, tiled=True)  12.3 us
    all_to_all x1, starting transfers between devices, gather_rows(): got = lax.all_to_all(spread, axis, split_axis=0, concat_axis=0, tiled=True)  10 us
    dot_general x4, matrix products, shards(): t = jnp.dot(h, w, preferred_element_type=jnp.float32)  6 us
    dot_general x4, matrix products, shards(): jnp.dot(full_tokens, w[1], preferred_element_type=jnp.float32)  5.99 us
  transfers between devices with their start and end apart: 20, of which 9 were waited for; matrix products, arithmetic and copies ran while one was open for 23% of the time, Pallas kernels for 0%

profile of v11, /device:TPU:8, one launch (start us, length us, event | category | flops | bytes accessed | tf_op | source)
XLA Modules:
  0.0 191.2 jit_solution(6467564071598653337)
XLA Ops:
  1.4 1.6 broadcast_in_dim.66
  3.0 10.0 %all-to-all-start = ((bf16[32,8,2,2048]{3,1,2,0:T(8,128)(2,1)}), bf16[32,8,2,2048]{3,1,2,0:T(8,128)(2,1)}, u32[]{:S(2)}, u32[]{:S(2)}) async-start(bf16[32,8,2,2048]{3,1,2,0:T(8,128)(2,1)} %broadcast_in_dim.66), calls=%async_computation | async-start | bytes 4194304 | tf_op jit(solution)/shard_map/all_to_all | solution.py:21
  13.0 2.0 %dynamic-slice_bitcast_fusion.2 = (bf16[1,2048,112]{1,2,0:T(8,128)(2,1)S(1)}, bf16[1,2048,112]{1,2,0:T(8,128)(2,1)S(1)}, bf16[1,2048,112]{1,2,0:T(8,128)(2,1)S(1...) fusion(bf16[8192,112]{0,1:T(8,128)(2,1)} %param.7, ...), kind=kLoop, calls=%fused_computation.59 | loop fusion | bytes 5505036 | tf_op jit(solution)/shard_map/stack | solution.py:82
  20.2 2.6 %constant_dynamic-slice_fusion.10 = (bf16[112,2048]{1,0:T(8,128)(2,1)}, bf16[112,2048]{1,0:T(8,128)(2,1)}, bf16[112,2048]{1,0:T(8,128)(2,1)S(1)}, bf16[112,2048]{1,0:T(8,128)(2,1)}) fusion(bf16[112,8192]{1,0:T(8,128)(2,1)} %param.8, s32[]{:T(128)S(6)} %select_n.82, s32[]{:T(128)S(6)} %select_n.38, s32[]{:T(128)S(6)} %select_n.36, s32[]{:T(128)S(6)} %select_n.40), kind=kLoop, calls=%fused_computation.139 | loop fusion | bytes 3670032 | tf_op jit(solution)/shard_map/dynamic_slice | solution.py:36
  22.8 35.8 %collective-permute-done.1 = bf16[2,2048,112]{1,2,0:T(8,128)(2,1)} collective-permute-done((bf16[2,2048,112]{1,2,0:T(8,128)(2,1)}, bf16[2,2048,112]{1,2,0:T(8,128)(2,1)}, u32[]{:S(2)}, u32[]{:S(2)}) %collective-permute-start.1) | collective-permute-done | bytes 917536 | tf_op jit(solution)/shard_map/ppermute | solution.py:32
  58.7 1.7 collective-permute-start.11
  60.5 1.8 copy.82
  73.4 2.6 %collective-permute-done.2 = bf16[2,2048,112]{1,2,0:T(8,128)(2,1)} collective-permute-done((bf16[2,2048,112]{1,2,0:T(8,128)(2,1)}, bf16[2,2048,112]{1,2,0:T(8,128)(2,1)}, u32[]{:S(2)}, u32[]{:S(2)}) %collective-permute-start.2) | collective-permute-done | bytes 917536 | tf_op jit(solution)/shard_map/ppermute | solution.py:32
  79.7 1.8 copy.56
  82.5 2.1 %collective-permute-start.3 = (f32[64,4,224]{2,0,1:T(8,128)S(1)}, f32[64,4,224]{2,0,1:T(8,128)S(1)}, u32[]{:S(2)}, u32[]{:S(2)}) collective-permute-start(f32[64,4,224]{2,0,1:T(8,128)S(1)} %get-tuple-element.29), channel_id=1, source_target_pairs={{0,1},{1,0},{2,3},{3,2},{4,5},{5,4},{6,7},{7,6},{8,9},{9,8},{10,11... | collective-permute-start | bytes 688136 | tf_op jit(solution)/shard_map/ppermute | solution.py:32
  89.6 6.1 %collective-permute-done.11 = bf16[112,2048]{1,0:T(8,128)(2,1)} collective-permute-done((bf16[112,2048]{1,0:T(8,128)(2,1)}, bf16[112,2048]{1,0:T(8,128)(2,1)}, u32[]{:S(2)}, u32[]{:S(2)}) %collective-permute-start.11) | collective-permute-done | bytes 458784 | tf_op jit(solution)/shard_map/ppermute | solution.py:32
  97.2 2.1 %collective-permute-start.12 = (f32[64,4,112]{2,0,1:T(8,128)S(1)}, f32[64,4,112]{2,0,1:T(8,128)S(1)}, u32[]{:S(2)}, u32[]{:S(2)}) collective-permute-start(f32[64,4,112]{2,0,1:T(8,128)S(1)} %get-tuple-element.36), channel_id=1, source_target_pairs={{0,1},{1,0},{2,3},{3,2},{4,5},{5,4},{6,7},{7,6},{8,9},{9,8},{10,11... | collective-permute-start | bytes 344072 | tf_op jit(solution)/shard_map/ppermute | solution.py:32
  100.8 2.7 %collective-permute-done.4 = f32[64,4,224]{2,0,1:T(8,128)S(1)} collective-permute-done((f32[64,4,224]{2,0,1:T(8,128)S(1)}, f32[64,4,224]{2,0,1:T(8,128)S(1)}, u32[]{:S(2)}, u32[]{:S(2)}) %collective-permute-start.4) | collective-permute-done | bytes 229408 | tf_op jit(solution)/shard_map/ppermute | solution.py:32
  103.4 3.4 %collective-permute-done.5 = f32[64,4,224]{2,0,1:T(8,128)S(1)} collective-permute-done((f32[64,4,224]{2,0,1:T(8,128)S(1)}, f32[64,4,224]{2,0,1:T(8,128)S(1)}, u32[]{:S(2)}, u32[]{:S(2)}) %collective-permute-start.5) | collective-permute-done | bytes 229408 | tf_op jit(solution)/shard_map/ppermute | solution.py:32
  106.9 5.0 %collective-permute-done.13 = f32[64,4,112]{2,0,1:T(8,128)S(1)} collective-permute-done((f32[64,4,112]{2,0,1:T(8,128)S(1)}, f32[64,4,112]{2,0,1:T(8,128)S(1)}, u32[]{:S(2)}, u32[]{:S(2)}) %collective-permute-start.13) | collective-permute-done | bytes 114720 | tf_op jit(solution)/shard_map/ppermute | solution.py:32
  127.4 2.8 %convolution_add_fusion.3 = f32[256,2048]{1,0:T(8,128)} fusion(f32[256,2048]{1,0:T(8,128)S(1)} %fusion.43, bf16[8192,112]{0,1:T(8,128)(2,1)} %param.7, s32[]{:T(128)S(6)} %select_n.36, bf16[256,224]{0,1:T(8,128)(2,1)S(1)} %bitcast.168), kind=kOutput, calls=%fused_computation.6 | convolution fusion | flops 117964800 | bytes 4710404 | tf_op jit(solution)/shard_map/dot_general | solution.py:8
  131.8 2.8 %convolution_add_fusion.1 = f32[256,2048]{1,0:T(8,128)} fusion(f32[256,2048]{1,0:T(8,128)S(1)} %fusion.32, bf16[2,2048,112]{1,2,0:T(8,128)(2,1)} %collective-permute-done.1, bf16[256,224]{0,1:T(8,128)(2,1)S(1)} %bitcast.170), kind=kOutput, calls=%fused_computation.4 | convolution fusion | flops 117964800 | bytes 4710400 | tf_op jit(solution)/shard_map/dot_general | solution.py:8
  137.7 1.6 convolution_add_fusion
  140.1 1.7 fusion.8
  143.3 12.3 %all-to-all-start.1 = ((bf16[32,8,2,2048]{3,1,2,0:T(8,128)(2,1)}), bf16[32,8,2,2048]{3,1,2,0:T(8,128)(2,1)}, u32[]{:S(2)}, u32[]{:S(2)}) async-start(bf16[32,8,2,2048]{3,1,2,0:T(8,128)(2,1)} %pad_maximum_fusion), calls=%async_computation.1 | async-start | bytes 4194304 | tf_op jit(solution)/shard_map/all_to_all | solution.py:27
  155.6 1.9 convolution_convert_fusion.1
  159.2 2.3 %fusion.80 = (bf16[2048,4,112]{0,2,1:T(8,128)(2,1)}, bf16[2048,4,112]{0,2,1:T(8,128)(2,1)}) fusion(bf16[2048,4,224]{0,2,1:T(8,128)(2,1)S(1)} %convolution_convert_fusion), kind=kLoop, calls=%fused_computation.148 | loop fusion | bytes 7340032 | tf_op jit(solution)/shard_map/slice | solution.py:143
  161.6 27.0 %all-to-all-done.1 = bf16[32,8,2,2048]{3,1,2,0:T(8,128)(2,1)} async-done(((bf16[32,8,2,2048]{3,1,2,0:T(8,128)(2,1)}), bf16[32,8,2,2048]{3,1,2,0:T(8,128)(2,1)}, u32[]{:S(2)}, u32[]{:S(2)}) %all-to-all-start.1) | async-done | bytes 2097184 | tf_op jit(solution)/shard_map/all_to_all | solution.py:27
  188.6 1.9 %convert_reduce_fusion = f32[8,2,2048]{2,0,1:T(8,128)S(1)} fusion(bf16[32,8,2,2048]{3,1,2,0:T(8,128)(2,1)} %all-to-all-done.1), kind=kLoop, calls=%fused_computation | loop fusion | flops 2064384 | bytes 2228224 | tf_op jit(solution)/shard_map/reduce_sum | solution.py:28
  (107 shorter events, 54.3 us)
Async XLA Ops:
  3.0 57.5 %all-to-all-start = ((bf16[32,8,2,2048]{3,1,2,0:T(8,128)(2,1)}), bf16[32,8,2,2048]{3,1,2,0:T(8,128)(2,1)}, u32[]{:S(2)}, u32[]{:S(2)}) async-start(bf16[32,8,2,2048]{3,1,2,0:T(8,128)(2,1)} %broadcast_in_dim.66), calls=%async_computation | async-start | bytes 4194304 | tf_op jit(solution)/shard_map/all_to_all | solution.py:21
  16.1 42.5 %collective-permute-start.1 = (bf16[2,2048,112]{1,2,0:T(8,128)(2,1)}, bf16[2,2048,112]{1,2,0:T(8,128)(2,1)}, u32[]{:S(2)}, u32[]{:S(2)}) collective-permute-start(bf16[2,2048,112]{1,2,0:T(8,128)(2,1)} %pad_maximum_fusion.2), channel_id=1, source_target_pairs={{0,2},{1,3},{2,0},{3,1},{4,6},{5,7},{6,4},{7,5},{8,10},{9,11},{10,... | collective-permute-start | bytes 2752520 | tf_op jit(solution)/shard_map/ppermute | solution.py:32
  18.4 47.0 %collective-permute-start = (bf16[2,2048,112]{1,2,0:T(8,128)(2,1)}, bf16[2,2048,112]{1,2,0:T(8,128)(2,1)}, u32[]{:S(2)}, u32[]{:S(2)}) collective-permute-start(bf16[2,2048,112]{1,2,0:T(8,128)(2,1)} %pad_maximum_fusion.1), channel_id=1, source_target_pairs={{0,1},{1,0},{2,3},{3,2},{4,5},{5,4},{6,7},{7,6},{8,9},{9,8},{10,11... | collective-permute-start | bytes 2752520 | tf_op jit(solution)/shard_map/ppermute | solution.py:32
  19.4 56.6 %collective-permute-start.2 = (bf16[2,2048,112]{1,2,0:T(8,128)(2,1)}, bf16[2,2048,112]{1,2,0:T(8,128)(2,1)}, u32[]{:S(2)}, u32[]{:S(2)}) collective-permute-start(bf16[2,2048,112]{1,2,0:T(8,128)(2,1)} %pad_maximum_fusion.3), channel_id=1, source_target_pairs={{0,3},{1,2},{2,1},{3,0},{4,7},{5,6},{6,5},{7,4},{8,11},{9,10},{10,... | collective-permute-start | bytes 2752520 | tf_op jit(solution)/shard_map/ppermute | solution.py:32
  58.6 26.7 %collective-permute-start.9 = (bf16[112,2048]{1,0:T(8,128)(2,1)}, bf16[112,2048]{1,0:T(8,128)(2,1)}, u32[]{:S(2)}, u32[]{:S(2)}) collective-permute-start(bf16[112,2048]{1,0:T(8,128)(2,1)} %get-tuple-element.12), channel_id=1, source_target_pairs={{0,1},{1,0},{2,3},{3,2},{4,5},{5,4},{6,7},{7,6},{8,9},{9,8},{10,11... | collective-permute-start | bytes 1376264 | tf_op jit(solution)/shard_map/ppermute | solution.py:32
  58.6 29.6 %collective-permute-start.10 = (bf16[112,2048]{1,0:T(8,128)(2,1)}, bf16[112,2048]{1,0:T(8,128)(2,1)}, u32[]{:S(2)}, u32[]{:S(2)}) collective-permute-start(bf16[112,2048]{1,0:T(8,128)(2,1)} %get-tuple-element.13), channel_id=1, source_target_pairs={{0,2},{1,3},{2,0},{3,1},{4,6},{5,7},{6,4},{7,5},{8,10},{9,11},{10,... | collective-permute-start | bytes 1376264 | tf_op jit(solution)/shard_map/ppermute | solution.py:32
  58.7 37.0 %collective-permute-start.11 = (bf16[112,2048]{1,0:T(8,128)(2,1)}, bf16[112,2048]{1,0:T(8,128)(2,1)}, u32[]{:S(2)}, u32[]{:S(2)}) collective-permute-start(bf16[112,2048]{1,0:T(8,128)(2,1)} %get-tuple-element.14), channel_id=1, source_target_pairs={{0,3},{1,2},{2,1},{3,0},{4,7},{5,6},{6,5},{7,4},{8,11},{9,10},{10,... | collective-permute-start | bytes 1376264 | tf_op jit(solution)/shard_map/ppermute | solution.py:32
  81.5 0.9 copy-start.3
  82.5 16.9 %collective-permute-start.3 = (f32[64,4,224]{2,0,1:T(8,128)S(1)}, f32[64,4,224]{2,0,1:T(8,128)S(1)}, u32[]{:S(2)}, u32[]{:S(2)}) collective-permute-start(f32[64,4,224]{2,0,1:T(8,128)S(1)} %get-tuple-element.29), channel_id=1, source_target_pairs={{0,1},{1,0},{2,3},{3,2},{4,5},{5,4},{6,7},{7,6},{8,9},{9,8},{10,11... | collective-permute-start | bytes 688136 | tf_op jit(solution)/shard_map/ppermute | solution.py:32
  84.7 18.7 %collective-permute-start.4 = (f32[64,4,224]{2,0,1:T(8,128)S(1)}, f32[64,4,224]{2,0,1:T(8,128)S(1)}, u32[]{:S(2)}, u32[]{:S(2)}) collective-permute-start(f32[64,4,224]{2,0,1:T(8,128)S(1)} %get-tuple-element.31), channel_id=1, source_target_pairs={{0,2},{1,3},{2,0},{3,1},{4,6},{5,7},{6,4},{7,5},{8,10},{9,11},{10,... | collective-permute-start | bytes 688136 | tf_op jit(solution)/shard_map/ppermute | solution.py:32
  85.3 21.5 %collective-permute-start.5 = (f32[64,4,224]{2,0,1:T(8,128)S(1)}, f32[64,4,224]{2,0,1:T(8,128)S(1)}, u32[]{:S(2)}, u32[]{:S(2)}) collective-permute-start(f32[64,4,224]{2,0,1:T(8,128)S(1)} %get-tuple-element.30), channel_id=1, source_target_pairs={{0,3},{1,2},{2,1},{3,0},{4,7},{5,6},{6,5},{7,4},{8,11},{9,10},{10,... | collective-permute-start | bytes 688136 | tf_op jit(solution)/shard_map/ppermute | solution.py:32
  97.2 9.7 %collective-permute-start.12 = (f32[64,4,112]{2,0,1:T(8,128)S(1)}, f32[64,4,112]{2,0,1:T(8,128)S(1)}, u32[]{:S(2)}, u32[]{:S(2)}) collective-permute-start(f32[64,4,112]{2,0,1:T(8,128)S(1)} %get-tuple-element.36), channel_id=1, source_target_pairs={{0,1},{1,0},{2,3},{3,2},{4,5},{5,4},{6,7},{7,6},{8,9},{9,8},{10,11... | collective-permute-start | bytes 344072 | tf_op jit(solution)/shard_map/ppermute | solution.py:32
  99.3 12.5 %collective-permute-start.13 = (f32[64,4,112]{2,0,1:T(8,128)S(1)}, f32[64,4,112]{2,0,1:T(8,128)S(1)}, u32[]{:S(2)}, u32[]{:S(2)}) collective-permute-start(f32[64,4,112]{2,0,1:T(8,128)S(1)} %get-tuple-element.38), channel_id=1, source_target_pairs={{0,2},{1,3},{2,0},{3,1},{4,6},{5,7},{6,4},{7,5},{8,10},{9,11},{10,... | collective-permute-start | bytes 344072 | tf_op jit(solution)/shard_map/ppermute | solution.py:32
  99.4 13.0 %collective-permute-start.14 = (f32[64,4,112]{2,0,1:T(8,128)S(1)}, f32[64,4,112]{2,0,1:T(8,128)S(1)}, u32[]{:S(2)}, u32[]{:S(2)}) collective-permute-start(f32[64,4,112]{2,0,1:T(8,128)S(1)} %get-tuple-element.37), channel_id=1, source_target_pairs={{0,3},{1,2},{2,1},{3,0},{4,7},{5,6},{6,5},{7,4},{8,11},{9,10},{10,... | collective-permute-start | bytes 344072 | tf_op jit(solution)/shard_map/ppermute | solution.py:32
  113.4 3.9 %collective-permute-start.6 = (bf16[64,448]{1,0:T(8,128)(2,1)S(1)}, bf16[64,448]{1,0:T(8,128)(2,1)S(1)}, u32[]{:S(2)}, u32[]{:S(2)}) collective-permute-start(bf16[64,448]{1,0:T(8,128)(2,1)S(1)} %multiply_convert_fusion.2), channel_id=1, source_target_pairs={{0,1},{1,0},{2,3},{3,2},{4,5},{5,4},{6,7},{7,6},{8,9},{9,8},{10,11... | collective-permute-start | bytes 172040 | tf_op jit(solution)/shard_map/ppermute | solution.py:32
  114.4 4.8 %collective-permute-start.7 = (bf16[64,448]{1,0:T(8,128)(2,1)S(1)}, bf16[64,448]{1,0:T(8,128)(2,1)S(1)}, u32[]{:S(2)}, u32[]{:S(2)}) collective-permute-start(bf16[64,448]{1,0:T(8,128)(2,1)S(1)} %multiply_convert_fusion.2), channel_id=1, source_target_pairs={{0,2},{1,3},{2,0},{3,1},{4,6},{5,7},{6,4},{7,5},{8,10},{9,11},{10,... | collective-permute-start | bytes 172040 | tf_op jit(solution)/shard_map/ppermute | solution.py:32
  114.5 4.7 %collective-permute-start.8 = (bf16[64,448]{1,0:T(8,128)(2,1)S(1)}, bf16[64,448]{1,0:T(8,128)(2,1)S(1)}, u32[]{:S(2)}, u32[]{:S(2)}) collective-permute-start(bf16[64,448]{1,0:T(8,128)(2,1)S(1)} %multiply_convert_fusion.2), channel_id=1, source_target_pairs={{0,3},{1,2},{2,1},{3,0},{4,7},{5,6},{6,5},{7,4},{8,11},{9,10},{10,... | collective-permute-start | bytes 172040 | tf_op jit(solution)/shard_map/ppermute | solution.py:32
  116.0 9.3 %collective-permute-start.15 = (bf16[64,4,224]{2,0,1:T(8,128)(2,1)S(1)}, bf16[64,4,224]{2,0,1:T(8,128)(2,1)S(1)}, u32[]{:S(2)}, u32[]{:S(2)}) collective-permute-start(bf16[64,4,224]{2,0,1:T(8,128)(2,1)S(1)} %get-tuple-element.44), channel_id=1, source_target_pairs={{0,1},{1,0},{2,3},{3,2},{4,5},{5,4},{6,7},{7,6},{8,9},{9,8},{10,11... | collective-permute-start | bytes 344072 | tf_op jit(solution)/shard_map/ppermute | solution.py:32
  116.7 8.6 %collective-permute-start.16 = (bf16[64,4,224]{2,0,1:T(8,128)(2,1)S(1)}, bf16[64,4,224]{2,0,1:T(8,128)(2,1)S(1)}, u32[]{:S(2)}, u32[]{:S(2)}) collective-permute-start(bf16[64,4,224]{2,0,1:T(8,128)(2,1)S(1)} %get-tuple-element.44), channel_id=1, source_target_pairs={{0,2},{1,3},{2,0},{3,1},{4,6},{5,7},{6,4},{7,5},{8,10},{9,11},{10,... | collective-permute-start | bytes 344072 | tf_op jit(solution)/shard_map/ppermute | solution.py:32
  117.3 8.2 %collective-permute-start.17 = (bf16[64,4,224]{2,0,1:T(8,128)(2,1)S(1)}, bf16[64,4,224]{2,0,1:T(8,128)(2,1)S(1)}, u32[]{:S(2)}, u32[]{:S(2)}) collective-permute-start(bf16[64,4,224]{2,0,1:T(8,128)(2,1)S(1)} %get-tuple-element.44), channel_id=1, source_target_pairs={{0,3},{1,2},{2,1},{3,0},{4,7},{5,6},{6,5},{7,4},{8,11},{9,10},{10,... | collective-permute-start | bytes 344072 | tf_op jit(solution)/shard_map/ppermute | solution.py:32
  137.7 1.7 copy-start
  137.7 2.4 %copy-start.1 = (f32[256,2048]{1,0:T(8,128)S(1)}, f32[256,2048]{1,0:T(8,128)}, u32[]{:S(2)}) copy-start(f32[256,2048]{1,0:T(8,128)} %convolution_add_fusion.1) | copy-start | bytes 6291460
  140.1 1.7 copy-start.2
  143.3 45.3 %all-to-all-start.1 = ((bf16[32,8,2,2048]{3,1,2,0:T(8,128)(2,1)}), bf16[32,8,2,2048]{3,1,2,0:T(8,128)(2,1)}, u32[]{:S(2)}, u32[]{:S(2)}) async-start(bf16[32,8,2,2048]{3,1,2,0:T(8,128)(2,1)} %pad_maximum_fusion), calls=%async_computation.1 | async-start | bytes 4194304 | tf_op jit(solution)/shard_map/all_to_all | solution.py:27

commit v12 on v6

--- a/solution.py
+++ b/solution.py
@@ -111,11 +111,11 @@
     )
     grads = col_gather(joined_grad, n_col).reshape(count, n_col, 2 * unit)
 
-    in_part = None
-    for k, w in enumerate(gu_rel):
-        g = lax.dynamic_index_in_dim(grads, me ^ k, 1, keepdims=False)
-        t = contract_last(g, w)
-        in_part = t if in_part is None else in_part + t
+    gu_cat = jnp.concatenate(gu_rel, axis=1)
+    g_rel = jnp.concatenate(
+        [lax.dynamic_index_in_dim(grads, me ^ k, 1, keepdims=False) for k in range(n_col)], axis=1
+    )
+    in_part = contract_last(g_rel, gu_cat)
     summed = reduce_rows(jnp.stack([term, in_part], axis=1), "row", n_row)
     output = summed[:, 0]
     input_grad = summed[:, 1]

time: 180 us -> 187 us (1.039)
  local copies, waits for them, and re-layouts: 17.4 us -> 21.4 us
  waiting for transfers between devices: 96.1 us -> 99.6 us
  matrix products: 23.8 us -> 20.5 us
  starting transfers between devices: 36.3 us -> 38.4 us
    ppermute x18, waiting for transfers between devices: 50.2 us -> 53.8 us  [swap(): return lax.ppermute(x, 'col', perm=[(i, i ^ k) for i in range(n)])]
    dot_general x8 -> x5, matrix products: 10.3 us -> 7.14 us  [contract_last(): lax.dot_general(left, right, (((1,), (1,)), ((), ())), preferred_element_...]
    ppermute x18, starting transfers between devices: 14.3 us -> 17 us  [swap(): return lax.ppermute(x, 'col', perm=[(i, i ^ k) for i in range(n)])]
    dynamic_update_slice x8, local copies, waits for them, and re-layouts: 0.59 us -> 3.29 us  [place(): out = lax.dynamic_update_slice(out, jnp.expand_dims(p, axis), start)]
  transfers between devices with their start and end apart: 20 -> 20, of which waited for: 9 -> 13; matrix products, arithmetic and copies ran while one was open for 18% -> 19% of each run, Pallas kernels for 0% -> 0%
where the time goes in v12:
time: 187 us; the launch traced here: 186 us
  waiting for transfers between devices  99.6 us (53%)
  starting transfers between devices  38.4 us (21%)
  local copies, waits for them, and re-layouts  21.4 us (11%)
  matrix products  20.5 us (11%)
  other arithmetic  5.36 us (3%)
    ppermute x18, waiting for transfers between devices, swap(): return lax.ppermute(x, 'col', perm=[(i, i ^ k) for i in range(n)])  53.8 us
    all_to_all x1, waiting for transfers between devices, reduce_rows(): got = lax.all_to_all(pieces, axis, split_axis=0, concat_axis=0, tiled=True)  27 us
    all_to_all x1, waiting for transfers between devices, gather_rows(): got = lax.all_to_all(spread, axis, split_axis=0, concat_axis=0, tiled=True)  18.8 us
    ppermute x18, starting transfers between devices, swap(): return lax.ppermute(x, 'col', perm=[(i, i ^ k) for i in range(n)])  17 us
    all_to_all x1, starting transfers between devices, reduce_rows(): got = lax.all_to_all(pieces, axis, split_axis=0, concat_axis=0, tiled=True)  11.3 us
    all_to_all x1, starting transfers between devices, gather_rows(): got = lax.all_to_all(spread, axis, split_axis=0, concat_axis=0, tiled=True)  10.2 us
    dot_general x5, matrix products, contract_last(): lax.dot_general(left, right, (((1,), (1,)), ((), ())), preferred_element_...  7.14 us
    dot_general x4, matrix products, shards(): jnp.dot(full_tokens, w, preferred_element_type=jnp.float32)  5.38 us
  transfers between devices with their start and end apart: 20, of which 13 were waited for; matrix products, arithmetic and copies ran while one was open for 19% of the time, Pallas kernels for 0%

profile of v12, /device:TPU:8, one launch (start us, length us, event | category | flops | bytes accessed | tf_op | source)
XLA Modules:
  0.0 186.4 jit_solution(3330375836163282142)
XLA Ops:
  3.0 10.2 %all-to-all-start = ((bf16[32,8,2,2048]{3,1,2,0:T(8,128)(2,1)}), bf16[32,8,2,2048]{3,1,2,0:T(8,128)(2,1)}, u32[]{:S(2)}, u32[]{:S(2)}) async-start(bf16[32,8,2,2048]{3,1,2,0:T(8,128)(2,1)} %broadcast_in_dim.66), calls=%async_computation | async-start | bytes 4194304 | tf_op jit(solution)/shard_map/all_to_all | solution.py:21
  14.6 2.9 %constant_dynamic-update-slice_fusion = bf16[8192,224]{0,1:T(8,128)(2,1)} fusion(bf16[8192,224]{0,1:T(8,128)(2,1)} %constant_dynamic-update-slice_fusion.1, bf16[8192,112]{0,1:T(8,128)(2,1)} %param.7), kind=kLoop, calls=%fused_computation.103 | loop fusion | bytes 3670016 | tf_op jit(solution)/shard_map/concatenate | solution.py:79
  17.4 3.8 %constant_dynamic-slice_fusion.16 = (bf16[2048,224]{0,1:T(8,128)(2,1)S(1)}, bf16[2048,224]{0,1:T(8,128)(2,1)}, bf16[2048,224]{0,1:T(8,128)(2,1)}, bf16[2048,224]{0,1:T(8,128)(2,1)}) fusion(bf16[8192,224]{0,1:T(8,128)(2,1)} %constant_dynamic-update-slice_fusion, s32[]{:T(128)S(6)} %select_n.36, s32[]{:T(128)S(6)} %select_n.79, s32[]{:T(128)S(6)} %select_n.77, ...), kind=kLoop, calls=%fused_computation.102 | loop fusion | bytes 7340048 | tf_op jit(solution)/shard_map/dynamic_slice | solution.py:36
  25.9 18.8 %all-to-all-done = bf16[32,8,2,2048]{3,1,2,0:T(8,128)(2,1)} async-done(((bf16[32,8,2,2048]{3,1,2,0:T(8,128)(2,1)}), bf16[32,8,2,2048]{3,1,2,0:T(8,128)(2,1)}, u32[]{:S(2)}, u32[]{:S(2)}) %all-to-all-start) | async-done | bytes 2097184 | tf_op jit(solution)/shard_map/all_to_all | solution.py:21
  44.7 1.8 copy.82
  49.2 9.5 %collective-permute-done.1 = bf16[2048,224]{0,1:T(8,128)(2,1)} collective-permute-done((bf16[2048,224]{0,1:T(8,128)(2,1)}, bf16[2048,224]{0,1:T(8,128)(2,1)}, u32[]{:S(2)}, u32[]{:S(2)}) %collective-permute-start.1) | collective-permute-done | bytes 917536 | tf_op jit(solution)/shard_map/ppermute | solution.py:32
  60.4 15.8 %collective-permute-done.2 = bf16[2048,224]{0,1:T(8,128)(2,1)} collective-permute-done((bf16[2048,224]{0,1:T(8,128)(2,1)}, bf16[2048,224]{0,1:T(8,128)(2,1)}, u32[]{:S(2)}, u32[]{:S(2)}) %collective-permute-start.2) | collective-permute-done | bytes 917536 | tf_op jit(solution)/shard_map/ppermute | solution.py:32
  77.9 1.8 collective-permute-start.5
  79.7 1.9 %collective-permute-start.4 = (f32[64,4,224]{2,0,1:T(8,128)S(1)}, f32[64,4,224]{2,0,1:T(8,128)S(1)}, u32[]{:S(2)}, u32[]{:S(2)}) collective-permute-start(f32[64,4,224]{2,0,1:T(8,128)S(1)} %get-tuple-element.18), channel_id=1, source_target_pairs={{0,2},{1,3},{2,0},{3,1},{4,6},{5,7},{6,4},{7,5},{8,10},{9,11},{10,... | collective-permute-start | bytes 688136 | tf_op jit(solution)/shard_map/ppermute | solution.py:32
  84.7 3.4 %collective-permute-done.10 = bf16[112,2048]{1,0:T(8,128)(2,1)S(1)} collective-permute-done((bf16[112,2048]{1,0:T(8,128)(2,1)}, bf16[112,2048]{1,0:T(8,128)(2,1)S(1)}, u32[]{:S(2)}, u32[]{:S(2)}) %collective-permute-start.10) | collective-permute-done | bytes 458784 | tf_op jit(solution)/shard_map/ppermute | solution.py:32
  88.6 7.2 %collective-permute-done.11 = bf16[112,2048]{1,0:T(8,128)(2,1)S(1)} collective-permute-done((bf16[112,2048]{1,0:T(8,128)(2,1)S(1)}, bf16[112,2048]{1,0:T(8,128)(2,1)S(1)}, u32[]{:S(2)}, u32[]{:S(2)}) %collective-permute-start.11) | collective-permute-done | bytes 458784 | tf_op jit(solution)/shard_map/ppermute | solution.py:32
  96.2 2.1 %collective-permute-start.14 = (f32[64,4,112]{2,0,1:T(8,128)S(1)}, f32[64,4,112]{2,0,1:T(8,128)S(1)}, u32[]{:S(2)}, u32[]{:S(2)}) collective-permute-start(f32[64,4,112]{2,0,1:T(8,128)S(1)} %get-tuple-element.24), channel_id=1, source_target_pairs={{0,3},{1,2},{2,1},{3,0},{4,7},{5,6},{6,5},{7,4},{8,11},{9,10},{10,... | collective-permute-start | bytes 344072 | tf_op jit(solution)/shard_map/ppermute | solution.py:32
  98.4 1.9 %collective-permute-start.13 = (f32[64,4,112]{2,0,1:T(8,128)S(1)}, f32[64,4,112]{2,0,1:T(8,128)S(1)}, u32[]{:S(2)}, u32[]{:S(2)}) collective-permute-start(f32[64,4,112]{2,0,1:T(8,128)S(1)} %get-tuple-element.25), channel_id=1, source_target_pairs={{0,2},{1,3},{2,0},{3,1},{4,6},{5,7},{6,4},{7,5},{8,10},{9,11},{10,... | collective-permute-start | bytes 344072 | tf_op jit(solution)/shard_map/ppermute | solution.py:32
  101.3 2.1 %collective-permute-start.12 = (f32[64,4,112]{2,0,1:T(8,128)S(1)}, f32[64,4,112]{2,0,1:T(8,128)S(1)}, u32[]{:S(2)}, u32[]{:S(2)}) collective-permute-start(f32[64,4,112]{2,0,1:T(8,128)S(1)} %get-tuple-element.23), channel_id=1, source_target_pairs={{0,1},{1,0},{2,3},{3,2},{4,5},{5,4},{6,7},{7,6},{8,9},{9,8},{10,11... | collective-permute-start | bytes 344072 | tf_op jit(solution)/shard_map/ppermute | solution.py:32
  103.4 5.8 %collective-permute-done.4 = f32[64,4,224]{2,0,1:T(8,128)S(1)} collective-permute-done((f32[64,4,224]{2,0,1:T(8,128)S(1)}, f32[64,4,224]{2,0,1:T(8,128)S(1)}, u32[]{:S(2)}, u32[]{:S(2)}) %collective-permute-start.4) | collective-permute-done | bytes 229408 | tf_op jit(solution)/shard_map/ppermute | solution.py:32
  109.8 3.9 %collective-permute-done.13 = f32[64,4,112]{2,0,1:T(8,128)S(1)} collective-permute-done((f32[64,4,112]{2,0,1:T(8,128)S(1)}, f32[64,4,112]{2,0,1:T(8,128)S(1)}, u32[]{:S(2)}, u32[]{:S(2)}) %collective-permute-start.13) | collective-permute-done | bytes 114720 | tf_op jit(solution)/shard_map/ppermute | solution.py:32
  114.8 1.7 collective-permute-start.17
  119.9 5.6 %collective-permute-done.7 = bf16[64,448]{1,0:T(8,128)(2,1)S(1)} collective-permute-done((bf16[64,448]{1,0:T(8,128)(2,1)S(1)}, bf16[64,448]{1,0:T(8,128)(2,1)S(1)}, u32[]{:S(2)}, u32[]{:S(2)}) %collective-permute-start.7) | collective-permute-done | bytes 57376 | tf_op jit(solution)/shard_map/ppermute | solution.py:32
  134.7 3.4 %fusion.14 = bf16[32,8,1,2048]{3,1,2,0:T(8,128)(2,1)S(1)} fusion(bf16[2048,224]{0,1:T(8,128)(2,1)} %collective-permute-done.2, bf16[2048,224]{0,1:T(8,128)(2,1)} %collective-permute-done.1, bf16[2048,224]{0,1:T(8,128)(2,1)} %collective-permute-done, bf16[2048,224]{0,1:T(8,128)(2,1)} %copy-done.3, bf16[256,224]{0,1:T(8,128)(2,1)S(1)} %bitcast.129, ...), kind=kOutput, calls=%fused_computation.17 | convolution fusion | flops 956563456 | bytes 5177344 | tf_op jit(solution)/shard_map/dot_general | solution.py:8
  139.6 11.3 %all-to-all-start.1 = ((bf16[32,8,2,2048]{3,1,2,0:T(8,128)(2,1)}), bf16[32,8,2,2048]{3,1,2,0:T(8,128)(2,1)}, u32[]{:S(2)}, u32[]{:S(2)}) async-start(bf16[32,8,2,2048]{3,1,2,0:T(8,128)(2,1)} %pad_maximum_fusion), calls=%async_computation.1 | async-start | bytes 4194304 | tf_op jit(solution)/shard_map/all_to_all | solution.py:27
  150.9 1.9 %convolution_convert_fusion.1 = bf16[448,2048]{1,0:T(8,128)(2,1)} fusion(bf16[256,448]{1,0:T(8,128)(2,1)S(1)} %bitcast.123, bf16[256,2,2048]{2,0,1:T(8,128)(2,1)S(1)} %bitcast.117), kind=kOutput, calls=%fused_computation.10 | convolution fusion | flops 470679552 | bytes 3145728 | tf_op jit(solution)/shard_map/dot_general | solution.py:14
  154.5 2.3 %fusion.58 = (bf16[2048,4,112]{0,2,1:T(8,128)(2,1)}, bf16[2048,4,112]{0,2,1:T(8,128)(2,1)}) fusion(bf16[2048,4,224]{0,2,1:T(8,128)(2,1)S(1)} %convolution_convert_fusion), kind=kLoop, calls=%fused_computation.107 | loop fusion | bytes 7340032 | tf_op jit(solution)/shard_map/slice | solution.py:125
  156.8 27.0 %all-to-all-done.1 = bf16[32,8,2,2048]{3,1,2,0:T(8,128)(2,1)} async-done(((bf16[32,8,2,2048]{3,1,2,0:T(8,128)(2,1)}), bf16[32,8,2,2048]{3,1,2,0:T(8,128)(2,1)}, u32[]{:S(2)}, u32[]{:S(2)}) %all-to-all-start.1) | async-done | bytes 2097184 | tf_op jit(solution)/shard_map/all_to_all | solution.py:27
  183.8 1.9 %convert_reduce_fusion = f32[8,2,2048]{2,0,1:T(8,128)S(1)} fusion(bf16[32,8,2,2048]{3,1,2,0:T(8,128)(2,1)} %all-to-all-done.1), kind=kLoop, calls=%fused_computation | loop fusion | flops 2064384 | bytes 2228224 | tf_op jit(solution)/shard_map/reduce_sum | solution.py:28
  (89 shorter events, 37.3 us)
Async XLA Ops:
  3.0 10.2 %copy-start.2 = (bf16[8192,112]{0,1:T(8,128)(2,1)S(1)}, bf16[8192,112]{0,1:T(8,128)(2,1)}, u32[]{:S(2)}) copy-start(bf16[8192,112]{0,1:T(8,128)(2,1)} %param.6) | copy-start | bytes 5505028
  3.0 41.7 %all-to-all-start = ((bf16[32,8,2,2048]{3,1,2,0:T(8,128)(2,1)}), bf16[32,8,2,2048]{3,1,2,0:T(8,128)(2,1)}, u32[]{:S(2)}, u32[]{:S(2)}) async-start(bf16[32,8,2,2048]{3,1,2,0:T(8,128)(2,1)} %broadcast_in_dim.66), calls=%async_computation | async-start | bytes 4194304 | tf_op jit(solution)/shard_map/all_to_all | solution.py:21
  17.4 5.6 %copy-start.1 = (bf16[112,8192]{1,0:T(8,128)(2,1)S(1)}, bf16[112,8192]{1,0:T(8,128)(2,1)}, u32[]{:S(2)}) copy-start(bf16[112,8192]{1,0:T(8,128)(2,1)} %param.8) | copy-start | bytes 5505028
  21.2 25.4 %copy-start.3 = (bf16[2048,224]{0,1:T(8,128)(2,1)}, bf16[2048,224]{0,1:T(8,128)(2,1)S(1)}, u32[]{:S(2)}) copy-start(bf16[2048,224]{0,1:T(8,128)(2,1)S(1)} %get-tuple-element.9) | copy-start | bytes 2752516
  21.2 25.9 %collective-permute-start = (bf16[2048,224]{0,1:T(8,128)(2,1)}, bf16[2048,224]{0,1:T(8,128)(2,1)}, u32[]{:S(2)}, u32[]{:S(2)}) collective-permute-start(bf16[2048,224]{0,1:T(8,128)(2,1)} %get-tuple-element.12), channel_id=1, source_target_pairs={{0,1},{1,0},{2,3},{3,2},{4,5},{5,4},{6,7},{7,6},{8,9},{9,8},{10,11... | collective-permute-start | bytes 2752520 | tf_op jit(solution)/shard_map/ppermute | solution.py:32
  21.2 37.5 %collective-permute-start.1 = (bf16[2048,224]{0,1:T(8,128)(2,1)}, bf16[2048,224]{0,1:T(8,128)(2,1)}, u32[]{:S(2)}, u32[]{:S(2)}) collective-permute-start(bf16[2048,224]{0,1:T(8,128)(2,1)} %get-tuple-element.11), channel_id=1, source_target_pairs={{0,2},{1,3},{2,0},{3,1},{4,6},{5,7},{6,4},{7,5},{8,10},{9,11},{10,... | collective-permute-start | bytes 2752520 | tf_op jit(solution)/shard_map/ppermute | solution.py:32
  22.6 53.6 %collective-permute-start.2 = (bf16[2048,224]{0,1:T(8,128)(2,1)}, bf16[2048,224]{0,1:T(8,128)(2,1)}, u32[]{:S(2)}, u32[]{:S(2)}) collective-permute-start(bf16[2048,224]{0,1:T(8,128)(2,1)} %get-tuple-element.10), channel_id=1, source_target_pairs={{0,3},{1,2},{2,1},{3,0},{4,7},{5,6},{6,5},{7,4},{8,11},{9,10},{10,... | collective-permute-start | bytes 2752520 | tf_op jit(solution)/shard_map/ppermute | solution.py:32
  24.3 58.9 %collective-permute-start.9 = (bf16[112,2048]{1,0:T(8,128)(2,1)}, bf16[112,2048]{1,0:T(8,128)(2,1)}, u32[]{:S(2)}, u32[]{:S(2)}) collective-permute-start(bf16[112,2048]{1,0:T(8,128)(2,1)} %get-tuple-element.14), channel_id=1, source_target_pairs={{0,1},{1,0},{2,3},{3,2},{4,5},{5,4},{6,7},{7,6},{8,9},{9,8},{10,11... | collective-permute-start | bytes 1376264 | tf_op jit(solution)/shard_map/ppermute | solution.py:32
  24.5 63.6 %collective-permute-start.10 = (bf16[112,2048]{1,0:T(8,128)(2,1)}, bf16[112,2048]{1,0:T(8,128)(2,1)S(1)}, u32[]{:S(2)}, u32[]{:S(2)}) collective-permute-start(bf16[112,2048]{1,0:T(8,128)(2,1)} %get-tuple-element.15), channel_id=1, source_target_pairs={{0,2},{1,3},{2,0},{3,1},{4,6},{5,7},{6,4},{7,5},{8,10},{9,11},{10,... | collective-permute-start | bytes 1376264 | tf_op jit(solution)/shard_map/ppermute | solution.py:32
  47.6 48.2 %collective-permute-start.11 = (bf16[112,2048]{1,0:T(8,128)(2,1)S(1)}, bf16[112,2048]{1,0:T(8,128)(2,1)S(1)}, u32[]{:S(2)}, u32[]{:S(2)}) collective-permute-start(bf16[112,2048]{1,0:T(8,128)(2,1)S(1)} %copy-done.6), channel_id=1, source_target_pairs={{0,3},{1,2},{2,1},{3,0},{4,7},{5,6},{6,5},{7,4},{8,11},{9,10},{10,... | collective-permute-start | bytes 1376264 | tf_op jit(solution)/shard_map/ppermute | solution.py:32
  77.9 23.4 %collective-permute-start.5 = (f32[64,4,224]{2,0,1:T(8,128)S(1)}, f32[64,4,224]{2,0,1:T(8,128)S(1)}, u32[]{:S(2)}, u32[]{:S(2)}) collective-permute-start(f32[64,4,224]{2,0,1:T(8,128)S(1)} %get-tuple-element.17), channel_id=1, source_target_pairs={{0,3},{1,2},{2,1},{3,0},{4,7},{5,6},{6,5},{7,4},{8,11},{9,10},{10,... | collective-permute-start | bytes 688136 | tf_op jit(solution)/shard_map/ppermute | solution.py:32
  79.7 29.4 %collective-permute-start.4 = (f32[64,4,224]{2,0,1:T(8,128)S(1)}, f32[64,4,224]{2,0,1:T(8,128)S(1)}, u32[]{:S(2)}, u32[]{:S(2)}) collective-permute-start(f32[64,4,224]{2,0,1:T(8,128)S(1)} %get-tuple-element.18), channel_id=1, source_target_pairs={{0,2},{1,3},{2,0},{3,1},{4,6},{5,7},{6,4},{7,5},{8,10},{9,11},{10,... | collective-permute-start | bytes 688136 | tf_op jit(solution)/shard_map/ppermute | solution.py:32
  83.2 26.0 %collective-permute-start.3 = (f32[64,4,224]{2,0,1:T(8,128)S(1)}, f32[64,4,224]{2,0,1:T(8,128)S(1)}, u32[]{:S(2)}, u32[]{:S(2)}) collective-permute-start(f32[64,4,224]{2,0,1:T(8,128)S(1)} %get-tuple-element.16), channel_id=1, source_target_pairs={{0,1},{1,0},{2,3},{3,2},{4,5},{5,4},{6,7},{7,6},{8,9},{9,8},{10,11... | collective-permute-start | bytes 688136 | tf_op jit(solution)/shard_map/ppermute | solution.py:32
  95.7 18.1 %copy-start.4 = (bf16[112,2048]{1,0:T(8,128)(2,1)}, bf16[112,2048]{1,0:T(8,128)(2,1)S(1)}, u32[]{:S(2)}) copy-start(bf16[112,2048]{1,0:T(8,128)(2,1)S(1)} %collective-permute-done.11) | copy-start | bytes 1376260
  96.2 13.6 %collective-permute-start.14 = (f32[64,4,112]{2,0,1:T(8,128)S(1)}, f32[64,4,112]{2,0,1:T(8,128)S(1)}, u32[]{:S(2)}, u32[]{:S(2)}) collective-permute-start(f32[64,4,112]{2,0,1:T(8,128)S(1)} %get-tuple-element.24), channel_id=1, source_target_pairs={{0,3},{1,2},{2,1},{3,0},{4,7},{5,6},{6,5},{7,4},{8,11},{9,10},{10,... | collective-permute-start | bytes 344072 | tf_op jit(solution)/shard_map/ppermute | solution.py:32
  98.4 15.3 %collective-permute-start.13 = (f32[64,4,112]{2,0,1:T(8,128)S(1)}, f32[64,4,112]{2,0,1:T(8,128)S(1)}, u32[]{:S(2)}, u32[]{:S(2)}) collective-permute-start(f32[64,4,112]{2,0,1:T(8,128)S(1)} %get-tuple-element.25), channel_id=1, source_target_pairs={{0,2},{1,3},{2,0},{3,1},{4,6},{5,7},{6,4},{7,5},{8,10},{9,11},{10,... | collective-permute-start | bytes 344072 | tf_op jit(solution)/shard_map/ppermute | solution.py:32
  101.3 12.4 %collective-permute-start.12 = (f32[64,4,112]{2,0,1:T(8,128)S(1)}, f32[64,4,112]{2,0,1:T(8,128)S(1)}, u32[]{:S(2)}, u32[]{:S(2)}) collective-permute-start(f32[64,4,112]{2,0,1:T(8,128)S(1)} %get-tuple-element.23), channel_id=1, source_target_pairs={{0,1},{1,0},{2,3},{3,2},{4,5},{5,4},{6,7},{7,6},{8,9},{9,8},{10,11... | collective-permute-start | bytes 344072 | tf_op jit(solution)/shard_map/ppermute | solution.py:32
  114.7 16.3 %collective-permute-start.15 = (bf16[64,4,224]{2,0,1:T(8,128)(2,1)}, bf16[64,4,224]{2,0,1:T(8,128)(2,1)}, u32[]{:S(2)}, u32[]{:S(2)}) collective-permute-start(bf16[64,4,224]{2,0,1:T(8,128)(2,1)} %get-tuple-element.31), channel_id=1, source_target_pairs={{0,1},{1,0},{2,3},{3,2},{4,5},{5,4},{6,7},{7,6},{8,9},{9,8},{10,11... | collective-permute-start | bytes 344072 | tf_op jit(solution)/shard_map/ppermute | solution.py:32
  114.7 17.4 %collective-permute-start.16 = (bf16[64,4,224]{2,0,1:T(8,128)(2,1)}, bf16[64,4,224]{2,0,1:T(8,128)(2,1)}, u32[]{:S(2)}, u32[]{:S(2)}) collective-permute-start(bf16[64,4,224]{2,0,1:T(8,128)(2,1)} %get-tuple-element.31), channel_id=1, source_target_pairs={{0,2},{1,3},{2,0},{3,1},{4,6},{5,7},{6,4},{7,5},{8,10},{9,11},{10,... | collective-permute-start | bytes 344072 | tf_op jit(solution)/shard_map/ppermute | solution.py:32
  114.8 18.3 %collective-permute-start.17 = (bf16[64,4,224]{2,0,1:T(8,128)(2,1)}, bf16[64,4,224]{2,0,1:T(8,128)(2,1)}, u32[]{:S(2)}, u32[]{:S(2)}) collective-permute-start(bf16[64,4,224]{2,0,1:T(8,128)(2,1)} %get-tuple-element.31), channel_id=1, source_target_pairs={{0,3},{1,2},{2,1},{3,0},{4,7},{5,6},{6,5},{7,4},{8,11},{9,10},{10,... | collective-permute-start | bytes 344072 | tf_op jit(solution)/shard_map/ppermute | solution.py:32
  117.3 1.3 collective-permute-start.6
  117.7 7.8 %collective-permute-start.7 = (bf16[64,448]{1,0:T(8,128)(2,1)S(1)}, bf16[64,448]{1,0:T(8,128)(2,1)S(1)}, u32[]{:S(2)}, u32[]{:S(2)}) collective-permute-start(bf16[64,448]{1,0:T(8,128)(2,1)S(1)} %multiply_convert_fusion.2), channel_id=1, source_target_pairs={{0,2},{1,3},{2,0},{3,1},{4,6},{5,7},{6,4},{7,5},{8,10},{9,11},{10,... | collective-permute-start | bytes 172040 | tf_op jit(solution)/shard_map/ppermute | solution.py:32
  118.6 7.3 %collective-permute-start.8 = (bf16[64,448]{1,0:T(8,128)(2,1)S(1)}, bf16[64,448]{1,0:T(8,128)(2,1)S(1)}, u32[]{:S(2)}, u32[]{:S(2)}) collective-permute-start(bf16[64,448]{1,0:T(8,128)(2,1)S(1)} %multiply_convert_fusion.2), channel_id=1, source_target_pairs={{0,3},{1,2},{2,1},{3,0},{4,7},{5,6},{6,5},{7,4},{8,11},{9,10},{10,... | collective-permute-start | bytes 172040 | tf_op jit(solution)/shard_map/ppermute | solution.py:32
  139.6 44.2 %all-to-all-start.1 = ((bf16[32,8,2,2048]{3,1,2,0:T(8,128)(2,1)}), bf16[32,8,2,2048]{3,1,2,0:T(8,128)(2,1)}, u32[]{:S(2)}, u32[]{:S(2)}) async-start(bf16[32,8,2,2048]{3,1,2,0:T(8,128)(2,1)} %pad_maximum_fusion), calls=%async_computation.1 | async-start | bytes 4194304 | tf_op jit(solution)/shard_map/all_to_all | solution.py:27
  (3 other events, 6.0 us)

commit v13 on v6

--- a/solution.py
+++ b/solution.py
@@ -92,24 +92,27 @@
     up_sum = gu_sum[:, :, unit:].reshape(share, n_col * unit)
     sig = jax.nn.sigmoid(gate_sum)
     hidden_share = (gate_sum * sig * up_sum).astype(jnp.bfloat16)
-    hidden = col_gather(hidden_share, n_col).reshape(count, n_col * unit)
 
-    term = None
-    for k, w in enumerate(down_rel):
-        h = lax.dynamic_slice_in_dim(hidden, (me ^ k) * unit, unit, 1)
-        t = jnp.dot(h, w, preferred_element_type=jnp.float32)
-        term = t if term is None else term + t
 
     dh_part = place([contract_last(grad_full, w) for w in down_rel], me, 1)
     hidden_grad = col_reduce(dh_part, n_col).reshape(share, n_col * unit)
-    grad_down = contract_first(hidden, grad_full).astype(jnp.bfloat16)
 
     gate_grad = (hidden_grad * up_sum * sig * (1.0 + gate_sum * (1.0 - sig))).astype(jnp.bfloat16)
     up_grad = (hidden_grad * gate_sum * sig).astype(jnp.bfloat16)
     joined_grad = jnp.concatenate(
         [gate_grad.reshape(share, n_col, unit), up_grad.reshape(share, n_col, unit)], axis=2
     )
-    grads = col_gather(joined_grad, n_col).reshape(count, n_col, 2 * unit)
+    both_col = col_gather(
+        jnp.concatenate([hidden_share, joined_grad.reshape(share, n_col * 2 * unit)], axis=1), n_col
+    ).reshape(count, n_col * 3 * unit)
+    hidden = both_col[:, : n_col * unit]
+    grads = both_col[:, n_col * unit :].reshape(count, n_col, 2 * unit)
+    grad_down = contract_first(hidden, grad_full).astype(jnp.bfloat16)
+    term = None
+    for k, w in enumerate(down_rel):
+        h = lax.dynamic_slice_in_dim(hidden, (me ^ k) * unit, unit, 1)
+        t = jnp.dot(h, w, preferred_element_type=jnp.float32)
+        term = t if term is None else term + t
 
     in_part = None
     for k, w in enumerate(gu_rel):

time: 180 us -> 187 us (1.039)
  waiting for transfers between devices: 96.1 us -> 101 us
  local copies, waits for them, and re-layouts: 17.4 us -> 20.6 us
  matrix products: 23.8 us -> 21.8 us
    ppermute x18 -> x15, waiting for transfers between devices: 50.2 us -> 55.6 us  [swap(): return lax.ppermute(x, 'col', perm=[(i, i ^ k) for i in range(n)])]
    dot_general x1 -> x2, local copies, waits for them, and re-layouts: 0.21 us -> 2.19 us  [contract_first(): lax.dot_general(left, right, (((0,), (0,)), ((), ())), preferred_element_...]
    ppermute x18 -> x15, starting transfers between devices: 14.3 us -> 15.5 us  [swap(): return lax.ppermute(x, 'col', perm=[(i, i ^ k) for i in range(n)])]
  transfers between devices with their start and end apart: 20 -> 17, of which waited for: 9 -> 12; matrix products, arithmetic and copies ran while one was open for 18% -> 14% of each run, Pallas kernels for 0% -> 0%
where the time goes in v13:
time: 187 us
  waiting for transfers between devices  101 us (54%)
  starting transfers between devices  36.9 us (20%)
  matrix products  21.8 us (12%)
  local copies, waits for them, and re-layouts  20.6 us (11%)
  other arithmetic  4.88 us (3%)
    ppermute x15, waiting for transfers between devices, swap(): return lax.ppermute(x, 'col', perm=[(i, i ^ k) for i in range(n)])  55.6 us
    all_to_all x1, waiting for transfers between devices, reduce_rows(): got = lax.all_to_all(pieces, axis, split_axis=0, concat_axis=0, tiled=True)  26.4 us
    all_to_all x1, waiting for transfers between devices, gather_rows(): got = lax.all_to_all(spread, axis, split_axis=0, concat_axis=0, tiled=True)  19.3 us
    ppermute x15, starting transfers between devices, swap(): return lax.ppermute(x, 'col', perm=[(i, i ^ k) for i in range(n)])  15.5 us
    all_to_all x1, starting transfers between devices, reduce_rows(): got = lax.all_to_all(pieces, axis, split_axis=0, concat_axis=0, tiled=True)  11.2 us
    all_to_all x1, starting transfers between devices, gather_rows(): got = lax.all_to_all(spread, axis, split_axis=0, concat_axis=0, tiled=True)  10.2 us
    dot_general x8, matrix products, contract_last(): lax.dot_general(left, right, (((1,), (1,)), ((), ())), preferred_element_...  9.35 us
    dot_general x4, matrix products, shards(): jnp.dot(full_tokens, w, preferred_element_type=jnp.float32)  5.43 us
  transfers between devices with their start and end apart: 17, of which 12 were waited for; matrix products, arithmetic and copies ran while one was open for 14% of the time, Pallas kernels for 0%

profile of v13, /device:TPU:8, one launch (start us, length us, event | category | flops | bytes accessed | tf_op | source)
XLA Modules:
  0.0 186.5 jit_solution(328864523920332744)
XLA Ops:
  3.0 10.2 %all-to-all-start = ((bf16[32,8,2,2048]{3,1,2,0:T(8,128)(2,1)}), bf16[32,8,2,2048]{3,1,2,0:T(8,128)(2,1)}, u32[]{:S(2)}, u32[]{:S(2)}) async-start(bf16[32,8,2,2048]{3,1,2,0:T(8,128)(2,1)} %broadcast_in_dim.53), calls=%async_computation | async-start | bytes 4194304 | tf_op jit(solution)/shard_map/all_to_all | solution.py:21
  14.6 2.9 %constant_dynamic-update-slice_fusion = bf16[8192,224]{0,1:T(8,128)(2,1)} fusion(bf16[8192,224]{0,1:T(8,128)(2,1)} %constant_dynamic-update-slice_fusion.1, bf16[8192,112]{0,1:T(8,128)(2,1)} %param.7), kind=kLoop, calls=%fused_computation.99 | loop fusion | bytes 3670016 | tf_op jit(solution)/shard_map/concatenate | solution.py:79
  17.4 3.5 %constant_dynamic-slice_fusion.10 = (bf16[2048,224]{0,1:T(8,128)(2,1)}, bf16[2048,224]{0,1:T(8,128)(2,1)}, bf16[2048,224]{0,1:T(8,128)(2,1)}) fusion(bf16[8192,224]{0,1:T(8,128)(2,1)} %constant_dynamic-update-slice_fusion, s32[]{:T(128)S(6)} %select_n.73, s32[]{:T(128)S(6)} %select_n.75, s32[]{:T(128)S(6)} %select_n.71), kind=kLoop, calls=%fused_computation.95 | loop fusion | bytes 5505036 | tf_op jit(solution)/shard_map/dynamic_slice | solution.py:36
  25.5 19.3 %all-to-all-done = bf16[32,8,2,2048]{3,1,2,0:T(8,128)(2,1)} async-done(((bf16[32,8,2,2048]{3,1,2,0:T(8,128)(2,1)}), bf16[32,8,2,2048]{3,1,2,0:T(8,128)(2,1)}, u32[]{:S(2)}, u32[]{:S(2)}) %all-to-all-start) | async-done | bytes 2097184 | tf_op jit(solution)/shard_map/all_to_all | solution.py:21
  44.8 1.7 copy.98
  50.1 8.5 %collective-permute-done.1 = bf16[2048,224]{0,1:T(8,128)(2,1)S(1)} collective-permute-done((bf16[2048,224]{0,1:T(8,128)(2,1)}, bf16[2048,224]{0,1:T(8,128)(2,1)S(1)}, u32[]{:S(2)}, u32[]{:S(2)}) %collective-permute-start.1) | collective-permute-done | bytes 917536 | tf_op jit(solution)/shard_map/ppermute | solution.py:32
  59.1 17.1 %collective-permute-done.2 = bf16[2048,224]{0,1:T(8,128)(2,1)} collective-permute-done((bf16[2048,224]{0,1:T(8,128)(2,1)}, bf16[2048,224]{0,1:T(8,128)(2,1)}, u32[]{:S(2)}, u32[]{:S(2)}) %collective-permute-start.2) | collective-permute-done | bytes 917536 | tf_op jit(solution)/shard_map/ppermute | solution.py:32
  77.9 1.8 collective-permute-start.5
  79.8 1.9 %collective-permute-start.4 = (f32[64,4,224]{2,0,1:T(8,128)S(1)}, f32[64,4,224]{2,0,1:T(8,128)S(1)}, u32[]{:S(2)}, u32[]{:S(2)}) collective-permute-start(f32[64,4,224]{2,0,1:T(8,128)S(1)} %get-tuple-element.17), channel_id=1, source_target_pairs={{0,2},{1,3},{2,0},{3,1},{4,6},{5,7},{6,4},{7,5},{8,10},{9,11},{10,... | collective-permute-start | bytes 688136 | tf_op jit(solution)/shard_map/ppermute | solution.py:32
  83.7 4.5 %collective-permute-done.7 = bf16[112,2048]{1,0:T(8,128)(2,1)} collective-permute-done((bf16[112,2048]{1,0:T(8,128)(2,1)}, bf16[112,2048]{1,0:T(8,128)(2,1)}, u32[]{:S(2)}, u32[]{:S(2)}) %collective-permute-start.7) | collective-permute-done | bytes 458784 | tf_op jit(solution)/shard_map/ppermute | solution.py:32
  89.7 6.0 %collective-permute-done.8 = bf16[112,2048]{1,0:T(8,128)(2,1)S(1)} collective-permute-done((bf16[112,2048]{1,0:T(8,128)(2,1)S(1)}, bf16[112,2048]{1,0:T(8,128)(2,1)S(1)}, u32[]{:S(2)}, u32[]{:S(2)}) %collective-permute-start.8) | collective-permute-done | bytes 458784 | tf_op jit(solution)/shard_map/ppermute | solution.py:32
  96.2 2.1 %collective-permute-start.11 = (f32[64,4,112]{2,0,1:T(8,128)S(1)}, f32[64,4,112]{2,0,1:T(8,128)S(1)}, u32[]{:S(2)}, u32[]{:S(2)}) collective-permute-start(f32[64,4,112]{2,0,1:T(8,128)S(1)} %get-tuple-element.21), channel_id=1, source_target_pairs={{0,3},{1,2},{2,1},{3,0},{4,7},{5,6},{6,5},{7,4},{8,11},{9,10},{10,... | collective-permute-start | bytes 344072 | tf_op jit(solution)/shard_map/ppermute | solution.py:32
  98.4 1.9 %collective-permute-start.10 = (f32[64,4,112]{2,0,1:T(8,128)S(1)}, f32[64,4,112]{2,0,1:T(8,128)S(1)}, u32[]{:S(2)}, u32[]{:S(2)}) collective-permute-start(f32[64,4,112]{2,0,1:T(8,128)S(1)} %get-tuple-element.22), channel_id=1, source_target_pairs={{0,2},{1,3},{2,0},{3,1},{4,6},{5,7},{6,4},{7,5},{8,10},{9,11},{10,... | collective-permute-start | bytes 344072 | tf_op jit(solution)/shard_map/ppermute | solution.py:32
  101.4 2.1 %collective-permute-start.9 = (f32[64,4,112]{2,0,1:T(8,128)S(1)}, f32[64,4,112]{2,0,1:T(8,128)S(1)}, u32[]{:S(2)}, u32[]{:S(2)}) collective-permute-start(f32[64,4,112]{2,0,1:T(8,128)S(1)} %get-tuple-element.20), channel_id=1, source_target_pairs={{0,1},{1,0},{2,3},{3,2},{4,5},{5,4},{6,7},{7,6},{8,9},{9,8},{10,11... | collective-permute-start | bytes 344072 | tf_op jit(solution)/shard_map/ppermute | solution.py:32
  103.4 5.8 %collective-permute-done.4 = f32[64,4,224]{2,0,1:T(8,128)S(1)} collective-permute-done((f32[64,4,224]{2,0,1:T(8,128)S(1)}, f32[64,4,224]{2,0,1:T(8,128)S(1)}, u32[]{:S(2)}, u32[]{:S(2)}) %collective-permute-start.4) | collective-permute-done | bytes 229408 | tf_op jit(solution)/shard_map/ppermute | solution.py:32
  109.8 3.9 %collective-permute-done.10 = f32[64,4,112]{2,0,1:T(8,128)S(1)} collective-permute-done((f32[64,4,112]{2,0,1:T(8,128)S(1)}, f32[64,4,112]{2,0,1:T(8,128)S(1)}, u32[]{:S(2)}, u32[]{:S(2)}) %collective-permute-start.10) | collective-permute-done | bytes 114720 | tf_op jit(solution)/shard_map/ppermute | solution.py:32
  117.1 5.4 %collective-permute-done.13 = bf16[64,1344]{1,0:T(8,128)(2,1)S(1)} collective-permute-done((bf16[64,1344]{1,0:T(8,128)(2,1)S(1)}, bf16[64,1344]{1,0:T(8,128)(2,1)S(1)}, u32[]{:S(2)}, u32[]{:S(2)}) %collective-permute-start.13) | collective-permute-done | bytes 172064 | tf_op jit(solution)/shard_map/ppermute | solution.py:32
  122.5 2.7 %collective-permute-done.14 = bf16[64,1344]{1,0:T(8,128)(2,1)S(1)} collective-permute-done((bf16[64,1344]{1,0:T(8,128)(2,1)S(1)}, bf16[64,1344]{1,0:T(8,128)(2,1)S(1)}, u32[]{:S(2)}, u32[]{:S(2)}) %collective-permute-start.14) | collective-permute-done | bytes 172064 | tf_op jit(solution)/shard_map/ppermute | solution.py:32
  127.3 1.7 fusion.19
  139.7 11.2 %all-to-all-start.1 = ((bf16[32,8,2,2048]{3,1,2,0:T(8,128)(2,1)}), bf16[32,8,2,2048]{3,1,2,0:T(8,128)(2,1)}, u32[]{:S(2)}, u32[]{:S(2)}) async-start(bf16[32,8,2,2048]{3,1,2,0:T(8,128)(2,1)} %pad_maximum_fusion), calls=%async_computation.1 | async-start | bytes 4194304 | tf_op jit(solution)/shard_map/all_to_all | solution.py:27
  152.1 1.9 %convolution_convert_fusion.1 = bf16[448,2048]{1,0:T(8,128)(2,1)} fusion(bf16[256,2,2048]{2,0,1:T(8,128)(2,1)S(1)} %bitcast.116, bf16[256,1344]{1,0:T(8,128)(2,1)S(1)} %bitcast.120), kind=kOutput, calls=%fused_computation.2 | convolution fusion | flops 470679552 | bytes 3145728 | tf_op jit(solution)/shard_map/dot_general | solution.py:14
  155.2 2.3 %fusion.55 = (bf16[2048,4,112]{0,2,1:T(8,128)(2,1)}, bf16[2048,4,112]{0,2,1:T(8,128)(2,1)}) fusion(bf16[2048,4,224]{0,2,1:T(8,128)(2,1)S(1)} %convolution_convert_fusion), kind=kLoop, calls=%fused_computation.103 | loop fusion | bytes 7340032 | tf_op jit(solution)/shard_map/slice | solution.py:128
  157.5 26.4 %all-to-all-done.1 = bf16[32,8,2,2048]{3,1,2,0:T(8,128)(2,1)} async-done(((bf16[32,8,2,2048]{3,1,2,0:T(8,128)(2,1)}), bf16[32,8,2,2048]{3,1,2,0:T(8,128)(2,1)}, u32[]{:S(2)}, u32[]{:S(2)}) %all-to-all-start.1) | async-done | bytes 2097184 | tf_op jit(solution)/shard_map/all_to_all | solution.py:27
  183.9 1.9 %convert_reduce_fusion = f32[8,2,2048]{2,0,1:T(8,128)S(1)} fusion(bf16[32,8,2,2048]{3,1,2,0:T(8,128)(2,1)} %all-to-all-done.1), kind=kLoop, calls=%fused_computation | loop fusion | flops 2064384 | bytes 2228224 | tf_op jit(solution)/shard_map/reduce_sum | solution.py:28
  (84 shorter events, 38.5 us)
Async XLA Ops:
  3.0 10.2 %copy-start = (bf16[8192,112]{0,1:T(8,128)(2,1)S(1)}, bf16[8192,112]{0,1:T(8,128)(2,1)}, u32[]{:S(2)}) copy-start(bf16[8192,112]{0,1:T(8,128)(2,1)} %param.6) | copy-start | bytes 5505028
  3.0 41.8 %all-to-all-start = ((bf16[32,8,2,2048]{3,1,2,0:T(8,128)(2,1)}), bf16[32,8,2,2048]{3,1,2,0:T(8,128)(2,1)}, u32[]{:S(2)}, u32[]{:S(2)}) async-start(bf16[32,8,2,2048]{3,1,2,0:T(8,128)(2,1)} %broadcast_in_dim.53), calls=%async_computation | async-start | bytes 4194304 | tf_op jit(solution)/shard_map/all_to_all | solution.py:21
  17.4 5.4 %copy-start.1 = (bf16[112,8192]{1,0:T(8,128)(2,1)S(1)}, bf16[112,8192]{1,0:T(8,128)(2,1)}, u32[]{:S(2)}) copy-start(bf16[112,8192]{1,0:T(8,128)(2,1)} %param.8) | copy-start | bytes 5505028
  20.9 27.4 %collective-permute-start = (bf16[2048,224]{0,1:T(8,128)(2,1)}, bf16[2048,224]{0,1:T(8,128)(2,1)}, u32[]{:S(2)}, u32[]{:S(2)}) collective-permute-start(bf16[2048,224]{0,1:T(8,128)(2,1)} %get-tuple-element.11), channel_id=1, source_target_pairs={{0,1},{1,0},{2,3},{3,2},{4,5},{5,4},{6,7},{7,6},{8,9},{9,8},{10,11... | collective-permute-start | bytes 2752520 | tf_op jit(solution)/shard_map/ppermute | solution.py:32
  20.9 37.7 %collective-permute-start.1 = (bf16[2048,224]{0,1:T(8,128)(2,1)}, bf16[2048,224]{0,1:T(8,128)(2,1)S(1)}, u32[]{:S(2)}, u32[]{:S(2)}) collective-permute-start(bf16[2048,224]{0,1:T(8,128)(2,1)} %get-tuple-element.9), channel_id=1, source_target_pairs={{0,2},{1,3},{2,0},{3,1},{4,6},{5,7},{6,4},{7,5},{8,10},{9,11},{10,... | collective-permute-start | bytes 2752520 | tf_op jit(solution)/shard_map/ppermute | solution.py:32
  22.3 53.9 %collective-permute-start.2 = (bf16[2048,224]{0,1:T(8,128)(2,1)}, bf16[2048,224]{0,1:T(8,128)(2,1)}, u32[]{:S(2)}, u32[]{:S(2)}) collective-permute-start(bf16[2048,224]{0,1:T(8,128)(2,1)} %get-tuple-element.10), channel_id=1, source_target_pairs={{0,3},{1,2},{2,1},{3,0},{4,7},{5,6},{6,5},{7,4},{8,11},{9,10},{10,... | collective-permute-start | bytes 2752520 | tf_op jit(solution)/shard_map/ppermute | solution.py:32
  23.9 59.3 %collective-permute-start.6 = (bf16[112,2048]{1,0:T(8,128)(2,1)}, bf16[112,2048]{1,0:T(8,128)(2,1)S(1)}, u32[]{:S(2)}, u32[]{:S(2)}) collective-permute-start(bf16[112,2048]{1,0:T(8,128)(2,1)} %get-tuple-element.13), channel_id=1, source_target_pairs={{0,1},{1,0},{2,3},{3,2},{4,5},{5,4},{6,7},{7,6},{8,9},{9,8},{10,11... | collective-permute-start | bytes 1376264 | tf_op jit(solution)/shard_map/ppermute | solution.py:32
  24.2 64.1 %collective-permute-start.7 = (bf16[112,2048]{1,0:T(8,128)(2,1)}, bf16[112,2048]{1,0:T(8,128)(2,1)}, u32[]{:S(2)}, u32[]{:S(2)}) collective-permute-start(bf16[112,2048]{1,0:T(8,128)(2,1)} %get-tuple-element.14), channel_id=1, source_target_pairs={{0,2},{1,3},{2,0},{3,1},{4,6},{5,7},{6,4},{7,5},{8,10},{9,11},{10,... | collective-permute-start | bytes 1376264 | tf_op jit(solution)/shard_map/ppermute | solution.py:32
  46.5 1.8 copy-start.9
  48.3 47.4 %collective-permute-start.8 = (bf16[112,2048]{1,0:T(8,128)(2,1)S(1)}, bf16[112,2048]{1,0:T(8,128)(2,1)S(1)}, u32[]{:S(2)}, u32[]{:S(2)}) collective-permute-start(bf16[112,2048]{1,0:T(8,128)(2,1)S(1)} %copy-done.9), channel_id=1, source_target_pairs={{0,3},{1,2},{2,1},{3,0},{4,7},{5,6},{6,5},{7,4},{8,11},{9,10},{10,... | collective-permute-start | bytes 1376264 | tf_op jit(solution)/shard_map/ppermute | solution.py:32
  58.6 19.2 %copy-start.3 = (bf16[2048,224]{0,1:T(8,128)(2,1)}, bf16[2048,224]{0,1:T(8,128)(2,1)S(1)}, u32[]{:S(2)}) copy-start(bf16[2048,224]{0,1:T(8,128)(2,1)S(1)} %collective-permute-done.1) | copy-start | bytes 2752516
  77.9 23.4 %collective-permute-start.5 = (f32[64,4,224]{2,0,1:T(8,128)S(1)}, f32[64,4,224]{2,0,1:T(8,128)S(1)}, u32[]{:S(2)}, u32[]{:S(2)}) collective-permute-start(f32[64,4,224]{2,0,1:T(8,128)S(1)} %get-tuple-element.16), channel_id=1, source_target_pairs={{0,3},{1,2},{2,1},{3,0},{4,7},{5,6},{6,5},{7,4},{8,11},{9,10},{10,... | collective-permute-start | bytes 688136 | tf_op jit(solution)/shard_map/ppermute | solution.py:32
  79.8 29.4 %collective-permute-start.4 = (f32[64,4,224]{2,0,1:T(8,128)S(1)}, f32[64,4,224]{2,0,1:T(8,128)S(1)}, u32[]{:S(2)}, u32[]{:S(2)}) collective-permute-start(f32[64,4,224]{2,0,1:T(8,128)S(1)} %get-tuple-element.17), channel_id=1, source_target_pairs={{0,2},{1,3},{2,0},{3,1},{4,6},{5,7},{6,4},{7,5},{8,10},{9,11},{10,... | collective-permute-start | bytes 688136 | tf_op jit(solution)/shard_map/ppermute | solution.py:32
  83.2 13.0 %copy-start.5 = (bf16[112,2048]{1,0:T(8,128)(2,1)}, bf16[112,2048]{1,0:T(8,128)(2,1)S(1)}, u32[]{:S(2)}) copy-start(bf16[112,2048]{1,0:T(8,128)(2,1)S(1)} %collective-permute-done.6) | copy-start | bytes 1376260
  83.2 26.0 %collective-permute-start.3 = (f32[64,4,224]{2,0,1:T(8,128)S(1)}, f32[64,4,224]{2,0,1:T(8,128)S(1)}, u32[]{:S(2)}, u32[]{:S(2)}) collective-permute-start(f32[64,4,224]{2,0,1:T(8,128)S(1)} %get-tuple-element.15), channel_id=1, source_target_pairs={{0,1},{1,0},{2,3},{3,2},{4,5},{5,4},{6,7},{7,6},{8,9},{9,8},{10,11... | collective-permute-start | bytes 688136 | tf_op jit(solution)/shard_map/ppermute | solution.py:32
  95.7 18.1 %copy-start.7 = (bf16[112,2048]{1,0:T(8,128)(2,1)}, bf16[112,2048]{1,0:T(8,128)(2,1)S(1)}, u32[]{:S(2)}) copy-start(bf16[112,2048]{1,0:T(8,128)(2,1)S(1)} %collective-permute-done.8) | copy-start | bytes 1376260
  96.2 13.5 %collective-permute-start.11 = (f32[64,4,112]{2,0,1:T(8,128)S(1)}, f32[64,4,112]{2,0,1:T(8,128)S(1)}, u32[]{:S(2)}, u32[]{:S(2)}) collective-permute-start(f32[64,4,112]{2,0,1:T(8,128)S(1)} %get-tuple-element.21), channel_id=1, source_target_pairs={{0,3},{1,2},{2,1},{3,0},{4,7},{5,6},{6,5},{7,4},{8,11},{9,10},{10,... | collective-permute-start | bytes 344072 | tf_op jit(solution)/shard_map/ppermute | solution.py:32
  98.4 15.3 %collective-permute-start.10 = (f32[64,4,112]{2,0,1:T(8,128)S(1)}, f32[64,4,112]{2,0,1:T(8,128)S(1)}, u32[]{:S(2)}, u32[]{:S(2)}) collective-permute-start(f32[64,4,112]{2,0,1:T(8,128)S(1)} %get-tuple-element.22), channel_id=1, source_target_pairs={{0,2},{1,3},{2,0},{3,1},{4,6},{5,7},{6,4},{7,5},{8,10},{9,11},{10,... | collective-permute-start | bytes 344072 | tf_op jit(solution)/shard_map/ppermute | solution.py:32
  101.4 12.4 %collective-permute-start.9 = (f32[64,4,112]{2,0,1:T(8,128)S(1)}, f32[64,4,112]{2,0,1:T(8,128)S(1)}, u32[]{:S(2)}, u32[]{:S(2)}) collective-permute-start(f32[64,4,112]{2,0,1:T(8,128)S(1)} %get-tuple-element.20), channel_id=1, source_target_pairs={{0,1},{1,0},{2,3},{3,2},{4,5},{5,4},{6,7},{7,6},{8,9},{9,8},{10,11... | collective-permute-start | bytes 344072 | tf_op jit(solution)/shard_map/ppermute | solution.py:32
  114.9 2.1 %collective-permute-start.12 = (bf16[64,1344]{1,0:T(8,128)(2,1)S(1)}, bf16[64,1344]{1,0:T(8,128)(2,1)S(1)}, u32[]{:S(2)}, u32[]{:S(2)}) collective-permute-start(bf16[64,1344]{1,0:T(8,128)(2,1)S(1)} %pad_maximum_fusion.1), channel_id=1, source_target_pairs={{0,1},{1,0},{2,3},{3,2},{4,5},{5,4},{6,7},{7,6},{8,9},{9,8},{10,11... | collective-permute-start | bytes 516104 | tf_op jit(solution)/shard_map/ppermute | solution.py:32
  115.0 7.5 %collective-permute-start.13 = (bf16[64,1344]{1,0:T(8,128)(2,1)S(1)}, bf16[64,1344]{1,0:T(8,128)(2,1)S(1)}, u32[]{:S(2)}, u32[]{:S(2)}) collective-permute-start(bf16[64,1344]{1,0:T(8,128)(2,1)S(1)} %pad_maximum_fusion.1), channel_id=1, source_target_pairs={{0,2},{1,3},{2,0},{3,1},{4,6},{5,7},{6,4},{7,5},{8,10},{9,11},{10,... | collective-permute-start | bytes 516104 | tf_op jit(solution)/shard_map/ppermute | solution.py:32
  115.2 10.1 %collective-permute-start.14 = (bf16[64,1344]{1,0:T(8,128)(2,1)S(1)}, bf16[64,1344]{1,0:T(8,128)(2,1)S(1)}, u32[]{:S(2)}, u32[]{:S(2)}) collective-permute-start(bf16[64,1344]{1,0:T(8,128)(2,1)S(1)} %pad_maximum_fusion.1), channel_id=1, source_target_pairs={{0,3},{1,2},{2,1},{3,0},{4,7},{5,6},{6,5},{7,4},{8,11},{9,10},{10,... | collective-permute-start | bytes 516104 | tf_op jit(solution)/shard_map/ppermute | solution.py:32
  127.3 3.3 %copy-start.2 = (bf16[256,896]{0,1:T(8,128)(2,1)S(1)}, bf16[256,896]{0,1:T(8,128)(2,1)}, u32[]{:S(2)}) copy-start(bf16[256,896]{0,1:T(8,128)(2,1)} %copy.85) | copy-start | bytes 1376260
  139.7 44.3 %all-to-all-start.1 = ((bf16[32,8,2,2048]{3,1,2,0:T(8,128)(2,1)}), bf16[32,8,2,2048]{3,1,2,0:T(8,128)(2,1)}, u32[]{:S(2)}, u32[]{:S(2)}) async-start(bf16[32,8,2,2048]{3,1,2,0:T(8,128)(2,1)} %pad_maximum_fusion), calls=%async_computation.1 | async-start | bytes 4194304 | tf_op jit(solution)/shard_map/all_to_all | solution.py:27
  (3 other events, 3.9 us)

commit v14 on v12

--- a/solution.py
+++ b/solution.py
@@ -109,13 +109,18 @@
     joined_grad = jnp.concatenate(
         [gate_grad.reshape(share, n_col, unit), up_grad.reshape(share, n_col, unit)], axis=2
     )
-    grads = col_gather(joined_grad, n_col).reshape(count, n_col, 2 * unit)
+    arrived = [joined_grad] + [swap(joined_grad, k, n_col) for k in range(1, n_col)]
+    grads = place(arrived, me, 0).reshape(count, n_col, 2 * unit)
 
-    gu_cat = jnp.concatenate(gu_rel, axis=1)
-    g_rel = jnp.concatenate(
-        [lax.dynamic_index_in_dim(grads, me ^ k, 1, keepdims=False) for k in range(n_col)], axis=1
-    )
-    in_part = contract_last(g_rel, gu_cat)
+    blocks = []
+    for g_blk in arrived:
+        acc = None
+        for k, w in enumerate(gu_rel):
+            g = lax.dynamic_index_in_dim(g_blk, me ^ k, 1, keepdims=False)
+            t = contract_last(g, w)
+            acc = t if acc is None else acc + t
+        blocks.append(acc)
+    in_part = place(blocks, me, 0).reshape(count, -1)
     summed = reduce_rows(jnp.stack([term, in_part], axis=1), "row", n_row)
     output = summed[:, 0]
     input_grad = summed[:, 1]

time: 187 us -> 198 us (1.059)
  matrix products: 20.5 us -> 26.8 us
  local copies, waits for them, and re-layouts: 21.4 us -> 25.8 us
  waiting for transfers between devices: 99.6 us -> 95.3 us
  starting transfers between devices: 38.4 us -> 40.7 us
    dot_general x5 -> x20, matrix products: 7.14 us -> 17.8 us  [contract_last(): lax.dot_general(left, right, (((1,), (1,)), ((), ())), preferred_element_...]
    dot_general x4, matrix products: 5.38 us -> 1.85 us  [shards(): jnp.dot(full_tokens, w, preferred_element_type=jnp.float32)]
    all_to_all x1, waiting for transfers between devices: 27 us -> 23.7 us  [reduce_rows(): got = lax.all_to_all(pieces, axis, split_axis=0, concat_axis=0, tiled=True)]
  transfers between devices with their start and end apart: 20 -> 20, of which waited for: 13 -> 12; matrix products, arithmetic and copies ran while one was open for 19% -> 22% of each run, Pallas kernels for 0% -> 0%
where the time goes in v14:
time: 198 us; the launch traced here: 197 us
  waiting for transfers between devices  95.3 us (48%)
  starting transfers between devices  40.7 us (21%)
  matrix products  26.8 us (14%)
  local copies, waits for them, and re-layouts  25.8 us (13%)
  other arithmetic  6.98 us (4%)
    ppermute x18, waiting for transfers between devices, swap(): return lax.ppermute(x, 'col', perm=[(i, i ^ k) for i in range(n)])  52.4 us
    all_to_all x1, waiting for transfers between devices, reduce_rows(): got = lax.all_to_all(pieces, axis, split_axis=0, concat_axis=0, tiled=True)  23.7 us
    all_to_all x1, waiting for transfers between devices, gather_rows(): got = lax.all_to_all(spread, axis, split_axis=0, concat_axis=0, tiled=True)  19.2 us
    dot_general x20, matrix products, contract_last(): lax.dot_general(left, right, (((1,), (1,)), ((), ())), preferred_element_...  17.8 us
    ppermute x18, starting transfers between devices, swap(): return lax.ppermute(x, 'col', perm=[(i, i ^ k) for i in range(n)])  17.5 us
    all_to_all x1, starting transfers between devices, reduce_rows(): got = lax.all_to_all(pieces, axis, split_axis=0, concat_axis=0, tiled=True)  13.1 us
    all_to_all x1, starting transfers between devices, gather_rows(): got = lax.all_to_all(spread, axis, split_axis=0, concat_axis=0, tiled=True)  10.2 us
    dynamic_slice x4, local copies, waits for them, and re-layouts, piece(): return lax.dynamic_slice_in_dim(x, index * size, size, axis)  4.74 us
  transfers between devices with their start and end apart: 20, of which 12 were waited for; matrix products, arithmetic and copies ran while one was open for 22% of the time, Pallas kernels for 0%

profile of v14, /device:TPU:8, one launch (start us, length us, event | category | flops | bytes accessed | tf_op | source)
XLA Modules:
  0.0 196.8 jit_solution(10462029596166283529)
XLA Ops:
  3.0 10.2 %all-to-all-start = ((bf16[32,8,2,2048]{3,1,2,0:T(8,128)(2,1)}), bf16[32,8,2,2048]{3,1,2,0:T(8,128)(2,1)}, u32[]{:S(2)}, u32[]{:S(2)}) async-start(bf16[32,8,2,2048]{3,1,2,0:T(8,128)(2,1)} %broadcast_in_dim.81), calls=%async_computation | async-start | bytes 4194304 | tf_op jit(solution)/shard_map/all_to_all | solution.py:21
  14.6 2.9 %constant_dynamic-update-slice_fusion = bf16[8192,224]{0,1:T(8,128)(2,1)} fusion(bf16[8192,224]{0,1:T(8,128)(2,1)} %constant_dynamic-update-slice_fusion.1, bf16[8192,112]{0,1:T(8,128)(2,1)} %param.7), kind=kLoop, calls=%fused_computation.174 | loop fusion | bytes 3670016 | tf_op jit(solution)/shard_map/concatenate | solution.py:79
  17.5 3.5 %constant_dynamic-slice_fusion.10 = (bf16[2048,224]{0,1:T(8,128)(2,1)}, bf16[2048,224]{0,1:T(8,128)(2,1)}, bf16[2048,224]{0,1:T(8,128)(2,1)}) fusion(bf16[8192,224]{0,1:T(8,128)(2,1)} %constant_dynamic-update-slice_fusion, s32[]{:T(128)S(6)} %select_n.93, s32[]{:T(128)S(6)} %select_n.95, s32[]{:T(128)S(6)} %select_n.91), kind=kLoop, calls=%fused_computation.170 | loop fusion | bytes 5505036 | tf_op jit(solution)/shard_map/dynamic_slice | solution.py:36
  25.6 19.2 %all-to-all-done = bf16[32,8,2,2048]{3,1,2,0:T(8,128)(2,1)} async-done(((bf16[32,8,2,2048]{3,1,2,0:T(8,128)(2,1)}), bf16[32,8,2,2048]{3,1,2,0:T(8,128)(2,1)}, u32[]{:S(2)}, u32[]{:S(2)}) %all-to-all-start) | async-done | bytes 2097184 | tf_op jit(solution)/shard_map/all_to_all | solution.py:21
  44.8 1.9 copy.64
  48.7 9.9 %collective-permute-done.1 = bf16[2048,224]{0,1:T(8,128)(2,1)S(1)} collective-permute-done((bf16[2048,224]{0,1:T(8,128)(2,1)}, bf16[2048,224]{0,1:T(8,128)(2,1)S(1)}, u32[]{:S(2)}, u32[]{:S(2)}) %collective-permute-start.1) | collective-permute-done | bytes 917536 | tf_op jit(solution)/shard_map/ppermute | solution.py:32
  59.1 17.0 %collective-permute-done.2 = bf16[2048,224]{0,1:T(8,128)(2,1)S(1)} collective-permute-done((bf16[2048,224]{0,1:T(8,128)(2,1)}, bf16[2048,224]{0,1:T(8,128)(2,1)S(1)}, u32[]{:S(2)}, u32[]{:S(2)}) %collective-permute-start.2) | collective-permute-done | bytes 917536 | tf_op jit(solution)/shard_map/ppermute | solution.py:32
  76.6 1.8 collective-permute-start.5
  78.5 1.9 collective-permute-start.4
  83.5 4.7 %collective-permute-done.10 = bf16[112,2048]{1,0:T(8,128)(2,1)S(1)} collective-permute-done((bf16[112,2048]{1,0:T(8,128)(2,1)}, bf16[112,2048]{1,0:T(8,128)(2,1)S(1)}, u32[]{:S(2)}, u32[]{:S(2)}) %collective-permute-start.10) | collective-permute-done | bytes 458784 | tf_op jit(solution)/shard_map/ppermute | solution.py:32
  88.6 7.2 %collective-permute-done.11 = bf16[112,2048]{1,0:T(8,128)(2,1)S(1)} collective-permute-done((bf16[112,2048]{1,0:T(8,128)(2,1)S(1)}, bf16[112,2048]{1,0:T(8,128)(2,1)S(1)}, u32[]{:S(2)}, u32[]{:S(2)}) %collective-permute-start.11) | collective-permute-done | bytes 458784 | tf_op jit(solution)/shard_map/ppermute | solution.py:32
  96.3 2.1 %collective-permute-start.14 = (f32[64,4,112]{2,0,1:T(8,128)S(1)}, f32[64,4,112]{2,0,1:T(8,128)S(1)}, u32[]{:S(2)}, u32[]{:S(2)}) collective-permute-start(f32[64,4,112]{2,0,1:T(8,128)S(1)} %get-tuple-element.19), channel_id=1, source_target_pairs={{0,3},{1,2},{2,1},{3,0},{4,7},{5,6},{6,5},{7,4},{8,11},{9,10},{10,... | collective-permute-start | bytes 344072 | tf_op jit(solution)/shard_map/ppermute | solution.py:32
  98.4 1.9 collective-permute-start.13
  101.4 2.1 %collective-permute-start.12 = (f32[64,4,112]{2,0,1:T(8,128)S(1)}, f32[64,4,112]{2,0,1:T(8,128)S(1)}, u32[]{:S(2)}, u32[]{:S(2)}) collective-permute-start(f32[64,4,112]{2,0,1:T(8,128)S(1)} %get-tuple-element.18), channel_id=1, source_target_pairs={{0,1},{1,0},{2,3},{3,2},{4,5},{5,4},{6,7},{7,6},{8,9},{9,8},{10,11... | collective-permute-start | bytes 344072 | tf_op jit(solution)/shard_map/ppermute | solution.py:32
  103.4 5.8 %collective-permute-done.4 = f32[64,4,224]{2,0,1:T(8,128)S(1)} collective-permute-done((f32[64,4,224]{2,0,1:T(8,128)S(1)}, f32[64,4,224]{2,0,1:T(8,128)S(1)}, u32[]{:S(2)}, u32[]{:S(2)}) %collective-permute-start.4) | collective-permute-done | bytes 229408 | tf_op jit(solution)/shard_map/ppermute | solution.py:32
  109.8 3.9 %collective-permute-done.13 = f32[64,4,112]{2,0,1:T(8,128)S(1)} collective-permute-done((f32[64,4,112]{2,0,1:T(8,128)S(1)}, f32[64,4,112]{2,0,1:T(8,128)S(1)}, u32[]{:S(2)}, u32[]{:S(2)}) %collective-permute-start.13) | collective-permute-done | bytes 114720 | tf_op jit(solution)/shard_map/ppermute | solution.py:32
  115.8 1.7 collective-permute-start.17
  124.9 1.7 collective-permute-start.8
  127.4 1.7 collective-permute-done.8
  148.1 13.1 %all-to-all-start.1 = ((bf16[32,8,2,2048]{3,1,2,0:T(8,128)(2,1)}), bf16[32,8,2,2048]{3,1,2,0:T(8,128)(2,1)}, u32[]{:S(2)}, u32[]{:S(2)}) async-start(bf16[32,8,2,2048]{3,1,2,0:T(8,128)(2,1)} %pad_maximum_fusion), calls=%async_computation.1 | async-start | bytes 4194304 | tf_op jit(solution)/shard_map/all_to_all | solution.py:27
  161.5 1.9 convolution_convert_fusion.1
  168.2 2.3 %fusion.124 = (bf16[2048,4,112]{0,2,1:T(8,128)(2,1)}, bf16[2048,4,112]{0,2,1:T(8,128)(2,1)}) fusion(bf16[2048,4,224]{0,2,1:T(8,128)(2,1)S(1)} %convolution_convert_fusion), kind=kLoop, calls=%fused_computation.181 | loop fusion | bytes 7340032 | tf_op jit(solution)/shard_map/slice | solution.py:130
  170.5 23.7 %all-to-all-done.1 = bf16[32,8,2,2048]{3,1,2,0:T(8,128)(2,1)} async-done(((bf16[32,8,2,2048]{3,1,2,0:T(8,128)(2,1)}), bf16[32,8,2,2048]{3,1,2,0:T(8,128)(2,1)}, u32[]{:S(2)}, u32[]{:S(2)}) %all-to-all-start.1) | async-done | bytes 2097184 | tf_op jit(solution)/shard_map/all_to_all | solution.py:27
  194.2 1.9 convert_reduce_fusion
  (113 shorter events, 51.7 us)
Async XLA Ops:
  3.0 41.8 %all-to-all-start = ((bf16[32,8,2,2048]{3,1,2,0:T(8,128)(2,1)}), bf16[32,8,2,2048]{3,1,2,0:T(8,128)(2,1)}, u32[]{:S(2)}, u32[]{:S(2)}) async-start(bf16[32,8,2,2048]{3,1,2,0:T(8,128)(2,1)} %broadcast_in_dim.81), calls=%async_computation | async-start | bytes 4194304 | tf_op jit(solution)/shard_map/all_to_all | solution.py:21
  21.0 27.0 %collective-permute-start = (bf16[2048,224]{0,1:T(8,128)(2,1)}, bf16[2048,224]{0,1:T(8,128)(2,1)S(1)}, u32[]{:S(2)}, u32[]{:S(2)}) collective-permute-start(bf16[2048,224]{0,1:T(8,128)(2,1)} %get-tuple-element.11), channel_id=1, source_target_pairs={{0,1},{1,0},{2,3},{3,2},{4,5},{5,4},{6,7},{7,6},{8,9},{9,8},{10,11... | collective-permute-start | bytes 2752520 | tf_op jit(solution)/shard_map/ppermute | solution.py:32
  21.0 37.7 %collective-permute-start.1 = (bf16[2048,224]{0,1:T(8,128)(2,1)}, bf16[2048,224]{0,1:T(8,128)(2,1)S(1)}, u32[]{:S(2)}, u32[]{:S(2)}) collective-permute-start(bf16[2048,224]{0,1:T(8,128)(2,1)} %get-tuple-element.9), channel_id=1, source_target_pairs={{0,2},{1,3},{2,0},{3,1},{4,6},{5,7},{6,4},{7,5},{8,10},{9,11},{10,... | collective-permute-start | bytes 2752520 | tf_op jit(solution)/shard_map/ppermute | solution.py:32
  22.3 53.8 %collective-permute-start.2 = (bf16[2048,224]{0,1:T(8,128)(2,1)}, bf16[2048,224]{0,1:T(8,128)(2,1)S(1)}, u32[]{:S(2)}, u32[]{:S(2)}) collective-permute-start(bf16[2048,224]{0,1:T(8,128)(2,1)} %get-tuple-element.10), channel_id=1, source_target_pairs={{0,3},{1,2},{2,1},{3,0},{4,7},{5,6},{6,5},{7,4},{8,11},{9,10},{10,... | collective-permute-start | bytes 2752520 | tf_op jit(solution)/shard_map/ppermute | solution.py:32
  24.0 58.0 %collective-permute-start.9 = (bf16[112,2048]{1,0:T(8,128)(2,1)}, bf16[112,2048]{1,0:T(8,128)(2,1)}, u32[]{:S(2)}, u32[]{:S(2)}) collective-permute-start(bf16[112,2048]{1,0:T(8,128)(2,1)} %get-tuple-element.13), channel_id=1, source_target_pairs={{0,1},{1,0},{2,3},{3,2},{4,5},{5,4},{6,7},{7,6},{8,9},{9,8},{10,11... | collective-permute-start | bytes 1376264 | tf_op jit(solution)/shard_map/ppermute | solution.py:32
  24.2 63.9 %collective-permute-start.10 = (bf16[112,2048]{1,0:T(8,128)(2,1)}, bf16[112,2048]{1,0:T(8,128)(2,1)S(1)}, u32[]{:S(2)}, u32[]{:S(2)}) collective-permute-start(bf16[112,2048]{1,0:T(8,128)(2,1)} %get-tuple-element.14), channel_id=1, source_target_pairs={{0,2},{1,3},{2,0},{3,1},{4,6},{5,7},{6,4},{7,5},{8,10},{9,11},{10,... | collective-permute-start | bytes 1376264 | tf_op jit(solution)/shard_map/ppermute | solution.py:32
  46.7 49.0 %copy-start.2 = (bf16[32,8,2,2048]{3,1,0,2:T(8,128)(2,1)}, bf16[32,8,2,2048]{3,1,0,2:T(8,128)(2,1)S(1)}, u32[]{:S(2)}) copy-start(bf16[32,8,2,2048]{3,1,0,2:T(8,128)(2,1)S(1)} %copy.64) | copy-start | bytes 6291460
  48.3 47.5 %collective-permute-start.11 = (bf16[112,2048]{1,0:T(8,128)(2,1)S(1)}, bf16[112,2048]{1,0:T(8,128)(2,1)S(1)}, u32[]{:S(2)}, u32[]{:S(2)}) collective-permute-start(bf16[112,2048]{1,0:T(8,128)(2,1)S(1)} %copy-done.13), channel_id=1, source_target_pairs={{0,3},{1,2},{2,1},{3,0},{4,7},{5,6},{6,5},{7,4},{8,11},{9,10},{10,... | collective-permute-start | bytes 1376264 | tf_op jit(solution)/shard_map/ppermute | solution.py:32
  76.6 24.7 %collective-permute-start.5 = (f32[64,4,224]{2,0,1:T(8,128)S(1)}, f32[64,4,224]{2,0,1:T(8,128)S(1)}, u32[]{:S(2)}, u32[]{:S(2)}) collective-permute-start(f32[64,4,224]{2,0,1:T(8,128)S(1)} %get-tuple-element.16), channel_id=1, source_target_pairs={{0,3},{1,2},{2,1},{3,0},{4,7},{5,6},{6,5},{7,4},{8,11},{9,10},{10,... | collective-permute-start | bytes 688136 | tf_op jit(solution)/shard_map/ppermute | solution.py:32
  78.5 30.7 %collective-permute-start.4 = (f32[64,4,224]{2,0,1:T(8,128)S(1)}, f32[64,4,224]{2,0,1:T(8,128)S(1)}, u32[]{:S(2)}, u32[]{:S(2)}) collective-permute-start(f32[64,4,224]{2,0,1:T(8,128)S(1)} %get-tuple-element.17), channel_id=1, source_target_pairs={{0,2},{1,3},{2,0},{3,1},{4,6},{5,7},{6,4},{7,5},{8,10},{9,11},{10,... | collective-permute-start | bytes 688136 | tf_op jit(solution)/shard_map/ppermute | solution.py:32
  81.9 27.3 %collective-permute-start.3 = (f32[64,4,224]{2,0,1:T(8,128)S(1)}, f32[64,4,224]{2,0,1:T(8,128)S(1)}, u32[]{:S(2)}, u32[]{:S(2)}) collective-permute-start(f32[64,4,224]{2,0,1:T(8,128)S(1)} %get-tuple-element.15), channel_id=1, source_target_pairs={{0,1},{1,0},{2,3},{3,2},{4,5},{5,4},{6,7},{7,6},{8,9},{9,8},{10,11... | collective-permute-start | bytes 688136 | tf_op jit(solution)/shard_map/ppermute | solution.py:32
  95.7 18.7 %copy-start.11 = (bf16[112,2048]{1,0:T(8,128)(2,1)}, bf16[112,2048]{1,0:T(8,128)(2,1)S(1)}, u32[]{:S(2)}) copy-start(bf16[112,2048]{1,0:T(8,128)(2,1)S(1)} %collective-permute-done.11) | copy-start | bytes 1376260
  96.3 13.5 %collective-permute-start.14 = (f32[64,4,112]{2,0,1:T(8,128)S(1)}, f32[64,4,112]{2,0,1:T(8,128)S(1)}, u32[]{:S(2)}, u32[]{:S(2)}) collective-permute-start(f32[64,4,112]{2,0,1:T(8,128)S(1)} %get-tuple-element.19), channel_id=1, source_target_pairs={{0,3},{1,2},{2,1},{3,0},{4,7},{5,6},{6,5},{7,4},{8,11},{9,10},{10,... | collective-permute-start | bytes 344072 | tf_op jit(solution)/shard_map/ppermute | solution.py:32
  98.4 15.3 %collective-permute-start.13 = (f32[64,4,112]{2,0,1:T(8,128)S(1)}, f32[64,4,112]{2,0,1:T(8,128)S(1)}, u32[]{:S(2)}, u32[]{:S(2)}) collective-permute-start(f32[64,4,112]{2,0,1:T(8,128)S(1)} %get-tuple-element.20), channel_id=1, source_target_pairs={{0,2},{1,3},{2,0},{3,1},{4,6},{5,7},{6,4},{7,5},{8,10},{9,11},{10,... | collective-permute-start | bytes 344072 | tf_op jit(solution)/shard_map/ppermute | solution.py:32
  101.4 12.4 %collective-permute-start.12 = (f32[64,4,112]{2,0,1:T(8,128)S(1)}, f32[64,4,112]{2,0,1:T(8,128)S(1)}, u32[]{:S(2)}, u32[]{:S(2)}) collective-permute-start(f32[64,4,112]{2,0,1:T(8,128)S(1)} %get-tuple-element.18), channel_id=1, source_target_pairs={{0,1},{1,0},{2,3},{3,2},{4,5},{5,4},{6,7},{7,6},{8,9},{9,8},{10,11... | collective-permute-start | bytes 344072 | tf_op jit(solution)/shard_map/ppermute | solution.py:32
  115.7 18.1 %collective-permute-start.15 = (bf16[64,4,224]{2,0,1:T(8,128)(2,1)}, bf16[64,4,224]{2,0,1:T(8,128)(2,1)}, u32[]{:S(2)}, u32[]{:S(2)}) collective-permute-start(bf16[64,4,224]{2,0,1:T(8,128)(2,1)} %get-tuple-element.24), channel_id=1, source_target_pairs={{0,1},{1,0},{2,3},{3,2},{4,5},{5,4},{6,7},{7,6},{8,9},{9,8},{10,11... | collective-permute-start | bytes 344072 | tf_op jit(solution)/shard_map/ppermute | solution.py:32
  115.7 21.3 %collective-permute-start.16 = (bf16[64,4,224]{2,0,1:T(8,128)(2,1)}, bf16[64,4,224]{2,0,1:T(8,128)(2,1)}, u32[]{:S(2)}, u32[]{:S(2)}) collective-permute-start(bf16[64,4,224]{2,0,1:T(8,128)(2,1)} %get-tuple-element.24), channel_id=1, source_target_pairs={{0,2},{1,3},{2,0},{3,1},{4,6},{5,7},{6,4},{7,5},{8,10},{9,11},{10,... | collective-permute-start | bytes 344072 | tf_op jit(solution)/shard_map/ppermute | solution.py:32
  115.8 24.3 %collective-permute-start.17 = (bf16[64,4,224]{2,0,1:T(8,128)(2,1)}, bf16[64,4,224]{2,0,1:T(8,128)(2,1)}, u32[]{:S(2)}, u32[]{:S(2)}) collective-permute-start(bf16[64,4,224]{2,0,1:T(8,128)(2,1)} %get-tuple-element.24), channel_id=1, source_target_pairs={{0,3},{1,2},{2,1},{3,0},{4,7},{5,6},{6,5},{7,4},{8,11},{9,10},{10,... | collective-permute-start | bytes 344072 | tf_op jit(solution)/shard_map/ppermute | solution.py:32
  122.7 2.2 %collective-permute-start.6 = (bf16[64,448]{1,0:T(8,128)(2,1)S(1)}, bf16[64,448]{1,0:T(8,128)(2,1)S(1)}, u32[]{:S(2)}, u32[]{:S(2)}) collective-permute-start(bf16[64,448]{1,0:T(8,128)(2,1)S(1)} %multiply_convert_fusion.2), channel_id=1, source_target_pairs={{0,1},{1,0},{2,3},{3,2},{4,5},{5,4},{6,7},{7,6},{8,9},{9,8},{10,11... | collective-permute-start | bytes 172040 | tf_op jit(solution)/shard_map/ppermute | solution.py:32
  123.1 4.3 %collective-permute-start.7 = (bf16[64,448]{1,0:T(8,128)(2,1)S(1)}, bf16[64,448]{1,0:T(8,128)(2,1)S(1)}, u32[]{:S(2)}, u32[]{:S(2)}) collective-permute-start(bf16[64,448]{1,0:T(8,128)(2,1)S(1)} %multiply_convert_fusion.2), channel_id=1, source_target_pairs={{0,2},{1,3},{2,0},{3,1},{4,6},{5,7},{6,4},{7,5},{8,10},{9,11},{10,... | collective-permute-start | bytes 172040 | tf_op jit(solution)/shard_map/ppermute | solution.py:32
  124.9 4.2 %collective-permute-start.8 = (bf16[64,448]{1,0:T(8,128)(2,1)S(1)}, bf16[64,448]{1,0:T(8,128)(2,1)S(1)}, u32[]{:S(2)}, u32[]{:S(2)}) collective-permute-start(bf16[64,448]{1,0:T(8,128)(2,1)S(1)} %multiply_convert_fusion.2), channel_id=1, source_target_pairs={{0,3},{1,2},{2,1},{3,0},{4,7},{5,6},{6,5},{7,4},{8,11},{9,10},{10,... | collective-permute-start | bytes 172040 | tf_op jit(solution)/shard_map/ppermute | solution.py:32
  148.1 13.2 %copy-start.6 = (bf16[1,64,4,224]{3,1,2,0:T(8,128)(2,1)S(1)}, bf16[1,64,4,224]{3,1,2,0:T(8,128)(2,1)}, u32[]{:S(2)}) copy-start(bf16[1,64,4,224]{3,1,2,0:T(8,128)(2,1)} %get-tuple-element.23) | copy-start | bytes 344068
  148.1 13.4 %copy-start.3 = (bf16[32,8,2,2048]{3,1,0,2:T(8,128)(2,1)S(1)}, bf16[32,8,2,2048]{3,1,0,2:T(8,128)(2,1)}, u32[]{:S(2)}) copy-start(bf16[32,8,2,2048]{3,1,0,2:T(8,128)(2,1)} %copy-done.2) | copy-start | bytes 6291460
  148.1 46.1 %all-to-all-start.1 = ((bf16[32,8,2,2048]{3,1,2,0:T(8,128)(2,1)}), bf16[32,8,2,2048]{3,1,2,0:T(8,128)(2,1)}, u32[]{:S(2)}, u32[]{:S(2)}) async-start(bf16[32,8,2,2048]{3,1,2,0:T(8,128)(2,1)} %pad_maximum_fusion), calls=%async_computation.1 | async-start | bytes 4194304 | tf_op jit(solution)/shard_map/all_to_all | solution.py:27
  (10 other events, 35.6 us)
